TPU v7x, 512 devices: a whole 4x8x8 slice. The times are simulated.
512 devices in a mesh: wide: 64 (over z, x, core), narrow: 8 (over y).
Axes of the slice: x: 4, y: 8, z: 8, core: 2. Of those that a mesh axis runs over, the one named last changes fastest.
Arguments:
- hidden_in: bfloat16 [16384, 2048], P('wide', 'narrow'), may hold values from -6 to 6
- segment_ids: int32 [16384], P('wide'), may hold values from 0 to 31, never falling along the last dimension, each value on 1 to 2048 neighbouring positions
- page_table: int32 [1024], P('wide'), may hold values from 0 to 1023, as said below
- wq: bfloat16 [2048, 2048], P('wide', 'narrow')
- wk: bfloat16 [2048, 2048], P('wide', 'narrow')
- wv: bfloat16 [2048, 2048], P('wide', 'narrow'), may hold values from -0.125 to 0.125
- wo: bfloat16 [2048, 2048], P('narrow', 'wide'), may hold values from -0.125 to 0.125
- wg: bfloat16 [2048, 4096], P('wide', 'narrow'), may hold values from -0.125 to 0.125
- wu: bfloat16 [2048, 4096], P('wide', 'narrow'), may hold values from -0.125 to 0.125
- wd: bfloat16 [4096, 2048], P('narrow', 'wide'), may hold values from -0.09375 to 0.09375
Outputs:
- result: bfloat16 [16384, 2048], P('wide', 'narrow')
- kv_cache: bfloat16 [2, 1024, 16, 2048], P(None, 'wide', None, 'narrow')
Inputs may be any that keep to these rules, and one draw needn't show every extreme that they name: `page_table`: entries 16 * w to 16 * (w + 1) - 1 of the table are a permutation of those same numbers, for every w.
All inputs are finite; a program needn't handle non-finite values.
Results may differ from a plain program's by a relative error of at most 0.017.
Values may be sent and summed in bfloat16 or wider, within the bound.
No kernel may reach another device: no remote copies, remote signals or barrier semaphores. Data moves between devices by JAX's collectives and lax.ppermute only.
A program may use at most 64 MiB of HBM per device.

v0:
```python
import jax
import jax.numpy as jnp
from jax import lax
from jax.sharding import PartitionSpec as P

HEAD_DIM = 128
REACH = 8
PAGE = 16


epsilon = 1e-05
rope_base = 10000.0


def prefix(value, axis, join, neutral):
    count, mine = (lax.axis_size(axis), lax.axis_index(axis))
    pieces = jax.tree.map(lambda part: lax.all_gather(part, axis), value)
    running = jax.tree.map(
        lambda part, zero: jnp.full_like(part, 0) + jnp.asarray(zero, part.dtype), value, neutral
    )

    def lap(position, running):
        longer = join(running, jax.tree.map(lambda part: part[position], pieces))
        return jax.tree.map(lambda new, old: jnp.where(position < mine, new, old), longer, running)

    return lax.fori_loop(0, count - 1, lap, running)


def shifted(value, axis, steps):
    count = lax.axis_size(axis)
    first, last = (max(0, -steps), min(count, count - steps))
    return lax.ppermute(value, axis, [(source, source + steps) for source in range(first, last)])


def norm_rows(source):
    widened = source.astype(jnp.float32)
    center = widened - jnp.mean(widened, axis=-1, keepdims=True)
    spread = jnp.mean(center * center, axis=-1, keepdims=True)
    return (center * lax.rsqrt(spread + epsilon)).astype(jnp.bfloat16)


def rotate(projected, positions):
    head_size = projected.shape[-1]
    half_dim = head_size // 2
    frequency = jnp.power(rope_base, -jnp.arange(half_dim, dtype=jnp.float32) * 2.0 / head_size)
    angles = positions.astype(jnp.float32)[:, None] * frequency[None, :]
    cosine = jnp.cos(angles)[:, None, :]
    sine_part = jnp.sin(angles)[:, None, :]
    first_half = projected[..., :half_dim]
    second_half = projected[..., half_dim:]
    return jnp.concatenate(
        [
            first_half * cosine - second_half * sine_part,
            second_half * cosine + first_half * sine_part,
        ],
        axis=-1,
    )


def join_runs(earlier, later):
    early_last, early_trailing, early_single = earlier
    late_last, late_trailing, late_single = later
    late_empty = late_trailing == 0
    same_id = (early_last == late_last).astype(jnp.int32)
    linked = (late_single == 1) & (same_id == 1) & (early_trailing > 0)
    last_id = jnp.where(late_empty, early_last, late_last)
    trailing = jnp.where(
        late_empty, early_trailing, late_trailing + jnp.where(linked, early_trailing, 0)
    )
    single = jnp.where(
        late_empty,
        early_single,
        jnp.where(early_trailing == 0, late_single, late_single * early_single * same_id),
    )
    return (last_id, trailing, single)


def add_rows(source, piece):
    return jnp.dot(source, piece, preferred_element_type=jnp.float32)


def per_device(hidden_in, segment_ids, page_table, wq, wk, wv, wo, wg, wu, wd):
    tok_rows = hidden_in.shape[0]
    wide_rank = lax.axis_index("wide")
    local_index = jnp.arange(tok_rows, dtype=jnp.int32)
    run_last = segment_ids[tok_rows - 1]
    run_trailing = jnp.sum((segment_ids == run_last).astype(jnp.int32))
    run_single = (segment_ids[0] == run_last).astype(jnp.int32)
    earlier = prefix(
        (run_last, run_trailing, run_single),
        "wide",
        join_runs,
        (jnp.int32(-1), jnp.int32(0), jnp.int32(1)),
    )
    lower_count = jnp.sum((segment_ids[None, :] < segment_ids[:, None]).astype(jnp.int32), axis=1)
    carried = jnp.where(
        (segment_ids == earlier[0]) & (segment_ids == segment_ids[0]), earlier[1], 0
    )
    positions = local_index - lower_count + carried
    global_index = wide_rank * tok_rows + local_index
    query_start = global_index - positions
    whole = lax.all_gather(hidden_in, "narrow", axis=1, tiled=True)
    normed = norm_rows(whole)
    local_width = wq.shape[1]
    head_count = local_width // HEAD_DIM

    def add_normed(piece):
        return add_rows(normed, piece)

    q_proj = add_normed(lax.all_gather(wq, "wide", axis=0, tiled=True))
    k_proj = add_normed(lax.all_gather(wk, "wide", axis=0, tiled=True))
    v_proj = add_normed(lax.all_gather(wv, "wide", axis=0, tiled=True))
    queries = rotate(q_proj.reshape(tok_rows, head_count, HEAD_DIM), positions).astype(jnp.bfloat16)
    keys_rot = rotate(k_proj.reshape(tok_rows, head_count, HEAD_DIM), positions).astype(
        jnp.bfloat16
    )
    values = v_proj.astype(jnp.bfloat16).reshape(tok_rows, head_count, HEAD_DIM)
    current = (keys_rot, values)
    blocks = [current]
    for step_back in range(REACH):
        current = shifted((current[0], current[1]), "wide", 1)
        blocks.append(current)
    score_scale = HEAD_DIM ** (-0.5)
    ordered = blocks[::-1]
    key_all = jnp.concatenate([member[0] for member in ordered], axis=0)
    value_all = jnp.concatenate([member[1] for member in ordered], axis=0)
    key_index = (wide_rank - REACH) * tok_rows + jnp.arange((REACH + 1) * tok_rows, dtype=jnp.int32)
    allowed = (key_index[None, :] >= query_start[:, None]) & (
        key_index[None, :] <= global_index[:, None]
    )
    scores = (
        jnp.einsum("qhd,khd->hqk", queries, key_all, preferred_element_type=jnp.float32)
        * score_scale
    )
    scores = jnp.where(allowed[None], scores, -1e30)
    row_peak = jnp.max(scores, axis=-1, keepdims=True)
    exps = jnp.where(allowed[None], jnp.exp(scores - row_peak), 0.0)
    attn_probs = (exps / jnp.sum(exps, axis=-1, keepdims=True)).astype(jnp.bfloat16)
    mixed = jnp.einsum("hqk,khd->qhd", attn_probs, value_all, preferred_element_type=jnp.float32)
    attended = mixed.astype(jnp.bfloat16).reshape(tok_rows, local_width)
    attn_terms = jnp.dot(
        attended, lax.all_gather(wo, "wide", axis=1, tiled=True), preferred_element_type=jnp.float32
    )
    attn_sum = lax.psum_scatter(
        attn_terms.astype(jnp.bfloat16), "narrow", scatter_dimension=1, tiled=True
    ).astype(jnp.float32)
    first_res = (hidden_in.astype(jnp.float32) + attn_sum).astype(jnp.bfloat16)
    whole_two = lax.all_gather(first_res, "narrow", axis=1, tiled=True)
    normed_two = norm_rows(whole_two)

    def add_second(piece):
        return add_rows(normed_two, piece)

    gate_proj = add_second(lax.all_gather(wg, "wide", axis=0, tiled=True))
    up_proj = add_second(lax.all_gather(wu, "wide", axis=0, tiled=True))
    hidden = (jax.nn.silu(gate_proj) * up_proj).astype(jnp.bfloat16)
    down_terms = jnp.dot(
        hidden, lax.all_gather(wd, "wide", axis=1, tiled=True), preferred_element_type=jnp.float32
    )
    down_sum = lax.psum_scatter(
        down_terms.astype(jnp.bfloat16), "narrow", scatter_dimension=1, tiled=True
    ).astype(jnp.float32)
    result = (first_res.astype(jnp.float32) + down_sum).astype(jnp.bfloat16)
    page_count = tok_rows // PAGE
    slots = page_table - wide_rank * page_count
    pairs = jnp.stack(
        [
            keys_rot.reshape(page_count, PAGE, local_width),
            values.reshape(page_count, PAGE, local_width),
        ],
        axis=0,
    )
    kv_cache = jnp.zeros_like(pairs).at[:, slots].set(pairs)
    return (result, kv_cache)


def solution(mesh):
    return jax.shard_map(
        per_device,
        mesh=mesh,
        in_specs=(
            P("wide", "narrow"),
            P("wide"),
            P("wide"),
            P("wide", "narrow"),
            P("wide", "narrow"),
            P("wide", "narrow"),
            P("narrow", "wide"),
            P("wide", "narrow"),
            P("wide", "narrow"),
            P("narrow", "wide"),
        ),
        out_specs=(P("wide", "narrow"), P(None, "wide", None, "narrow")),
        check_vma=False,
    )
```

profile of v0, /device:TPU:6, one launch (start us, length us, event | category | flops | bytes accessed | tf_op | source)
XLA Modules:
  0.0 878.4 jit_solution(14633172779645840433)
XLA Ops:
  12.3 2.0 fusion.47
  14.3 2.0 fusion.27
  19.8 25.0 %all-reduce.3 = (s32[64]{0:T(128)S(1)}, s32[64]{0:T(128)S(1)}, s32[64]{0:T(128)S(1)}) all-reduce(s32[64]{0:T(128)S(1)} %dynamic-update-slice, s32[64]{0:T(128)S(1)} %get-tuple-element.159, s32[64]{0:T(128)S(1)} %dynamic-update-slice.2), channel_id=1, replica_groups=mesh['wide'=64,'narrow'=8] {'wide'}, use_global_device_ids=true, to_apply=%add | all-reduce | flops 192 | bytes 1536
  44.7 335.9 %while.15 = (s32[]{:T(128)}, s32[]{:T(128)}, s32[]{:T(128)}, s32[]{:T(128)}, s32[64]{0:T(128)S(1)}, /*index=5*/s32[64]{0:T(128)S(1)}, s32[64]{0:T(128)S(1)}, s32[]{:T(128)}, s32[]{:T(128)}, s32[1]{0:T(128)}) while((s32[]{:T(128)}, s32[]{:T(128)}, s32[]{:T(128)}, s32[]{:T(128)}, s32[64]{0:T(128)S(1)}, /*index=5*/s32[64]{0:T(128)S(1)}, ...), condition=%wide.region_5.6_spmd, body=%wide.region_4.5_spmd.sunk | while | flops 17 | bytes 279 | solution.py:26
  387.1 1.9 collective-permute-start.8
  390.9 4.4 collective-permute-start
  395.3 1.9 collective-permute-start.9
  397.2 4.6 collective-permute-start.1
  401.9 3.7 collective-permute-start.10
  405.7 4.6 collective-permute-start.2
  410.4 3.6 collective-permute-start.11
  414.0 4.6 collective-permute-start.3
  418.7 3.7 collective-permute-start.12
  423.0 4.7 collective-permute-start.4
  427.7 3.2 collective-permute-start.13
  432.7 5.0 collective-permute-start.5
  437.7 1.9 collective-permute-start.14
  439.9 5.0 collective-permute-start.6
  444.9 3.3 collective-permute-start.15
  449.0 5.0 collective-permute-start.7
  459.7 5.9 fusion.48
  465.6 3.7 fusion.15
  469.3 18.0 %all-gather.18.cloned.1.call-done = bf16[256,2048]{0,1:T(8,128)(2,1)} async-done(((bf16[256,32]{0,1:T(8,128)(2,1)}), bf16[256,2048]{0,1:T(8,128)(2,1)}) %all-gather.18.cloned.1.call-update) | async-done | bytes 1048592 | tf_op jit(solution)/shard_map/all_gather | solution.py:142
  487.3 2.7 convolution_convert_fusion.1
  490.1 39.2 %reduce-scatter.3.cloned.1.call-done = bf16[256,256]{1,0:T(8,128)(2,1)} async-done(((bf16[256,2048]{1,0:T(8,128)(2,1)}), bf16[256,256]{1,0:T(8,128)(2,1)}) %reduce-scatter.3.cloned.1.call-update) | async-done | bytes 131088 | tf_op jit(solution)/shard_map/reduce_scatter | solution.py:144
  533.2 40.0 %all-gather.20.cloned.1.call-done = bf16[256,2048]{1,0:T(8,128)(2,1)} async-done(((bf16[256,256]{1,0:T(8,128)(2,1)}), bf16[256,2048]{1,0:T(8,128)(2,1)}) %all-gather.20.cloned.1.call-update) | async-done | bytes 1048592 | tf_op jit(solution)/shard_map/all_gather | solution.py:148
  575.1 83.4 %all-gather.22.cloned.1.call-done = bf16[2048,512]{1,0:T(8,128)(2,1)} async-done(((bf16[32,512]{1,0:T(8,128)(2,1)}), bf16[2048,512]{1,0:T(8,128)(2,1)}) %all-gather.22.cloned.1.call-update) | async-done | bytes 2097168 | tf_op jit(solution)/shard_map/all_gather | solution.py:154
  658.5 2.4 fusion.41
  660.9 81.6 %all-gather.24.cloned.1.call-done = bf16[2048,512]{1,0:T(8,128)(2,1)} async-done(((bf16[32,512]{1,0:T(8,128)(2,1)}), bf16[2048,512]{1,0:T(8,128)(2,1)}) %all-gather.24.cloned.1.call-update) | async-done | bytes 2097168 | tf_op jit(solution)/shard_map/all_gather | solution.py:155
  742.5 83.8 %all-gather.26.cloned.1.call-done = bf16[512,2048]{0,1:T(8,128)(2,1)} async-done(((bf16[512,32]{0,1:T(8,128)(2,1)}), bf16[512,2048]{0,1:T(8,128)(2,1)}) %all-gather.26.cloned.1.call-update) | async-done | bytes 2097168 | tf_op jit(solution)/shard_map/all_gather | solution.py:158
  826.4 4.7 convolution_convert_fusion
  832.6 37.6 %reduce-scatter.5.cloned.1.call-done = bf16[256,256]{1,0:T(8,128)(2,1)} async-done(((bf16[256,2048]{1,0:T(8,128)(2,1)}), bf16[256,256]{1,0:T(8,128)(2,1)}) %reduce-scatter.5.cloned.1.call-update) | async-done | bytes 131088 | tf_op jit(solution)/shard_map/reduce_scatter | solution.py:160
  (313 shorter events, 157.2 us)
Async XLA Ops:
  7.2 375.3 %all-gather.10.cloned.1.call-start = ((), (), s32[]{:S(2)}) async-start(), calls=%async_computation.2 | async-start | bytes 1179648 | tf_op jit(solution)/shard_map/all_gather | solution.py:102
  7.9 377.0 %all-gather.16.cloned.1.call-start = ((), (), s32[]{:S(2)}) async-start(), calls=%async_computation.5 | async-start | bytes 1064960 | tf_op jit(solution)/shard_map/all_gather | solution.py:111
  8.6 380.4 %all-gather.12.cloned.1.call-start = ((), (), s32[]{:S(2)}) async-start(), calls=%async_computation.3 | async-start | bytes 1064960 | tf_op jit(solution)/shard_map/all_gather | solution.py:112
  9.4 421.5 %all-gather.14.cloned.1.call-start = ((), (), s32[]{:S(2)}) async-start(), calls=%async_computation.4 | async-start | bytes 1064960 | tf_op jit(solution)/shard_map/all_gather | solution.py:110
  10.0 477.3 %all-gather.18.cloned.1.call-start = ((), (), s32[]{:S(2)}) async-start(), calls=%async_computation.6 | async-start | bytes 1064960 | tf_op jit(solution)/shard_map/all_gather | solution.py:142
  387.1 8.2 collective-permute-start.8
  390.9 6.4 collective-permute-start
  395.3 6.6 collective-permute-start.9
  397.2 8.5 collective-permute-start.1
  401.9 8.5 collective-permute-start.10
  405.6 123.6 %reduce-scatter.3.cloned.1.call-start = ((), (), s32[]{:S(2)}) async-start(), calls=%async_computation.7 | async-start | bytes 1179648 | tf_op jit(solution)/shard_map/reduce_scatter | solution.py:144
  405.7 8.3 collective-permute-start.2
  410.4 8.3 collective-permute-start.11
  414.0 8.9 %collective-permute-start.3 = (bf16[256,2,128]{0,2,1:T(8,128)(2,1)S(1)}, bf16[256,2,128]{0,2,1:T(8,128)(2,1)S(1)}, u32[]{:S(2)}, u32[]{:S(2)}) collective-permute-start(bf16[256,2,128]{0,2,1:T(8,128)(2,1)S(1)} %collective-permute-done.2), channel_id=1, source_target_pairs={{0,8},{8,16},{16,24},{24,32},{32,40},{40,48},{48,56},{56,64},{64,7... | collective-permute-start | bytes 393224 | tf_op jit(solution)/shard_map/ppermute | solution.py:32
  418.7 9.0 %collective-permute-start.12 = (bf16[256,2,128]{2,0,1:T(8,128)(2,1)}, bf16[256,2,128]{2,0,1:T(8,128)(2,1)}, u32[]{:S(2)}, u32[]{:S(2)}) collective-permute-start(bf16[256,2,128]{2,0,1:T(8,128)(2,1)} %collective-permute-done.11), channel_id=1, source_target_pairs={{0,8},{8,16},{16,24},{24,32},{32,40},{40,48},{48,56},{56,64},{64,7... | collective-permute-start | bytes 393224 | tf_op jit(solution)/shard_map/ppermute | solution.py:32
  423.0 9.7 %collective-permute-start.4 = (bf16[256,2,128]{0,2,1:T(8,128)(2,1)S(1)}, bf16[256,2,128]{0,2,1:T(8,128)(2,1)}, u32[]{:S(2)}, u32[]{:S(2)}) collective-permute-start(bf16[256,2,128]{0,2,1:T(8,128)(2,1)S(1)} %collective-permute-done.3), channel_id=1, source_target_pairs={{0,8},{8,16},{16,24},{24,32},{32,40},{40,48},{48,56},{56,64},{64,7... | collective-permute-start | bytes 393224 | tf_op jit(solution)/shard_map/ppermute | solution.py:32
  427.7 10.0 %collective-permute-start.13 = (bf16[256,2,128]{2,0,1:T(8,128)(2,1)}, bf16[256,2,128]{2,0,1:T(8,128)(2,1)}, u32[]{:S(2)}, u32[]{:S(2)}) collective-permute-start(bf16[256,2,128]{2,0,1:T(8,128)(2,1)} %collective-permute-done.12), channel_id=1, source_target_pairs={{0,8},{8,16},{16,24},{24,32},{32,40},{40,48},{48,56},{56,64},{64,7... | collective-permute-start | bytes 393224 | tf_op jit(solution)/shard_map/ppermute | solution.py:32
  432.7 7.2 collective-permute-start.5
  437.7 7.2 collective-permute-start.14
  439.9 9.1 %collective-permute-start.6 = (bf16[256,2,128]{0,2,1:T(8,128)(2,1)S(1)}, bf16[256,2,128]{0,2,1:T(8,128)(2,1)S(1)}, u32[]{:S(2)}, u32[]{:S(2)}) collective-permute-start(bf16[256,2,128]{0,2,1:T(8,128)(2,1)S(1)} %collective-permute-done.5), channel_id=1, source_target_pairs={{0,8},{8,16},{16,24},{24,32},{32,40},{40,48},{48,56},{56,64},{64,7... | collective-permute-start | bytes 393224 | tf_op jit(solution)/shard_map/ppermute | solution.py:32
  444.9 9.1 %collective-permute-start.15 = (bf16[256,2,128]{2,0,1:T(8,128)(2,1)S(1)}, bf16[256,2,128]{2,0,1:T(8,128)(2,1)S(1)}, u32[]{:S(2)}, u32[]{:S(2)}) collective-permute-start(bf16[256,2,128]{2,0,1:T(8,128)(2,1)S(1)} %collective-permute-done.14), channel_id=1, source_target_pairs={{0,8},{8,16},{16,24},{24,32},{32,40},{40,48},{48,56},{56,64},{64,7... | collective-permute-start | bytes 393224 | tf_op jit(solution)/shard_map/ppermute | solution.py:32
  449.0 8.1 collective-permute-start.7
  457.1 2.6 copy-start.5
  487.3 42.0 %copy-start.4 = (bf16[256,256]{1,0:T(8,128)(2,1)S(1)}, bf16[256,256]{1,0:T(8,128)(2,1)}, u32[]{:S(2)}) copy-start(bf16[256,256]{1,0:T(8,128)(2,1)} %param.12) | copy-start | bytes 393220
  490.0 83.1 %all-gather.20.cloned.1.call-start = ((), (), s32[]{:S(2)}) async-start(), calls=%async_computation.8 | async-start | bytes 1179648 | tf_op jit(solution)/shard_map/all_gather | solution.py:148
  530.9 127.6 %all-gather.22.cloned.1.call-start = ((), (), s32[]{:S(2)}) async-start(), calls=%async_computation.9 | async-start | bytes 2129920 | tf_op jit(solution)/shard_map/all_gather | solution.py:154
  531.7 210.9 %all-gather.24.cloned.1.call-start = ((), (), s32[]{:S(2)}) async-start(), calls=%async_computation.10 | async-start | bytes 2129920 | tf_op jit(solution)/shard_map/all_gather | solution.py:155
  532.4 294.0 %all-gather.26.cloned.1.call-start = ((), (), s32[]{:S(2)}) async-start(), calls=%async_computation.11 | async-start | bytes 2129920 | tf_op jit(solution)/shard_map/all_gather | solution.py:158
  533.0 337.3 %reduce-scatter.5.cloned.1.call-start = ((), (), s32[]{:S(2)}) async-start(), calls=%async_computation.12 | async-start | bytes 1179648 | tf_op jit(solution)/shard_map/reduce_scatter | solution.py:160
  660.9 170.2 %copy-start.9 = (s32[16]{0:T(128)S(1)}, s32[16]{0:T(128)}, u32[]{:S(2)}) copy-start(s32[16]{0:T(128)} %param.14) | copy-start | bytes 196
  831.2 39.1 %copy-start.2 = (bf16[256,256]{1,0:T(8,128)(2,1)S(1)}, bf16[256,256]{1,0:T(8,128)(2,1)}, u32[]{:S(2)}) copy-start(bf16[256,256]{1,0:T(8,128)(2,1)} %add_convert_fusion.1) | copy-start | bytes 393220
  832.6 39.3 %copy-start.3 = (bf16[2,16,16,256]{3,2,1,0:T(8,128)(2,1)}, bf16[2,16,16,256]{3,2,1,0:T(8,128)(2,1)S(1)}, u32[]{:S(2)}) copy-start(bf16[2,16,16,256]{3,2,1,0:T(8,128)(2,1)S(1)} %scatter_fusion) | copy-start | bytes 786436
  (5 other events, 8.3 us)
Sparse Core Ops, SparseCore 0:
  10.0 46.6 all-gather.9
  60.0 81.1 all-gather.15
  144.6 79.7 all-gather.11
  227.7 79.7 all-gather.13
  405.8 81.4 all-gather.17
  490.2 39.0 reduce-scatter.2
  531.9 41.2 all-gather.19
  576.5 81.9 all-gather.21
  661.9 80.5 all-gather.23
  745.7 80.5 all-gather.25
  831.2 39.0 reduce-scatter.4
where the time goes:
time: 882 us; the launch traced here: 878 us
  waiting for transfers between devices  388 us (44%)
  loops' own time  212 us (24%)
  local copies, waits for them, and re-layouts  137 us (16%)
  starting transfers between devices  61.9 us (7%)
  blocking collectives  25 us (3%)
  matrix products  24.5 us (3%)
  between operations  15.9 us (2%)
  other arithmetic  13.9 us (2%)
    another operation x1, loops' own time, prefix(): return lax.fori_loop(0, count - 1, lap, running)  212 us
    dynamic_slice x189, local copies, waits for them, and re-layouts, lap(): longer = join(running, jax.tree.map(lambda part: part[position], pieces))  124 us
    all_gather x1, waiting for transfers between devices, per_device(): lax.all_gather(wd, 'wide', axis=1, tiled=True)  83.8 us
    all_gather x1, waiting for transfers between devices, per_device(): gate_proj = add_second(lax.all_gather(wg, 'wide', axis=0, tiled=True))  83.4 us
    all_gather x1, waiting for transfers between devices, per_device(): up_proj = add_second(lax.all_gather(wu, 'wide', axis=0, tiled=True))  81.6 us
    ppermute x16, starting transfers between devices, shifted(): lax.ppermute(value, axis, [(source, source + steps) for source in range(f...  61.3 us
    all_gather x1, waiting for transfers between devices, per_device(): whole_two = lax.all_gather(first_res, 'narrow', axis=1, tiled=True)  40 us
    reduce_scatter x1, waiting for transfers between devices, per_device(): lax.psum_scatter(attn_terms.astype(jnp.bfloat16), 'narrow', scatter_dimen...  39.2 us
  transfers between devices with their start and end apart: 27, of which 7 were waited for; matrix products, arithmetic and copies ran while one was open for 19% of the time, Pallas kernels for 0%

commit v1 on v0

v1 whole, which is shorter than its diff:
```python
import jax
import jax.numpy as jnp
from jax import lax
from jax.sharding import PartitionSpec as P

HEAD_DIM = 128
REACH = 8
PAGE = 16


epsilon = 1e-05
rope_base = 10000.0


def shifted(value, axis, steps):
    count = lax.axis_size(axis)
    first, last = (max(0, -steps), min(count, count - steps))
    return lax.ppermute(value, axis, [(source, source + steps) for source in range(first, last)])


def norm_rows(source):
    widened = source.astype(jnp.float32)
    center = widened - jnp.mean(widened, axis=-1, keepdims=True)
    spread = jnp.mean(center * center, axis=-1, keepdims=True)
    return (center * lax.rsqrt(spread + epsilon)).astype(jnp.bfloat16)


def rotate(projected, positions):
    head_size = projected.shape[-1]
    half_dim = head_size // 2
    frequency = jnp.power(rope_base, -jnp.arange(half_dim, dtype=jnp.float32) * 2.0 / head_size)
    angles = positions.astype(jnp.float32)[:, None] * frequency[None, :]
    cosine = jnp.cos(angles)[:, None, :]
    sine_part = jnp.sin(angles)[:, None, :]
    first_half = projected[..., :half_dim]
    second_half = projected[..., half_dim:]
    return jnp.concatenate(
        [
            first_half * cosine - second_half * sine_part,
            second_half * cosine + first_half * sine_part,
        ],
        axis=-1,
    )


def add_rows(source, piece):
    return jnp.dot(source, piece, preferred_element_type=jnp.float32)


def per_device(hidden_in, segment_ids, page_table, wq, wk, wv, wo, wg, wu, wd):
    tok_rows = hidden_in.shape[0]
    wide_rank = lax.axis_index("wide")
    local_index = jnp.arange(tok_rows, dtype=jnp.int32)

    attn_width = wq.shape[1]
    ff_width = wg.shape[1]
    pieces = [wq, wk, wv, wo.T, wg, wu, wd.T]
    widths = [piece.shape[1] for piece in pieces]
    gathered = lax.all_gather(jnp.concatenate(pieces, axis=1), "wide", axis=0, tiled=True)
    offsets = [sum(widths[:k]) for k in range(len(widths))]
    full = [gathered[:, o:o + w] for o, w in zip(offsets, widths)]
    wq_all, wk_all, wv_all, wo_t, wg_all, wu_all, wd_t = full

    id_blocks = []
    for step_back in range(REACH, 0, -1):
        got = shifted(segment_ids, "wide", step_back)
        id_blocks.append(jnp.where(wide_rank >= step_back, got, -1))
    id_blocks.append(segment_ids)
    window_ids = jnp.concatenate(id_blocks, axis=0)
    window_len = window_ids.shape[0]
    lead = REACH * tok_rows
    window_index = jnp.arange(window_len, dtype=jnp.int32)
    same = window_ids[None, :] == segment_ids[:, None]
    allowed = same & (window_index[None, :] <= lead + local_index[:, None])
    earlier = same & (window_index[None, :] < lead + local_index[:, None])
    positions = jnp.sum(earlier.astype(jnp.int32), axis=1)

    whole = lax.all_gather(hidden_in, "narrow", axis=1, tiled=True)
    normed = norm_rows(whole)
    local_width = attn_width
    head_count = local_width // HEAD_DIM

    q_proj = add_rows(normed, wq_all)
    k_proj = add_rows(normed, wk_all)
    v_proj = add_rows(normed, wv_all)
    queries = rotate(q_proj.reshape(tok_rows, head_count, HEAD_DIM), positions).astype(jnp.bfloat16)
    keys_rot = rotate(k_proj.reshape(tok_rows, head_count, HEAD_DIM), positions).astype(
        jnp.bfloat16
    )
    values = v_proj.astype(jnp.bfloat16).reshape(tok_rows, head_count, HEAD_DIM)
    blocks = []
    for step_back in range(REACH, 0, -1):
        blocks.append(shifted((keys_rot, values), "wide", step_back))
    blocks.append((keys_rot, values))
    score_scale = HEAD_DIM ** (-0.5)
    key_all = jnp.concatenate([member[0] for member in blocks], axis=0)
    value_all = jnp.concatenate([member[1] for member in blocks], axis=0)
    scores = (
        jnp.einsum("qhd,khd->hqk", queries, key_all, preferred_element_type=jnp.float32)
        * score_scale
    )
    scores = jnp.where(allowed[None], scores, -1e30)
    row_peak = jnp.max(scores, axis=-1, keepdims=True)
    exps = jnp.where(allowed[None], jnp.exp(scores - row_peak), 0.0)
    attn_probs = (exps / jnp.sum(exps, axis=-1, keepdims=True)).astype(jnp.bfloat16)
    mixed = jnp.einsum("hqk,khd->qhd", attn_probs, value_all, preferred_element_type=jnp.float32)
    attended = mixed.astype(jnp.bfloat16).reshape(tok_rows, local_width)
    attn_terms = lax.dot_general(
        attended, wo_t, (((1,), (1,)), ((), ())), preferred_element_type=jnp.float32
    )
    attn_sum = lax.psum_scatter(
        attn_terms.astype(jnp.bfloat16), "narrow", scatter_dimension=1, tiled=True
    ).astype(jnp.float32)
    first_res = (hidden_in.astype(jnp.float32) + attn_sum).astype(jnp.bfloat16)
    whole_two = lax.all_gather(first_res, "narrow", axis=1, tiled=True)
    normed_two = norm_rows(whole_two)

    gate_proj = add_rows(normed_two, wg_all)
    up_proj = add_rows(normed_two, wu_all)
    hidden = (jax.nn.silu(gate_proj) * up_proj).astype(jnp.bfloat16)
    down_terms = lax.dot_general(
        hidden, wd_t, (((1,), (1,)), ((), ())), preferred_element_type=jnp.float32
    )
    down_sum = lax.psum_scatter(
        down_terms.astype(jnp.bfloat16), "narrow", scatter_dimension=1, tiled=True
    ).astype(jnp.float32)
    result = (first_res.astype(jnp.float32) + down_sum).astype(jnp.bfloat16)
    page_count = tok_rows // PAGE
    slots = page_table - wide_rank * page_count
    pairs = jnp.stack(
        [
            keys_rot.reshape(page_count, PAGE, local_width),
            values.reshape(page_count, PAGE, local_width),
        ],
        axis=0,
    )
    kv_cache = jnp.zeros_like(pairs).at[:, slots].set(pairs)
    return (result, kv_cache)


def solution(mesh):
    return jax.shard_map(
        per_device,
        mesh=mesh,
        in_specs=(
            P("wide", "narrow"),
            P("wide"),
            P("wide"),
            P("wide", "narrow"),
            P("wide", "narrow"),
            P("wide", "narrow"),
            P("narrow", "wide"),
            P("wide", "narrow"),
            P("wide", "narrow"),
            P("narrow", "wide"),
        ),
        out_specs=(P("wide", "narrow"), P(None, "wide", None, "narrow")),
        check_vma=False,
    )
```

time: 882 us -> 367 us (0.42)
  loops' own time: 212 us -> 0 us
  waiting for transfers between devices: 388 us -> 219 us
  local copies, waits for them, and re-layouts: 137 us -> 11 us
  blocking collectives: 25 us -> 0 us
  starting transfers between devices: 61.9 us -> 84.2 us
    another operation x1 -> x0, loops' own time: 212 us -> none  [prefix(): return lax.fori_loop(0, count - 1, lap, running)]
    all_gather x7 -> x1, waiting for transfers between devices: 267 us -> 90.5 us  [per_device(): lax.all_gather(jnp.concatenate(pieces, axis=1), 'wide', axis=0, tiled=True)]
    dynamic_slice x189 -> x0, local copies, waits for them, and re-layouts: 124 us -> none  [lap(): longer = join(running, jax.tree.map(lambda part: part[position], pieces))]
    unnamed x1 -> x0, blocking collectives: 25 us -> none
    ppermute x16 -> x24, starting transfers between devices: 61.3 us -> 83.8 us  [shifted(): lax.ppermute(value, axis, [(source, source + steps) for source in range(f...]
  transfers between devices with their start and end apart: 27 -> 29, of which waited for: 7 -> 8; matrix products, arithmetic and copies ran while one was open for 19% -> 5% of each run, Pallas kernels for 0% -> 0%
where the time goes in v1:
time: 367 us; the launch traced here: 365 us
  waiting for transfers between devices  219 us (60%)
  starting transfers between devices  84.2 us (23%)
  matrix products  23.6 us (6%)
  between operations  14.6 us (4%)
  other arithmetic  13.2 us (4%)
  local copies, waits for them, and re-layouts  11 us (3%)
    all_gather x1, waiting for transfers between devices, per_device(): lax.all_gather(jnp.concatenate(pieces, axis=1), 'wide', axis=0, tiled=True)  90.5 us
    ppermute x24, starting transfers between devices, shifted(): lax.ppermute(value, axis, [(source, source + steps) for source in range(f...  83.8 us
    all_gather x1, waiting for transfers between devices, per_device(): whole_two = lax.all_gather(first_res, 'narrow', axis=1, tiled=True)  42 us
    reduce_scatter x1, waiting for transfers between devices, per_device(): lax.psum_scatter(down_terms.astype(jnp.bfloat16), 'narrow', scatter_dimen...  39.1 us
    reduce_scatter x1, waiting for transfers between devices, per_device(): lax.psum_scatter(attn_terms.astype(jnp.bfloat16), 'narrow', scatter_dimen...  37.6 us
    unnamed x46, local copies, waits for them, and re-layouts  7.88 us
    dot_general x4, matrix products, add_rows(): return jnp.dot(source, piece, preferred_element_type=jnp.float32)  7.84 us
  transfers between devices with their start and end apart: 29, of which 8 were waited for; matrix products, arithmetic and copies ran while one was open for 5% of the time, Pallas kernels for 0%

profile of v1, /device:TPU:6, one launch (start us, length us, event | category | flops | bytes accessed | tf_op | source)
XLA Modules:
  0.0 365.4 jit_solution(13922790470429218336)
XLA Ops:
  13.8 4.3 %collective-permute-start.8 = (s32[256]{0:T(256)}, s32[256]{0:T(256)S(1)}, u32[]{:S(2)}, u32[]{:S(2)}) collective-permute-start(s32[256]{0:T(256)} %param.11), channel_id=1, source_target_pairs={{0,64},{8,72},{16,80},{24,88},{32,96},{40,104},{48,112},{56,120},{... | collective-permute-start | bytes 3080 | tf_op jit(solution)/shard_map/ppermute | solution.py:18
  18.1 3.7 %collective-permute-start.9 = (s32[256]{0:T(256)}, s32[256]{0:T(256)S(1)}, u32[]{:S(2)}, u32[]{:S(2)}) collective-permute-start(s32[256]{0:T(256)} %param.11), channel_id=1, source_target_pairs={{0,56},{8,64},{16,72},{24,80},{32,88},{40,96},{48,104},{56,112},{6... | collective-permute-start | bytes 3080 | tf_op jit(solution)/shard_map/ppermute | solution.py:18
  21.8 4.3 %collective-permute-start.10 = (s32[256]{0:T(256)}, s32[256]{0:T(256)S(1)}, u32[]{:S(2)}, u32[]{:S(2)}) collective-permute-start(s32[256]{0:T(256)} %param.11), channel_id=1, source_target_pairs={{0,48},{8,56},{16,64},{24,72},{32,80},{40,88},{48,96},{56,104},{64... | collective-permute-start | bytes 3080 | tf_op jit(solution)/shard_map/ppermute | solution.py:18
  26.1 6.4 %collective-permute-start.11 = (s32[256]{0:T(256)}, s32[256]{0:T(256)S(1)}, u32[]{:S(2)}, u32[]{:S(2)}) collective-permute-start(s32[256]{0:T(256)} %param.11), channel_id=1, source_target_pairs={{0,40},{8,48},{16,56},{24,64},{32,72},{40,80},{48,88},{56,96},{64,... | collective-permute-start | bytes 3080 | tf_op jit(solution)/shard_map/ppermute | solution.py:18
  32.5 4.3 %collective-permute-start.12 = (s32[256]{0:T(256)}, s32[256]{0:T(256)S(1)}, u32[]{:S(2)}, u32[]{:S(2)}) collective-permute-start(s32[256]{0:T(256)} %param.11), channel_id=1, source_target_pairs={{0,32},{8,40},{16,48},{24,56},{32,64},{40,72},{48,80},{56,88},{64,... | collective-permute-start | bytes 3080 | tf_op jit(solution)/shard_map/ppermute | solution.py:18
  36.9 3.5 collective-permute-start.13
  40.4 2.8 collective-permute-start.14
  43.2 3.4 collective-permute-start.15
  52.2 4.4 %all-gather.4.cloned.1.call-done = bf16[256,2048]{1,0:T(8,128)(2,1)} async-done(((bf16[256,256]{1,0:T(8,128)(2,1)}), bf16[256,2048]{1,0:T(8,128)(2,1)}) %all-gather.4.cloned.1.call-update) | async-done | bytes 1048592 | tf_op jit(solution)/shard_map/all_gather | solution.py:78
  59.9 90.5 %all-gather.6.cloned.1.call-done = bf16[2048,2560]{1,0:T(8,128)(2,1)} async-done(((bf16[32,2560]{1,0:T(8,128)(2,1)}), bf16[2048,2560]{1,0:T(8,128)(2,1)}) %all-gather.6.cloned.1.call-update) | async-done | bytes 10485776 | tf_op jit(solution)/shard_map/all_gather | solution.py:59
  152.8 3.4 collective-permute-start.16
  156.2 2.5 collective-permute-start.17
  158.7 4.2 %collective-permute-start.18 = (bf16[256,2,128]{2,0,1:T(8,128)(2,1)S(1)}, bf16[256,2,128]{2,0,1:T(8,128)(2,1)S(1)}, u32[]{:S(2)}, u32[]{:S(2)}) collective-permute-start(bf16[256,2,128]{2,0,1:T(8,128)(2,1)S(1)} %maximum_convert_fusion), channel_id=1, source_target_pairs={{0,48},{8,56},{16,64},{24,72},{32,80},{40,88},{48,96},{56,104},{64... | collective-permute-start | bytes 393224 | tf_op jit(solution)/shard_map/ppermute | solution.py:18
  163.0 4.1 %collective-permute-start.19 = (bf16[256,2,128]{2,0,1:T(8,128)(2,1)S(1)}, bf16[256,2,128]{2,0,1:T(8,128)(2,1)S(1)}, u32[]{:S(2)}, u32[]{:S(2)}) collective-permute-start(bf16[256,2,128]{2,0,1:T(8,128)(2,1)S(1)} %maximum_convert_fusion), channel_id=1, source_target_pairs={{0,40},{8,48},{16,56},{24,64},{32,72},{40,80},{48,88},{56,96},{64,... | collective-permute-start | bytes 393224 | tf_op jit(solution)/shard_map/ppermute | solution.py:18
  167.0 2.8 collective-permute-start.20
  173.9 3.6 collective-permute-start.21
  177.5 3.5 collective-permute-start.22
  181.1 3.0 collective-permute-start.23
  184.2 2.4 collective-permute-start
  186.6 3.4 collective-permute-start.1
  190.1 3.2 collective-permute-start.2
  195.6 3.6 collective-permute-start.4
  200.2 3.5 collective-permute-start.5
  206.1 3.5 collective-permute-start.7
  213.8 4.7 %fusion.62 = (f32[2,256]{1,0:T(2,128)S(1)}, f32[2,256,2304]{2,1,0:T(8,128)}) fusion(bf16[2304,2,128]{2,0,1:T(8,128)(2,1)S(1)} %copy-done.7, pred[256,2304]{1,0:T(8,128)(4,1)S(1)} %compare_and_fusion.1, bf16[256,2,64]{2,0,1:T(8,128)(2,1)S(1)} %get-tuple-element.3, bf16[256,2,64]{2,0,1:T(8,128)(2,1)S(1)} %get-tuple-element.2), kind=kOutput, calls=%fused_computation.111 | convolution fusion | flops 308152576 | bytes 6621184 | tf_op jit(solution)/shard_map/sub | solution.py:104
  218.5 3.7 %fusion.27 = bf16[2,128,256]{2,1,0:T(8,128)(2,1)S(1)} fusion(bf16[2304,2,128]{0,2,1:T(8,128)(2,1)} %copy-done.8, f32[2,256,2304]{2,1,0:T(8,128)} %get-tuple-element.13, f32[2,256]{1,0:T(2,128)S(1)} %get-tuple-element.12), kind=kOutput, calls=%fused_computation.35 | convolution fusion | flops 304414720 | bytes 6031360 | tf_op jit(solution)/shard_map/hqk,khd->qhd/dot_general | solution.py:106
  222.2 2.8 convolution_convert_fusion.1
  225.0 37.6 %reduce-scatter.3.cloned.1.call-done = bf16[256,256]{1,0:T(8,128)(2,1)} async-done(((bf16[256,2048]{1,0:T(8,128)(2,1)}), bf16[256,256]{1,0:T(8,128)(2,1)}) %reduce-scatter.3.cloned.1.call-update) | async-done | bytes 131088 | tf_op jit(solution)/shard_map/reduce_scatter | solution.py:111
  264.4 42.0 %all-gather.8.cloned.1.call-done = bf16[256,2048]{1,0:T(8,128)(2,1)} async-done(((bf16[256,256]{1,0:T(8,128)(2,1)}), bf16[256,2048]{1,0:T(8,128)(2,1)}) %all-gather.8.cloned.1.call-update) | async-done | bytes 1048592 | tf_op jit(solution)/shard_map/all_gather | solution.py:115
  309.6 2.3 fusion.17
  312.0 4.7 %convolution_convert_fusion = bf16[256,2048]{1,0:T(8,128)(2,1)} fusion(bf16[2048,2560]{1,0:T(8,128)(2,1)} %all-gather.6.cloned.1.call-done, f32[256,512]{1,0:T(8,128)S(1)} %fusion.17, bf16[256,2048]{1,0:T(8,128)(2,1)S(1)} %copy-done.1, f32[256]{0:T(256)S(1)} %add_rsqrt_fusion, f32[256]{0:T(256)S(1)} %broadcast_multiply_fusion), kind=kOutput, calls=%fused_computation.14 | convolution fusion | flops 1077149696 | bytes 6817792 | tf_op jit(solution)/shard_map/dot_general | solution.py:121
  318.2 39.1 %reduce-scatter.5.cloned.1.call-done = bf16[256,256]{1,0:T(8,128)(2,1)} async-done(((bf16[256,2048]{1,0:T(8,128)(2,1)}), bf16[256,256]{1,0:T(8,128)(2,1)}) %reduce-scatter.5.cloned.1.call-update) | async-done | bytes 131088 | tf_op jit(solution)/shard_map/reduce_scatter | solution.py:124
  (127 shorter events, 39.8 us)
Async XLA Ops:
  7.2 49.5 %all-gather.4.cloned.1.call-start = ((), (), s32[]{:S(2)}) async-start(), calls=%async_computation.2 | async-start | bytes 1179648 | tf_op jit(solution)/shard_map/all_gather | solution.py:78
  7.9 142.5 %all-gather.6.cloned.1.call-start = ((), (), s32[]{:S(2)}) async-start(), calls=%async_computation.3 | async-start | bytes 10649600 | tf_op jit(solution)/shard_map/all_gather | solution.py:59
  13.8 248.8 %reduce-scatter.3.cloned.1.call-start = ((), (), s32[]{:S(2)}) async-start(), calls=%async_computation.4 | async-start | bytes 1179648 | tf_op jit(solution)/shard_map/reduce_scatter | solution.py:111
  13.8 23.0 %collective-permute-start.8 = (s32[256]{0:T(256)}, s32[256]{0:T(256)S(1)}, u32[]{:S(2)}, u32[]{:S(2)}) collective-permute-start(s32[256]{0:T(256)} %param.11), channel_id=1, source_target_pairs={{0,64},{8,72},{16,80},{24,88},{32,96},{40,104},{48,112},{56,120},{... | collective-permute-start | bytes 3080 | tf_op jit(solution)/shard_map/ppermute | solution.py:18
  18.1 22.2 %collective-permute-start.9 = (s32[256]{0:T(256)}, s32[256]{0:T(256)S(1)}, u32[]{:S(2)}, u32[]{:S(2)}) collective-permute-start(s32[256]{0:T(256)} %param.11), channel_id=1, source_target_pairs={{0,56},{8,64},{16,72},{24,80},{32,88},{40,96},{48,104},{56,112},{6... | collective-permute-start | bytes 3080 | tf_op jit(solution)/shard_map/ppermute | solution.py:18
  21.8 21.3 %collective-permute-start.10 = (s32[256]{0:T(256)}, s32[256]{0:T(256)S(1)}, u32[]{:S(2)}, u32[]{:S(2)}) collective-permute-start(s32[256]{0:T(256)} %param.11), channel_id=1, source_target_pairs={{0,48},{8,56},{16,64},{24,72},{32,80},{40,88},{48,96},{56,104},{64... | collective-permute-start | bytes 3080 | tf_op jit(solution)/shard_map/ppermute | solution.py:18
  26.1 20.5 %collective-permute-start.11 = (s32[256]{0:T(256)}, s32[256]{0:T(256)S(1)}, u32[]{:S(2)}, u32[]{:S(2)}) collective-permute-start(s32[256]{0:T(256)} %param.11), channel_id=1, source_target_pairs={{0,40},{8,48},{16,56},{24,64},{32,72},{40,80},{48,88},{56,96},{64,... | collective-permute-start | bytes 3080 | tf_op jit(solution)/shard_map/ppermute | solution.py:18
  32.5 14.2 %collective-permute-start.12 = (s32[256]{0:T(256)}, s32[256]{0:T(256)S(1)}, u32[]{:S(2)}, u32[]{:S(2)}) collective-permute-start(s32[256]{0:T(256)} %param.11), channel_id=1, source_target_pairs={{0,32},{8,40},{16,48},{24,56},{32,64},{40,72},{48,80},{56,88},{64,... | collective-permute-start | bytes 3080 | tf_op jit(solution)/shard_map/ppermute | solution.py:18
  36.9 9.8 %collective-permute-start.13 = (s32[256]{0:T(256)}, s32[256]{0:T(256)S(1)}, u32[]{:S(2)}, u32[]{:S(2)}) collective-permute-start(s32[256]{0:T(256)} %param.11), channel_id=1, source_target_pairs={{0,24},{8,32},{16,40},{24,48},{32,56},{40,64},{48,72},{56,80},{64,... | collective-permute-start | bytes 3080 | tf_op jit(solution)/shard_map/ppermute | solution.py:18
  40.4 6.3 %collective-permute-start.14 = (s32[256]{0:T(256)}, s32[256]{0:T(256)S(1)}, u32[]{:S(2)}, u32[]{:S(2)}) collective-permute-start(s32[256]{0:T(256)} %param.11), channel_id=1, source_target_pairs={{0,16},{8,24},{16,32},{24,40},{32,48},{40,56},{48,64},{56,72},{64,... | collective-permute-start | bytes 3080 | tf_op jit(solution)/shard_map/ppermute | solution.py:18
  43.2 5.1 %collective-permute-start.15 = (s32[256]{0:T(256)}, s32[256]{0:T(256)S(1)}, u32[]{:S(2)}, u32[]{:S(2)}) collective-permute-start(s32[256]{0:T(256)} %param.11), channel_id=1, source_target_pairs={{0,8},{8,16},{16,24},{24,32},{32,40},{40,48},{48,56},{56,64},{64,7... | collective-permute-start | bytes 3080 | tf_op jit(solution)/shard_map/ppermute | solution.py:18
  56.7 93.7 %copy-start = (bf16[256,2048]{1,0:T(8,128)(2,1)S(1)}, bf16[256,2048]{1,0:T(8,128)(2,1)}, u32[]{:S(2)}) copy-start(bf16[256,2048]{1,0:T(8,128)(2,1)} %all-gather.4.cloned.1.call-done) | copy-start | bytes 3145732
  152.8 21.1 %collective-permute-start.16 = (bf16[256,2,128]{2,0,1:T(8,128)(2,1)S(1)}, bf16[256,2,128]{2,0,1:T(8,128)(2,1)S(1)}, u32[]{:S(2)}, u32[]{:S(2)}) collective-permute-start(bf16[256,2,128]{2,0,1:T(8,128)(2,1)S(1)} %maximum_convert_fusion), channel_id=1, source_target_pairs={{0,64},{8,72},{16,80},{24,88},{32,96},{40,104},{48,112},{56,120},{... | collective-permute-start | bytes 393224 | tf_op jit(solution)/shard_map/ppermute | solution.py:18
  156.2 21.3 %collective-permute-start.17 = (bf16[256,2,128]{2,0,1:T(8,128)(2,1)S(1)}, bf16[256,2,128]{2,0,1:T(8,128)(2,1)S(1)}, u32[]{:S(2)}, u32[]{:S(2)}) collective-permute-start(bf16[256,2,128]{2,0,1:T(8,128)(2,1)S(1)} %maximum_convert_fusion), channel_id=1, source_target_pairs={{0,56},{8,64},{16,72},{24,80},{32,88},{40,96},{48,104},{56,112},{6... | collective-permute-start | bytes 393224 | tf_op jit(solution)/shard_map/ppermute | solution.py:18
  158.7 22.3 %collective-permute-start.18 = (bf16[256,2,128]{2,0,1:T(8,128)(2,1)S(1)}, bf16[256,2,128]{2,0,1:T(8,128)(2,1)S(1)}, u32[]{:S(2)}, u32[]{:S(2)}) collective-permute-start(bf16[256,2,128]{2,0,1:T(8,128)(2,1)S(1)} %maximum_convert_fusion), channel_id=1, source_target_pairs={{0,48},{8,56},{16,64},{24,72},{32,80},{40,88},{48,96},{56,104},{64... | collective-permute-start | bytes 393224 | tf_op jit(solution)/shard_map/ppermute | solution.py:18
  163.0 21.2 %collective-permute-start.19 = (bf16[256,2,128]{2,0,1:T(8,128)(2,1)S(1)}, bf16[256,2,128]{2,0,1:T(8,128)(2,1)S(1)}, u32[]{:S(2)}, u32[]{:S(2)}) collective-permute-start(bf16[256,2,128]{2,0,1:T(8,128)(2,1)S(1)} %maximum_convert_fusion), channel_id=1, source_target_pairs={{0,40},{8,48},{16,56},{24,64},{32,72},{40,80},{48,88},{56,96},{64,... | collective-permute-start | bytes 393224 | tf_op jit(solution)/shard_map/ppermute | solution.py:18
  167.0 19.5 %collective-permute-start.20 = (bf16[256,2,128]{2,0,1:T(8,128)(2,1)S(1)}, bf16[256,2,128]{2,0,1:T(8,128)(2,1)S(1)}, u32[]{:S(2)}, u32[]{:S(2)}) collective-permute-start(bf16[256,2,128]{2,0,1:T(8,128)(2,1)S(1)} %maximum_convert_fusion), channel_id=1, source_target_pairs={{0,32},{8,40},{16,48},{24,56},{32,64},{40,72},{48,80},{56,88},{64,... | collective-permute-start | bytes 393224 | tf_op jit(solution)/shard_map/ppermute | solution.py:18
  173.9 16.1 %collective-permute-start.21 = (bf16[256,2,128]{2,0,1:T(8,128)(2,1)S(1)}, bf16[256,2,128]{2,0,1:T(8,128)(2,1)S(1)}, u32[]{:S(2)}, u32[]{:S(2)}) collective-permute-start(bf16[256,2,128]{2,0,1:T(8,128)(2,1)S(1)} %maximum_convert_fusion), channel_id=1, source_target_pairs={{0,24},{8,32},{16,40},{24,48},{32,56},{40,64},{48,72},{56,80},{64,... | collective-permute-start | bytes 393224 | tf_op jit(solution)/shard_map/ppermute | solution.py:18
  177.5 15.7 %collective-permute-start.22 = (bf16[256,2,128]{2,0,1:T(8,128)(2,1)S(1)}, bf16[256,2,128]{2,0,1:T(8,128)(2,1)S(1)}, u32[]{:S(2)}, u32[]{:S(2)}) collective-permute-start(bf16[256,2,128]{2,0,1:T(8,128)(2,1)S(1)} %maximum_convert_fusion), channel_id=1, source_target_pairs={{0,16},{8,24},{16,32},{24,40},{32,48},{40,56},{48,64},{56,72},{64,... | collective-permute-start | bytes 393224 | tf_op jit(solution)/shard_map/ppermute | solution.py:18
  181.1 14.5 %collective-permute-start.23 = (bf16[256,2,128]{2,0,1:T(8,128)(2,1)S(1)}, bf16[256,2,128]{2,0,1:T(8,128)(2,1)S(1)}, u32[]{:S(2)}, u32[]{:S(2)}) collective-permute-start(bf16[256,2,128]{2,0,1:T(8,128)(2,1)S(1)} %maximum_convert_fusion), channel_id=1, source_target_pairs={{0,8},{8,16},{16,24},{24,32},{32,40},{40,48},{48,56},{56,64},{64,7... | collective-permute-start | bytes 393224 | tf_op jit(solution)/shard_map/ppermute | solution.py:18
  184.2 16.1 %collective-permute-start = (bf16[256,2,128]{0,2,1:T(8,128)(2,1)S(1)}, bf16[256,2,128]{0,2,1:T(8,128)(2,1)S(1)}, u32[]{:S(2)}, u32[]{:S(2)}) collective-permute-start(bf16[256,2,128]{0,2,1:T(8,128)(2,1)S(1)} %bitcast.16), channel_id=1, source_target_pairs={{0,64},{8,72},{16,80},{24,88},{32,96},{40,104},{48,112},{56,120},{... | collective-permute-start | bytes 393224 | tf_op jit(solution)/shard_map/ppermute | solution.py:18
  186.6 17.2 %collective-permute-start.1 = (bf16[256,2,128]{0,2,1:T(8,128)(2,1)S(1)}, bf16[256,2,128]{0,2,1:T(8,128)(2,1)S(1)}, u32[]{:S(2)}, u32[]{:S(2)}) collective-permute-start(bf16[256,2,128]{0,2,1:T(8,128)(2,1)S(1)} %bitcast.17), channel_id=1, source_target_pairs={{0,56},{8,64},{16,72},{24,80},{32,88},{40,96},{48,104},{56,112},{6... | collective-permute-start | bytes 393224 | tf_op jit(solution)/shard_map/ppermute | solution.py:18
  190.1 16.0 %collective-permute-start.2 = (bf16[256,2,128]{0,2,1:T(8,128)(2,1)S(1)}, bf16[256,2,128]{0,2,1:T(8,128)(2,1)S(1)}, u32[]{:S(2)}, u32[]{:S(2)}) collective-permute-start(bf16[256,2,128]{0,2,1:T(8,128)(2,1)S(1)} %bitcast.18), channel_id=1, source_target_pairs={{0,48},{8,56},{16,64},{24,72},{32,80},{40,88},{48,96},{56,104},{64... | collective-permute-start | bytes 393224 | tf_op jit(solution)/shard_map/ppermute | solution.py:18
  193.3 16.4 %collective-permute-start.3 = (bf16[256,2,128]{0,2,1:T(8,128)(2,1)S(1)}, bf16[256,2,128]{0,2,1:T(8,128)(2,1)S(1)}, u32[]{:S(2)}, u32[]{:S(2)}) collective-permute-start(bf16[256,2,128]{0,2,1:T(8,128)(2,1)S(1)} %bitcast.19), channel_id=1, source_target_pairs={{0,40},{8,48},{16,56},{24,64},{32,72},{40,80},{48,88},{56,96},{64,... | collective-permute-start | bytes 393224 | tf_op jit(solution)/shard_map/ppermute | solution.py:18
  195.6 14.2 %collective-permute-start.4 = (bf16[256,2,128]{0,2,1:T(8,128)(2,1)S(1)}, bf16[256,2,128]{0,2,1:T(8,128)(2,1)S(1)}, u32[]{:S(2)}, u32[]{:S(2)}) collective-permute-start(bf16[256,2,128]{0,2,1:T(8,128)(2,1)S(1)} %bitcast.20), channel_id=1, source_target_pairs={{0,32},{8,40},{16,48},{24,56},{32,64},{40,72},{48,80},{56,88},{64,... | collective-permute-start | bytes 393224 | tf_op jit(solution)/shard_map/ppermute | solution.py:18
  200.2 9.5 %collective-permute-start.5 = (bf16[256,2,128]{0,2,1:T(8,128)(2,1)S(1)}, bf16[256,2,128]{0,2,1:T(8,128)(2,1)S(1)}, u32[]{:S(2)}, u32[]{:S(2)}) collective-permute-start(bf16[256,2,128]{0,2,1:T(8,128)(2,1)S(1)} %bitcast.21), channel_id=1, source_target_pairs={{0,24},{8,32},{16,40},{24,48},{32,56},{40,64},{48,72},{56,80},{64,... | collective-permute-start | bytes 393224 | tf_op jit(solution)/shard_map/ppermute | solution.py:18
  203.8 7.8 %collective-permute-start.6 = (bf16[256,2,128]{0,2,1:T(8,128)(2,1)S(1)}, bf16[256,2,128]{0,2,1:T(8,128)(2,1)S(1)}, u32[]{:S(2)}, u32[]{:S(2)}) collective-permute-start(bf16[256,2,128]{0,2,1:T(8,128)(2,1)S(1)} %bitcast.22), channel_id=1, source_target_pairs={{0,16},{8,24},{16,32},{24,40},{32,48},{40,56},{48,64},{56,72},{64,... | collective-permute-start | bytes 393224 | tf_op jit(solution)/shard_map/ppermute | solution.py:18
  206.1 6.6 %collective-permute-start.7 = (bf16[256,2,128]{0,2,1:T(8,128)(2,1)S(1)}, bf16[256,2,128]{0,2,1:T(8,128)(2,1)S(1)}, u32[]{:S(2)}, u32[]{:S(2)}) collective-permute-start(bf16[256,2,128]{0,2,1:T(8,128)(2,1)S(1)} %bitcast.23), channel_id=1, source_target_pairs={{0,8},{8,16},{16,24},{24,32},{32,40},{40,48},{48,56},{56,64},{64,7... | collective-permute-start | bytes 393224 | tf_op jit(solution)/shard_map/ppermute | solution.py:18
  225.0 81.4 %all-gather.8.cloned.1.call-start = ((), (), s32[]{:S(2)}) async-start(), calls=%async_computation.5 | async-start | bytes 1179648 | tf_op jit(solution)/shard_map/all_gather | solution.py:115
  264.2 93.1 %reduce-scatter.5.cloned.1.call-start = ((), (), s32[]{:S(2)}) async-start(), calls=%async_computation.6 | async-start | bytes 1179648 | tf_op jit(solution)/shard_map/reduce_scatter | solution.py:124
  316.6 40.7 %copy-start.2 = (bf16[256,256]{1,0:T(8,128)(2,1)S(1)}, bf16[256,256]{1,0:T(8,128)(2,1)}, u32[]{:S(2)}) copy-start(bf16[256,256]{1,0:T(8,128)(2,1)} %add_convert_fusion.1) | copy-start | bytes 393220
  318.2 40.7 %copy-start.3 = (bf16[2,16,16,256]{3,2,1,0:T(8,128)(2,1)}, bf16[2,16,16,256]{3,2,1,0:T(8,128)(2,1)S(1)}, u32[]{:S(2)}) copy-start(bf16[2,16,16,256]{3,2,1,0:T(8,128)(2,1)S(1)} %scatter_fusion) | copy-start | bytes 786436
  (7 other events, 64.6 us)
Sparse Core Ops, SparseCore 0:
  10.0 46.6 all-gather.3
  60.6 89.7 all-gather.5
  225.1 37.4 reduce-scatter.2
  265.0 41.3 all-gather.7
  316.8 40.5 reduce-scatter.4

commit v2 on v1

--- a/solution.py
+++ b/solution.py
@@ -16,6 +16,20 @@
     count = lax.axis_size(axis)
     first, last = (max(0, -steps), min(count, count - steps))
     return lax.ppermute(value, axis, [(source, source + steps) for source in range(first, last)])
+
+
+def ring_gather(value, axis, dim):
+    count, mine = (lax.axis_size(axis), lax.axis_index(axis))
+    got = [value]
+    for steps in range(1, count):
+        got.append(lax.ppermute(value, axis, [(source, (source + steps) % count) for source in range(count)]))
+    stacked = jnp.stack(got, axis=0)
+    order = (mine - jnp.arange(count, dtype=jnp.int32)) % count
+    ordered = jnp.take(stacked, order, axis=0)
+    ordered = jnp.moveaxis(ordered, 0, dim)
+    shape = list(value.shape)
+    shape[dim] = shape[dim] * count
+    return ordered.reshape(shape)
 
 
 def norm_rows(source):
@@ -75,7 +89,7 @@
     earlier = same & (window_index[None, :] < lead + local_index[:, None])
     positions = jnp.sum(earlier.astype(jnp.int32), axis=1)
 
-    whole = lax.all_gather(hidden_in, "narrow", axis=1, tiled=True)
+    whole = ring_gather(hidden_in, "narrow", 1)
     normed = norm_rows(whole)
     local_width = attn_width
     head_count = local_width // HEAD_DIM
@@ -88,13 +102,15 @@
         jnp.bfloat16
     )
     values = v_proj.astype(jnp.bfloat16).reshape(tok_rows, head_count, HEAD_DIM)
+    packed = jnp.concatenate([keys_rot, values], axis=2)
     blocks = []
     for step_back in range(REACH, 0, -1):
-        blocks.append(shifted((keys_rot, values), "wide", step_back))
-    blocks.append((keys_rot, values))
+        blocks.append(shifted(packed, "wide", step_back))
+    blocks.append(packed)
     score_scale = HEAD_DIM ** (-0.5)
-    key_all = jnp.concatenate([member[0] for member in blocks], axis=0)
-    value_all = jnp.concatenate([member[1] for member in blocks], axis=0)
+    kv_all = jnp.concatenate(blocks, axis=0)
+    key_all = kv_all[:, :, :HEAD_DIM]
+    value_all = kv_all[:, :, HEAD_DIM:]
     scores = (
         jnp.einsum("qhd,khd->hqk", queries, key_all, preferred_element_type=jnp.float32)
         * score_scale
@@ -108,11 +124,11 @@
     attn_terms = lax.dot_general(
         attended, wo_t, (((1,), (1,)), ((), ())), preferred_element_type=jnp.float32
     )
-    attn_sum = lax.psum_scatter(
-        attn_terms.astype(jnp.bfloat16), "narrow", scatter_dimension=1, tiled=True
-    ).astype(jnp.float32)
-    first_res = (hidden_in.astype(jnp.float32) + attn_sum).astype(jnp.bfloat16)
-    whole_two = lax.all_gather(first_res, "narrow", axis=1, tiled=True)
+    attn_sum = lax.psum(attn_terms.astype(jnp.bfloat16), "narrow").astype(jnp.float32)
+    whole_two = (whole.astype(jnp.float32) + attn_sum).astype(jnp.bfloat16)
+    narrow_rank = lax.axis_index("narrow")
+    feat = hidden_in.shape[1]
+    first_res = lax.dynamic_slice_in_dim(whole_two, narrow_rank * feat, feat, axis=1)
     normed_two = norm_rows(whole_two)
 
     gate_proj = add_rows(normed_two, wg_all)

time: 367 us -> 327 us (0.89)
  waiting for transfers between devices: 219 us -> 164 us
  local copies, waits for them, and re-layouts: 11 us -> 24.3 us
  starting transfers between devices: 84.2 us -> 88.7 us
    all_gather x1, waiting for transfers between devices: 90.5 us -> 3.18 us  [per_device(): lax.all_gather(jnp.concatenate(pieces, axis=1), 'wide', axis=0, tiled=True)]
    psum x0 -> x1, waiting for transfers between devices: none -> 82.7 us  [per_device(): lax.psum(attn_terms.astype(jnp.bfloat16), 'narrow').astype(jnp.float32)]
    all_gather x2 -> x0, waiting for transfers between devices: 46.4 us -> none  [the longest x1 42 us: per_device(): whole_two = lax.all_gather(first_res, 'narrow', axis=1, tiled=True)]
    reduce_scatter x1 -> x0, waiting for transfers between devices: 37.6 us -> none  [per_device(): lax.psum_scatter(attn_terms.astype(jnp.bfloat16), 'narrow', scatter_dimen...]
    ppermute x0 -> x7, starting transfers between devices: none -> 28.2 us  [ring_gather(): lax.ppermute(value, axis, [(source, (source + steps) % count) for source...]
    ppermute x24 -> x16, starting transfers between devices: 83.8 us -> 60.2 us  [shifted(): lax.ppermute(value, axis, [(source, source + steps) for source in range(f...]
    ppermute x0 -> x7, waiting for transfers between devices: none -> 17.4 us  [ring_gather(): lax.ppermute(value, axis, [(source, (source + steps) % count) for source...]
    ppermute x24 -> x16, waiting for transfers between devices: 4.52 us -> 21.6 us  [shifted(): lax.ppermute(value, axis, [(source, source + steps) for source in range(f...]
  transfers between devices with their start and end apart: 29 -> 26, of which waited for: 8 -> 12; matrix products, arithmetic and copies ran while one was open for 5% -> 6% of each run, Pallas kernels for 0% -> 0%
where the time goes in v2:
time: 327 us; the launch traced here: 325 us
  waiting for transfers between devices  164 us (50%)
  starting transfers between devices  88.7 us (27%)
  local copies, waits for them, and re-layouts  24.3 us (7%)
  matrix products  24.3 us (7%)
  between operations  14.5 us (4%)
  other arithmetic  9.85 us (3%)
    psum x1, waiting for transfers between devices, per_device(): lax.psum(attn_terms.astype(jnp.bfloat16), 'narrow').astype(jnp.float32)  82.7 us
    ppermute x16, starting transfers between devices, shifted(): lax.ppermute(value, axis, [(source, source + steps) for source in range(f...  60.2 us
    reduce_scatter x1, waiting for transfers between devices, per_device(): lax.psum_scatter(down_terms.astype(jnp.bfloat16), 'narrow', scatter_dimen...  38.6 us
    ppermute x7, starting transfers between devices, ring_gather(): lax.ppermute(value, axis, [(source, (source + steps) % count) for source...  28.2 us
    ppermute x16, waiting for transfers between devices, shifted(): lax.ppermute(value, axis, [(source, source + steps) for source in range(f...  21.6 us
    ppermute x7, waiting for transfers between devices, ring_gather(): lax.ppermute(value, axis, [(source, (source + steps) % count) for source...  17.4 us
    unnamed x39, local copies, waits for them, and re-layouts  12.4 us
    dot_general x3, local copies, waits for them, and re-layouts, add_rows(): return jnp.dot(source, piece, preferred_element_type=jnp.float32)  7.58 us
  transfers between devices with their start and end apart: 26, of which 12 were waited for; matrix products, arithmetic and copies ran while one was open for 6% of the time, Pallas kernels for 0%

profile of v2, /device:TPU:6, one launch (start us, length us, event | category | flops | bytes accessed | tf_op | source)
XLA Modules:
  0.0 325.4 jit_solution(10156077091598197644)
XLA Ops:
  15.0 4.2 %collective-permute-start.13 = (s32[256]{0:T(256)}, s32[256]{0:T(256)S(1)}, u32[]{:S(2)}, u32[]{:S(2)}) collective-permute-start(s32[256]{0:T(256)} %param.11), channel_id=1, source_target_pairs={{0,16},{8,24},{16,32},{24,40},{32,48},{40,56},{48,64},{56,72},{64,... | collective-permute-start | bytes 3080 | tf_op jit(solution)/shard_map/ppermute | solution.py:18
  19.2 4.3 %collective-permute-start.12 = (s32[256]{0:T(256)}, s32[256]{0:T(256)S(1)}, u32[]{:S(2)}, u32[]{:S(2)}) collective-permute-start(s32[256]{0:T(256)} %param.11), channel_id=1, source_target_pairs={{0,24},{8,32},{16,40},{24,48},{32,56},{40,64},{48,72},{56,80},{64,... | collective-permute-start | bytes 3080 | tf_op jit(solution)/shard_map/ppermute | solution.py:18
  23.6 4.8 %collective-permute-start.11 = (s32[256]{0:T(256)}, s32[256]{0:T(256)S(1)}, u32[]{:S(2)}, u32[]{:S(2)}) collective-permute-start(s32[256]{0:T(256)} %param.11), channel_id=1, source_target_pairs={{0,32},{8,40},{16,48},{24,56},{32,64},{40,72},{48,80},{56,88},{64,... | collective-permute-start | bytes 3080 | tf_op jit(solution)/shard_map/ppermute | solution.py:18
  28.4 4.3 %collective-permute-start.7 = (s32[256]{0:T(256)}, s32[256]{0:T(256)S(1)}, u32[]{:S(2)}, u32[]{:S(2)}) collective-permute-start(s32[256]{0:T(256)} %param.11), channel_id=1, source_target_pairs={{0,64},{8,72},{16,80},{24,88},{32,96},{40,104},{48,112},{56,120},{... | collective-permute-start | bytes 3080 | tf_op jit(solution)/shard_map/ppermute | solution.py:18
  37.9 5.7 %collective-permute-start.9 = (s32[256]{0:T(256)}, s32[256]{0:T(256)S(1)}, u32[]{:S(2)}, u32[]{:S(2)}) collective-permute-start(s32[256]{0:T(256)} %param.11), channel_id=1, source_target_pairs={{0,48},{8,56},{16,64},{24,72},{32,80},{40,88},{48,96},{56,104},{64... | collective-permute-start | bytes 3080 | tf_op jit(solution)/shard_map/ppermute | solution.py:18
  45.1 4.9 %collective-permute-start.10 = (s32[256]{0:T(256)}, s32[256]{0:T(256)S(1)}, u32[]{:S(2)}, u32[]{:S(2)}) collective-permute-start(s32[256]{0:T(256)} %param.11), channel_id=1, source_target_pairs={{0,40},{8,48},{16,56},{24,64},{32,72},{40,80},{48,88},{56,96},{64,... | collective-permute-start | bytes 3080 | tf_op jit(solution)/shard_map/ppermute | solution.py:18
  51.5 6.9 %collective-permute-start.4 = (bf16[256,256]{1,0:T(8,128)(2,1)}, bf16[256,256]{1,0:T(8,128)(2,1)S(1)}, u32[]{:S(2)}, u32[]{:S(2)}) collective-permute-start(bf16[256,256]{1,0:T(8,128)(2,1)} %param.10), channel_id=1, source_target_pairs={{0,5},{1,6},{2,7},{3,0},{4,1},{5,2},{6,3},{7,4},{8,13},{9,14},{10,... | collective-permute-start | bytes 393224 | tf_op jit(solution)/shard_map/ppermute | solution.py:25
  58.5 2.9 collective-permute-start.3
  61.5 5.5 %collective-permute-start.2 = (bf16[256,256]{1,0:T(8,128)(2,1)}, bf16[256,256]{1,0:T(8,128)(2,1)S(1)}, u32[]{:S(2)}, u32[]{:S(2)}) collective-permute-start(bf16[256,256]{1,0:T(8,128)(2,1)} %param.10), channel_id=1, source_target_pairs={{0,3},{1,4},{2,5},{3,6},{4,7},{5,0},{6,1},{7,2},{8,11},{9,12},{10,... | collective-permute-start | bytes 393224 | tf_op jit(solution)/shard_map/ppermute | solution.py:25
  67.0 3.9 %collective-permute-start.1 = (bf16[256,256]{1,0:T(8,128)(2,1)}, bf16[256,256]{1,0:T(8,128)(2,1)S(1)}, u32[]{:S(2)}, u32[]{:S(2)}) collective-permute-start(bf16[256,256]{1,0:T(8,128)(2,1)} %param.10), channel_id=1, source_target_pairs={{0,2},{1,3},{2,4},{3,5},{4,6},{5,7},{6,0},{7,1},{8,10},{9,11},{10,... | collective-permute-start | bytes 393224 | tf_op jit(solution)/shard_map/ppermute | solution.py:25
  71.0 2.6 collective-permute-start
  78.1 10.9 %collective-permute-done = bf16[256,256]{1,0:T(8,128)(2,1)S(1)} collective-permute-done((bf16[256,256]{1,0:T(8,128)(2,1)}, bf16[256,256]{1,0:T(8,128)(2,1)S(1)}, u32[]{:S(2)}, u32[]{:S(2)}) %collective-permute-start) | collective-permute-done | bytes 131104 | tf_op jit(solution)/shard_map/ppermute | solution.py:25
  91.2 4.1 %collective-permute-start.5 = (bf16[256,256]{1,0:T(8,128)(2,1)}, bf16[256,256]{1,0:T(8,128)(2,1)S(1)}, u32[]{:S(2)}, u32[]{:S(2)}) collective-permute-start(bf16[256,256]{1,0:T(8,128)(2,1)} %param.10), channel_id=1, source_target_pairs={{0,6},{1,7},{2,0},{3,1},{4,2},{5,3},{6,4},{7,5},{8,14},{9,15},{10,... | collective-permute-start | bytes 393224 | tf_op jit(solution)/shard_map/ppermute | solution.py:25
  95.5 6.5 %collective-permute-done.5 = bf16[256,256]{1,0:T(8,128)(2,1)S(1)} collective-permute-done((bf16[256,256]{1,0:T(8,128)(2,1)}, bf16[256,256]{1,0:T(8,128)(2,1)S(1)}, u32[]{:S(2)}, u32[]{:S(2)}) %collective-permute-start.5) | collective-permute-done | bytes 131104 | tf_op jit(solution)/shard_map/ppermute | solution.py:25
  105.0 3.2 all-gather.2.cloned.1.call-done
  110.0 3.0 slice_bitcast_fusion
  113.0 2.3 copy.32
  119.9 5.2 %collective-permute-start.21 = (bf16[256,2,256]{0,2,1:T(8,128)(2,1)}, bf16[256,2,256]{0,2,1:T(8,128)(2,1)}, u32[]{:S(2)}, u32[]{:S(2)}) collective-permute-start(bf16[256,2,256]{0,2,1:T(8,128)(2,1)} %pad_maximum_fusion), channel_id=1, source_target_pairs={{0,16},{8,24},{16,32},{24,40},{32,48},{40,56},{48,64},{56,72},{64,... | collective-permute-start | bytes 786440 | tf_op jit(solution)/shard_map/ppermute | solution.py:18
  127.1 3.7 %collective-permute-start.16 = (bf16[256,2,256]{0,2,1:T(8,128)(2,1)}, bf16[256,2,256]{0,2,1:T(8,128)(2,1)}, u32[]{:S(2)}, u32[]{:S(2)}) collective-permute-start(bf16[256,2,256]{0,2,1:T(8,128)(2,1)} %pad_maximum_fusion), channel_id=1, source_target_pairs={{0,56},{8,64},{16,72},{24,80},{32,88},{40,96},{48,104},{56,112},{6... | collective-permute-start | bytes 786440 | tf_op jit(solution)/shard_map/ppermute | solution.py:18
  130.7 3.9 %collective-permute-start.15 = (bf16[256,2,256]{0,2,1:T(8,128)(2,1)}, bf16[256,2,256]{0,2,1:T(8,128)(2,1)}, u32[]{:S(2)}, u32[]{:S(2)}) collective-permute-start(bf16[256,2,256]{0,2,1:T(8,128)(2,1)} %pad_maximum_fusion), channel_id=1, source_target_pairs={{0,64},{8,72},{16,80},{24,88},{32,96},{40,104},{48,112},{56,120},{... | collective-permute-start | bytes 786440 | tf_op jit(solution)/shard_map/ppermute | solution.py:18
  134.7 2.3 copy.35
  138.7 10.3 %collective-permute-done.15 = bf16[256,2,256]{0,2,1:T(8,128)(2,1)} collective-permute-done((bf16[256,2,256]{0,2,1:T(8,128)(2,1)}, bf16[256,2,256]{0,2,1:T(8,128)(2,1)}, u32[]{:S(2)}, u32[]{:S(2)}) %collective-permute-start.15) | collective-permute-done | bytes 262176 | tf_op jit(solution)/shard_map/ppermute | solution.py:18
  151.9 7.0 %collective-permute-start.19 = (bf16[256,2,256]{0,2,1:T(8,128)(2,1)}, bf16[256,2,256]{0,2,1:T(8,128)(2,1)S(1)}, u32[]{:S(2)}, u32[]{:S(2)}) collective-permute-start(bf16[256,2,256]{0,2,1:T(8,128)(2,1)} %pad_maximum_fusion), channel_id=1, source_target_pairs={{0,32},{8,40},{16,48},{24,56},{32,64},{40,72},{48,80},{56,88},{64,... | collective-permute-start | bytes 786440 | tf_op jit(solution)/shard_map/ppermute | solution.py:18
  162.9 3.7 %collective-permute-done.18 = bf16[256,2,256]{0,2,1:T(8,128)(2,1)S(1)} collective-permute-done((bf16[256,2,256]{0,2,1:T(8,128)(2,1)}, bf16[256,2,256]{0,2,1:T(8,128)(2,1)S(1)}, u32[]{:S(2)}, u32[]{:S(2)}) %collective-permute-start.18) | collective-permute-done | bytes 262176 | tf_op jit(solution)/shard_map/ppermute | solution.py:18
  166.6 2.8 collective-permute-done.20
  172.8 5.8 %fusion.54 = (f32[2,256]{1,0:T(2,128)S(1)}, f32[2,256,2304]{2,1,0:T(8,128)}) fusion(pred[256,2304]{1,0:T(8,128)(4,1)S(1)} %copy-done.1, bf16[2304,2,256]{0,2,1:T(8,128)(2,1)} %copy-done.7, bf16[256,2,64]{0,2,1:T(8,128)(2,1)S(1)} %get-tuple-element.7, bf16[256,2,64]{0,2,1:T(8,128)(2,1)S(1)} %get-tuple-element.6), kind=kOutput, calls=%fused_computation.125 | convolution fusion | flops 308152576 | bytes 7211008 | tf_op jit(solution)/shard_map/sub | solution.py:120
  178.6 3.7 %fusion.29 = bf16[2,128,256]{2,1,0:T(8,128)(2,1)S(1)} fusion(f32[2,256,2304]{2,1,0:T(8,128)} %get-tuple-element.13, f32[2,256]{1,0:T(2,128)S(1)} %get-tuple-element.12, bf16[2304,2,256]{0,2,1:T(8,128)(2,1)} %copy-done.7), kind=kOutput, calls=%fused_computation.41 | convolution fusion | flops 304414720 | bytes 6031360 | tf_op jit(solution)/shard_map/hqk,khd->qhd/dot_general | solution.py:122
  182.3 2.7 convolution_convert_fusion.1
  185.2 82.7 %all-reduce.2.cloned.1.call-done = bf16[256,2048]{1,0:T(8,128)(2,1)} async-done(((bf16[256,2048]{1,0:T(8,128)(2,1)}), bf16[256,2048]{1,0:T(8,128)(2,1)}) %all-reduce.2.cloned.1.call-update) | async-done | bytes 1048592 | tf_op jit(solution)/shard_map/psum | solution.py:127
  270.0 2.3 fusion.17
  272.3 4.6 %convolution_convert_fusion = bf16[256,2048]{1,0:T(8,128)(2,1)} fusion(bf16[2048,2560]{1,0:T(8,128)(2,1)} %all-gather.2.cloned.1.call-done, f32[256,512]{1,0:T(8,128)S(1)} %fusion.17, bf16[256,2048]{1,0:T(8,128)(2,1)S(1)} %get-tuple-element.3, f32[256]{0:T(256)S(1)} %add_rsqrt_fusion, f32[256]{0:T(256)S(1)} %broadcast_multiply_fusion), kind=kOutput, calls=%fused_computation.16 | convolution fusion | flops 1077149696 | bytes 6817792 | tf_op jit(solution)/shard_map/dot_general | solution.py:137
  278.6 38.6 %reduce-scatter.2.cloned.1.call-done = bf16[256,256]{1,0:T(8,128)(2,1)} async-done(((bf16[256,2048]{1,0:T(8,128)(2,1)}), bf16[256,256]{1,0:T(8,128)(2,1)}) %reduce-scatter.2.cloned.1.call-update) | async-done | bytes 131088 | tf_op jit(solution)/shard_map/reduce_scatter | solution.py:140
  (121 shorter events, 51.2 us)
Async XLA Ops:
  7.2 101.0 %all-gather.2.cloned.1.call-start = ((), (), s32[]{:S(2)}) async-start(), calls=%async_computation.1 | async-start | bytes 10649600 | tf_op jit(solution)/shard_map/all_gather | solution.py:73
  13.1 254.9 %all-reduce.2.cloned.1.call-start = ((), (), s32[]{:S(2)}) async-start(), calls=%async_computation.2 | async-start | bytes 2097152 | tf_op jit(solution)/shard_map/psum | solution.py:127
  13.1 57.8 %collective-permute-start.14 = (s32[256]{0:T(256)}, s32[256]{0:T(256)S(1)}, u32[]{:S(2)}, u32[]{:S(2)}) collective-permute-start(s32[256]{0:T(256)} %param.11), channel_id=1, source_target_pairs={{0,8},{8,16},{16,24},{24,32},{32,40},{40,48},{48,56},{56,64},{64,7... | collective-permute-start | bytes 3080 | tf_op jit(solution)/shard_map/ppermute | solution.py:18
  15.0 52.0 %collective-permute-start.13 = (s32[256]{0:T(256)}, s32[256]{0:T(256)S(1)}, u32[]{:S(2)}, u32[]{:S(2)}) collective-permute-start(s32[256]{0:T(256)} %param.11), channel_id=1, source_target_pairs={{0,16},{8,24},{16,32},{24,40},{32,48},{40,56},{48,64},{56,72},{64,... | collective-permute-start | bytes 3080 | tf_op jit(solution)/shard_map/ppermute | solution.py:18
  19.2 42.2 %collective-permute-start.12 = (s32[256]{0:T(256)}, s32[256]{0:T(256)S(1)}, u32[]{:S(2)}, u32[]{:S(2)}) collective-permute-start(s32[256]{0:T(256)} %param.11), channel_id=1, source_target_pairs={{0,24},{8,32},{16,40},{24,48},{32,56},{40,64},{48,72},{56,80},{64,... | collective-permute-start | bytes 3080 | tf_op jit(solution)/shard_map/ppermute | solution.py:18
  23.6 34.9 %collective-permute-start.11 = (s32[256]{0:T(256)}, s32[256]{0:T(256)S(1)}, u32[]{:S(2)}, u32[]{:S(2)}) collective-permute-start(s32[256]{0:T(256)} %param.11), channel_id=1, source_target_pairs={{0,32},{8,40},{16,48},{24,56},{32,64},{40,72},{48,80},{56,88},{64,... | collective-permute-start | bytes 3080 | tf_op jit(solution)/shard_map/ppermute | solution.py:18
  28.4 5.8 %collective-permute-start.7 = (s32[256]{0:T(256)}, s32[256]{0:T(256)S(1)}, u32[]{:S(2)}, u32[]{:S(2)}) collective-permute-start(s32[256]{0:T(256)} %param.11), channel_id=1, source_target_pairs={{0,64},{8,72},{16,80},{24,88},{32,96},{40,104},{48,112},{56,120},{... | collective-permute-start | bytes 3080 | tf_op jit(solution)/shard_map/ppermute | solution.py:18
  34.2 3.7 %collective-permute-start.8 = (s32[256]{0:T(256)}, s32[256]{0:T(256)S(1)}, u32[]{:S(2)}, u32[]{:S(2)}) collective-permute-start(s32[256]{0:T(256)} %param.11), channel_id=1, source_target_pairs={{0,56},{8,64},{16,72},{24,80},{32,88},{40,96},{48,104},{56,112},{6... | collective-permute-start | bytes 3080 | tf_op jit(solution)/shard_map/ppermute | solution.py:18
  37.9 7.2 %collective-permute-start.9 = (s32[256]{0:T(256)}, s32[256]{0:T(256)S(1)}, u32[]{:S(2)}, u32[]{:S(2)}) collective-permute-start(s32[256]{0:T(256)} %param.11), channel_id=1, source_target_pairs={{0,48},{8,56},{16,64},{24,72},{32,80},{40,88},{48,96},{56,104},{64... | collective-permute-start | bytes 3080 | tf_op jit(solution)/shard_map/ppermute | solution.py:18
  45.1 6.4 %collective-permute-start.10 = (s32[256]{0:T(256)}, s32[256]{0:T(256)S(1)}, u32[]{:S(2)}, u32[]{:S(2)}) collective-permute-start(s32[256]{0:T(256)} %param.11), channel_id=1, source_target_pairs={{0,40},{8,48},{16,56},{24,64},{32,72},{40,80},{48,88},{56,96},{64,... | collective-permute-start | bytes 3080 | tf_op jit(solution)/shard_map/ppermute | solution.py:18
  51.5 43.9 %collective-permute-start.4 = (bf16[256,256]{1,0:T(8,128)(2,1)}, bf16[256,256]{1,0:T(8,128)(2,1)S(1)}, u32[]{:S(2)}, u32[]{:S(2)}) collective-permute-start(bf16[256,256]{1,0:T(8,128)(2,1)} %param.10), channel_id=1, source_target_pairs={{0,5},{1,6},{2,7},{3,0},{4,1},{5,2},{6,3},{7,4},{8,13},{9,14},{10,... | collective-permute-start | bytes 393224 | tf_op jit(solution)/shard_map/ppermute | solution.py:25
  58.5 36.9 %collective-permute-start.3 = (bf16[256,256]{1,0:T(8,128)(2,1)}, bf16[256,256]{1,0:T(8,128)(2,1)S(1)}, u32[]{:S(2)}, u32[]{:S(2)}) collective-permute-start(bf16[256,256]{1,0:T(8,128)(2,1)} %param.10), channel_id=1, source_target_pairs={{0,4},{1,5},{2,6},{3,7},{4,0},{5,1},{6,2},{7,3},{8,12},{9,13},{10,... | collective-permute-start | bytes 393224 | tf_op jit(solution)/shard_map/ppermute | solution.py:25
  61.5 33.9 %collective-permute-start.2 = (bf16[256,256]{1,0:T(8,128)(2,1)}, bf16[256,256]{1,0:T(8,128)(2,1)S(1)}, u32[]{:S(2)}, u32[]{:S(2)}) collective-permute-start(bf16[256,256]{1,0:T(8,128)(2,1)} %param.10), channel_id=1, source_target_pairs={{0,3},{1,4},{2,5},{3,6},{4,7},{5,0},{6,1},{7,2},{8,11},{9,12},{10,... | collective-permute-start | bytes 393224 | tf_op jit(solution)/shard_map/ppermute | solution.py:25
  67.0 24.2 %collective-permute-start.1 = (bf16[256,256]{1,0:T(8,128)(2,1)}, bf16[256,256]{1,0:T(8,128)(2,1)S(1)}, u32[]{:S(2)}, u32[]{:S(2)}) collective-permute-start(bf16[256,256]{1,0:T(8,128)(2,1)} %param.10), channel_id=1, source_target_pairs={{0,2},{1,3},{2,4},{3,5},{4,6},{5,7},{6,0},{7,1},{8,10},{9,11},{10,... | collective-permute-start | bytes 393224 | tf_op jit(solution)/shard_map/ppermute | solution.py:25
  71.0 18.0 %collective-permute-start = (bf16[256,256]{1,0:T(8,128)(2,1)}, bf16[256,256]{1,0:T(8,128)(2,1)S(1)}, u32[]{:S(2)}, u32[]{:S(2)}) collective-permute-start(bf16[256,256]{1,0:T(8,128)(2,1)} %param.10), channel_id=1, source_target_pairs={{0,1},{1,2},{2,3},{3,4},{4,5},{5,6},{6,7},{7,0},{8,9},{9,10},{10,1... | collective-permute-start | bytes 393224 | tf_op jit(solution)/shard_map/ppermute | solution.py:25
  78.1 38.8 %copy-start.2 = (f32[256,64]{0,1:T(8,128)}, f32[256,64]{0,1:T(8,128)S(1)}, u32[]{:S(2)}) copy-start(f32[256,64]{0,1:T(8,128)S(1)} %get-tuple-element.10) | copy-start | bytes 196612
  78.1 38.8 %copy-start.4 = (f32[256,64]{0,1:T(8,128)}, f32[256,64]{0,1:T(8,128)S(1)}, u32[]{:S(2)}) copy-start(f32[256,64]{0,1:T(8,128)S(1)} %get-tuple-element.11) | copy-start | bytes 196612
  89.0 13.1 %collective-permute-start.6 = (bf16[256,256]{1,0:T(8,128)(2,1)}, bf16[256,256]{1,0:T(8,128)(2,1)S(1)}, u32[]{:S(2)}, u32[]{:S(2)}) collective-permute-start(bf16[256,256]{1,0:T(8,128)(2,1)} %param.10), channel_id=1, source_target_pairs={{0,7},{1,0},{2,1},{3,2},{4,3},{5,4},{6,5},{7,6},{8,15},{9,8},{10,9... | collective-permute-start | bytes 393224 | tf_op jit(solution)/shard_map/ppermute | solution.py:25
  91.2 10.8 %collective-permute-start.5 = (bf16[256,256]{1,0:T(8,128)(2,1)}, bf16[256,256]{1,0:T(8,128)(2,1)S(1)}, u32[]{:S(2)}, u32[]{:S(2)}) collective-permute-start(bf16[256,256]{1,0:T(8,128)(2,1)} %param.10), channel_id=1, source_target_pairs={{0,6},{1,7},{2,0},{3,1},{4,2},{5,3},{6,4},{7,5},{8,14},{9,15},{10,... | collective-permute-start | bytes 393224 | tf_op jit(solution)/shard_map/ppermute | solution.py:25
  117.7 52.6 %collective-permute-start.22 = (bf16[256,2,256]{0,2,1:T(8,128)(2,1)}, bf16[256,2,256]{0,2,1:T(8,128)(2,1)}, u32[]{:S(2)}, u32[]{:S(2)}) collective-permute-start(bf16[256,2,256]{0,2,1:T(8,128)(2,1)} %pad_maximum_fusion), channel_id=1, source_target_pairs={{0,8},{8,16},{16,24},{24,32},{32,40},{40,48},{48,56},{56,64},{64,7... | collective-permute-start | bytes 786440 | tf_op jit(solution)/shard_map/ppermute | solution.py:18
  119.9 49.5 %collective-permute-start.21 = (bf16[256,2,256]{0,2,1:T(8,128)(2,1)}, bf16[256,2,256]{0,2,1:T(8,128)(2,1)}, u32[]{:S(2)}, u32[]{:S(2)}) collective-permute-start(bf16[256,2,256]{0,2,1:T(8,128)(2,1)} %pad_maximum_fusion), channel_id=1, source_target_pairs={{0,16},{8,24},{16,32},{24,40},{32,48},{40,56},{48,64},{56,72},{64,... | collective-permute-start | bytes 786440 | tf_op jit(solution)/shard_map/ppermute | solution.py:18
  125.1 34.8 %collective-permute-start.17 = (bf16[256,2,256]{0,2,1:T(8,128)(2,1)}, bf16[256,2,256]{0,2,1:T(8,128)(2,1)}, u32[]{:S(2)}, u32[]{:S(2)}) collective-permute-start(bf16[256,2,256]{0,2,1:T(8,128)(2,1)} %pad_maximum_fusion), channel_id=1, source_target_pairs={{0,48},{8,56},{16,64},{24,72},{32,80},{40,88},{48,96},{56,104},{64... | collective-permute-start | bytes 786440 | tf_op jit(solution)/shard_map/ppermute | solution.py:18
  127.1 24.9 %collective-permute-start.16 = (bf16[256,2,256]{0,2,1:T(8,128)(2,1)}, bf16[256,2,256]{0,2,1:T(8,128)(2,1)}, u32[]{:S(2)}, u32[]{:S(2)}) collective-permute-start(bf16[256,2,256]{0,2,1:T(8,128)(2,1)} %pad_maximum_fusion), channel_id=1, source_target_pairs={{0,56},{8,64},{16,72},{24,80},{32,88},{40,96},{48,104},{56,112},{6... | collective-permute-start | bytes 786440 | tf_op jit(solution)/shard_map/ppermute | solution.py:18
  130.7 18.3 %collective-permute-start.15 = (bf16[256,2,256]{0,2,1:T(8,128)(2,1)}, bf16[256,2,256]{0,2,1:T(8,128)(2,1)}, u32[]{:S(2)}, u32[]{:S(2)}) collective-permute-start(bf16[256,2,256]{0,2,1:T(8,128)(2,1)} %pad_maximum_fusion), channel_id=1, source_target_pairs={{0,64},{8,72},{16,80},{24,88},{32,96},{40,104},{48,112},{56,120},{... | collective-permute-start | bytes 786440 | tf_op jit(solution)/shard_map/ppermute | solution.py:18
  137.0 1.7 copy-start.5
  138.7 34.0 %copy-start.1 = (pred[256,2304]{1,0:T(8,128)(4,1)S(1)}, pred[256,2304]{1,0:T(8,128)(4,1)}, u32[]{:S(2)}) copy-start(pred[256,2304]{1,0:T(8,128)(4,1)} %compare_and_fusion) | copy-start | bytes 1769476
  149.0 17.5 %collective-permute-start.18 = (bf16[256,2,256]{0,2,1:T(8,128)(2,1)}, bf16[256,2,256]{0,2,1:T(8,128)(2,1)S(1)}, u32[]{:S(2)}, u32[]{:S(2)}) collective-permute-start(bf16[256,2,256]{0,2,1:T(8,128)(2,1)} %pad_maximum_fusion), channel_id=1, source_target_pairs={{0,40},{8,48},{16,56},{24,64},{32,72},{40,80},{48,88},{56,96},{64,... | collective-permute-start | bytes 786440 | tf_op jit(solution)/shard_map/ppermute | solution.py:18
  151.9 14.7 %collective-permute-start.19 = (bf16[256,2,256]{0,2,1:T(8,128)(2,1)}, bf16[256,2,256]{0,2,1:T(8,128)(2,1)S(1)}, u32[]{:S(2)}, u32[]{:S(2)}) collective-permute-start(bf16[256,2,256]{0,2,1:T(8,128)(2,1)} %pad_maximum_fusion), channel_id=1, source_target_pairs={{0,32},{8,40},{16,48},{24,56},{32,64},{40,72},{48,80},{56,88},{64,... | collective-permute-start | bytes 786440 | tf_op jit(solution)/shard_map/ppermute | solution.py:18
  160.0 9.4 %collective-permute-start.20 = (bf16[256,2,256]{0,2,1:T(8,128)(2,1)}, bf16[256,2,256]{0,2,1:T(8,128)(2,1)S(1)}, u32[]{:S(2)}, u32[]{:S(2)}) collective-permute-start(bf16[256,2,256]{0,2,1:T(8,128)(2,1)} %pad_maximum_fusion), channel_id=1, source_target_pairs={{0,24},{8,32},{16,40},{24,48},{32,56},{40,64},{48,72},{56,80},{64,... | collective-permute-start | bytes 786440 | tf_op jit(solution)/shard_map/ppermute | solution.py:18
  185.0 132.2 %reduce-scatter.2.cloned.1.call-start = ((), (), s32[]{:S(2)}) async-start(), calls=%async_computation.3 | async-start | bytes 1179648 | tf_op jit(solution)/shard_map/reduce_scatter | solution.py:140
  272.3 4.7 %copy-start.8 = (s32[16]{0:T(128)S(1)}, s32[16]{0:T(128)}, u32[]{:S(2)}) copy-start(s32[16]{0:T(128)} %param.12) | copy-start | bytes 196
  278.6 40.3 %copy-start = (bf16[2,16,16,256]{3,2,1,0:T(8,128)(2,1)}, bf16[2,16,16,256]{3,2,1,0:T(8,128)(2,1)S(1)}, u32[]{:S(2)}) copy-start(bf16[2,16,16,256]{3,2,1,0:T(8,128)(2,1)S(1)} %scatter_fusion) | copy-start | bytes 786436
  (3 other events, 3.8 us)
Sparse Core Ops, SparseCore 0:
  13.2 94.9 all-gather.1
  185.1 82.8 all-reduce.1
  277.1 40.0 reduce-scatter.1

commit v3 on v1

--- a/solution.py
+++ b/solution.py
@@ -16,6 +16,23 @@
     count = lax.axis_size(axis)
     first, last = (max(0, -steps), min(count, count - steps))
     return lax.ppermute(value, axis, [(source, source + steps) for source in range(first, last)])
+
+
+def swap_gather(value, axis):
+    count = lax.axis_size(axis)
+    rows, cols = value.shape
+    copies = jnp.broadcast_to(value[None], (count, rows, cols))
+    got = lax.all_to_all(copies, axis, 0, 0, tiled=True)
+    return jnp.moveaxis(got, 0, 1).reshape(rows, cols * count)
+
+
+def swap_sum(value, axis):
+    count = lax.axis_size(axis)
+    rows, width = value.shape
+    cols = width // count
+    pieces = jnp.moveaxis(value.reshape(rows, count, cols), 1, 0)
+    got = lax.all_to_all(pieces, axis, 0, 0, tiled=True)
+    return jnp.sum(got.astype(jnp.float32), axis=0)
 
 
 def norm_rows(source):
@@ -75,7 +92,7 @@
     earlier = same & (window_index[None, :] < lead + local_index[:, None])
     positions = jnp.sum(earlier.astype(jnp.int32), axis=1)
 
-    whole = lax.all_gather(hidden_in, "narrow", axis=1, tiled=True)
+    whole = swap_gather(hidden_in, "narrow")
     normed = norm_rows(whole)
     local_width = attn_width
     head_count = local_width // HEAD_DIM
@@ -88,13 +105,15 @@
         jnp.bfloat16
     )
     values = v_proj.astype(jnp.bfloat16).reshape(tok_rows, head_count, HEAD_DIM)
+    packed = jnp.concatenate([keys_rot, values], axis=2)
     blocks = []
     for step_back in range(REACH, 0, -1):
-        blocks.append(shifted((keys_rot, values), "wide", step_back))
-    blocks.append((keys_rot, values))
+        blocks.append(shifted(packed, "wide", step_back))
+    blocks.append(packed)
     score_scale = HEAD_DIM ** (-0.5)
-    key_all = jnp.concatenate([member[0] for member in blocks], axis=0)
-    value_all = jnp.concatenate([member[1] for member in blocks], axis=0)
+    kv_all = jnp.concatenate(blocks, axis=0)
+    key_all = kv_all[:, :, :HEAD_DIM]
+    value_all = kv_all[:, :, HEAD_DIM:]
     scores = (
         jnp.einsum("qhd,khd->hqk", queries, key_all, preferred_element_type=jnp.float32)
         * score_scale
@@ -108,11 +127,9 @@
     attn_terms = lax.dot_general(
         attended, wo_t, (((1,), (1,)), ((), ())), preferred_element_type=jnp.float32
     )
-    attn_sum = lax.psum_scatter(
-        attn_terms.astype(jnp.bfloat16), "narrow", scatter_dimension=1, tiled=True
-    ).astype(jnp.float32)
+    attn_sum = swap_sum(attn_terms.astype(jnp.bfloat16), "narrow")
     first_res = (hidden_in.astype(jnp.float32) + attn_sum).astype(jnp.bfloat16)
-    whole_two = lax.all_gather(first_res, "narrow", axis=1, tiled=True)
+    whole_two = swap_gather(first_res, "narrow")
     normed_two = norm_rows(whole_two)
 
     gate_proj = add_rows(normed_two, wg_all)
@@ -121,9 +138,7 @@
     down_terms = lax.dot_general(
         hidden, wd_t, (((1,), (1,)), ((), ())), preferred_element_type=jnp.float32
     )
-    down_sum = lax.psum_scatter(
-        down_terms.astype(jnp.bfloat16), "narrow", scatter_dimension=1, tiled=True
-    ).astype(jnp.float32)
+    down_sum = swap_sum(down_terms.astype(jnp.bfloat16), "narrow")
     result = (first_res.astype(jnp.float32) + down_sum).astype(jnp.bfloat16)
     page_count = tok_rows // PAGE
     slots = page_table - wide_rank * page_count

time: 367 us -> 297 us (0.81)
  the two profiles are of different devices: /device:TPU:6 before, /device:TPU:64 now
where the time goes in v3:
time: 297 us; the launch traced here: 295 us
  waiting for transfers between devices  92.1 us (31%)
  starting transfers between devices  73.3 us (25%)
  blocking collectives  68.3 us (23%)
  local copies, waits for them, and re-layouts  21.3 us (7%)
  matrix products  18.1 us (6%)
  between operations  14.7 us (5%)
  other arithmetic  7.17 us (2%)
    ppermute x16, starting transfers between devices, shifted(): lax.ppermute(value, axis, [(source, source + steps) for source in range(f...  62.6 us
    all_gather x1, waiting for transfers between devices, per_device(): lax.all_gather(jnp.concatenate(pieces, axis=1), 'wide', axis=0, tiled=True)  38.1 us
    all_to_all x1, blocking collectives, swap_sum(): got = lax.all_to_all(pieces, axis, 0, 0, tiled=True)  36.6 us
    all_to_all x1, blocking collectives, swap_gather(): got = lax.all_to_all(copies, axis, 0, 0, tiled=True)  31.7 us
    all_to_all x1, waiting for transfers between devices, swap_sum(): got = lax.all_to_all(pieces, axis, 0, 0, tiled=True)  27.1 us
    ppermute x16, waiting for transfers between devices, shifted(): lax.ppermute(value, axis, [(source, source + steps) for source in range(f...  20.7 us
    unnamed x34, local copies, waits for them, and re-layouts  10.4 us
    all_to_all x1, starting transfers between devices, swap_gather(): got = lax.all_to_all(copies, axis, 0, 0, tiled=True)  7.12 us
  transfers between devices with their start and end apart: 19, of which 8 were waited for; matrix products, arithmetic and copies ran while one was open for 5% of the time, Pallas kernels for 0%

profile of v3, /device:TPU:64, one launch (start us, length us, event | category | flops | bytes accessed | tf_op | source)
XLA Modules:
  0.0 295.0 jit_solution(77051576578544907)
XLA Ops:
  13.1 1.9 collective-permute-start.7
  15.0 3.4 %collective-permute-start.6 = (s32[256]{0:T(256)}, s32[256]{0:T(256)S(1)}, u32[]{:S(2)}, u32[]{:S(2)}) collective-permute-start(s32[256]{0:T(256)} %param.11), channel_id=1, source_target_pairs={{0,16},{8,24},{16,32},{24,40},{32,48},{40,56},{48,64},{56,72},{64,... | collective-permute-start | bytes 3080 | tf_op jit(solution)/shard_map/ppermute | solution.py:18
  18.4 4.0 %collective-permute-start.5 = (s32[256]{0:T(256)}, s32[256]{0:T(256)S(1)}, u32[]{:S(2)}, u32[]{:S(2)}) collective-permute-start(s32[256]{0:T(256)} %param.11), channel_id=1, source_target_pairs={{0,24},{8,32},{16,40},{24,48},{32,56},{40,64},{48,72},{56,80},{64,... | collective-permute-start | bytes 3080 | tf_op jit(solution)/shard_map/ppermute | solution.py:18
  22.4 5.7 %collective-permute-start.4 = (s32[256]{0:T(256)}, s32[256]{0:T(256)S(1)}, u32[]{:S(2)}, u32[]{:S(2)}) collective-permute-start(s32[256]{0:T(256)} %param.11), channel_id=1, source_target_pairs={{0,32},{8,40},{16,48},{24,56},{32,64},{40,72},{48,80},{56,88},{64,... | collective-permute-start | bytes 3080 | tf_op jit(solution)/shard_map/ppermute | solution.py:18
  28.2 4.3 %collective-permute-start = (s32[256]{0:T(256)}, s32[256]{0:T(256)S(1)}, u32[]{:S(2)}, u32[]{:S(2)}) collective-permute-start(s32[256]{0:T(256)} %param.11), channel_id=1, source_target_pairs={{0,64},{8,72},{16,80},{24,88},{32,96},{40,104},{48,112},{56,120},{... | collective-permute-start | bytes 3080 | tf_op jit(solution)/shard_map/ppermute | solution.py:18
  32.5 1.9 broadcast_in_dim.37
  34.4 7.1 %all-to-all-start = ((bf16[8,256,256]{2,1,0:T(8,128)(2,1)}), bf16[8,256,256]{2,1,0:T(8,128)(2,1)S(1)}, u32[]{:S(2)}, u32[]{:S(2)}) async-start(bf16[8,256,256]{2,1,0:T(8,128)(2,1)} %broadcast_in_dim.37), calls=%async_computation | async-start | bytes 2097152 | tf_op jit(solution)/shard_map/all_to_all | solution.py:25
  41.6 4.9 %collective-permute-start.1 = (s32[256]{0:T(256)S(1)}, s32[256]{0:T(256)S(1)}, u32[]{:S(2)}, u32[]{:S(2)}) collective-permute-start(s32[256]{0:T(256)S(1)} %copy-done.8), channel_id=1, source_target_pairs={{0,56},{8,64},{16,72},{24,80},{32,88},{40,96},{48,104},{56,112},{6... | collective-permute-start | bytes 3080 | tf_op jit(solution)/shard_map/ppermute | solution.py:18
  47.8 4.7 %collective-permute-start.2 = (s32[256]{0:T(256)S(1)}, s32[256]{0:T(256)S(1)}, u32[]{:S(2)}, u32[]{:S(2)}) collective-permute-start(s32[256]{0:T(256)S(1)} %copy-done.8), channel_id=1, source_target_pairs={{0,48},{8,56},{16,64},{24,72},{32,80},{40,88},{48,96},{56,104},{64... | collective-permute-start | bytes 3080 | tf_op jit(solution)/shard_map/ppermute | solution.py:18
  54.2 2.3 collective-permute-start.3
  56.5 3.5 %collective-permute-done.3 = s32[256]{0:T(256)S(1)} collective-permute-done((s32[256]{0:T(256)S(1)}, s32[256]{0:T(256)S(1)}, u32[]{:S(2)}, u32[]{:S(2)}) %collective-permute-start.3) | collective-permute-done | bytes 1056 | tf_op jit(solution)/shard_map/ppermute | solution.py:18
  63.3 6.1 %all-to-all-done = bf16[8,256,256]{2,1,0:T(8,128)(2,1)S(1)} async-done(((bf16[8,256,256]{2,1,0:T(8,128)(2,1)}), bf16[8,256,256]{2,1,0:T(8,128)(2,1)S(1)}, u32[]{:S(2)}, u32[]{:S(2)}) %all-to-all-start) | async-done | bytes 1048608 | tf_op jit(solution)/shard_map/all_to_all | solution.py:25
  71.1 38.1 %all-gather.2.cloned.1.call-done = bf16[2048,2560]{1,0:T(8,128)(2,1)} async-done(((bf16[32,2560]{1,0:T(8,128)(2,1)}), bf16[2048,2560]{1,0:T(8,128)(2,1)}) %all-gather.2.cloned.1.call-update) | async-done | bytes 10485776 | tf_op jit(solution)/shard_map/all_gather | solution.py:76
  111.0 2.7 slice_bitcast_fusion
  116.4 2.2 collective-permute-start.15
  118.6 2.1 collective-permute-start.14
  120.7 4.8 %collective-permute-start.10 = (bf16[256,2,256]{0,2,1:T(8,128)(2,1)}, bf16[256,2,256]{0,2,1:T(8,128)(2,1)}, u32[]{:S(2)}, u32[]{:S(2)}) collective-permute-start(bf16[256,2,256]{0,2,1:T(8,128)(2,1)} %pad_maximum_fusion), channel_id=1, source_target_pairs={{0,48},{8,56},{16,64},{24,72},{32,80},{40,88},{48,96},{56,104},{64... | collective-permute-start | bytes 786440 | tf_op jit(solution)/shard_map/ppermute | solution.py:18
  125.5 4.3 %collective-permute-start.9 = (bf16[256,2,256]{0,2,1:T(8,128)(2,1)}, bf16[256,2,256]{0,2,1:T(8,128)(2,1)}, u32[]{:S(2)}, u32[]{:S(2)}) collective-permute-start(bf16[256,2,256]{0,2,1:T(8,128)(2,1)} %pad_maximum_fusion), channel_id=1, source_target_pairs={{0,56},{8,64},{16,72},{24,80},{32,88},{40,96},{48,104},{56,112},{6... | collective-permute-start | bytes 786440 | tf_op jit(solution)/shard_map/ppermute | solution.py:18
  129.8 2.4 collective-permute-start.8
  133.8 6.2 %collective-permute-done.8 = bf16[256,2,256]{0,2,1:T(8,128)(2,1)} collective-permute-done((bf16[256,2,256]{0,2,1:T(8,128)(2,1)}, bf16[256,2,256]{0,2,1:T(8,128)(2,1)}, u32[]{:S(2)}, u32[]{:S(2)}) %collective-permute-start.8) | collective-permute-done | bytes 262176 | tf_op jit(solution)/shard_map/ppermute | solution.py:18
  140.0 6.7 %collective-permute-start.11 = (bf16[256,2,256]{0,2,1:T(8,128)(2,1)}, bf16[256,2,256]{0,2,1:T(8,128)(2,1)S(1)}, u32[]{:S(2)}, u32[]{:S(2)}) collective-permute-start(bf16[256,2,256]{0,2,1:T(8,128)(2,1)} %pad_maximum_fusion), channel_id=1, source_target_pairs={{0,40},{8,48},{16,56},{24,64},{32,72},{40,80},{48,88},{56,96},{64,... | collective-permute-start | bytes 786440 | tf_op jit(solution)/shard_map/ppermute | solution.py:18
  147.7 2.6 collective-permute-start.12
  151.3 6.2 %collective-permute-start.13 = (bf16[256,2,256]{0,2,1:T(8,128)(2,1)}, bf16[256,2,256]{0,2,1:T(8,128)(2,1)S(1)}, u32[]{:S(2)}, u32[]{:S(2)}) collective-permute-start(bf16[256,2,256]{0,2,1:T(8,128)(2,1)} %pad_maximum_fusion), channel_id=1, source_target_pairs={{0,24},{8,32},{16,40},{24,48},{32,56},{40,64},{48,72},{56,80},{64,... | collective-permute-start | bytes 786440 | tf_op jit(solution)/shard_map/ppermute | solution.py:18
  158.6 8.1 %collective-permute-done.13 = bf16[256,2,256]{0,2,1:T(8,128)(2,1)S(1)} collective-permute-done((bf16[256,2,256]{0,2,1:T(8,128)(2,1)}, bf16[256,2,256]{0,2,1:T(8,128)(2,1)S(1)}, u32[]{:S(2)}, u32[]{:S(2)}) %collective-permute-start.13) | collective-permute-done | bytes 262176 | tf_op jit(solution)/shard_map/ppermute | solution.py:18
  168.8 4.6 %fusion.41 = (f32[2,256]{1,0:T(2,128)S(1)}, f32[2,256,2304]{2,1,0:T(8,128)}) fusion(pred[256,2304]{1,0:T(8,128)(4,1)S(1)} %copy-done.1, bf16[2304,2,256]{0,2,1:T(8,128)(2,1)S(1)} %constant_dynamic-update-slice_fusion.8, bf16[256,2,64]{0,2,1:T(8,128)(2,1)S(1)} %get-tuple-element.5, bf16[256,2,64]{0,2,1:T(8,128)(2,1)S(1)} %get-tuple-element.4), kind=kOutput, calls=%fused_computation.100 | convolution fusion | flops 308152576 | bytes 7211008 | tf_op jit(solution)/shard_map/sub | solution.py:123
  173.3 3.3 %fusion.25 = bf16[2,128,256]{2,1,0:T(8,128)(2,1)S(1)} fusion(f32[2,256,2304]{2,1,0:T(8,128)} %get-tuple-element.11, f32[2,256]{1,0:T(2,128)S(1)} %get-tuple-element.10, bf16[2304,2,256]{0,2,1:T(8,128)(2,1)S(1)} %constant_dynamic-update-slice_fusion.8), kind=kOutput, calls=%fused_computation.37 | convolution fusion | flops 304414720 | bytes 6031360 | tf_op jit(solution)/shard_map/hqk,khd->qhd/dot_general | solution.py:125
  178.5 36.6 %all_to_all.20 = bf16[8,256,256]{2,1,0:T(8,128)(2,1)S(1)} all-to-all(bf16[8,256,256]{2,1,0:T(8,128)(2,1)S(1)} %bitcast.67), channel_id=1, replica_groups=mesh['wide'=64,'narrow'=8] {'narrow'}, dimensions={0} | all-to-all | bytes 2097152 | tf_op jit(solution)/shard_map/all_to_all | solution.py:34
  215.4 31.7 %all_to_all.21 = bf16[8,256,256]{1,2,0:T(8,128)(2,1)S(1)} all-to-all(bf16[8,256,256]{1,2,0:T(8,128)(2,1)S(1)} %broadcast_in_dim.74), channel_id=1, replica_groups=mesh['wide'=64,'narrow'=8] {'narrow'}, dimensions={0} | all-to-all | bytes 2097152 | tf_op jit(solution)/shard_map/all_to_all | solution.py:25
  248.0 2.3 fusion.9
  250.3 3.6 %convolution_convert_fusion = bf16[256,2048]{1,0:T(8,128)(2,1)S(1)} fusion(bf16[2048,2560]{1,0:T(8,128)(2,1)} %all-gather.2.cloned.1.call-done, bf16[256,2048]{0,1:T(8,128)(2,1)S(1)} %fusion.12, f32[256,512]{1,0:T(8,128)S(1)} %fusion.9), kind=kOutput, calls=%fused_computation.10 | convolution fusion | flops 1075052544 | bytes 6815744 | tf_op jit(solution)/shard_map/dot_general | solution.py:138
  255.0 3.6 %all-to-all-start.3 = ((bf16[8,256,256]{2,1,0:T(8,128)(2,1)}), bf16[8,256,256]{2,1,0:T(8,128)(2,1)S(1)}, u32[]{:S(2)}, u32[]{:S(2)}) async-start(bf16[8,256,256]{2,1,0:T(8,128)(2,1)} %bitcast.58), calls=%async_computation.3 | async-start | bytes 2097152 | tf_op jit(solution)/shard_map/all_to_all | solution.py:34
  260.2 27.1 %all-to-all-done.3 = bf16[8,256,256]{2,1,0:T(8,128)(2,1)S(1)} async-done(((bf16[8,256,256]{2,1,0:T(8,128)(2,1)}), bf16[8,256,256]{2,1,0:T(8,128)(2,1)S(1)}, u32[]{:S(2)}, u32[]{:S(2)}) %all-to-all-start.3) | async-done | bytes 1048608 | tf_op jit(solution)/shard_map/all_to_all | solution.py:34
  (105 shorter events, 31.1 us)
Async XLA Ops:
  7.2 34.4 %copy-start.8 = (s32[256]{0:T(256)S(1)}, s32[256]{0:T(256)}, u32[]{:S(2)}) copy-start(s32[256]{0:T(256)} %param.11) | copy-start | bytes 3076
  7.2 102.0 %all-gather.2.cloned.1.call-start = ((), (), s32[]{:S(2)}) async-start(), calls=%async_computation.4 | async-start | bytes 10649600 | tf_op jit(solution)/shard_map/all_gather | solution.py:76
  12.4 0.7 copy-start.7
  13.1 47.0 %collective-permute-start.7 = (s32[256]{0:T(256)}, s32[256]{0:T(256)S(1)}, u32[]{:S(2)}, u32[]{:S(2)}) collective-permute-start(s32[256]{0:T(256)} %param.11), channel_id=1, source_target_pairs={{0,8},{8,16},{16,24},{24,32},{32,40},{40,48},{48,56},{56,64},{64,7... | collective-permute-start | bytes 3080 | tf_op jit(solution)/shard_map/ppermute | solution.py:18
  15.0 45.0 %collective-permute-start.6 = (s32[256]{0:T(256)}, s32[256]{0:T(256)S(1)}, u32[]{:S(2)}, u32[]{:S(2)}) collective-permute-start(s32[256]{0:T(256)} %param.11), channel_id=1, source_target_pairs={{0,16},{8,24},{16,32},{24,40},{32,48},{40,56},{48,64},{56,72},{64,... | collective-permute-start | bytes 3080 | tf_op jit(solution)/shard_map/ppermute | solution.py:18
  18.4 41.6 %collective-permute-start.5 = (s32[256]{0:T(256)}, s32[256]{0:T(256)S(1)}, u32[]{:S(2)}, u32[]{:S(2)}) collective-permute-start(s32[256]{0:T(256)} %param.11), channel_id=1, source_target_pairs={{0,24},{8,32},{16,40},{24,48},{32,56},{40,64},{48,72},{56,80},{64,... | collective-permute-start | bytes 3080 | tf_op jit(solution)/shard_map/ppermute | solution.py:18
  22.4 37.5 %collective-permute-start.4 = (s32[256]{0:T(256)}, s32[256]{0:T(256)S(1)}, u32[]{:S(2)}, u32[]{:S(2)}) collective-permute-start(s32[256]{0:T(256)} %param.11), channel_id=1, source_target_pairs={{0,32},{8,40},{16,48},{24,56},{32,64},{40,72},{48,80},{56,88},{64,... | collective-permute-start | bytes 3080 | tf_op jit(solution)/shard_map/ppermute | solution.py:18
  28.2 13.4 %collective-permute-start = (s32[256]{0:T(256)}, s32[256]{0:T(256)S(1)}, u32[]{:S(2)}, u32[]{:S(2)}) collective-permute-start(s32[256]{0:T(256)} %param.11), channel_id=1, source_target_pairs={{0,64},{8,72},{16,80},{24,88},{32,96},{40,104},{48,112},{56,120},{... | collective-permute-start | bytes 3080 | tf_op jit(solution)/shard_map/ppermute | solution.py:18
  34.4 35.0 %all-to-all-start = ((bf16[8,256,256]{2,1,0:T(8,128)(2,1)}), bf16[8,256,256]{2,1,0:T(8,128)(2,1)S(1)}, u32[]{:S(2)}, u32[]{:S(2)}) async-start(bf16[8,256,256]{2,1,0:T(8,128)(2,1)} %broadcast_in_dim.37), calls=%async_computation | async-start | bytes 2097152 | tf_op jit(solution)/shard_map/all_to_all | solution.py:25
  41.6 6.2 %collective-permute-start.1 = (s32[256]{0:T(256)S(1)}, s32[256]{0:T(256)S(1)}, u32[]{:S(2)}, u32[]{:S(2)}) collective-permute-start(s32[256]{0:T(256)S(1)} %copy-done.8), channel_id=1, source_target_pairs={{0,56},{8,64},{16,72},{24,80},{32,88},{40,96},{48,104},{56,112},{6... | collective-permute-start | bytes 3080 | tf_op jit(solution)/shard_map/ppermute | solution.py:18
  47.8 6.3 %collective-permute-start.2 = (s32[256]{0:T(256)S(1)}, s32[256]{0:T(256)S(1)}, u32[]{:S(2)}, u32[]{:S(2)}) collective-permute-start(s32[256]{0:T(256)S(1)} %copy-done.8), channel_id=1, source_target_pairs={{0,48},{8,56},{16,64},{24,72},{32,80},{40,88},{48,96},{56,104},{64... | collective-permute-start | bytes 3080 | tf_op jit(solution)/shard_map/ppermute | solution.py:18
  54.2 5.8 %collective-permute-start.3 = (s32[256]{0:T(256)S(1)}, s32[256]{0:T(256)S(1)}, u32[]{:S(2)}, u32[]{:S(2)}) collective-permute-start(s32[256]{0:T(256)S(1)} %copy-done.8), channel_id=1, source_target_pairs={{0,40},{8,48},{16,56},{24,64},{32,72},{40,80},{48,88},{56,96},{64,... | collective-permute-start | bytes 3080 | tf_op jit(solution)/shard_map/ppermute | solution.py:18
  113.6 2.0 copy-start.2
  113.6 2.0 copy-start.4
  116.4 51.3 %collective-permute-start.15 = (bf16[256,2,256]{0,2,1:T(8,128)(2,1)}, bf16[256,2,256]{0,2,1:T(8,128)(2,1)}, u32[]{:S(2)}, u32[]{:S(2)}) collective-permute-start(bf16[256,2,256]{0,2,1:T(8,128)(2,1)} %pad_maximum_fusion), channel_id=1, source_target_pairs={{0,8},{8,16},{16,24},{24,32},{32,40},{40,48},{48,56},{56,64},{64,7... | collective-permute-start | bytes 786440 | tf_op jit(solution)/shard_map/ppermute | solution.py:18
  118.6 48.2 %collective-permute-start.14 = (bf16[256,2,256]{0,2,1:T(8,128)(2,1)}, bf16[256,2,256]{0,2,1:T(8,128)(2,1)}, u32[]{:S(2)}, u32[]{:S(2)}) collective-permute-start(bf16[256,2,256]{0,2,1:T(8,128)(2,1)} %pad_maximum_fusion), channel_id=1, source_target_pairs={{0,16},{8,24},{16,32},{24,40},{32,48},{40,56},{48,64},{56,72},{64,... | collective-permute-start | bytes 786440 | tf_op jit(solution)/shard_map/ppermute | solution.py:18
  120.7 30.6 %collective-permute-start.10 = (bf16[256,2,256]{0,2,1:T(8,128)(2,1)}, bf16[256,2,256]{0,2,1:T(8,128)(2,1)}, u32[]{:S(2)}, u32[]{:S(2)}) collective-permute-start(bf16[256,2,256]{0,2,1:T(8,128)(2,1)} %pad_maximum_fusion), channel_id=1, source_target_pairs={{0,48},{8,56},{16,64},{24,72},{32,80},{40,88},{48,96},{56,104},{64... | collective-permute-start | bytes 786440 | tf_op jit(solution)/shard_map/ppermute | solution.py:18
  125.5 22.2 %collective-permute-start.9 = (bf16[256,2,256]{0,2,1:T(8,128)(2,1)}, bf16[256,2,256]{0,2,1:T(8,128)(2,1)}, u32[]{:S(2)}, u32[]{:S(2)}) collective-permute-start(bf16[256,2,256]{0,2,1:T(8,128)(2,1)} %pad_maximum_fusion), channel_id=1, source_target_pairs={{0,56},{8,64},{16,72},{24,80},{32,88},{40,96},{48,104},{56,112},{6... | collective-permute-start | bytes 786440 | tf_op jit(solution)/shard_map/ppermute | solution.py:18
  129.8 10.2 %collective-permute-start.8 = (bf16[256,2,256]{0,2,1:T(8,128)(2,1)}, bf16[256,2,256]{0,2,1:T(8,128)(2,1)}, u32[]{:S(2)}, u32[]{:S(2)}) collective-permute-start(bf16[256,2,256]{0,2,1:T(8,128)(2,1)} %pad_maximum_fusion), channel_id=1, source_target_pairs={{0,64},{8,72},{16,80},{24,88},{32,96},{40,104},{48,112},{56,120},{... | collective-permute-start | bytes 786440 | tf_op jit(solution)/shard_map/ppermute | solution.py:18
  132.9 0.8 copy-start.3
  132.9 0.9 copy-start.5
  133.8 35.0 %copy-start.1 = (pred[256,2304]{1,0:T(8,128)(4,1)S(1)}, pred[256,2304]{1,0:T(8,128)(4,1)}, u32[]{:S(2)}) copy-start(pred[256,2304]{1,0:T(8,128)(4,1)} %compare_and_fusion) | copy-start | bytes 1769476
  140.0 18.5 %collective-permute-start.11 = (bf16[256,2,256]{0,2,1:T(8,128)(2,1)}, bf16[256,2,256]{0,2,1:T(8,128)(2,1)S(1)}, u32[]{:S(2)}, u32[]{:S(2)}) collective-permute-start(bf16[256,2,256]{0,2,1:T(8,128)(2,1)} %pad_maximum_fusion), channel_id=1, source_target_pairs={{0,40},{8,48},{16,56},{24,64},{32,72},{40,80},{48,88},{56,96},{64,... | collective-permute-start | bytes 786440 | tf_op jit(solution)/shard_map/ppermute | solution.py:18
  147.7 10.9 %collective-permute-start.12 = (bf16[256,2,256]{0,2,1:T(8,128)(2,1)}, bf16[256,2,256]{0,2,1:T(8,128)(2,1)S(1)}, u32[]{:S(2)}, u32[]{:S(2)}) collective-permute-start(bf16[256,2,256]{0,2,1:T(8,128)(2,1)} %pad_maximum_fusion), channel_id=1, source_target_pairs={{0,32},{8,40},{16,48},{24,56},{32,64},{40,72},{48,80},{56,88},{64,... | collective-permute-start | bytes 786440 | tf_op jit(solution)/shard_map/ppermute | solution.py:18
  151.3 15.4 %collective-permute-start.13 = (bf16[256,2,256]{0,2,1:T(8,128)(2,1)}, bf16[256,2,256]{0,2,1:T(8,128)(2,1)S(1)}, u32[]{:S(2)}, u32[]{:S(2)}) collective-permute-start(bf16[256,2,256]{0,2,1:T(8,128)(2,1)} %pad_maximum_fusion), channel_id=1, source_target_pairs={{0,24},{8,32},{16,40},{24,48},{32,56},{40,64},{48,72},{56,80},{64,... | collective-permute-start | bytes 786440 | tf_op jit(solution)/shard_map/ppermute | solution.py:18
  178.4 36.8 %copy-start.6 = (bf16[256,256]{1,0:T(8,128)(2,1)S(1)}, bf16[256,256]{1,0:T(8,128)(2,1)}, u32[]{:S(2)}) copy-start(bf16[256,256]{1,0:T(8,128)(2,1)} %param.10) | copy-start | bytes 393220
  254.0 4.6 %copy-start.9 = (s32[16]{0:T(128)S(1)}, s32[16]{0:T(128)}, u32[]{:S(2)}) copy-start(s32[16]{0:T(128)} %param.12) | copy-start | bytes 196
  255.0 32.3 %all-to-all-start.3 = ((bf16[8,256,256]{2,1,0:T(8,128)(2,1)}), bf16[8,256,256]{2,1,0:T(8,128)(2,1)S(1)}, u32[]{:S(2)}, u32[]{:S(2)}) async-start(bf16[8,256,256]{2,1,0:T(8,128)(2,1)} %bitcast.58), calls=%async_computation.3 | async-start | bytes 2097152 | tf_op jit(solution)/shard_map/all_to_all | solution.py:34
  260.1 28.0 %copy-start = (bf16[2,16,16,256]{3,2,1,0:T(8,128)(2,1)}, bf16[2,16,16,256]{3,2,1,0:T(8,128)(2,1)S(1)}, u32[]{:S(2)}) copy-start(bf16[2,16,16,256]{3,2,1,0:T(8,128)(2,1)S(1)} %scatter_fusion) | copy-start | bytes 786436
Sparse Core Ops, SparseCore 0:
  13.2 95.9 all-gather.1

commit v4 on v3

--- a/solution.py
+++ b/solution.py
@@ -106,12 +106,14 @@
     )
     values = v_proj.astype(jnp.bfloat16).reshape(tok_rows, head_count, HEAD_DIM)
     packed = jnp.concatenate([keys_rot, values], axis=2)
-    blocks = []
-    for step_back in range(REACH, 0, -1):
-        blocks.append(shifted(packed, "wide", step_back))
-    blocks.append(packed)
+    far = shifted(packed, "wide", REACH)
+    span = packed
+    steps = 1
+    while steps < REACH:
+        span = jnp.concatenate([shifted(span, "wide", steps), span], axis=0)
+        steps = steps * 2
     score_scale = HEAD_DIM ** (-0.5)
-    kv_all = jnp.concatenate(blocks, axis=0)
+    kv_all = jnp.concatenate([far, span], axis=0)
     key_all = kv_all[:, :, :HEAD_DIM]
     value_all = kv_all[:, :, HEAD_DIM:]
     scores = (

time: 297 us -> 293 us (0.987)
  the two profiles are of different devices: /device:TPU:64 before, /device:TPU:6 now
where the time goes in v4:
time: 293 us; the launch traced here: 292 us
  waiting for transfers between devices  110 us (38%)
  blocking collectives  62.9 us (21%)
  starting transfers between devices  58.8 us (20%)
  local copies, waits for them, and re-layouts  18.8 us (6%)
  matrix products  18.1 us (6%)
  between operations  14.7 us (5%)
  other arithmetic  8.4 us (3%)
    ppermute x12, starting transfers between devices, shifted(): lax.ppermute(value, axis, [(source, source + steps) for source in range(f...  48.1 us
    ppermute x12, waiting for transfers between devices, shifted(): lax.ppermute(value, axis, [(source, source + steps) for source in range(f...  40.5 us
    all_gather x1, waiting for transfers between devices, per_device(): lax.all_gather(jnp.concatenate(pieces, axis=1), 'wide', axis=0, tiled=True)  36.3 us
    all_to_all x1, blocking collectives, swap_sum(): got = lax.all_to_all(pieces, axis, 0, 0, tiled=True)  34 us
    all_to_all x1, blocking collectives, swap_gather(): got = lax.all_to_all(copies, axis, 0, 0, tiled=True)  28.9 us
    all_to_all x1, waiting for transfers between devices, swap_sum(): got = lax.all_to_all(pieces, axis, 0, 0, tiled=True)  23.6 us
    all_to_all x1, waiting for transfers between devices, swap_gather(): got = lax.all_to_all(copies, axis, 0, 0, tiled=True)  9.64 us
    unnamed x42, local copies, waits for them, and re-layouts  7.84 us
  transfers between devices with their start and end apart: 15, of which 9 were waited for; matrix products, arithmetic and copies ran while one was open for 4% of the time, Pallas kernels for 0%

profile of v4, /device:TPU:6, one launch (start us, length us, event | category | flops | bytes accessed | tf_op | source)
XLA Modules:
  0.0 291.6 jit_solution(15510039855682386233)
XLA Ops:
  13.1 1.9 collective-permute-start.7
  15.0 4.2 %collective-permute-start.6 = (s32[256]{0:T(256)}, s32[256]{0:T(256)S(1)}, u32[]{:S(2)}, u32[]{:S(2)}) collective-permute-start(s32[256]{0:T(256)} %param.11), channel_id=1, source_target_pairs={{0,16},{8,24},{16,32},{24,40},{32,48},{40,56},{48,64},{56,72},{64,... | collective-permute-start | bytes 3080 | tf_op jit(solution)/shard_map/ppermute | solution.py:18
  19.2 4.3 %collective-permute-start.5 = (s32[256]{0:T(256)}, s32[256]{0:T(256)S(1)}, u32[]{:S(2)}, u32[]{:S(2)}) collective-permute-start(s32[256]{0:T(256)} %param.11), channel_id=1, source_target_pairs={{0,24},{8,32},{16,40},{24,48},{32,56},{40,64},{48,72},{56,80},{64,... | collective-permute-start | bytes 3080 | tf_op jit(solution)/shard_map/ppermute | solution.py:18
  23.5 4.8 %collective-permute-start.4 = (s32[256]{0:T(256)}, s32[256]{0:T(256)S(1)}, u32[]{:S(2)}, u32[]{:S(2)}) collective-permute-start(s32[256]{0:T(256)} %param.11), channel_id=1, source_target_pairs={{0,32},{8,40},{16,48},{24,56},{32,64},{40,72},{48,80},{56,88},{64,... | collective-permute-start | bytes 3080 | tf_op jit(solution)/shard_map/ppermute | solution.py:18
  28.4 4.3 %collective-permute-start = (s32[256]{0:T(256)}, s32[256]{0:T(256)S(1)}, u32[]{:S(2)}, u32[]{:S(2)}) collective-permute-start(s32[256]{0:T(256)} %param.11), channel_id=1, source_target_pairs={{0,64},{8,72},{16,80},{24,88},{32,96},{40,104},{48,112},{56,120},{... | collective-permute-start | bytes 3080 | tf_op jit(solution)/shard_map/ppermute | solution.py:18
  32.7 2.0 broadcast_in_dim.37
  34.6 7.1 %all-to-all-start = ((bf16[8,256,256]{2,1,0:T(8,128)(2,1)}), bf16[8,256,256]{2,1,0:T(8,128)(2,1)S(1)}, u32[]{:S(2)}, u32[]{:S(2)}) async-start(bf16[8,256,256]{2,1,0:T(8,128)(2,1)} %broadcast_in_dim.37), calls=%async_computation | async-start | bytes 2097152 | tf_op jit(solution)/shard_map/all_to_all | solution.py:25
  41.8 2.3 collective-permute-start.1
  45.4 5.7 %collective-permute-start.2 = (s32[256]{0:T(256)S(1)}, s32[256]{0:T(256)S(1)}, u32[]{:S(2)}, u32[]{:S(2)}) collective-permute-start(s32[256]{0:T(256)S(1)} %copy-done.12), channel_id=1, source_target_pairs={{0,48},{8,56},{16,64},{24,72},{32,80},{40,88},{48,96},{56,104},{64... | collective-permute-start | bytes 3080 | tf_op jit(solution)/shard_map/ppermute | solution.py:18
  52.5 5.1 %collective-permute-start.3 = (s32[256]{0:T(256)S(1)}, s32[256]{0:T(256)S(1)}, u32[]{:S(2)}, u32[]{:S(2)}) collective-permute-start(s32[256]{0:T(256)S(1)} %copy-done.12), channel_id=1, source_target_pairs={{0,40},{8,48},{16,56},{24,64},{32,72},{40,80},{48,88},{56,96},{64,... | collective-permute-start | bytes 3080 | tf_op jit(solution)/shard_map/ppermute | solution.py:18
  60.5 9.6 %all-to-all-done = bf16[8,256,256]{2,1,0:T(8,128)(2,1)S(1)} async-done(((bf16[8,256,256]{2,1,0:T(8,128)(2,1)}), bf16[8,256,256]{2,1,0:T(8,128)(2,1)S(1)}, u32[]{:S(2)}, u32[]{:S(2)}) %all-to-all-start) | async-done | bytes 1048608 | tf_op jit(solution)/shard_map/all_to_all | solution.py:25
  71.9 36.3 %all-gather.2.cloned.1.call-done = bf16[2048,2560]{1,0:T(8,128)(2,1)} async-done(((bf16[32,2560]{1,0:T(8,128)(2,1)}), bf16[2048,2560]{1,0:T(8,128)(2,1)}) %all-gather.2.cloned.1.call-update) | async-done | bytes 10485776 | tf_op jit(solution)/shard_map/all_gather | solution.py:76
  108.1 1.7 convolution_convert_fusion.2
  110.0 2.7 slice_bitcast_fusion
  112.6 1.5 copy.38
  115.4 2.2 collective-permute-start.9
  117.6 5.7 %collective-permute-done.9 = bf16[256,2,256]{0,2,1:T(8,128)(2,1)S(1)} collective-permute-done((bf16[256,2,256]{0,2,1:T(8,128)(2,1)}, bf16[256,2,256]{0,2,1:T(8,128)(2,1)S(1)}, u32[]{:S(2)}, u32[]{:S(2)}) %collective-permute-start.9) | collective-permute-done | bytes 262176 | tf_op jit(solution)/shard_map/ppermute | solution.py:18
  123.4 7.3 %collective-permute-start.10 = (bf16[512,2,256]{0,2,1:T(8,128)(2,1)S(1)}, bf16[512,2,256]{0,2,1:T(8,128)(2,1)S(1)}, u32[]{:S(2)}, u32[]{:S(2)}) collective-permute-start(bf16[512,2,256]{0,2,1:T(8,128)(2,1)S(1)} %maximum_maximum_fusion.1), channel_id=1, source_target_pairs={{0,16},{8,24},{16,32},{24,40},{32,48},{40,56},{48,64},{56,72},{64,... | collective-permute-start | bytes 1572872 | tf_op jit(solution)/shard_map/ppermute | solution.py:18
  130.7 9.3 %collective-permute-done.10 = bf16[512,2,256]{0,2,1:T(8,128)(2,1)S(1)} collective-permute-done((bf16[512,2,256]{0,2,1:T(8,128)(2,1)S(1)}, bf16[512,2,256]{0,2,1:T(8,128)(2,1)S(1)}, u32[]{:S(2)}, u32[]{:S(2)}) %collective-permute-start.10) | collective-permute-done | bytes 524320 | tf_op jit(solution)/shard_map/ppermute | solution.py:18
  141.1 2.9 collective-permute-start.11
  144.0 1.6 compare_and_fusion
  145.7 3.1 %collective-permute-start.8 = (bf16[256,2,256]{0,2,1:T(8,128)(2,1)}, bf16[256,2,256]{0,2,1:T(8,128)(2,1)}, u32[]{:S(2)}, u32[]{:S(2)}) collective-permute-start(bf16[256,2,256]{0,2,1:T(8,128)(2,1)} %pad_maximum_fusion), channel_id=1, source_target_pairs={{0,64},{8,72},{16,80},{24,88},{32,96},{40,104},{48,112},{56,120},{... | collective-permute-start | bytes 786440 | tf_op jit(solution)/shard_map/ppermute | solution.py:18
  150.3 21.7 %collective-permute-done.8 = bf16[256,2,256]{0,2,1:T(8,128)(2,1)} collective-permute-done((bf16[256,2,256]{0,2,1:T(8,128)(2,1)}, bf16[256,2,256]{0,2,1:T(8,128)(2,1)}, u32[]{:S(2)}, u32[]{:S(2)}) %collective-permute-start.8) | collective-permute-done | bytes 262176 | tf_op jit(solution)/shard_map/ppermute | solution.py:18
  174.4 4.6 %fusion.41 = (f32[2,256]{1,0:T(2,128)S(1)}, f32[2,256,2304]{2,1,0:T(8,128)}) fusion(pred[256,2304]{1,0:T(8,128)(4,1)S(1)} %copy-done.5, bf16[2304,2,256]{0,2,1:T(8,128)(2,1)S(1)} %constant_dynamic-update-slice_fusion.7, bf16[256,2,64]{0,2,1:T(8,128)(2,1)S(1)} %get-tuple-element.5, bf16[256,2,64]{0,2,1:T(8,128)(2,1)S(1)} %get-tuple-element.4), kind=kOutput, calls=%fused_computation.98 | convolution fusion | flops 308152576 | bytes 7211008 | tf_op jit(solution)/shard_map/sub | solution.py:125
  178.9 3.3 %fusion.25 = bf16[2,128,256]{2,1,0:T(8,128)(2,1)S(1)} fusion(f32[2,256,2304]{2,1,0:T(8,128)} %get-tuple-element.11, f32[2,256]{1,0:T(2,128)S(1)} %get-tuple-element.10, bf16[2304,2,256]{0,2,1:T(8,128)(2,1)S(1)} %constant_dynamic-update-slice_fusion.7), kind=kOutput, calls=%fused_computation.37 | convolution fusion | flops 304414720 | bytes 6031360 | tf_op jit(solution)/shard_map/hqk,khd->qhd/dot_general | solution.py:127
  182.2 1.7 convolution_convert_fusion.1
  184.0 34.0 %all_to_all.20 = bf16[8,256,256]{2,1,0:T(8,128)(2,1)S(1)} all-to-all(bf16[8,256,256]{2,1,0:T(8,128)(2,1)S(1)} %bitcast.67), channel_id=1, replica_groups=mesh['wide'=64,'narrow'=8] {'narrow'}, dimensions={0} | all-to-all | bytes 2097152 | tf_op jit(solution)/shard_map/all_to_all | solution.py:34
  218.4 28.9 %all_to_all.21 = bf16[8,256,256]{1,2,0:T(8,128)(2,1)S(1)} all-to-all(bf16[8,256,256]{1,2,0:T(8,128)(2,1)S(1)} %broadcast_in_dim.74), channel_id=1, replica_groups=mesh['wide'=64,'narrow'=8] {'narrow'}, dimensions={0} | all-to-all | bytes 2097152 | tf_op jit(solution)/shard_map/all_to_all | solution.py:25
  248.2 2.3 fusion.9
  250.5 3.6 %convolution_convert_fusion = bf16[256,2048]{1,0:T(8,128)(2,1)S(1)} fusion(bf16[2048,2560]{1,0:T(8,128)(2,1)} %all-gather.2.cloned.1.call-done, bf16[256,2048]{0,1:T(8,128)(2,1)S(1)} %fusion.12, f32[256,512]{1,0:T(8,128)S(1)} %fusion.9), kind=kOutput, calls=%fused_computation.10 | convolution fusion | flops 1075052544 | bytes 6815744 | tf_op jit(solution)/shard_map/dot_general | solution.py:140
  255.2 3.6 %all-to-all-start.3 = ((bf16[8,256,256]{2,1,0:T(8,128)(2,1)}), bf16[8,256,256]{2,1,0:T(8,128)(2,1)S(1)}, u32[]{:S(2)}, u32[]{:S(2)}) async-start(bf16[8,256,256]{2,1,0:T(8,128)(2,1)} %bitcast.58), calls=%async_computation.3 | async-start | bytes 2097152 | tf_op jit(solution)/shard_map/all_to_all | solution.py:34
  260.3 23.6 %all-to-all-done.3 = bf16[8,256,256]{2,1,0:T(8,128)(2,1)S(1)} async-done(((bf16[8,256,256]{2,1,0:T(8,128)(2,1)}), bf16[8,256,256]{2,1,0:T(8,128)(2,1)S(1)}, u32[]{:S(2)}, u32[]{:S(2)}) %all-to-all-start.3) | async-done | bytes 1048608 | tf_op jit(solution)/shard_map/all_to_all | solution.py:34
  (107 shorter events, 24.1 us)
Async XLA Ops:
  7.2 34.6 %copy-start.12 = (s32[256]{0:T(256)S(1)}, s32[256]{0:T(256)}, u32[]{:S(2)}) copy-start(s32[256]{0:T(256)} %param.11) | copy-start | bytes 3076
  7.2 101.0 %all-gather.2.cloned.1.call-start = ((), (), s32[]{:S(2)}) async-start(), calls=%async_computation.4 | async-start | bytes 10649600 | tf_op jit(solution)/shard_map/all_gather | solution.py:76
  12.4 0.7 copy-start.11
  13.1 45.8 %collective-permute-start.7 = (s32[256]{0:T(256)}, s32[256]{0:T(256)S(1)}, u32[]{:S(2)}, u32[]{:S(2)}) collective-permute-start(s32[256]{0:T(256)} %param.11), channel_id=1, source_target_pairs={{0,8},{8,16},{16,24},{24,32},{32,40},{40,48},{48,56},{56,64},{64,7... | collective-permute-start | bytes 3080 | tf_op jit(solution)/shard_map/ppermute | solution.py:18
  15.0 43.9 %collective-permute-start.6 = (s32[256]{0:T(256)}, s32[256]{0:T(256)S(1)}, u32[]{:S(2)}, u32[]{:S(2)}) collective-permute-start(s32[256]{0:T(256)} %param.11), channel_id=1, source_target_pairs={{0,16},{8,24},{16,32},{24,40},{32,48},{40,56},{48,64},{56,72},{64,... | collective-permute-start | bytes 3080 | tf_op jit(solution)/shard_map/ppermute | solution.py:18
  19.2 39.6 %collective-permute-start.5 = (s32[256]{0:T(256)}, s32[256]{0:T(256)S(1)}, u32[]{:S(2)}, u32[]{:S(2)}) collective-permute-start(s32[256]{0:T(256)} %param.11), channel_id=1, source_target_pairs={{0,24},{8,32},{16,40},{24,48},{32,56},{40,64},{48,72},{56,80},{64,... | collective-permute-start | bytes 3080 | tf_op jit(solution)/shard_map/ppermute | solution.py:18
  23.5 35.3 %collective-permute-start.4 = (s32[256]{0:T(256)}, s32[256]{0:T(256)S(1)}, u32[]{:S(2)}, u32[]{:S(2)}) collective-permute-start(s32[256]{0:T(256)} %param.11), channel_id=1, source_target_pairs={{0,32},{8,40},{16,48},{24,56},{32,64},{40,72},{48,80},{56,88},{64,... | collective-permute-start | bytes 3080 | tf_op jit(solution)/shard_map/ppermute | solution.py:18
  28.4 13.4 %collective-permute-start = (s32[256]{0:T(256)}, s32[256]{0:T(256)S(1)}, u32[]{:S(2)}, u32[]{:S(2)}) collective-permute-start(s32[256]{0:T(256)} %param.11), channel_id=1, source_target_pairs={{0,64},{8,72},{16,80},{24,88},{32,96},{40,104},{48,112},{56,120},{... | collective-permute-start | bytes 3080 | tf_op jit(solution)/shard_map/ppermute | solution.py:18
  34.6 35.6 %all-to-all-start = ((bf16[8,256,256]{2,1,0:T(8,128)(2,1)}), bf16[8,256,256]{2,1,0:T(8,128)(2,1)S(1)}, u32[]{:S(2)}, u32[]{:S(2)}) async-start(bf16[8,256,256]{2,1,0:T(8,128)(2,1)} %broadcast_in_dim.37), calls=%async_computation | async-start | bytes 2097152 | tf_op jit(solution)/shard_map/all_to_all | solution.py:25
  41.7 17.2 %copy-start.13 = (s32[256]{0:T(256)}, s32[256]{0:T(256)S(1)}, u32[]{:S(2)}) copy-start(s32[256]{0:T(256)S(1)} %iota_add_fusion) | copy-start | bytes 3076
  41.8 3.6 %collective-permute-start.1 = (s32[256]{0:T(256)S(1)}, s32[256]{0:T(256)S(1)}, u32[]{:S(2)}, u32[]{:S(2)}) collective-permute-start(s32[256]{0:T(256)S(1)} %copy-done.12), channel_id=1, source_target_pairs={{0,56},{8,64},{16,72},{24,80},{32,88},{40,96},{48,104},{56,112},{6... | collective-permute-start | bytes 3080 | tf_op jit(solution)/shard_map/ppermute | solution.py:18
  45.4 7.0 %collective-permute-start.2 = (s32[256]{0:T(256)S(1)}, s32[256]{0:T(256)S(1)}, u32[]{:S(2)}, u32[]{:S(2)}) collective-permute-start(s32[256]{0:T(256)S(1)} %copy-done.12), channel_id=1, source_target_pairs={{0,48},{8,56},{16,64},{24,72},{32,80},{40,88},{48,96},{56,104},{64... | collective-permute-start | bytes 3080 | tf_op jit(solution)/shard_map/ppermute | solution.py:18
  52.5 6.4 %collective-permute-start.3 = (s32[256]{0:T(256)S(1)}, s32[256]{0:T(256)S(1)}, u32[]{:S(2)}, u32[]{:S(2)}) collective-permute-start(s32[256]{0:T(256)S(1)} %copy-done.12), channel_id=1, source_target_pairs={{0,40},{8,48},{16,56},{24,64},{32,72},{40,80},{48,88},{56,96},{64,... | collective-permute-start | bytes 3080 | tf_op jit(solution)/shard_map/ppermute | solution.py:18
  112.6 2.0 copy-start.6
  112.6 2.0 copy-start.8
  114.6 29.4 %copy-start.14 = (s32[256]{0:T(256)S(1)}, s32[256]{0:T(256)}, u32[]{:S(2)}) copy-start(s32[256]{0:T(256)} %copy-done.13) | copy-start | bytes 3076
  115.4 7.9 %collective-permute-start.9 = (bf16[256,2,256]{0,2,1:T(8,128)(2,1)}, bf16[256,2,256]{0,2,1:T(8,128)(2,1)S(1)}, u32[]{:S(2)}, u32[]{:S(2)}) collective-permute-start(bf16[256,2,256]{0,2,1:T(8,128)(2,1)} %pad_maximum_fusion), channel_id=1, source_target_pairs={{0,8},{8,16},{16,24},{24,32},{32,40},{40,48},{48,56},{56,64},{64,7... | collective-permute-start | bytes 786440 | tf_op jit(solution)/shard_map/ppermute | solution.py:18
  123.3 25.4 %copy-start = (bf16[256,2,256]{0,2,1:T(8,128)(2,1)}, bf16[256,2,256]{0,2,1:T(8,128)(2,1)S(1)}, u32[]{:S(2)}) copy-start(bf16[256,2,256]{0,2,1:T(8,128)(2,1)S(1)} %collective-permute-done.9) | copy-start | bytes 786436
  123.4 16.6 %collective-permute-start.10 = (bf16[512,2,256]{0,2,1:T(8,128)(2,1)S(1)}, bf16[512,2,256]{0,2,1:T(8,128)(2,1)S(1)}, u32[]{:S(2)}, u32[]{:S(2)}) collective-permute-start(bf16[512,2,256]{0,2,1:T(8,128)(2,1)S(1)} %maximum_maximum_fusion.1), channel_id=1, source_target_pairs={{0,16},{8,24},{16,32},{24,40},{32,48},{40,56},{48,64},{56,72},{64,... | collective-permute-start | bytes 1572872 | tf_op jit(solution)/shard_map/ppermute | solution.py:18
  140.0 8.7 %copy-start.2 = (bf16[512,2,256]{0,2,1:T(8,128)(2,1)}, bf16[512,2,256]{0,2,1:T(8,128)(2,1)S(1)}, u32[]{:S(2)}) copy-start(bf16[512,2,256]{0,2,1:T(8,128)(2,1)S(1)} %collective-permute-done.10) | copy-start | bytes 1572868
  141.1 31.8 %collective-permute-start.11 = (bf16[1024,2,256]{0,2,1:T(8,128)(2,1)}, bf16[1024,2,256]{0,2,1:T(8,128)(2,1)}, u32[]{:S(2)}, u32[]{:S(2)}) collective-permute-start(bf16[1024,2,256]{0,2,1:T(8,128)(2,1)} %maximum_maximum_fusion), channel_id=1, source_target_pairs={{0,32},{8,40},{16,48},{24,56},{32,64},{40,72},{48,80},{56,88},{64,... | collective-permute-start | bytes 3145736 | tf_op jit(solution)/shard_map/ppermute | solution.py:18
  145.7 26.3 %collective-permute-start.8 = (bf16[256,2,256]{0,2,1:T(8,128)(2,1)}, bf16[256,2,256]{0,2,1:T(8,128)(2,1)}, u32[]{:S(2)}, u32[]{:S(2)}) collective-permute-start(bf16[256,2,256]{0,2,1:T(8,128)(2,1)} %pad_maximum_fusion), channel_id=1, source_target_pairs={{0,64},{8,72},{16,80},{24,88},{32,96},{40,104},{48,112},{56,120},{... | collective-permute-start | bytes 786440 | tf_op jit(solution)/shard_map/ppermute | solution.py:18
  149.4 0.8 copy-start.7
  149.4 0.9 copy-start.9
  149.4 24.9 %copy-start.3 = (bf16[512,2,256]{0,2,1:T(8,128)(2,1)S(1)}, bf16[512,2,256]{0,2,1:T(8,128)(2,1)}, u32[]{:S(2)}) copy-start(bf16[512,2,256]{0,2,1:T(8,128)(2,1)} %copy-done.2) | copy-start | bytes 1572868
  150.2 24.1 %copy-start.1 = (bf16[256,2,256]{0,2,1:T(8,128)(2,1)S(1)}, bf16[256,2,256]{0,2,1:T(8,128)(2,1)}, u32[]{:S(2)}) copy-start(bf16[256,2,256]{0,2,1:T(8,128)(2,1)} %copy-done) | copy-start | bytes 786436
  150.3 24.1 %copy-start.5 = (pred[256,2304]{1,0:T(8,128)(4,1)S(1)}, pred[256,2304]{1,0:T(8,128)(4,1)}, u32[]{:S(2)}) copy-start(pred[256,2304]{1,0:T(8,128)(4,1)} %compare_and_fusion) | copy-start | bytes 1769476
  184.0 34.2 %copy-start.10 = (bf16[256,256]{1,0:T(8,128)(2,1)S(1)}, bf16[256,256]{1,0:T(8,128)(2,1)}, u32[]{:S(2)}) copy-start(bf16[256,256]{1,0:T(8,128)(2,1)} %param.10) | copy-start | bytes 393220
  254.1 4.6 %copy-start.15 = (s32[16]{0:T(128)S(1)}, s32[16]{0:T(128)}, u32[]{:S(2)}) copy-start(s32[16]{0:T(128)} %param.12) | copy-start | bytes 196
  255.2 28.8 %all-to-all-start.3 = ((bf16[8,256,256]{2,1,0:T(8,128)(2,1)}), bf16[8,256,256]{2,1,0:T(8,128)(2,1)S(1)}, u32[]{:S(2)}, u32[]{:S(2)}) async-start(bf16[8,256,256]{2,1,0:T(8,128)(2,1)} %bitcast.58), calls=%async_computation.3 | async-start | bytes 2097152 | tf_op jit(solution)/shard_map/all_to_all | solution.py:34
  260.3 24.5 %copy-start.4 = (bf16[2,16,16,256]{3,2,1,0:T(8,128)(2,1)}, bf16[2,16,16,256]{3,2,1,0:T(8,128)(2,1)S(1)}, u32[]{:S(2)}) copy-start(bf16[2,16,16,256]{3,2,1,0:T(8,128)(2,1)S(1)} %scatter_fusion) | copy-start | bytes 786436
Sparse Core Ops, SparseCore 0:
  13.2 94.9 all-gather.1

commit v5 on v4

--- a/solution.py
+++ b/solution.py
@@ -70,22 +70,27 @@
     local_index = jnp.arange(tok_rows, dtype=jnp.int32)
 
     attn_width = wq.shape[1]
-    ff_width = wg.shape[1]
-    pieces = [wq, wk, wv, wo.T, wg, wu, wd.T]
+    pieces = [wq, wo.T, wg, wu, wd.T]
     widths = [piece.shape[1] for piece in pieces]
     gathered = lax.all_gather(jnp.concatenate(pieces, axis=1), "wide", axis=0, tiled=True)
     offsets = [sum(widths[:k]) for k in range(len(widths))]
-    full = [gathered[:, o:o + w] for o, w in zip(offsets, widths)]
-    wq_all, wk_all, wv_all, wo_t, wg_all, wu_all, wd_t = full
+    wq_all, wo_t, wg_all, wu_all, wd_t = [gathered[:, o:o + w] for o, w in zip(offsets, widths)]
 
-    id_blocks = []
-    for step_back in range(REACH, 0, -1):
-        got = shifted(segment_ids, "wide", step_back)
-        id_blocks.append(jnp.where(wide_rank >= step_back, got, -1))
-    id_blocks.append(segment_ids)
-    window_ids = jnp.concatenate(id_blocks, axis=0)
+    count = lax.axis_size("wide")
+    rows = wk.shape[0]
+    id_rows = segment_ids.astype(jnp.bfloat16).reshape(rows, tok_rows // rows)
+    early = jnp.concatenate([wk, wv, id_rows], axis=1)
+    early_all = lax.all_to_all(
+        jnp.broadcast_to(early[None], (count,) + early.shape), "wide", 0, 0, tiled=True
+    ).reshape(count * rows, early.shape[1])
+    wk_all = early_all[:, :attn_width]
+    wv_all = early_all[:, attn_width:2 * attn_width]
+    all_ids = early_all[:, 2 * attn_width:].reshape(-1).astype(jnp.int32)
+
+    lead = REACH * tok_rows
+    padded_ids = jnp.concatenate([jnp.full((lead,), -1, jnp.int32), all_ids], axis=0)
+    window_ids = lax.dynamic_slice_in_dim(padded_ids, wide_rank * tok_rows, lead + tok_rows)
     window_len = window_ids.shape[0]
-    lead = REACH * tok_rows
     window_index = jnp.arange(window_len, dtype=jnp.int32)
     same = window_ids[None, :] == segment_ids[:, None]
     allowed = same & (window_index[None, :] <= lead + local_index[:, None])

time: 293 us -> 325 us (1.11)
  waiting for transfers between devices: 110 us -> 169 us
  starting transfers between devices: 58.8 us -> 37.1 us
  blocking collectives: 62.9 us -> 56.2 us
    all_to_all x0 -> x1, waiting for transfers between devices: none -> 80.4 us  [per_device(): lax.all_to_all(jnp.broadcast_to(early[None], (count,) + early.shape), 'wi...]
    all_gather x1, waiting for transfers between devices: 36.3 us -> 0.01 us  [per_device(): lax.all_gather(jnp.concatenate(pieces, axis=1), 'wide', axis=0, tiled=True)]
    ppermute x12 -> x4, starting transfers between devices: 48.1 us -> 12.4 us  [shifted(): lax.ppermute(value, axis, [(source, source + steps) for source in range(f...]
    all_to_all x1, waiting for transfers between devices: 9.64 us -> 28.6 us  [swap_gather(): got = lax.all_to_all(copies, axis, 0, 0, tiled=True)]
    all_to_all x0 -> x1, starting transfers between devices: none -> 14 us  [per_device(): lax.all_to_all(jnp.broadcast_to(early[None], (count,) + early.shape), 'wi...]
    all_to_all x1, blocking collectives: 34 us -> 28.2 us  [swap_sum(): got = lax.all_to_all(pieces, axis, 0, 0, tiled=True)]
    ppermute x12 -> x4, waiting for transfers between devices: 40.5 us -> 37.6 us  [shifted(): lax.ppermute(value, axis, [(source, source + steps) for source in range(f...]
    unnamed x42 -> x32, local copies, waits for them, and re-layouts: 7.84 us -> 7.71 us
  transfers between devices with their start and end apart: 15 -> 8, of which waited for: 9 -> 6; matrix products, arithmetic and copies ran while one was open for 4% -> 6% of each run, Pallas kernels for 0% -> 0%
where the time goes in v5:
time: 325 us; the launch traced here: 324 us
  waiting for transfers between devices  169 us (52%)
  blocking collectives  56.2 us (17%)
  starting transfers between devices  37.1 us (11%)
  local copies, waits for them, and re-layouts  21.2 us (7%)
  matrix products  19.7 us (6%)
  between operations  14.5 us (4%)
  other arithmetic  6.82 us (2%)
    all_to_all x1, waiting for transfers between devices, per_device(): lax.all_to_all(jnp.broadcast_to(early[None], (count,) + early.shape), 'wi...  80.4 us
    ppermute x4, waiting for transfers between devices, shifted(): lax.ppermute(value, axis, [(source, source + steps) for source in range(f...  37.6 us
    all_to_all x1, waiting for transfers between devices, swap_gather(): got = lax.all_to_all(copies, axis, 0, 0, tiled=True)  28.6 us
    all_to_all x1, blocking collectives, swap_sum(): got = lax.all_to_all(pieces, axis, 0, 0, tiled=True)  28.2 us
    all_to_all x1, blocking collectives, swap_gather(): got = lax.all_to_all(copies, axis, 0, 0, tiled=True)  28 us
    all_to_all x1, waiting for transfers between devices, swap_sum(): got = lax.all_to_all(pieces, axis, 0, 0, tiled=True)  22.3 us
    all_to_all x1, starting transfers between devices, per_device(): lax.all_to_all(jnp.broadcast_to(early[None], (count,) + early.shape), 'wi...  14 us
    ppermute x4, starting transfers between devices, shifted(): lax.ppermute(value, axis, [(source, source + steps) for source in range(f...  12.4 us
  transfers between devices with their start and end apart: 8, of which 6 were waited for; matrix products, arithmetic and copies ran while one was open for 6% of the time, Pallas kernels for 0%

profile of v5, /device:TPU:6, one launch (start us, length us, event | category | flops | bytes accessed | tf_op | source)
XLA Modules:
  0.0 324.3 jit_solution(4909236512495025155)
XLA Ops:
  11.6 2.0 broadcast_in_dim.24
  13.7 7.1 %all-to-all-start = ((bf16[8,256,256]{2,1,0:T(8,128)(2,1)}), bf16[8,256,256]{2,1,0:T(8,128)(2,1)S(1)}, u32[]{:S(2)}, u32[]{:S(2)}) async-start(bf16[8,256,256]{2,1,0:T(8,128)(2,1)} %broadcast_in_dim.24), calls=%async_computation | async-start | bytes 2097152 | tf_op jit(solution)/shard_map/all_to_all | solution.py:25
  20.9 28.6 %all-to-all-done = bf16[8,256,256]{2,1,0:T(8,128)(2,1)S(1)} async-done(((bf16[8,256,256]{2,1,0:T(8,128)(2,1)}), bf16[8,256,256]{2,1,0:T(8,128)(2,1)S(1)}, u32[]{:S(2)}, u32[]{:S(2)}) %all-to-all-start) | async-done | bytes 1048608 | tf_op jit(solution)/shard_map/all_to_all | solution.py:25
  49.5 1.8 broadcast_in_dim.25
  51.3 14.0 %all-to-all-start.1 = ((bf16[64,32,520]{2,1,0:T(8,128)(2,1)}), bf16[64,32,520]{2,1,0:T(8,128)(2,1)}, u32[]{:S(2)}, u32[]{:S(2)}) async-start(bf16[64,32,520]{2,1,0:T(8,128)(2,1)} %broadcast_in_dim.25), calls=%async_computation.1 | async-start | bytes 5242880 | tf_op jit(solution)/shard_map/all_to_all | solution.py:83
  67.0 80.4 %all-to-all-done.1 = bf16[64,32,520]{2,1,0:T(8,128)(2,1)} async-done(((bf16[64,32,520]{2,1,0:T(8,128)(2,1)}), bf16[64,32,520]{2,1,0:T(8,128)(2,1)}, u32[]{:S(2)}, u32[]{:S(2)}) %all-to-all-start.1) | async-done | bytes 2129952 | tf_op jit(solution)/shard_map/all_to_all | solution.py:83
  147.4 1.1 slice.58
  148.5 1.7 convolution_convert_fusion.2
  150.8 1.3 slice_bitcast_fusion.1
  154.4 1.9 collective-permute-start.1
  156.3 5.8 %collective-permute-done.1 = bf16[256,2,256]{0,2,1:T(8,128)(2,1)S(1)} collective-permute-done((bf16[256,2,256]{0,2,1:T(8,128)(2,1)S(1)}, bf16[256,2,256]{0,2,1:T(8,128)(2,1)S(1)}, u32[]{:S(2)}, u32[]{:S(2)}) %collective-permute-start.1) | collective-permute-done | bytes 262176 | tf_op jit(solution)/shard_map/ppermute | solution.py:18
  162.1 4.6 %collective-permute-start.2 = (bf16[512,2,256]{0,2,1:T(8,128)(2,1)S(1)}, bf16[512,2,256]{0,2,1:T(8,128)(2,1)S(1)}, u32[]{:S(2)}, u32[]{:S(2)}) collective-permute-start(bf16[512,2,256]{0,2,1:T(8,128)(2,1)S(1)} %maximum_maximum_fusion.1), channel_id=1, source_target_pairs={{0,16},{8,24},{16,32},{24,40},{32,48},{40,56},{48,64},{56,72},{64,... | collective-permute-start | bytes 1572872 | tf_op jit(solution)/shard_map/ppermute | solution.py:18
  166.7 9.3 %collective-permute-done.2 = bf16[512,2,256]{0,2,1:T(8,128)(2,1)S(1)} collective-permute-done((bf16[512,2,256]{0,2,1:T(8,128)(2,1)S(1)}, bf16[512,2,256]{0,2,1:T(8,128)(2,1)S(1)}, u32[]{:S(2)}, u32[]{:S(2)}) %collective-permute-start.2) | collective-permute-done | bytes 524320 | tf_op jit(solution)/shard_map/ppermute | solution.py:18
  176.2 4.3 %collective-permute-start.3 = (bf16[1024,2,256]{0,2,1:T(8,128)(2,1)S(1)}, bf16[1024,2,256]{0,2,1:T(8,128)(2,1)S(1)}, u32[]{:S(2)}, u32[]{:S(2)}) collective-permute-start(bf16[1024,2,256]{0,2,1:T(8,128)(2,1)S(1)} %maximum_maximum_fusion), channel_id=1, source_target_pairs={{0,32},{8,40},{16,48},{24,56},{32,64},{40,72},{48,80},{56,88},{64,... | collective-permute-start | bytes 3145736 | tf_op jit(solution)/shard_map/ppermute | solution.py:18
  180.5 1.6 collective-permute-start
  182.1 1.6 compare_and_fusion
  183.8 22.5 %collective-permute-done = bf16[256,2,256]{0,2,1:T(8,128)(2,1)S(1)} collective-permute-done((bf16[256,2,256]{0,2,1:T(8,128)(2,1)S(1)}, bf16[256,2,256]{0,2,1:T(8,128)(2,1)S(1)}, u32[]{:S(2)}, u32[]{:S(2)}) %collective-permute-start) | collective-permute-done | bytes 262176 | tf_op jit(solution)/shard_map/ppermute | solution.py:18
  207.0 1.1 constant_dynamic-update-slice_fusion.3
  208.1 0.9 constant_dynamic-update-slice_fusion.2
  209.0 0.8 constant_dynamic-update-slice_fusion.1
  210.5 1.3 slice_bitcast_fusion
  213.5 5.8 %fusion.42 = (f32[2,256]{1,0:T(2,128)S(1)}, f32[2,256,2304]{2,1,0:T(8,128)}) fusion(pred[256,2304]{1,0:T(8,128)(4,1)S(1)} %copy-done.1, bf16[2304,2,256]{0,2,1:T(8,128)(2,1)} %constant_dynamic-update-slice_fusion, bf16[256,2,64]{0,2,1:T(8,128)(2,1)S(1)} %get-tuple-element.3, bf16[256,2,64]{0,2,1:T(8,128)(2,1)S(1)} %get-tuple-element.2), kind=kOutput, calls=%fused_computation.90 | convolution fusion | flops 308152576 | bytes 7211008 | tf_op jit(solution)/shard_map/sub | solution.py:130
  219.3 3.7 %fusion.25 = bf16[2,128,256]{2,1,0:T(8,128)(2,1)S(1)} fusion(f32[2,256,2304]{2,1,0:T(8,128)} %get-tuple-element.9, f32[2,256]{1,0:T(2,128)S(1)} %get-tuple-element.8, bf16[2304,2,256]{0,2,1:T(8,128)(2,1)} %constant_dynamic-update-slice_fusion), kind=kOutput, calls=%fused_computation.37 | convolution fusion | flops 304414720 | bytes 6031360 | tf_op jit(solution)/shard_map/hqk,khd->qhd/dot_general | solution.py:132
  223.0 1.7 convolution_convert_fusion.1
  224.8 28.2 %all_to_all.25 = bf16[8,256,256]{2,1,0:T(8,128)(2,1)S(1)} all-to-all(bf16[8,256,256]{2,1,0:T(8,128)(2,1)S(1)} %bitcast.68), channel_id=1, replica_groups=mesh['wide'=64,'narrow'=8] {'narrow'}, dimensions={0} | all-to-all | bytes 2097152 | tf_op jit(solution)/shard_map/all_to_all | solution.py:34
  253.4 28.0 %all_to_all.26 = bf16[8,256,256]{1,2,0:T(8,128)(2,1)S(1)} all-to-all(bf16[8,256,256]{1,2,0:T(8,128)(2,1)S(1)} %broadcast_in_dim.29), channel_id=1, replica_groups=mesh['wide'=64,'narrow'=8] {'narrow'}, dimensions={0} | all-to-all | bytes 2097152 | tf_op jit(solution)/shard_map/all_to_all | solution.py:25
  282.3 2.3 fusion.9
  284.6 3.6 %convolution_convert_fusion = bf16[256,2048]{1,0:T(8,128)(2,1)S(1)} fusion(bf16[2048,2048]{1,0:T(8,128)(2,1)} %all-gather.2.cloned.1.call-done, bf16[256,2048]{0,1:T(8,128)(2,1)S(1)} %fusion.12, f32[256,512]{1,0:T(8,128)S(1)} %fusion.9), kind=kOutput, calls=%fused_computation.10 | convolution fusion | flops 1075052544 | bytes 6815744 | tf_op jit(solution)/shard_map/dot_general | solution.py:145
  288.2 1.1 copy.60
  289.3 3.6 %all-to-all-start.4 = ((bf16[8,256,256]{2,1,0:T(8,128)(2,1)}), bf16[8,256,256]{2,1,0:T(8,128)(2,1)S(1)}, u32[]{:S(2)}, u32[]{:S(2)}) async-start(bf16[8,256,256]{2,1,0:T(8,128)(2,1)} %bitcast.59), calls=%async_computation.4 | async-start | bytes 2097152 | tf_op jit(solution)/shard_map/all_to_all | solution.py:34
  293.2 1.2 scatter_fusion
  294.4 22.3 %all-to-all-done.4 = bf16[8,256,256]{2,1,0:T(8,128)(2,1)S(1)} async-done(((bf16[8,256,256]{2,1,0:T(8,128)(2,1)}), bf16[8,256,256]{2,1,0:T(8,128)(2,1)S(1)}, u32[]{:S(2)}, u32[]{:S(2)}) %all-to-all-start.4) | async-done | bytes 1048608 | tf_op jit(solution)/shard_map/all_to_all | solution.py:34
  (81 shorter events, 14.8 us)
Async XLA Ops:
  7.2 13.6 %copy-start.10 = (s32[256]{0:T(256)S(1)}, s32[256]{0:T(256)}, u32[]{:S(2)}) copy-start(s32[256]{0:T(256)} %param.11) | copy-start | bytes 3076
  7.2 13.7 %copy-start.8 = (bf16[32,256]{1,0:T(8,128)(2,1)S(1)}, bf16[32,256]{1,0:T(8,128)(2,1)}, u32[]{:S(2)}) copy-start(bf16[32,256]{1,0:T(8,128)(2,1)} %param.15) | copy-start | bytes 49156
  7.2 13.7 %copy-start.9 = (bf16[32,256]{1,0:T(8,128)(2,1)S(1)}, bf16[32,256]{1,0:T(8,128)(2,1)}, u32[]{:S(2)}) copy-start(bf16[32,256]{1,0:T(8,128)(2,1)} %param.14) | copy-start | bytes 49156
  7.2 203.3 %all-gather.2.cloned.1.call-start = ((), (), s32[]{:S(2)}) async-start(), calls=%async_computation.5 | async-start | bytes 8519680 | tf_op jit(solution)/shard_map/all_gather | solution.py:75
  11.0 0.7 copy-start.7
  13.7 35.8 %all-to-all-start = ((bf16[8,256,256]{2,1,0:T(8,128)(2,1)}), bf16[8,256,256]{2,1,0:T(8,128)(2,1)S(1)}, u32[]{:S(2)}, u32[]{:S(2)}) async-start(bf16[8,256,256]{2,1,0:T(8,128)(2,1)} %broadcast_in_dim.24), calls=%async_computation | async-start | bytes 2097152 | tf_op jit(solution)/shard_map/all_to_all | solution.py:25
  51.3 96.1 %all-to-all-start.1 = ((bf16[64,32,520]{2,1,0:T(8,128)(2,1)}), bf16[64,32,520]{2,1,0:T(8,128)(2,1)}, u32[]{:S(2)}, u32[]{:S(2)}) async-start(bf16[64,32,520]{2,1,0:T(8,128)(2,1)} %broadcast_in_dim.25), calls=%async_computation.1 | async-start | bytes 5242880 | tf_op jit(solution)/shard_map/all_to_all | solution.py:83
  153.8 8.3 %copy-start.2 = (f32[256,64]{0,1:T(8,128)}, f32[256,64]{0,1:T(8,128)S(1)}, u32[]{:S(2)}) copy-start(f32[256,64]{0,1:T(8,128)S(1)} %get-tuple-element.6) | copy-start | bytes 196612
  153.8 8.3 %copy-start.4 = (f32[256,64]{0,1:T(8,128)}, f32[256,64]{0,1:T(8,128)S(1)}, u32[]{:S(2)}) copy-start(f32[256,64]{0,1:T(8,128)S(1)} %get-tuple-element.7) | copy-start | bytes 196612
  154.4 7.7 %collective-permute-start.1 = (bf16[256,2,256]{0,2,1:T(8,128)(2,1)S(1)}, bf16[256,2,256]{0,2,1:T(8,128)(2,1)S(1)}, u32[]{:S(2)}, u32[]{:S(2)}) collective-permute-start(bf16[256,2,256]{0,2,1:T(8,128)(2,1)S(1)} %pad_maximum_fusion), channel_id=1, source_target_pairs={{0,8},{8,16},{16,24},{24,32},{32,40},{40,48},{48,56},{56,64},{64,7... | collective-permute-start | bytes 786440 | tf_op jit(solution)/shard_map/ppermute | solution.py:18
  162.1 13.9 %collective-permute-start.2 = (bf16[512,2,256]{0,2,1:T(8,128)(2,1)S(1)}, bf16[512,2,256]{0,2,1:T(8,128)(2,1)S(1)}, u32[]{:S(2)}, u32[]{:S(2)}) collective-permute-start(bf16[512,2,256]{0,2,1:T(8,128)(2,1)S(1)} %maximum_maximum_fusion.1), channel_id=1, source_target_pairs={{0,16},{8,24},{16,32},{24,40},{32,48},{40,56},{48,64},{56,72},{64,... | collective-permute-start | bytes 1572872 | tf_op jit(solution)/shard_map/ppermute | solution.py:18
  176.2 30.8 %collective-permute-start.3 = (bf16[1024,2,256]{0,2,1:T(8,128)(2,1)S(1)}, bf16[1024,2,256]{0,2,1:T(8,128)(2,1)S(1)}, u32[]{:S(2)}, u32[]{:S(2)}) collective-permute-start(bf16[1024,2,256]{0,2,1:T(8,128)(2,1)S(1)} %maximum_maximum_fusion), channel_id=1, source_target_pairs={{0,32},{8,40},{16,48},{24,56},{32,64},{40,72},{48,80},{56,88},{64,... | collective-permute-start | bytes 3145736 | tf_op jit(solution)/shard_map/ppermute | solution.py:18
  180.5 25.7 %collective-permute-start = (bf16[256,2,256]{0,2,1:T(8,128)(2,1)S(1)}, bf16[256,2,256]{0,2,1:T(8,128)(2,1)S(1)}, u32[]{:S(2)}, u32[]{:S(2)}) collective-permute-start(bf16[256,2,256]{0,2,1:T(8,128)(2,1)S(1)} %pad_maximum_fusion), channel_id=1, source_target_pairs={{0,64},{8,72},{16,80},{24,88},{32,96},{40,104},{48,112},{56,120},{... | collective-permute-start | bytes 786440 | tf_op jit(solution)/shard_map/ppermute | solution.py:18
  211.8 1.1 copy-start.3
  211.8 1.1 copy-start.5
  212.5 1.1 copy-start.1
  224.7 28.4 %copy-start.6 = (bf16[256,256]{1,0:T(8,128)(2,1)S(1)}, bf16[256,256]{1,0:T(8,128)(2,1)}, u32[]{:S(2)}) copy-start(bf16[256,256]{1,0:T(8,128)(2,1)} %param.10) | copy-start | bytes 393220
  288.2 4.6 %copy-start.11 = (s32[16]{0:T(128)S(1)}, s32[16]{0:T(128)}, u32[]{:S(2)}) copy-start(s32[16]{0:T(128)} %param.12) | copy-start | bytes 196
  289.3 27.4 %all-to-all-start.4 = ((bf16[8,256,256]{2,1,0:T(8,128)(2,1)}), bf16[8,256,256]{2,1,0:T(8,128)(2,1)S(1)}, u32[]{:S(2)}, u32[]{:S(2)}) async-start(bf16[8,256,256]{2,1,0:T(8,128)(2,1)} %bitcast.59), calls=%async_computation.4 | async-start | bytes 2097152 | tf_op jit(solution)/shard_map/all_to_all | solution.py:34
  294.4 23.1 %copy-start = (bf16[2,16,16,256]{3,2,1,0:T(8,128)(2,1)}, bf16[2,16,16,256]{3,2,1,0:T(8,128)(2,1)S(1)}, u32[]{:S(2)}) copy-start(bf16[2,16,16,256]{3,2,1,0:T(8,128)(2,1)S(1)} %scatter_fusion) | copy-start | bytes 786436
Sparse Core Ops, SparseCore 0:
  12.0 132.6 all-gather.1

commit v6 on v3

--- a/solution.py
+++ b/solution.py
@@ -88,7 +88,6 @@
     lead = REACH * tok_rows
     window_index = jnp.arange(window_len, dtype=jnp.int32)
     same = window_ids[None, :] == segment_ids[:, None]
-    allowed = same & (window_index[None, :] <= lead + local_index[:, None])
     earlier = same & (window_index[None, :] < lead + local_index[:, None])
     positions = jnp.sum(earlier.astype(jnp.int32), axis=1)
 
@@ -106,12 +105,29 @@
     )
     values = v_proj.astype(jnp.bfloat16).reshape(tok_rows, head_count, HEAD_DIM)
     packed = jnp.concatenate([keys_rot, values], axis=2)
-    blocks = []
-    for step_back in range(REACH, 0, -1):
-        blocks.append(shifted(packed, "wide", step_back))
-    blocks.append(packed)
+    pairs_per_chip = 2
+    chips_back = REACH // pairs_per_chip
+    line = [shifted(packed, "wide", pairs_per_chip * step) for step in range(1, chips_back + 1)]
+    count = lax.axis_size("wide")
+    partner = lax.ppermute(
+        jnp.stack(line + [packed], axis=0), "wide", [(i, i ^ 1) for i in range(count)]
+    )
+    partner_rank = wide_rank ^ 1
+    order = []
+    block_ids = []
+    for step in range(chips_back, 0, -1):
+        order += [line[step - 1], partner[step - 1]]
+        block_ids += [wide_rank - pairs_per_chip * step, partner_rank - pairs_per_chip * step]
+    order += [partner[chips_back], packed]
+    block_ids += [partner_rank, wide_rank]
+    kv_all = jnp.concatenate(order, axis=0)
+    key_index = (
+        jnp.stack(block_ids)[:, None] * tok_rows + local_index[None, :]
+    ).reshape(-1)
+    query_index = wide_rank * tok_rows + local_index
+    query_start = query_index - positions
+    allowed = (key_index[None, :] >= query_start[:, None]) & (key_index[None, :] <= query_index[:, None])
     score_scale = HEAD_DIM ** (-0.5)
-    kv_all = jnp.concatenate(blocks, axis=0)
     key_all = kv_all[:, :, :HEAD_DIM]
     value_all = kv_all[:, :, HEAD_DIM:]
     scores = (

time: 297 us -> 290 us (0.976)
  the two profiles are of different devices: /device:TPU:64 before, /device:TPU:6 now
where the time goes in v6:
time: 290 us; the launch traced here: 288 us
  waiting for transfers between devices  92.5 us (32%)
  blocking collectives  67.6 us (23%)
  starting transfers between devices  59.2 us (20%)
  local copies, waits for them, and re-layouts  25.7 us (9%)
  matrix products  20.4 us (7%)
  between operations  14.8 us (5%)
  other arithmetic  8.03 us (3%)
    ppermute x12, starting transfers between devices, shifted(): lax.ppermute(value, axis, [(source, source + steps) for source in range(f...  46.6 us
    all_gather x1, waiting for transfers between devices, per_device(): lax.all_gather(jnp.concatenate(pieces, axis=1), 'wide', axis=0, tiled=True)  36.3 us
    all_to_all x1, blocking collectives, swap_sum(): got = lax.all_to_all(pieces, axis, 0, 0, tiled=True)  35.9 us
    all_to_all x1, blocking collectives, swap_gather(): got = lax.all_to_all(copies, axis, 0, 0, tiled=True)  31.6 us
    all_to_all x1, waiting for transfers between devices, swap_sum(): got = lax.all_to_all(pieces, axis, 0, 0, tiled=True)  27.1 us
    ppermute x12, waiting for transfers between devices, shifted(): lax.ppermute(value, axis, [(source, source + steps) for source in range(f...  19.5 us
    unnamed x53, local copies, waits for them, and re-layouts  14.7 us
    all_to_all x1, waiting for transfers between devices, swap_gather(): got = lax.all_to_all(copies, axis, 0, 0, tiled=True)  9.54 us
  transfers between devices with their start and end apart: 16, of which 9 were waited for; matrix products, arithmetic and copies ran while one was open for 4% of the time, Pallas kernels for 0%

profile of v6, /device:TPU:6, one launch (start us, length us, event | category | flops | bytes accessed | tf_op | source)
XLA Modules:
  0.0 288.2 jit_solution(4574819859322242119)
XLA Ops:
  13.1 1.9 collective-permute-start.7
  15.0 4.2 %collective-permute-start.6 = (s32[256]{0:T(256)}, s32[256]{0:T(256)S(1)}, u32[]{:S(2)}, u32[]{:S(2)}) collective-permute-start(s32[256]{0:T(256)} %param.11), channel_id=1, source_target_pairs={{0,16},{8,24},{16,32},{24,40},{32,48},{40,56},{48,64},{56,72},{64,... | collective-permute-start | bytes 3080 | tf_op jit(solution)/shard_map/ppermute | solution.py:18
  19.2 4.3 %collective-permute-start.5 = (s32[256]{0:T(256)}, s32[256]{0:T(256)S(1)}, u32[]{:S(2)}, u32[]{:S(2)}) collective-permute-start(s32[256]{0:T(256)} %param.11), channel_id=1, source_target_pairs={{0,24},{8,32},{16,40},{24,48},{32,56},{40,64},{48,72},{56,80},{64,... | collective-permute-start | bytes 3080 | tf_op jit(solution)/shard_map/ppermute | solution.py:18
  23.5 4.8 %collective-permute-start.4 = (s32[256]{0:T(256)}, s32[256]{0:T(256)S(1)}, u32[]{:S(2)}, u32[]{:S(2)}) collective-permute-start(s32[256]{0:T(256)} %param.11), channel_id=1, source_target_pairs={{0,32},{8,40},{16,48},{24,56},{32,64},{40,72},{48,80},{56,88},{64,... | collective-permute-start | bytes 3080 | tf_op jit(solution)/shard_map/ppermute | solution.py:18
  28.4 4.3 %collective-permute-start = (s32[256]{0:T(256)}, s32[256]{0:T(256)S(1)}, u32[]{:S(2)}, u32[]{:S(2)}) collective-permute-start(s32[256]{0:T(256)} %param.11), channel_id=1, source_target_pairs={{0,64},{8,72},{16,80},{24,88},{32,96},{40,104},{48,112},{56,120},{... | collective-permute-start | bytes 3080 | tf_op jit(solution)/shard_map/ppermute | solution.py:18
  32.7 2.0 broadcast_in_dim.37
  34.6 7.1 %all-to-all-start = ((bf16[8,256,256]{2,1,0:T(8,128)(2,1)}), bf16[8,256,256]{2,1,0:T(8,128)(2,1)S(1)}, u32[]{:S(2)}, u32[]{:S(2)}) async-start(bf16[8,256,256]{2,1,0:T(8,128)(2,1)} %broadcast_in_dim.37), calls=%async_computation | async-start | bytes 2097152 | tf_op jit(solution)/shard_map/all_to_all | solution.py:25
  41.9 2.3 collective-permute-start.1
  45.5 5.7 %collective-permute-start.2 = (s32[256]{0:T(256)S(1)}, s32[256]{0:T(256)S(1)}, u32[]{:S(2)}, u32[]{:S(2)}) collective-permute-start(s32[256]{0:T(256)S(1)} %copy-done.15), channel_id=1, source_target_pairs={{0,48},{8,56},{16,64},{24,72},{32,80},{40,88},{48,96},{56,104},{64... | collective-permute-start | bytes 3080 | tf_op jit(solution)/shard_map/ppermute | solution.py:18
  52.6 5.1 %collective-permute-start.3 = (s32[256]{0:T(256)S(1)}, s32[256]{0:T(256)S(1)}, u32[]{:S(2)}, u32[]{:S(2)}) collective-permute-start(s32[256]{0:T(256)S(1)} %copy-done.15), channel_id=1, source_target_pairs={{0,40},{8,48},{16,56},{24,64},{32,72},{40,80},{48,88},{56,96},{64,... | collective-permute-start | bytes 3080 | tf_op jit(solution)/shard_map/ppermute | solution.py:18
  60.6 9.5 %all-to-all-done = bf16[8,256,256]{2,1,0:T(8,128)(2,1)S(1)} async-done(((bf16[8,256,256]{2,1,0:T(8,128)(2,1)}), bf16[8,256,256]{2,1,0:T(8,128)(2,1)S(1)}, u32[]{:S(2)}, u32[]{:S(2)}) %all-to-all-start) | async-done | bytes 1048608 | tf_op jit(solution)/shard_map/all_to_all | solution.py:25
  71.9 36.3 %all-gather.2.cloned.1.call-done = bf16[2048,2560]{1,0:T(8,128)(2,1)} async-done(((bf16[32,2560]{1,0:T(8,128)(2,1)}), bf16[2048,2560]{1,0:T(8,128)(2,1)}) %all-gather.2.cloned.1.call-update) | async-done | bytes 10485776 | tf_op jit(solution)/shard_map/all_gather | solution.py:76
  108.1 1.7 convolution_convert_fusion.2
  110.0 2.7 slice_bitcast_fusion
  112.7 1.5 copy.51
  114.7 5.2 %collective-permute-start.9 = (bf16[256,2,256]{0,2,1:T(8,128)(2,1)S(1)}, bf16[256,2,256]{0,2,1:T(8,128)(2,1)S(1)}, u32[]{:S(2)}, u32[]{:S(2)}) collective-permute-start(bf16[256,2,256]{0,2,1:T(8,128)(2,1)S(1)} %pad_maximum_fusion), channel_id=1, source_target_pairs={{0,16},{8,24},{16,32},{24,40},{32,48},{40,56},{48,64},{56,72},{64,... | collective-permute-start | bytes 786440 | tf_op jit(solution)/shard_map/ppermute | solution.py:18
  120.0 2.7 collective-permute-start.10
  122.8 2.0 collective-permute-start.11
  124.9 3.9 %collective-permute-start.8 = (bf16[256,2,256]{0,2,1:T(8,128)(2,1)S(1)}, bf16[256,2,256]{0,2,1:T(8,128)(2,1)S(1)}, u32[]{:S(2)}, u32[]{:S(2)}) collective-permute-start(bf16[256,2,256]{0,2,1:T(8,128)(2,1)S(1)} %pad_maximum_fusion), channel_id=1, source_target_pairs={{0,64},{8,72},{16,80},{24,88},{32,96},{40,104},{48,112},{56,120},{... | collective-permute-start | bytes 786440 | tf_op jit(solution)/shard_map/ppermute | solution.py:18
  129.6 6.7 %collective-permute-done.10 = bf16[256,2,256]{0,2,1:T(8,128)(2,1)S(1)} collective-permute-done((bf16[256,2,256]{0,2,1:T(8,128)(2,1)S(1)}, bf16[256,2,256]{0,2,1:T(8,128)(2,1)S(1)}, u32[]{:S(2)}, u32[]{:S(2)}) %collective-permute-start.10) | collective-permute-done | bytes 262176 | tf_op jit(solution)/shard_map/ppermute | solution.py:18
  137.1 4.8 %collective-permute-done.11 = bf16[256,2,256]{0,2,1:T(8,128)(2,1)S(1)} collective-permute-done((bf16[256,2,256]{0,2,1:T(8,128)(2,1)S(1)}, bf16[256,2,256]{0,2,1:T(8,128)(2,1)S(1)}, u32[]{:S(2)}, u32[]{:S(2)}) %collective-permute-start.11) | collective-permute-done | bytes 262176 | tf_op jit(solution)/shard_map/ppermute | solution.py:18
  142.7 4.2 %collective-permute-done.8 = bf16[256,2,256]{0,2,1:T(8,128)(2,1)S(1)} collective-permute-done((bf16[256,2,256]{0,2,1:T(8,128)(2,1)S(1)}, bf16[256,2,256]{0,2,1:T(8,128)(2,1)S(1)}, u32[]{:S(2)}, u32[]{:S(2)}) %collective-permute-start.8) | collective-permute-done | bytes 262176 | tf_op jit(solution)/shard_map/ppermute | solution.py:18
  148.3 1.9 collective-permute-start.12
  160.4 6.2 %fusion.46 = (f32[2,256]{1,0:T(2,128)S(1)}, f32[2,256,2560]{2,1,0:T(8,128)}) fusion(pred[256,2560]{1,0:T(8,128)(4,1)S(1)} %copy-done.9, bf16[2560,2,256]{0,2,1:T(8,128)(2,1)} %copy-done.14, bf16[256,2,64]{0,2,1:T(8,128)(2,1)S(1)} %get-tuple-element.5, bf16[256,2,64]{0,2,1:T(8,128)(2,1)S(1)} %get-tuple-element.4), kind=kOutput, calls=%fused_computation.113 | convolution fusion | flops 342362624 | bytes 7997440 | tf_op jit(solution)/shard_map/sub | solution.py:139
  166.6 4.0 %fusion.23 = bf16[2,128,256]{2,1,0:T(8,128)(2,1)S(1)} fusion(f32[2,256,2560]{2,1,0:T(8,128)} %get-tuple-element.13, f32[2,256]{1,0:T(2,128)S(1)} %get-tuple-element.12, bf16[2560,2,256]{0,2,1:T(8,128)(2,1)} %copy-done.14), kind=kOutput, calls=%fused_computation.34 | convolution fusion | flops 338231296 | bytes 6686720 | tf_op jit(solution)/shard_map/hqk,khd->qhd/dot_general | solution.py:141
  170.6 1.7 convolution_convert_fusion.1
  172.4 35.9 %all_to_all.20 = bf16[8,256,256]{2,1,0:T(8,128)(2,1)S(1)} all-to-all(bf16[8,256,256]{2,1,0:T(8,128)(2,1)S(1)} %bitcast.107), channel_id=1, replica_groups=mesh['wide'=64,'narrow'=8] {'narrow'}, dimensions={0} | all-to-all | bytes 2097152 | tf_op jit(solution)/shard_map/all_to_all | solution.py:34
  208.7 31.6 %all_to_all.21 = bf16[8,256,256]{1,2,0:T(8,128)(2,1)S(1)} all-to-all(bf16[8,256,256]{1,2,0:T(8,128)(2,1)S(1)} %broadcast_in_dim.42), channel_id=1, replica_groups=mesh['wide'=64,'narrow'=8] {'narrow'}, dimensions={0} | all-to-all | bytes 2097152 | tf_op jit(solution)/shard_map/all_to_all | solution.py:25
  241.3 2.3 fusion.7
  243.6 3.6 %convolution_convert_fusion = bf16[256,2048]{1,0:T(8,128)(2,1)S(1)} fusion(bf16[2048,2560]{1,0:T(8,128)(2,1)} %all-gather.2.cloned.1.call-done, bf16[256,2048]{0,1:T(8,128)(2,1)S(1)} %fusion.10, f32[256,512]{1,0:T(8,128)S(1)} %fusion.7), kind=kOutput, calls=%fused_computation.8 | convolution fusion | flops 1075052544 | bytes 6815744 | tf_op jit(solution)/shard_map/dot_general | solution.py:154
  248.2 3.6 %all-to-all-start.3 = ((bf16[8,256,256]{2,1,0:T(8,128)(2,1)}), bf16[8,256,256]{2,1,0:T(8,128)(2,1)S(1)}, u32[]{:S(2)}, u32[]{:S(2)}) async-start(bf16[8,256,256]{2,1,0:T(8,128)(2,1)} %bitcast.98), calls=%async_computation.3 | async-start | bytes 2097152 | tf_op jit(solution)/shard_map/all_to_all | solution.py:34
  253.4 27.1 %all-to-all-done.3 = bf16[8,256,256]{2,1,0:T(8,128)(2,1)S(1)} async-done(((bf16[8,256,256]{2,1,0:T(8,128)(2,1)}), bf16[8,256,256]{2,1,0:T(8,128)(2,1)S(1)}, u32[]{:S(2)}, u32[]{:S(2)}) %all-to-all-start.3) | async-done | bytes 1048608 | tf_op jit(solution)/shard_map/all_to_all | solution.py:34
  (124 shorter events, 32.3 us)
Async XLA Ops:
  7.2 34.7 %copy-start.15 = (s32[256]{0:T(256)S(1)}, s32[256]{0:T(256)}, u32[]{:S(2)}) copy-start(s32[256]{0:T(256)} %param.11) | copy-start | bytes 3076
  7.2 101.0 %all-gather.2.cloned.1.call-start = ((), (), s32[]{:S(2)}) async-start(), calls=%async_computation.4 | async-start | bytes 10649600 | tf_op jit(solution)/shard_map/all_gather | solution.py:76
  13.1 45.9 %collective-permute-start.7 = (s32[256]{0:T(256)}, s32[256]{0:T(256)S(1)}, u32[]{:S(2)}, u32[]{:S(2)}) collective-permute-start(s32[256]{0:T(256)} %param.11), channel_id=1, source_target_pairs={{0,8},{8,16},{16,24},{24,32},{32,40},{40,48},{48,56},{56,64},{64,7... | collective-permute-start | bytes 3080 | tf_op jit(solution)/shard_map/ppermute | solution.py:18
  15.0 44.0 %collective-permute-start.6 = (s32[256]{0:T(256)}, s32[256]{0:T(256)S(1)}, u32[]{:S(2)}, u32[]{:S(2)}) collective-permute-start(s32[256]{0:T(256)} %param.11), channel_id=1, source_target_pairs={{0,16},{8,24},{16,32},{24,40},{32,48},{40,56},{48,64},{56,72},{64,... | collective-permute-start | bytes 3080 | tf_op jit(solution)/shard_map/ppermute | solution.py:18
  19.2 39.7 %collective-permute-start.5 = (s32[256]{0:T(256)}, s32[256]{0:T(256)S(1)}, u32[]{:S(2)}, u32[]{:S(2)}) collective-permute-start(s32[256]{0:T(256)} %param.11), channel_id=1, source_target_pairs={{0,24},{8,32},{16,40},{24,48},{32,56},{40,64},{48,72},{56,80},{64,... | collective-permute-start | bytes 3080 | tf_op jit(solution)/shard_map/ppermute | solution.py:18
  23.5 35.4 %collective-permute-start.4 = (s32[256]{0:T(256)}, s32[256]{0:T(256)S(1)}, u32[]{:S(2)}, u32[]{:S(2)}) collective-permute-start(s32[256]{0:T(256)} %param.11), channel_id=1, source_target_pairs={{0,32},{8,40},{16,48},{24,56},{32,64},{40,72},{48,80},{56,88},{64,... | collective-permute-start | bytes 3080 | tf_op jit(solution)/shard_map/ppermute | solution.py:18
  28.4 13.5 %collective-permute-start = (s32[256]{0:T(256)}, s32[256]{0:T(256)S(1)}, u32[]{:S(2)}, u32[]{:S(2)}) collective-permute-start(s32[256]{0:T(256)} %param.11), channel_id=1, source_target_pairs={{0,64},{8,72},{16,80},{24,88},{32,96},{40,104},{48,112},{56,120},{... | collective-permute-start | bytes 3080 | tf_op jit(solution)/shard_map/ppermute | solution.py:18
  34.6 35.6 %all-to-all-start = ((bf16[8,256,256]{2,1,0:T(8,128)(2,1)}), bf16[8,256,256]{2,1,0:T(8,128)(2,1)S(1)}, u32[]{:S(2)}, u32[]{:S(2)}) async-start(bf16[8,256,256]{2,1,0:T(8,128)(2,1)} %broadcast_in_dim.37), calls=%async_computation | async-start | bytes 2097152 | tf_op jit(solution)/shard_map/all_to_all | solution.py:25
  41.9 3.6 %collective-permute-start.1 = (s32[256]{0:T(256)S(1)}, s32[256]{0:T(256)S(1)}, u32[]{:S(2)}, u32[]{:S(2)}) collective-permute-start(s32[256]{0:T(256)S(1)} %copy-done.15), channel_id=1, source_target_pairs={{0,56},{8,64},{16,72},{24,80},{32,88},{40,96},{48,104},{56,112},{6... | collective-permute-start | bytes 3080 | tf_op jit(solution)/shard_map/ppermute | solution.py:18
  45.5 7.0 %collective-permute-start.2 = (s32[256]{0:T(256)S(1)}, s32[256]{0:T(256)S(1)}, u32[]{:S(2)}, u32[]{:S(2)}) collective-permute-start(s32[256]{0:T(256)S(1)} %copy-done.15), channel_id=1, source_target_pairs={{0,48},{8,56},{16,64},{24,72},{32,80},{40,88},{48,96},{56,104},{64... | collective-permute-start | bytes 3080 | tf_op jit(solution)/shard_map/ppermute | solution.py:18
  52.6 6.4 %collective-permute-start.3 = (s32[256]{0:T(256)S(1)}, s32[256]{0:T(256)S(1)}, u32[]{:S(2)}, u32[]{:S(2)}) collective-permute-start(s32[256]{0:T(256)S(1)} %copy-done.15), channel_id=1, source_target_pairs={{0,40},{8,48},{16,56},{24,64},{32,72},{40,80},{48,88},{56,96},{64,... | collective-permute-start | bytes 3080 | tf_op jit(solution)/shard_map/ppermute | solution.py:18
  112.6 2.0 copy-start.10
  112.6 2.0 copy-start.11
  114.7 14.1 %collective-permute-start.9 = (bf16[256,2,256]{0,2,1:T(8,128)(2,1)S(1)}, bf16[256,2,256]{0,2,1:T(8,128)(2,1)S(1)}, u32[]{:S(2)}, u32[]{:S(2)}) collective-permute-start(bf16[256,2,256]{0,2,1:T(8,128)(2,1)S(1)} %pad_maximum_fusion), channel_id=1, source_target_pairs={{0,16},{8,24},{16,32},{24,40},{32,48},{40,56},{48,64},{56,72},{64,... | collective-permute-start | bytes 786440 | tf_op jit(solution)/shard_map/ppermute | solution.py:18
  120.0 16.2 %collective-permute-start.10 = (bf16[256,2,256]{0,2,1:T(8,128)(2,1)S(1)}, bf16[256,2,256]{0,2,1:T(8,128)(2,1)S(1)}, u32[]{:S(2)}, u32[]{:S(2)}) collective-permute-start(bf16[256,2,256]{0,2,1:T(8,128)(2,1)S(1)} %pad_maximum_fusion), channel_id=1, source_target_pairs={{0,32},{8,40},{16,48},{24,56},{32,64},{40,72},{48,80},{56,88},{64,... | collective-permute-start | bytes 786440 | tf_op jit(solution)/shard_map/ppermute | solution.py:18
  122.8 19.1 %collective-permute-start.11 = (bf16[256,2,256]{0,2,1:T(8,128)(2,1)S(1)}, bf16[256,2,256]{0,2,1:T(8,128)(2,1)S(1)}, u32[]{:S(2)}, u32[]{:S(2)}) collective-permute-start(bf16[256,2,256]{0,2,1:T(8,128)(2,1)S(1)} %pad_maximum_fusion), channel_id=1, source_target_pairs={{0,48},{8,56},{16,64},{24,72},{32,80},{40,88},{48,96},{56,104},{64... | collective-permute-start | bytes 786440 | tf_op jit(solution)/shard_map/ppermute | solution.py:18
  124.9 22.0 %collective-permute-start.8 = (bf16[256,2,256]{0,2,1:T(8,128)(2,1)S(1)}, bf16[256,2,256]{0,2,1:T(8,128)(2,1)S(1)}, u32[]{:S(2)}, u32[]{:S(2)}) collective-permute-start(bf16[256,2,256]{0,2,1:T(8,128)(2,1)S(1)} %pad_maximum_fusion), channel_id=1, source_target_pairs={{0,64},{8,72},{16,80},{24,88},{32,96},{40,104},{48,112},{56,120},{... | collective-permute-start | bytes 786440 | tf_op jit(solution)/shard_map/ppermute | solution.py:18
  128.8 22.9 %copy-start = (bf16[256,2,256]{0,2,1:T(8,128)(2,1)}, bf16[256,2,256]{0,2,1:T(8,128)(2,1)S(1)}, u32[]{:S(2)}) copy-start(bf16[256,2,256]{0,2,1:T(8,128)(2,1)S(1)} %collective-permute-done.9) | copy-start | bytes 786436
  136.3 15.4 %copy-start.2 = (bf16[256,2,256]{0,2,1:T(8,128)(2,1)}, bf16[256,2,256]{0,2,1:T(8,128)(2,1)S(1)}, u32[]{:S(2)}) copy-start(bf16[256,2,256]{0,2,1:T(8,128)(2,1)S(1)} %collective-permute-done.10) | copy-start | bytes 786436
  141.9 9.8 %copy-start.4 = (bf16[256,2,256]{0,2,1:T(8,128)(2,1)}, bf16[256,2,256]{0,2,1:T(8,128)(2,1)S(1)}, u32[]{:S(2)}) copy-start(bf16[256,2,256]{0,2,1:T(8,128)(2,1)S(1)} %collective-permute-done.11) | copy-start | bytes 786436
  146.8 4.9 %copy-start.6 = (bf16[256,2,256]{0,2,1:T(8,128)(2,1)}, bf16[256,2,256]{0,2,1:T(8,128)(2,1)S(1)}, u32[]{:S(2)}) copy-start(bf16[256,2,256]{0,2,1:T(8,128)(2,1)S(1)} %collective-permute-done.8) | copy-start | bytes 786436
  148.3 5.5 %collective-permute-start.12 = (bf16[5,256,2,256]{1,3,2,0:T(8,128)(2,1)}, bf16[5,256,2,256]{1,3,2,0:T(8,128)(2,1)}, u32[]{:S(2)}, u32[]{:S(2)}) collective-permute-start(bf16[5,256,2,256]{1,3,2,0:T(8,128)(2,1)} %bitcast_dynamic-update-slice_fusion), channel_id=1, source_target_pairs={{0,8},{8,0},{16,24},{24,16},{32,40},{40,32},{48,56},{56,48},{64,72... | collective-permute-start | bytes 3932168 | tf_op jit(solution)/shard_map/ppermute | solution.py:112
  152.4 1.4 copy-start.7
  152.4 2.5 copy-start.5
  152.4 3.5 %copy-start.3 = (bf16[256,2,256]{0,2,1:T(8,128)(2,1)S(1)}, bf16[256,2,256]{0,2,1:T(8,128)(2,1)}, u32[]{:S(2)}) copy-start(bf16[256,2,256]{0,2,1:T(8,128)(2,1)} %copy-done.2) | copy-start | bytes 786436
  152.4 4.5 %copy-start.1 = (bf16[256,2,256]{0,2,1:T(8,128)(2,1)S(1)}, bf16[256,2,256]{0,2,1:T(8,128)(2,1)}, u32[]{:S(2)}) copy-start(bf16[256,2,256]{0,2,1:T(8,128)(2,1)} %copy-done) | copy-start | bytes 786436
  153.8 6.6 %copy-start.9 = (pred[256,2560]{1,0:T(8,128)(4,1)S(1)}, pred[256,2560]{1,0:T(8,128)(4,1)}, u32[]{:S(2)}) copy-start(pred[256,2560]{1,0:T(8,128)(4,1)} %compare_and_fusion) | copy-start | bytes 1966084
  158.9 1.5 copy-start.14
  172.3 36.2 %copy-start.12 = (bf16[256,256]{1,0:T(8,128)(2,1)S(1)}, bf16[256,256]{1,0:T(8,128)(2,1)}, u32[]{:S(2)}) copy-start(bf16[256,256]{1,0:T(8,128)(2,1)} %param.10) | copy-start | bytes 393220
  247.2 4.6 %copy-start.16 = (s32[16]{0:T(128)S(1)}, s32[16]{0:T(128)}, u32[]{:S(2)}) copy-start(s32[16]{0:T(128)} %param.12) | copy-start | bytes 196
  248.2 32.3 %all-to-all-start.3 = ((bf16[8,256,256]{2,1,0:T(8,128)(2,1)}), bf16[8,256,256]{2,1,0:T(8,128)(2,1)S(1)}, u32[]{:S(2)}, u32[]{:S(2)}) async-start(bf16[8,256,256]{2,1,0:T(8,128)(2,1)} %bitcast.98), calls=%async_computation.3 | async-start | bytes 2097152 | tf_op jit(solution)/shard_map/all_to_all | solution.py:34
  253.4 28.0 %copy-start.8 = (bf16[2,16,16,256]{3,2,1,0:T(8,128)(2,1)}, bf16[2,16,16,256]{3,2,1,0:T(8,128)(2,1)S(1)}, u32[]{:S(2)}) copy-start(bf16[2,16,16,256]{3,2,1,0:T(8,128)(2,1)S(1)} %scatter_fusion) | copy-start | bytes 786436
  (1 other events, 0.7 us)
Sparse Core Ops, SparseCore 0:
  13.2 94.9 all-gather.1

commit v7 on v6

--- a/solution.py
+++ b/solution.py
@@ -70,13 +70,15 @@
     local_index = jnp.arange(tok_rows, dtype=jnp.int32)
 
     attn_width = wq.shape[1]
-    ff_width = wg.shape[1]
-    pieces = [wq, wk, wv, wo.T, wg, wu, wd.T]
-    widths = [piece.shape[1] for piece in pieces]
-    gathered = lax.all_gather(jnp.concatenate(pieces, axis=1), "wide", axis=0, tiled=True)
-    offsets = [sum(widths[:k]) for k in range(len(widths))]
-    full = [gathered[:, o:o + w] for o, w in zip(offsets, widths)]
-    wq_all, wk_all, wv_all, wo_t, wg_all, wu_all, wd_t = full
+
+    def gather_pieces(pieces):
+        widths = [piece.shape[1] for piece in pieces]
+        gathered = lax.all_gather(jnp.concatenate(pieces, axis=1), "wide", axis=0, tiled=True)
+        offsets = [sum(widths[:k]) for k in range(len(widths))]
+        return [gathered[:, o:o + w] for o, w in zip(offsets, widths)]
+
+    wq_all, wk_all, wv_all, wo_t = gather_pieces([wq, wk, wv, wo.T])
+    wg_all, wu_all, wd_t = gather_pieces([wg, wu, wd.T])
 
     id_blocks = []
     for step_back in range(REACH, 0, -1):

time: 290 us -> 283 us (0.976)
  local copies, waits for them, and re-layouts: 25.7 us -> 20.2 us
    all_gather x1 -> x2, waiting for transfers between devices: 36.3 us -> 29.2 us  [gather_pieces(): lax.all_gather(jnp.concatenate(pieces, axis=1), 'wide', axis=0, tiled=True)]
    all_to_all x1, waiting for transfers between devices: 9.54 us -> 15.4 us  [swap_gather(): got = lax.all_to_all(copies, axis, 0, 0, tiled=True)]
    unnamed x53, local copies, waits for them, and re-layouts: 14.7 us -> 9.67 us
  transfers between devices with their start and end apart: 16 -> 17, of which waited for: 9 -> 7; matrix products, arithmetic and copies ran while one was open for 4% -> 14% of each run, Pallas kernels for 0% -> 0%
where the time goes in v7:
time: 283 us; the launch traced here: 282 us
  waiting for transfers between devices  90.5 us (32%)
  blocking collectives  67.6 us (24%)
  starting transfers between devices  58.3 us (21%)
  matrix products  20.5 us (7%)
  local copies, waits for them, and re-layouts  20.2 us (7%)
  between operations  14.9 us (5%)
  other arithmetic  10.1 us (4%)
    ppermute x12, starting transfers between devices, shifted(): lax.ppermute(value, axis, [(source, source + steps) for source in range(f...  45.7 us
    all_to_all x1, blocking collectives, swap_sum(): got = lax.all_to_all(pieces, axis, 0, 0, tiled=True)  36 us
    all_to_all x1, blocking collectives, swap_gather(): got = lax.all_to_all(copies, axis, 0, 0, tiled=True)  31.6 us
    all_gather x2, waiting for transfers between devices, gather_pieces(): lax.all_gather(jnp.concatenate(pieces, axis=1), 'wide', axis=0, tiled=True)  29.2 us
    all_to_all x1, waiting for transfers between devices, swap_sum(): got = lax.all_to_all(pieces, axis, 0, 0, tiled=True)  27.1 us
    ppermute x12, waiting for transfers between devices, shifted(): lax.ppermute(value, axis, [(source, source + steps) for source in range(f...  18.7 us
    all_to_all x1, waiting for transfers between devices, swap_gather(): got = lax.all_to_all(copies, axis, 0, 0, tiled=True)  15.4 us
    unnamed x53, local copies, waits for them, and re-layouts  9.67 us
  transfers between devices with their start and end apart: 17, of which 7 were waited for; matrix products, arithmetic and copies ran while one was open for 14% of the time, Pallas kernels for 0%

profile of v7, /device:TPU:6, one launch (start us, length us, event | category | flops | bytes accessed | tf_op | source)
XLA Modules:
  0.0 282.0 jit_solution(1236416948706278077)
XLA Ops:
  8.7 4.3 %collective-permute-start = (s32[256]{0:T(256)}, s32[256]{0:T(256)S(1)}, u32[]{:S(2)}, u32[]{:S(2)}) collective-permute-start(s32[256]{0:T(256)} %param.11), channel_id=1, source_target_pairs={{0,64},{8,72},{16,80},{24,88},{32,96},{40,104},{48,112},{56,120},{... | collective-permute-start | bytes 3080 | tf_op jit(solution)/shard_map/ppermute | solution.py:18
  13.0 3.7 %collective-permute-start.1 = (s32[256]{0:T(256)}, s32[256]{0:T(256)S(1)}, u32[]{:S(2)}, u32[]{:S(2)}) collective-permute-start(s32[256]{0:T(256)} %param.11), channel_id=1, source_target_pairs={{0,56},{8,64},{16,72},{24,80},{32,88},{40,96},{48,104},{56,112},{6... | collective-permute-start | bytes 3080 | tf_op jit(solution)/shard_map/ppermute | solution.py:18
  16.7 4.3 %collective-permute-start.2 = (s32[256]{0:T(256)}, s32[256]{0:T(256)S(1)}, u32[]{:S(2)}, u32[]{:S(2)}) collective-permute-start(s32[256]{0:T(256)} %param.11), channel_id=1, source_target_pairs={{0,48},{8,56},{16,64},{24,72},{32,80},{40,88},{48,96},{56,104},{64... | collective-permute-start | bytes 3080 | tf_op jit(solution)/shard_map/ppermute | solution.py:18
  21.0 6.4 %collective-permute-start.3 = (s32[256]{0:T(256)}, s32[256]{0:T(256)S(1)}, u32[]{:S(2)}, u32[]{:S(2)}) collective-permute-start(s32[256]{0:T(256)} %param.11), channel_id=1, source_target_pairs={{0,40},{8,48},{16,56},{24,64},{32,72},{40,80},{48,88},{56,96},{64,... | collective-permute-start | bytes 3080 | tf_op jit(solution)/shard_map/ppermute | solution.py:18
  27.3 4.3 %collective-permute-start.4 = (s32[256]{0:T(256)}, s32[256]{0:T(256)S(1)}, u32[]{:S(2)}, u32[]{:S(2)}) collective-permute-start(s32[256]{0:T(256)} %param.11), channel_id=1, source_target_pairs={{0,32},{8,40},{16,48},{24,56},{32,64},{40,72},{48,80},{56,88},{64,... | collective-permute-start | bytes 3080 | tf_op jit(solution)/shard_map/ppermute | solution.py:18
  31.6 2.0 broadcast_in_dim.37
  33.6 7.1 %all-to-all-start = ((bf16[8,256,256]{2,1,0:T(8,128)(2,1)}), bf16[8,256,256]{2,1,0:T(8,128)(2,1)S(1)}, u32[]{:S(2)}, u32[]{:S(2)}) async-start(bf16[8,256,256]{2,1,0:T(8,128)(2,1)} %broadcast_in_dim.37), calls=%async_computation | async-start | bytes 2097152 | tf_op jit(solution)/shard_map/all_to_all | solution.py:25
  41.6 3.2 %collective-permute-start.5 = (s32[256]{0:T(256)S(1)}, s32[256]{0:T(256)S(1)}, u32[]{:S(2)}, u32[]{:S(2)}) collective-permute-start(s32[256]{0:T(256)S(1)} %copy-done.18), channel_id=1, source_target_pairs={{0,24},{8,32},{16,40},{24,48},{32,56},{40,64},{48,72},{56,80},{64,... | collective-permute-start | bytes 3080 | tf_op jit(solution)/shard_map/ppermute | solution.py:18
  44.9 3.0 %collective-permute-start.6 = (s32[256]{0:T(256)S(1)}, s32[256]{0:T(256)S(1)}, u32[]{:S(2)}, u32[]{:S(2)}) collective-permute-start(s32[256]{0:T(256)S(1)} %copy-done.18), channel_id=1, source_target_pairs={{0,16},{8,24},{16,32},{24,40},{32,48},{40,56},{48,64},{56,72},{64,... | collective-permute-start | bytes 3080 | tf_op jit(solution)/shard_map/ppermute | solution.py:18
  47.9 3.4 %collective-permute-start.7 = (s32[256]{0:T(256)S(1)}, s32[256]{0:T(256)S(1)}, u32[]{:S(2)}, u32[]{:S(2)}) collective-permute-start(s32[256]{0:T(256)S(1)} %copy-done.18), channel_id=1, source_target_pairs={{0,8},{8,16},{16,24},{24,32},{32,40},{40,48},{48,56},{56,64},{64,7... | collective-permute-start | bytes 3080 | tf_op jit(solution)/shard_map/ppermute | solution.py:18
  54.4 15.4 %all-to-all-done = bf16[8,256,256]{2,1,0:T(8,128)(2,1)S(1)} async-done(((bf16[8,256,256]{2,1,0:T(8,128)(2,1)}), bf16[8,256,256]{2,1,0:T(8,128)(2,1)S(1)}, u32[]{:S(2)}, u32[]{:S(2)}) %all-to-all-start) | async-done | bytes 1048608 | tf_op jit(solution)/shard_map/all_to_all | solution.py:25
  71.5 29.2 %all-gather.3.cloned.1.call-done = bf16[2048,1024]{1,0:T(8,128)(2,1)} async-done(((bf16[32,1024]{1,0:T(8,128)(2,1)}), bf16[2048,1024]{1,0:T(8,128)(2,1)}) %all-gather.3.cloned.1.call-update) | async-done | bytes 4194320 | tf_op jit(solution)/shard_map/all_gather | solution.py:76
  100.7 3.0 %slice_bitcast_fusion = (bf16[256,2048]{0,1:T(8,128)(2,1)}, bf16[256,2048]{0,1:T(8,128)(2,1)}) fusion(bf16[2048,1024]{1,0:T(8,128)(2,1)} %all-gather.3.cloned.1.call-done), kind=kLoop, calls=%fused_computation.39 | loop fusion | bytes 4194304 | tf_op jit(solution)/shard_map/dot_general | solution.py:64
  105.2 1.7 convolution_convert_fusion.2
  107.6 3.6 %collective-permute-start.9 = (bf16[256,2,256]{0,2,1:T(8,128)(2,1)S(1)}, bf16[256,2,256]{0,2,1:T(8,128)(2,1)S(1)}, u32[]{:S(2)}, u32[]{:S(2)}) collective-permute-start(bf16[256,2,256]{0,2,1:T(8,128)(2,1)S(1)} %pad_maximum_fusion), channel_id=1, source_target_pairs={{0,16},{8,24},{16,32},{24,40},{32,48},{40,56},{48,64},{56,72},{64,... | collective-permute-start | bytes 786440 | tf_op jit(solution)/shard_map/ppermute | solution.py:18
  111.3 3.3 %collective-permute-start.10 = (bf16[256,2,256]{0,2,1:T(8,128)(2,1)S(1)}, bf16[256,2,256]{0,2,1:T(8,128)(2,1)S(1)}, u32[]{:S(2)}, u32[]{:S(2)}) collective-permute-start(bf16[256,2,256]{0,2,1:T(8,128)(2,1)S(1)} %pad_maximum_fusion), channel_id=1, source_target_pairs={{0,32},{8,40},{16,48},{24,56},{32,64},{40,72},{48,80},{56,88},{64,... | collective-permute-start | bytes 786440 | tf_op jit(solution)/shard_map/ppermute | solution.py:18
  114.7 2.6 collective-permute-start.11
  117.3 3.6 %collective-permute-start.8 = (bf16[256,2,256]{0,2,1:T(8,128)(2,1)S(1)}, bf16[256,2,256]{0,2,1:T(8,128)(2,1)S(1)}, u32[]{:S(2)}, u32[]{:S(2)}) collective-permute-start(bf16[256,2,256]{0,2,1:T(8,128)(2,1)S(1)} %pad_maximum_fusion), channel_id=1, source_target_pairs={{0,64},{8,72},{16,80},{24,88},{32,96},{40,104},{48,112},{56,120},{... | collective-permute-start | bytes 786440 | tf_op jit(solution)/shard_map/ppermute | solution.py:18
  121.6 6.2 %collective-permute-done.10 = bf16[256,2,256]{0,2,1:T(8,128)(2,1)S(1)} collective-permute-done((bf16[256,2,256]{0,2,1:T(8,128)(2,1)S(1)}, bf16[256,2,256]{0,2,1:T(8,128)(2,1)S(1)}, u32[]{:S(2)}, u32[]{:S(2)}) %collective-permute-start.10) | collective-permute-done | bytes 262176 | tf_op jit(solution)/shard_map/ppermute | solution.py:18
  128.6 5.9 %collective-permute-done.11 = bf16[256,2,256]{0,2,1:T(8,128)(2,1)S(1)} collective-permute-done((bf16[256,2,256]{0,2,1:T(8,128)(2,1)S(1)}, bf16[256,2,256]{0,2,1:T(8,128)(2,1)S(1)}, u32[]{:S(2)}, u32[]{:S(2)}) %collective-permute-start.11) | collective-permute-done | bytes 262176 | tf_op jit(solution)/shard_map/ppermute | solution.py:18
  135.3 5.3 %collective-permute-done.8 = bf16[256,2,256]{0,2,1:T(8,128)(2,1)S(1)} collective-permute-done((bf16[256,2,256]{0,2,1:T(8,128)(2,1)S(1)}, bf16[256,2,256]{0,2,1:T(8,128)(2,1)S(1)}, u32[]{:S(2)}, u32[]{:S(2)}) %collective-permute-start.8) | collective-permute-done | bytes 262176 | tf_op jit(solution)/shard_map/ppermute | solution.py:18
  142.1 1.9 collective-permute-start.12
  152.7 1.5 copy-done.17
  154.2 6.2 %fusion.46 = (f32[2,256]{1,0:T(2,128)S(1)}, f32[2,256,2560]{2,1,0:T(8,128)}) fusion(pred[256,2560]{1,0:T(8,128)(4,1)S(1)} %copy-done.10, bf16[2560,2,256]{0,2,1:T(8,128)(2,1)} %copy-done.17, bf16[256,2,64]{0,2,1:T(8,128)(2,1)S(1)} %get-tuple-element.5, bf16[256,2,64]{0,2,1:T(8,128)(2,1)S(1)} %get-tuple-element.4), kind=kOutput, calls=%fused_computation.108 | convolution fusion | flops 342362624 | bytes 7997440 | tf_op jit(solution)/shard_map/sub | solution.py:141
  160.4 4.0 %fusion.23 = bf16[2,128,256]{2,1,0:T(8,128)(2,1)S(1)} fusion(f32[2,256,2560]{2,1,0:T(8,128)} %get-tuple-element.13, f32[2,256]{1,0:T(2,128)S(1)} %get-tuple-element.12, bf16[2560,2,256]{0,2,1:T(8,128)(2,1)} %copy-done.17), kind=kOutput, calls=%fused_computation.34 | convolution fusion | flops 338231296 | bytes 6686720 | tf_op jit(solution)/shard_map/hqk,khd->qhd/dot_general | solution.py:143
  164.4 1.7 convolution_convert_fusion.1
  166.2 36.0 %all_to_all.20 = bf16[8,256,256]{2,1,0:T(8,128)(2,1)S(1)} all-to-all(bf16[8,256,256]{2,1,0:T(8,128)(2,1)S(1)} %bitcast.104), channel_id=1, replica_groups=mesh['wide'=64,'narrow'=8] {'narrow'}, dimensions={0} | all-to-all | bytes 2097152 | tf_op jit(solution)/shard_map/all_to_all | solution.py:34
  202.5 31.6 %all_to_all.21 = bf16[8,256,256]{1,2,0:T(8,128)(2,1)S(1)} all-to-all(bf16[8,256,256]{1,2,0:T(8,128)(2,1)S(1)} %broadcast_in_dim.42), channel_id=1, replica_groups=mesh['wide'=64,'narrow'=8] {'narrow'}, dimensions={0} | all-to-all | bytes 2097152 | tf_op jit(solution)/shard_map/all_to_all | solution.py:25
  235.1 2.3 fusion.7
  237.4 3.6 %convolution_convert_fusion = bf16[256,2048]{1,0:T(8,128)(2,1)S(1)} fusion(bf16[2048,1536]{1,0:T(8,128)(2,1)} %all-gather.5.cloned.1.call-done, bf16[256,2048]{0,1:T(8,128)(2,1)S(1)} %fusion.10, f32[256,512]{1,0:T(8,128)S(1)} %fusion.7), kind=kOutput, calls=%fused_computation.8 | convolution fusion | flops 1075052544 | bytes 6815744 | tf_op jit(solution)/shard_map/dot_general | solution.py:156
  242.1 3.6 %all-to-all-start.3 = ((bf16[8,256,256]{2,1,0:T(8,128)(2,1)}), bf16[8,256,256]{2,1,0:T(8,128)(2,1)S(1)}, u32[]{:S(2)}, u32[]{:S(2)}) async-start(bf16[8,256,256]{2,1,0:T(8,128)(2,1)} %bitcast.96), calls=%async_computation.3 | async-start | bytes 2097152 | tf_op jit(solution)/shard_map/all_to_all | solution.py:34
  247.2 27.1 %all-to-all-done.3 = bf16[8,256,256]{2,1,0:T(8,128)(2,1)S(1)} async-done(((bf16[8,256,256]{2,1,0:T(8,128)(2,1)}), bf16[8,256,256]{2,1,0:T(8,128)(2,1)S(1)}, u32[]{:S(2)}, u32[]{:S(2)}) %all-to-all-start.3) | async-done | bytes 1048608 | tf_op jit(solution)/shard_map/all_to_all | solution.py:34
  (128 shorter events, 26.2 us)
Async XLA Ops:
  7.2 34.5 %copy-start.18 = (s32[256]{0:T(256)S(1)}, s32[256]{0:T(256)}, u32[]{:S(2)}) copy-start(s32[256]{0:T(256)} %param.11) | copy-start | bytes 3076
  7.2 33.6 %copy-start.14 = (bf16[512,32]{0,1:T(8,128)(2,1)S(1)}, bf16[512,32]{0,1:T(8,128)(2,1)}, u32[]{:S(2)}) copy-start(bf16[512,32]{0,1:T(8,128)(2,1)} %param.19) | copy-start | bytes 98308
  7.2 33.6 %copy-start.16 = (bf16[32,512]{1,0:T(8,128)(2,1)S(1)}, bf16[32,512]{1,0:T(8,128)(2,1)}, u32[]{:S(2)}) copy-start(bf16[32,512]{1,0:T(8,128)(2,1)} %param.17) | copy-start | bytes 98308
  7.2 33.6 %copy-start.15 = (bf16[32,512]{1,0:T(8,128)(2,1)S(1)}, bf16[32,512]{1,0:T(8,128)(2,1)}, u32[]{:S(2)}) copy-start(bf16[32,512]{1,0:T(8,128)(2,1)} %param.18) | copy-start | bytes 98308
  7.2 93.5 %all-gather.3.cloned.1.call-start = ((), (), s32[]{:S(2)}) async-start(), calls=%async_computation.4 | async-start | bytes 4259840 | tf_op jit(solution)/shard_map/all_gather | solution.py:76
  8.7 32.9 %collective-permute-start = (s32[256]{0:T(256)}, s32[256]{0:T(256)S(1)}, u32[]{:S(2)}, u32[]{:S(2)}) collective-permute-start(s32[256]{0:T(256)} %param.11), channel_id=1, source_target_pairs={{0,64},{8,72},{16,80},{24,88},{32,96},{40,104},{48,112},{56,120},{... | collective-permute-start | bytes 3080 | tf_op jit(solution)/shard_map/ppermute | solution.py:18
  13.0 31.9 %collective-permute-start.1 = (s32[256]{0:T(256)}, s32[256]{0:T(256)S(1)}, u32[]{:S(2)}, u32[]{:S(2)}) collective-permute-start(s32[256]{0:T(256)} %param.11), channel_id=1, source_target_pairs={{0,56},{8,64},{16,72},{24,80},{32,88},{40,96},{48,104},{56,112},{6... | collective-permute-start | bytes 3080 | tf_op jit(solution)/shard_map/ppermute | solution.py:18
  16.7 31.2 %collective-permute-start.2 = (s32[256]{0:T(256)}, s32[256]{0:T(256)S(1)}, u32[]{:S(2)}, u32[]{:S(2)}) collective-permute-start(s32[256]{0:T(256)} %param.11), channel_id=1, source_target_pairs={{0,48},{8,56},{16,64},{24,72},{32,80},{40,88},{48,96},{56,104},{64... | collective-permute-start | bytes 3080 | tf_op jit(solution)/shard_map/ppermute | solution.py:18
  21.0 30.4 %collective-permute-start.3 = (s32[256]{0:T(256)}, s32[256]{0:T(256)S(1)}, u32[]{:S(2)}, u32[]{:S(2)}) collective-permute-start(s32[256]{0:T(256)} %param.11), channel_id=1, source_target_pairs={{0,40},{8,48},{16,56},{24,64},{32,72},{40,80},{48,88},{56,96},{64,... | collective-permute-start | bytes 3080 | tf_op jit(solution)/shard_map/ppermute | solution.py:18
  27.3 24.1 %collective-permute-start.4 = (s32[256]{0:T(256)}, s32[256]{0:T(256)S(1)}, u32[]{:S(2)}, u32[]{:S(2)}) collective-permute-start(s32[256]{0:T(256)} %param.11), channel_id=1, source_target_pairs={{0,32},{8,40},{16,48},{24,56},{32,64},{40,72},{48,80},{56,88},{64,... | collective-permute-start | bytes 3080 | tf_op jit(solution)/shard_map/ppermute | solution.py:18
  33.6 36.2 %all-to-all-start = ((bf16[8,256,256]{2,1,0:T(8,128)(2,1)}), bf16[8,256,256]{2,1,0:T(8,128)(2,1)S(1)}, u32[]{:S(2)}, u32[]{:S(2)}) async-start(bf16[8,256,256]{2,1,0:T(8,128)(2,1)} %broadcast_in_dim.37), calls=%async_computation | async-start | bytes 2097152 | tf_op jit(solution)/shard_map/all_to_all | solution.py:25
  40.7 194.4 %all-gather.5.cloned.1.call-start = ((), (), s32[]{:S(2)}) async-start(), calls=%async_computation.5 | async-start | bytes 6389760 | tf_op jit(solution)/shard_map/all_gather | solution.py:76
  41.6 9.8 %collective-permute-start.5 = (s32[256]{0:T(256)S(1)}, s32[256]{0:T(256)S(1)}, u32[]{:S(2)}, u32[]{:S(2)}) collective-permute-start(s32[256]{0:T(256)S(1)} %copy-done.18), channel_id=1, source_target_pairs={{0,24},{8,32},{16,40},{24,48},{32,56},{40,64},{48,72},{56,80},{64,... | collective-permute-start | bytes 3080 | tf_op jit(solution)/shard_map/ppermute | solution.py:18
  44.9 6.6 %collective-permute-start.6 = (s32[256]{0:T(256)S(1)}, s32[256]{0:T(256)S(1)}, u32[]{:S(2)}, u32[]{:S(2)}) collective-permute-start(s32[256]{0:T(256)S(1)} %copy-done.18), channel_id=1, source_target_pairs={{0,16},{8,24},{16,32},{24,40},{32,48},{40,56},{48,64},{56,72},{64,... | collective-permute-start | bytes 3080 | tf_op jit(solution)/shard_map/ppermute | solution.py:18
  47.9 4.9 %collective-permute-start.7 = (s32[256]{0:T(256)S(1)}, s32[256]{0:T(256)S(1)}, u32[]{:S(2)}, u32[]{:S(2)}) collective-permute-start(s32[256]{0:T(256)S(1)} %copy-done.18), channel_id=1, source_target_pairs={{0,8},{8,16},{16,24},{24,32},{32,40},{40,48},{48,56},{56,64},{64,7... | collective-permute-start | bytes 3080 | tf_op jit(solution)/shard_map/ppermute | solution.py:18
  107.5 38.0 %copy-start = (bf16[256,2048]{0,1:T(8,128)(2,1)S(1)}, bf16[256,2048]{0,1:T(8,128)(2,1)}, u32[]{:S(2)}) copy-start(bf16[256,2048]{0,1:T(8,128)(2,1)} %get-tuple-element.2) | copy-start | bytes 3145732
  107.6 13.2 %collective-permute-start.9 = (bf16[256,2,256]{0,2,1:T(8,128)(2,1)S(1)}, bf16[256,2,256]{0,2,1:T(8,128)(2,1)S(1)}, u32[]{:S(2)}, u32[]{:S(2)}) collective-permute-start(bf16[256,2,256]{0,2,1:T(8,128)(2,1)S(1)} %pad_maximum_fusion), channel_id=1, source_target_pairs={{0,16},{8,24},{16,32},{24,40},{32,48},{40,56},{48,64},{56,72},{64,... | collective-permute-start | bytes 786440 | tf_op jit(solution)/shard_map/ppermute | solution.py:18
  111.3 16.4 %collective-permute-start.10 = (bf16[256,2,256]{0,2,1:T(8,128)(2,1)S(1)}, bf16[256,2,256]{0,2,1:T(8,128)(2,1)S(1)}, u32[]{:S(2)}, u32[]{:S(2)}) collective-permute-start(bf16[256,2,256]{0,2,1:T(8,128)(2,1)S(1)} %pad_maximum_fusion), channel_id=1, source_target_pairs={{0,32},{8,40},{16,48},{24,56},{32,64},{40,72},{48,80},{56,88},{64,... | collective-permute-start | bytes 786440 | tf_op jit(solution)/shard_map/ppermute | solution.py:18
  114.7 19.8 %collective-permute-start.11 = (bf16[256,2,256]{0,2,1:T(8,128)(2,1)S(1)}, bf16[256,2,256]{0,2,1:T(8,128)(2,1)S(1)}, u32[]{:S(2)}, u32[]{:S(2)}) collective-permute-start(bf16[256,2,256]{0,2,1:T(8,128)(2,1)S(1)} %pad_maximum_fusion), channel_id=1, source_target_pairs={{0,48},{8,56},{16,64},{24,72},{32,80},{40,88},{48,96},{56,104},{64... | collective-permute-start | bytes 786440 | tf_op jit(solution)/shard_map/ppermute | solution.py:18
  117.3 23.3 %collective-permute-start.8 = (bf16[256,2,256]{0,2,1:T(8,128)(2,1)S(1)}, bf16[256,2,256]{0,2,1:T(8,128)(2,1)S(1)}, u32[]{:S(2)}, u32[]{:S(2)}) collective-permute-start(bf16[256,2,256]{0,2,1:T(8,128)(2,1)S(1)} %pad_maximum_fusion), channel_id=1, source_target_pairs={{0,64},{8,72},{16,80},{24,88},{32,96},{40,104},{48,112},{56,120},{... | collective-permute-start | bytes 786440 | tf_op jit(solution)/shard_map/ppermute | solution.py:18
  120.8 24.6 %copy-start.1 = (bf16[256,2,256]{0,2,1:T(8,128)(2,1)}, bf16[256,2,256]{0,2,1:T(8,128)(2,1)S(1)}, u32[]{:S(2)}) copy-start(bf16[256,2,256]{0,2,1:T(8,128)(2,1)S(1)} %collective-permute-done.9) | copy-start | bytes 786436
  127.8 17.7 %copy-start.3 = (bf16[256,2,256]{0,2,1:T(8,128)(2,1)}, bf16[256,2,256]{0,2,1:T(8,128)(2,1)S(1)}, u32[]{:S(2)}) copy-start(bf16[256,2,256]{0,2,1:T(8,128)(2,1)S(1)} %collective-permute-done.10) | copy-start | bytes 786436
  134.5 11.0 %copy-start.5 = (bf16[256,2,256]{0,2,1:T(8,128)(2,1)}, bf16[256,2,256]{0,2,1:T(8,128)(2,1)S(1)}, u32[]{:S(2)}) copy-start(bf16[256,2,256]{0,2,1:T(8,128)(2,1)S(1)} %collective-permute-done.11) | copy-start | bytes 786436
  140.6 4.9 %copy-start.7 = (bf16[256,2,256]{0,2,1:T(8,128)(2,1)}, bf16[256,2,256]{0,2,1:T(8,128)(2,1)S(1)}, u32[]{:S(2)}) copy-start(bf16[256,2,256]{0,2,1:T(8,128)(2,1)S(1)} %collective-permute-done.8) | copy-start | bytes 786436
  142.1 5.5 %collective-permute-start.12 = (bf16[5,256,2,256]{1,3,2,0:T(8,128)(2,1)}, bf16[5,256,2,256]{1,3,2,0:T(8,128)(2,1)}, u32[]{:S(2)}, u32[]{:S(2)}) collective-permute-start(bf16[5,256,2,256]{1,3,2,0:T(8,128)(2,1)} %bitcast_dynamic-update-slice_fusion), channel_id=1, source_target_pairs={{0,8},{8,0},{16,24},{24,16},{32,40},{40,32},{48,56},{56,48},{64,72... | collective-permute-start | bytes 3932168 | tf_op jit(solution)/shard_map/ppermute | solution.py:114
  146.2 3.5 %copy-start.4 = (bf16[256,2,256]{0,2,1:T(8,128)(2,1)S(1)}, bf16[256,2,256]{0,2,1:T(8,128)(2,1)}, u32[]{:S(2)}) copy-start(bf16[256,2,256]{0,2,1:T(8,128)(2,1)} %copy-done.3) | copy-start | bytes 786436
  146.2 4.5 %copy-start.2 = (bf16[256,2,256]{0,2,1:T(8,128)(2,1)S(1)}, bf16[256,2,256]{0,2,1:T(8,128)(2,1)}, u32[]{:S(2)}) copy-start(bf16[256,2,256]{0,2,1:T(8,128)(2,1)} %copy-done.1) | copy-start | bytes 786436
  147.5 6.6 %copy-start.10 = (pred[256,2560]{1,0:T(8,128)(4,1)S(1)}, pred[256,2560]{1,0:T(8,128)(4,1)}, u32[]{:S(2)}) copy-start(pred[256,2560]{1,0:T(8,128)(4,1)} %compare_and_fusion) | copy-start | bytes 1966084
  166.1 36.2 %copy-start.13 = (bf16[256,256]{1,0:T(8,128)(2,1)S(1)}, bf16[256,256]{1,0:T(8,128)(2,1)}, u32[]{:S(2)}) copy-start(bf16[256,256]{1,0:T(8,128)(2,1)} %param.10) | copy-start | bytes 393220
  241.0 4.6 %copy-start.19 = (s32[16]{0:T(128)S(1)}, s32[16]{0:T(128)}, u32[]{:S(2)}) copy-start(s32[16]{0:T(128)} %param.12) | copy-start | bytes 196
  242.1 32.3 %all-to-all-start.3 = ((bf16[8,256,256]{2,1,0:T(8,128)(2,1)}), bf16[8,256,256]{2,1,0:T(8,128)(2,1)S(1)}, u32[]{:S(2)}, u32[]{:S(2)}) async-start(bf16[8,256,256]{2,1,0:T(8,128)(2,1)} %bitcast.96), calls=%async_computation.3 | async-start | bytes 2097152 | tf_op jit(solution)/shard_map/all_to_all | solution.py:34
  247.2 28.0 %copy-start.9 = (bf16[2,16,16,256]{3,2,1,0:T(8,128)(2,1)}, bf16[2,16,16,256]{3,2,1,0:T(8,128)(2,1)S(1)}, u32[]{:S(2)}) copy-start(bf16[2,16,16,256]{3,2,1,0:T(8,128)(2,1)S(1)} %scatter_fusion) | copy-start | bytes 786436
  (5 other events, 10.0 us)
Sparse Core Ops, SparseCore 0:
  12.0 88.6 all-gather.2
  104.6 90.4 all-gather.4

commit v8 on v7

--- a/solution.py
+++ b/solution.py
@@ -77,7 +77,9 @@
         offsets = [sum(widths[:k]) for k in range(len(widths))]
         return [gathered[:, o:o + w] for o, w in zip(offsets, widths)]
 
-    wq_all, wk_all, wv_all, wo_t = gather_pieces([wq, wk, wv, wo.T])
+    attn_pieces = [wq, wk, wv, wo.T]
+    attn_gathered = lax.all_gather(jnp.concatenate(attn_pieces, axis=1), "wide", axis=0, tiled=True)
+    wo_t = attn_gathered[:, 3 * attn_width:]
     wg_all, wu_all, wd_t = gather_pieces([wg, wu, wd.T])
 
     id_blocks = []
@@ -98,9 +100,10 @@
     local_width = attn_width
     head_count = local_width // HEAD_DIM
 
-    q_proj = add_rows(normed, wq_all)
-    k_proj = add_rows(normed, wk_all)
-    v_proj = add_rows(normed, wv_all)
+    projected = add_rows(normed, attn_gathered)
+    q_proj = projected[:, :attn_width]
+    k_proj = projected[:, attn_width:2 * attn_width]
+    v_proj = projected[:, 2 * attn_width:3 * attn_width]
     queries = rotate(q_proj.reshape(tok_rows, head_count, HEAD_DIM), positions).astype(jnp.bfloat16)
     keys_rot = rotate(k_proj.reshape(tok_rows, head_count, HEAD_DIM), positions).astype(
         jnp.bfloat16

time: 283 us -> 275 us (0.972)
  local copies, waits for them, and re-layouts: 20.2 us -> 16.3 us
    all_gather x0 -> x1, waiting for transfers between devices: none -> 29.8 us  [per_device(): lax.all_gather(jnp.concatenate(attn_pieces, axis=1), 'wide', axis=0, tile...]
    all_gather x2 -> x1, waiting for transfers between devices: 29.2 us -> 0.02 us  [gather_pieces(): lax.all_gather(jnp.concatenate(pieces, axis=1), 'wide', axis=0, tiled=True)]
    dot_general x3 -> x0, local copies, waits for them, and re-layouts: 5.13 us -> none  [add_rows(): return jnp.dot(source, piece, preferred_element_type=jnp.float32)]
    all_to_all x1, waiting for transfers between devices: 27.1 us -> 23.7 us  [swap_sum(): got = lax.all_to_all(pieces, axis, 0, 0, tiled=True)]
    dot_general x4 -> x2, matrix products: 4.93 us -> 5.77 us  [add_rows(): return jnp.dot(source, piece, preferred_element_type=jnp.float32)]
    unnamed x53 -> x30, local copies, waits for them, and re-layouts: 9.67 us -> 10.5 us
  transfers between devices with their start and end apart: 17 -> 17, of which waited for: 7 -> 8; matrix products, arithmetic and copies ran while one was open for 14% -> 14% of each run, Pallas kernels for 0% -> 0%
where the time goes in v8:
time: 275 us; the launch traced here: 274 us
  waiting for transfers between devices  88.1 us (32%)
  blocking collectives  66 us (24%)
  starting transfers between devices  58.2 us (21%)
  matrix products  21.7 us (8%)
  local copies, waits for them, and re-layouts  16.3 us (6%)
  between operations  14.7 us (5%)
  other arithmetic  9.43 us (3%)
    ppermute x12, starting transfers between devices, shifted(): lax.ppermute(value, axis, [(source, source + steps) for source in range(f...  45.5 us
    all_to_all x1, blocking collectives, swap_sum(): got = lax.all_to_all(pieces, axis, 0, 0, tiled=True)  35.6 us
    all_to_all x1, blocking collectives, swap_gather(): got = lax.all_to_all(copies, axis, 0, 0, tiled=True)  30.4 us
    all_gather x1, waiting for transfers between devices, per_device(): lax.all_gather(jnp.concatenate(attn_pieces, axis=1), 'wide', axis=0, tile...  29.8 us
    all_to_all x1, waiting for transfers between devices, swap_sum(): got = lax.all_to_all(pieces, axis, 0, 0, tiled=True)  23.7 us
    ppermute x12, waiting for transfers between devices, shifted(): lax.ppermute(value, axis, [(source, source + steps) for source in range(f...  18.2 us
    all_to_all x1, waiting for transfers between devices, swap_gather(): got = lax.all_to_all(copies, axis, 0, 0, tiled=True)  15.8 us
    unnamed x30, local copies, waits for them, and re-layouts  10.5 us
  transfers between devices with their start and end apart: 17, of which 8 were waited for; matrix products, arithmetic and copies ran while one was open for 14% of the time, Pallas kernels for 0%

profile of v8, /device:TPU:6, one launch (start us, length us, event | category | flops | bytes accessed | tf_op | source)
XLA Modules:
  0.0 274.4 jit_solution(7763055731733021395)
XLA Ops:
  7.3 1.4 pad_maximum_fusion.2
  8.7 4.3 %collective-permute-start = (s32[256]{0:T(256)}, s32[256]{0:T(256)S(1)}, u32[]{:S(2)}, u32[]{:S(2)}) collective-permute-start(s32[256]{0:T(256)} %param.11), channel_id=1, source_target_pairs={{0,64},{8,72},{16,80},{24,88},{32,96},{40,104},{48,112},{56,120},{... | collective-permute-start | bytes 3080 | tf_op jit(solution)/shard_map/ppermute | solution.py:18
  13.0 3.7 %collective-permute-start.1 = (s32[256]{0:T(256)}, s32[256]{0:T(256)S(1)}, u32[]{:S(2)}, u32[]{:S(2)}) collective-permute-start(s32[256]{0:T(256)} %param.11), channel_id=1, source_target_pairs={{0,56},{8,64},{16,72},{24,80},{32,88},{40,96},{48,104},{56,112},{6... | collective-permute-start | bytes 3080 | tf_op jit(solution)/shard_map/ppermute | solution.py:18
  16.7 4.3 %collective-permute-start.2 = (s32[256]{0:T(256)}, s32[256]{0:T(256)S(1)}, u32[]{:S(2)}, u32[]{:S(2)}) collective-permute-start(s32[256]{0:T(256)} %param.11), channel_id=1, source_target_pairs={{0,48},{8,56},{16,64},{24,72},{32,80},{40,88},{48,96},{56,104},{64... | collective-permute-start | bytes 3080 | tf_op jit(solution)/shard_map/ppermute | solution.py:18
  21.0 6.4 %collective-permute-start.3 = (s32[256]{0:T(256)}, s32[256]{0:T(256)S(1)}, u32[]{:S(2)}, u32[]{:S(2)}) collective-permute-start(s32[256]{0:T(256)} %param.11), channel_id=1, source_target_pairs={{0,40},{8,48},{16,56},{24,64},{32,72},{40,80},{48,88},{56,96},{64,... | collective-permute-start | bytes 3080 | tf_op jit(solution)/shard_map/ppermute | solution.py:18
  27.3 4.3 %collective-permute-start.4 = (s32[256]{0:T(256)}, s32[256]{0:T(256)S(1)}, u32[]{:S(2)}, u32[]{:S(2)}) collective-permute-start(s32[256]{0:T(256)} %param.11), channel_id=1, source_target_pairs={{0,32},{8,40},{16,48},{24,56},{32,64},{40,72},{48,80},{56,88},{64,... | collective-permute-start | bytes 3080 | tf_op jit(solution)/shard_map/ppermute | solution.py:18
  33.7 7.1 %all-to-all-start = ((bf16[8,256,256]{1,2,0:T(8,128)(2,1)}), bf16[8,256,256]{1,2,0:T(8,128)(2,1)S(1)}, u32[]{:S(2)}, u32[]{:S(2)}) async-start(bf16[8,256,256]{1,2,0:T(8,128)(2,1)} %broadcast_in_dim.37), calls=%async_computation | async-start | bytes 2097152 | tf_op jit(solution)/shard_map/all_to_all | solution.py:25
  41.7 3.2 %collective-permute-start.5 = (s32[256]{0:T(256)S(1)}, s32[256]{0:T(256)S(1)}, u32[]{:S(2)}, u32[]{:S(2)}) collective-permute-start(s32[256]{0:T(256)S(1)} %copy-done.6), channel_id=1, source_target_pairs={{0,24},{8,32},{16,40},{24,48},{32,56},{40,64},{48,72},{56,80},{64,... | collective-permute-start | bytes 3080 | tf_op jit(solution)/shard_map/ppermute | solution.py:18
  45.0 3.0 %collective-permute-start.6 = (s32[256]{0:T(256)S(1)}, s32[256]{0:T(256)S(1)}, u32[]{:S(2)}, u32[]{:S(2)}) collective-permute-start(s32[256]{0:T(256)S(1)} %copy-done.6), channel_id=1, source_target_pairs={{0,16},{8,24},{16,32},{24,40},{32,48},{40,56},{48,64},{56,72},{64,... | collective-permute-start | bytes 3080 | tf_op jit(solution)/shard_map/ppermute | solution.py:18
  48.0 3.4 %collective-permute-start.7 = (s32[256]{0:T(256)S(1)}, s32[256]{0:T(256)S(1)}, u32[]{:S(2)}, u32[]{:S(2)}) collective-permute-start(s32[256]{0:T(256)S(1)} %copy-done.6), channel_id=1, source_target_pairs={{0,8},{8,16},{16,24},{24,32},{32,40},{40,48},{48,56},{56,64},{64,7... | collective-permute-start | bytes 3080 | tf_op jit(solution)/shard_map/ppermute | solution.py:18
  51.6 1.3 collective-permute-done.7
  54.1 15.8 %all-to-all-done = bf16[8,256,256]{1,2,0:T(8,128)(2,1)S(1)} async-done(((bf16[8,256,256]{1,2,0:T(8,128)(2,1)}), bf16[8,256,256]{1,2,0:T(8,128)(2,1)S(1)}, u32[]{:S(2)}, u32[]{:S(2)}) %all-to-all-start) | async-done | bytes 1048608 | tf_op jit(solution)/shard_map/all_to_all | solution.py:25
  70.8 29.8 %all-gather.3.cloned.1.call-done = bf16[2048,1024]{1,0:T(8,128)(2,1)} async-done(((bf16[32,1024]{1,0:T(8,128)(2,1)}), bf16[2048,1024]{1,0:T(8,128)(2,1)}) %all-gather.3.cloned.1.call-update) | async-done | bytes 4194320 | tf_op jit(solution)/shard_map/all_gather | solution.py:81
  100.7 3.5 %fusion.53 = f32[256,1024]{1,0:T(8,128)S(1)} fusion(bf16[256,2048]{0,1:T(8,128)(2,1)S(1)} %fusion.12, bf16[2048,1024]{1,0:T(8,128)(2,1)} %all-gather.3.cloned.1.call-done), kind=kOutput, calls=%fused_computation.110 | convolution fusion | flops 1073741824 | bytes 6291456 | tf_op jit(solution)/shard_map/dot_general | solution.py:64
  105.0 3.5 %collective-permute-start.9 = (bf16[256,2,256]{2,0,1:T(8,128)(2,1)S(1)}, bf16[256,2,256]{2,0,1:T(8,128)(2,1)S(1)}, u32[]{:S(2)}, u32[]{:S(2)}) collective-permute-start(bf16[256,2,256]{2,0,1:T(8,128)(2,1)S(1)} %pad_maximum_fusion), channel_id=1, source_target_pairs={{0,16},{8,24},{16,32},{24,40},{32,48},{40,56},{48,64},{56,72},{64,... | collective-permute-start | bytes 786440 | tf_op jit(solution)/shard_map/ppermute | solution.py:18
  108.5 3.3 %collective-permute-start.10 = (bf16[256,2,256]{2,0,1:T(8,128)(2,1)S(1)}, bf16[256,2,256]{2,0,1:T(8,128)(2,1)S(1)}, u32[]{:S(2)}, u32[]{:S(2)}) collective-permute-start(bf16[256,2,256]{2,0,1:T(8,128)(2,1)S(1)} %pad_maximum_fusion), channel_id=1, source_target_pairs={{0,32},{8,40},{16,48},{24,56},{32,64},{40,72},{48,80},{56,88},{64,... | collective-permute-start | bytes 786440 | tf_op jit(solution)/shard_map/ppermute | solution.py:18
  111.9 2.5 collective-permute-start.11
  114.5 3.5 %collective-permute-start.8 = (bf16[256,2,256]{2,0,1:T(8,128)(2,1)S(1)}, bf16[256,2,256]{2,0,1:T(8,128)(2,1)S(1)}, u32[]{:S(2)}, u32[]{:S(2)}) collective-permute-start(bf16[256,2,256]{2,0,1:T(8,128)(2,1)S(1)} %pad_maximum_fusion), channel_id=1, source_target_pairs={{0,64},{8,72},{16,80},{24,88},{32,96},{40,104},{48,112},{56,120},{... | collective-permute-start | bytes 786440 | tf_op jit(solution)/shard_map/ppermute | solution.py:18
  118.7 5.6 %collective-permute-done.10 = bf16[256,2,256]{2,0,1:T(8,128)(2,1)S(1)} collective-permute-done((bf16[256,2,256]{2,0,1:T(8,128)(2,1)S(1)}, bf16[256,2,256]{2,0,1:T(8,128)(2,1)S(1)}, u32[]{:S(2)}, u32[]{:S(2)}) %collective-permute-start.10) | collective-permute-done | bytes 262176 | tf_op jit(solution)/shard_map/ppermute | solution.py:18
  125.0 6.0 %collective-permute-done.11 = bf16[256,2,256]{2,0,1:T(8,128)(2,1)S(1)} collective-permute-done((bf16[256,2,256]{2,0,1:T(8,128)(2,1)S(1)}, bf16[256,2,256]{2,0,1:T(8,128)(2,1)S(1)}, u32[]{:S(2)}, u32[]{:S(2)}) %collective-permute-start.11) | collective-permute-done | bytes 262176 | tf_op jit(solution)/shard_map/ppermute | solution.py:18
  131.8 5.3 %collective-permute-done.8 = bf16[256,2,256]{2,0,1:T(8,128)(2,1)S(1)} collective-permute-done((bf16[256,2,256]{2,0,1:T(8,128)(2,1)S(1)}, bf16[256,2,256]{2,0,1:T(8,128)(2,1)S(1)}, u32[]{:S(2)}, u32[]{:S(2)}) %collective-permute-start.8) | collective-permute-done | bytes 262176 | tf_op jit(solution)/shard_map/ppermute | solution.py:18
  138.5 1.9 collective-permute-start.12
  140.5 1.4 compare_and_fusion
  150.2 6.6 %fusion.48 = (f32[2,256]{1,0:T(2,128)S(1)}, f32[2,256,2560]{2,1,0:T(8,128)}) fusion(pred[256,2560]{1,0:T(8,128)(4,1)} %compare_and_fusion, bf16[2560,2,256]{2,0,1:T(8,128)(2,1)} %constant_dynamic-update-slice_fusion.1, bf16[256,2,64]{2,0,1:T(8,128)(2,1)S(1)} %get-tuple-element.5, bf16[256,2,64]{2,0,1:T(8,128)(2,1)S(1)} %get-tuple-element.4), kind=kOutput, calls=%fused_computation.108 | convolution fusion | flops 342362624 | bytes 7997440 | tf_op jit(solution)/shard_map/sub | solution.py:144
  156.9 4.0 %fusion.23 = bf16[2,128,256]{2,1,0:T(8,128)(2,1)S(1)} fusion(f32[2,256,2560]{2,1,0:T(8,128)} %get-tuple-element.17, f32[2,256]{1,0:T(2,128)S(1)} %get-tuple-element.16, bf16[2560,2,256]{2,0,1:T(8,128)(2,1)} %constant_dynamic-update-slice_fusion.1), kind=kOutput, calls=%fused_computation.32 | convolution fusion | flops 338231296 | bytes 6686720 | tf_op jit(solution)/shard_map/hqk,khd->qhd/dot_general | solution.py:146
  160.8 1.7 convolution_convert_fusion.1
  162.7 35.6 %all_to_all.20 = bf16[8,256,256]{2,1,0:T(8,128)(2,1)S(1)} all-to-all(bf16[8,256,256]{2,1,0:T(8,128)(2,1)S(1)} %bitcast.89), channel_id=1, replica_groups=mesh['wide'=64,'narrow'=8] {'narrow'}, dimensions={0} | all-to-all | bytes 2097152 | tf_op jit(solution)/shard_map/all_to_all | solution.py:34
  198.6 30.4 %all_to_all.21 = bf16[8,256,256]{1,2,0:T(8,128)(2,1)S(1)} all-to-all(bf16[8,256,256]{1,2,0:T(8,128)(2,1)S(1)} %broadcast_in_dim.42), channel_id=1, replica_groups=mesh['wide'=64,'narrow'=8] {'narrow'}, dimensions={0} | all-to-all | bytes 2097152 | tf_op jit(solution)/shard_map/all_to_all | solution.py:25
  229.9 2.3 fusion.7
  232.2 3.6 %convolution_convert_fusion = bf16[256,2048]{1,0:T(8,128)(2,1)S(1)} fusion(bf16[2048,1536]{1,0:T(8,128)(2,1)} %all-gather.5.cloned.1.call-done, bf16[256,2048]{0,1:T(8,128)(2,1)S(1)} %fusion.10, f32[256,512]{1,0:T(8,128)S(1)} %fusion.7), kind=kOutput, calls=%fused_computation.8 | convolution fusion | flops 1075052544 | bytes 6815744 | tf_op jit(solution)/shard_map/dot_general | solution.py:159
  236.9 3.6 %all-to-all-start.3 = ((bf16[8,256,256]{2,1,0:T(8,128)(2,1)}), bf16[8,256,256]{2,1,0:T(8,128)(2,1)S(1)}, u32[]{:S(2)}, u32[]{:S(2)}) async-start(bf16[8,256,256]{2,1,0:T(8,128)(2,1)} %bitcast.85), calls=%async_computation.3 | async-start | bytes 2097152 | tf_op jit(solution)/shard_map/all_to_all | solution.py:34
  243.0 23.7 %all-to-all-done.3 = bf16[8,256,256]{2,1,0:T(8,128)(2,1)S(1)} async-done(((bf16[8,256,256]{2,1,0:T(8,128)(2,1)}), bf16[8,256,256]{2,1,0:T(8,128)(2,1)S(1)}, u32[]{:S(2)}, u32[]{:S(2)}) %all-to-all-start.3) | async-done | bytes 1048608 | tf_op jit(solution)/shard_map/all_to_all | solution.py:34
  (104 shorter events, 23.5 us)
Async XLA Ops:
  7.2 34.6 %copy-start.6 = (s32[256]{0:T(256)S(1)}, s32[256]{0:T(256)}, u32[]{:S(2)}) copy-start(s32[256]{0:T(256)} %param.11) | copy-start | bytes 3076
  7.2 33.7 %copy-start.3 = (bf16[512,32]{0,1:T(8,128)(2,1)S(1)}, bf16[512,32]{0,1:T(8,128)(2,1)}, u32[]{:S(2)}) copy-start(bf16[512,32]{0,1:T(8,128)(2,1)} %param.19) | copy-start | bytes 98308
  7.2 33.7 %copy-start.5 = (bf16[32,512]{1,0:T(8,128)(2,1)S(1)}, bf16[32,512]{1,0:T(8,128)(2,1)}, u32[]{:S(2)}) copy-start(bf16[32,512]{1,0:T(8,128)(2,1)} %param.17) | copy-start | bytes 98308
  7.2 33.7 %copy-start.4 = (bf16[32,512]{1,0:T(8,128)(2,1)S(1)}, bf16[32,512]{1,0:T(8,128)(2,1)}, u32[]{:S(2)}) copy-start(bf16[32,512]{1,0:T(8,128)(2,1)} %param.18) | copy-start | bytes 98308
  7.2 93.5 %all-gather.3.cloned.1.call-start = ((), (), s32[]{:S(2)}) async-start(), calls=%async_computation.4 | async-start | bytes 4259840 | tf_op jit(solution)/shard_map/all_gather | solution.py:81
  8.7 33.1 %collective-permute-start = (s32[256]{0:T(256)}, s32[256]{0:T(256)S(1)}, u32[]{:S(2)}, u32[]{:S(2)}) collective-permute-start(s32[256]{0:T(256)} %param.11), channel_id=1, source_target_pairs={{0,64},{8,72},{16,80},{24,88},{32,96},{40,104},{48,112},{56,120},{... | collective-permute-start | bytes 3080 | tf_op jit(solution)/shard_map/ppermute | solution.py:18
  13.0 32.0 %collective-permute-start.1 = (s32[256]{0:T(256)}, s32[256]{0:T(256)S(1)}, u32[]{:S(2)}, u32[]{:S(2)}) collective-permute-start(s32[256]{0:T(256)} %param.11), channel_id=1, source_target_pairs={{0,56},{8,64},{16,72},{24,80},{32,88},{40,96},{48,104},{56,112},{6... | collective-permute-start | bytes 3080 | tf_op jit(solution)/shard_map/ppermute | solution.py:18
  16.7 31.4 %collective-permute-start.2 = (s32[256]{0:T(256)}, s32[256]{0:T(256)S(1)}, u32[]{:S(2)}, u32[]{:S(2)}) collective-permute-start(s32[256]{0:T(256)} %param.11), channel_id=1, source_target_pairs={{0,48},{8,56},{16,64},{24,72},{32,80},{40,88},{48,96},{56,104},{64... | collective-permute-start | bytes 3080 | tf_op jit(solution)/shard_map/ppermute | solution.py:18
  21.0 30.6 %collective-permute-start.3 = (s32[256]{0:T(256)}, s32[256]{0:T(256)S(1)}, u32[]{:S(2)}, u32[]{:S(2)}) collective-permute-start(s32[256]{0:T(256)} %param.11), channel_id=1, source_target_pairs={{0,40},{8,48},{16,56},{24,64},{32,72},{40,80},{48,88},{56,96},{64,... | collective-permute-start | bytes 3080 | tf_op jit(solution)/shard_map/ppermute | solution.py:18
  27.3 24.2 %collective-permute-start.4 = (s32[256]{0:T(256)}, s32[256]{0:T(256)S(1)}, u32[]{:S(2)}, u32[]{:S(2)}) collective-permute-start(s32[256]{0:T(256)} %param.11), channel_id=1, source_target_pairs={{0,32},{8,40},{16,48},{24,56},{32,64},{40,72},{48,80},{56,88},{64,... | collective-permute-start | bytes 3080 | tf_op jit(solution)/shard_map/ppermute | solution.py:18
  33.7 36.2 %all-to-all-start = ((bf16[8,256,256]{1,2,0:T(8,128)(2,1)}), bf16[8,256,256]{1,2,0:T(8,128)(2,1)S(1)}, u32[]{:S(2)}, u32[]{:S(2)}) async-start(bf16[8,256,256]{1,2,0:T(8,128)(2,1)} %broadcast_in_dim.37), calls=%async_computation | async-start | bytes 2097152 | tf_op jit(solution)/shard_map/all_to_all | solution.py:25
  40.8 189.1 %all-gather.5.cloned.1.call-start = ((), (), s32[]{:S(2)}) async-start(), calls=%async_computation.5 | async-start | bytes 6389760 | tf_op jit(solution)/shard_map/all_gather | solution.py:76
  41.7 9.8 %collective-permute-start.5 = (s32[256]{0:T(256)S(1)}, s32[256]{0:T(256)S(1)}, u32[]{:S(2)}, u32[]{:S(2)}) collective-permute-start(s32[256]{0:T(256)S(1)} %copy-done.6), channel_id=1, source_target_pairs={{0,24},{8,32},{16,40},{24,48},{32,56},{40,64},{48,72},{56,80},{64,... | collective-permute-start | bytes 3080 | tf_op jit(solution)/shard_map/ppermute | solution.py:18
  45.0 6.6 %collective-permute-start.6 = (s32[256]{0:T(256)S(1)}, s32[256]{0:T(256)S(1)}, u32[]{:S(2)}, u32[]{:S(2)}) collective-permute-start(s32[256]{0:T(256)S(1)} %copy-done.6), channel_id=1, source_target_pairs={{0,16},{8,24},{16,32},{24,40},{32,48},{40,56},{48,64},{56,72},{64,... | collective-permute-start | bytes 3080 | tf_op jit(solution)/shard_map/ppermute | solution.py:18
  48.0 4.9 %collective-permute-start.7 = (s32[256]{0:T(256)S(1)}, s32[256]{0:T(256)S(1)}, u32[]{:S(2)}, u32[]{:S(2)}) collective-permute-start(s32[256]{0:T(256)S(1)} %copy-done.6), channel_id=1, source_target_pairs={{0,8},{8,16},{16,24},{24,32},{32,40},{40,48},{48,56},{56,64},{64,7... | collective-permute-start | bytes 3080 | tf_op jit(solution)/shard_map/ppermute | solution.py:18
  104.2 14.6 %copy-start.1 = (f32[256,1024]{1,0:T(8,128)}, f32[256,1024]{1,0:T(8,128)S(1)}, u32[]{:S(2)}) copy-start(f32[256,1024]{1,0:T(8,128)S(1)} %fusion.53) | copy-start | bytes 3145732
  105.0 13.0 %collective-permute-start.9 = (bf16[256,2,256]{2,0,1:T(8,128)(2,1)S(1)}, bf16[256,2,256]{2,0,1:T(8,128)(2,1)S(1)}, u32[]{:S(2)}, u32[]{:S(2)}) collective-permute-start(bf16[256,2,256]{2,0,1:T(8,128)(2,1)S(1)} %pad_maximum_fusion), channel_id=1, source_target_pairs={{0,16},{8,24},{16,32},{24,40},{32,48},{40,56},{48,64},{56,72},{64,... | collective-permute-start | bytes 786440 | tf_op jit(solution)/shard_map/ppermute | solution.py:18
  108.5 15.9 %collective-permute-start.10 = (bf16[256,2,256]{2,0,1:T(8,128)(2,1)S(1)}, bf16[256,2,256]{2,0,1:T(8,128)(2,1)S(1)}, u32[]{:S(2)}, u32[]{:S(2)}) collective-permute-start(bf16[256,2,256]{2,0,1:T(8,128)(2,1)S(1)} %pad_maximum_fusion), channel_id=1, source_target_pairs={{0,32},{8,40},{16,48},{24,56},{32,64},{40,72},{48,80},{56,88},{64,... | collective-permute-start | bytes 786440 | tf_op jit(solution)/shard_map/ppermute | solution.py:18
  111.9 19.1 %collective-permute-start.11 = (bf16[256,2,256]{2,0,1:T(8,128)(2,1)S(1)}, bf16[256,2,256]{2,0,1:T(8,128)(2,1)S(1)}, u32[]{:S(2)}, u32[]{:S(2)}) collective-permute-start(bf16[256,2,256]{2,0,1:T(8,128)(2,1)S(1)} %pad_maximum_fusion), channel_id=1, source_target_pairs={{0,48},{8,56},{16,64},{24,72},{32,80},{40,88},{48,96},{56,104},{64... | collective-permute-start | bytes 786440 | tf_op jit(solution)/shard_map/ppermute | solution.py:18
  114.5 22.6 %collective-permute-start.8 = (bf16[256,2,256]{2,0,1:T(8,128)(2,1)S(1)}, bf16[256,2,256]{2,0,1:T(8,128)(2,1)S(1)}, u32[]{:S(2)}, u32[]{:S(2)}) collective-permute-start(bf16[256,2,256]{2,0,1:T(8,128)(2,1)S(1)} %pad_maximum_fusion), channel_id=1, source_target_pairs={{0,64},{8,72},{16,80},{24,88},{32,96},{40,104},{48,112},{56,120},{... | collective-permute-start | bytes 786440 | tf_op jit(solution)/shard_map/ppermute | solution.py:18
  138.5 5.1 %collective-permute-start.12 = (bf16[5,256,2,256]{3,1,2,0:T(8,128)(2,1)}, bf16[5,256,2,256]{3,1,2,0:T(8,128)(2,1)S(1)}, u32[]{:S(2)}, u32[]{:S(2)}) collective-permute-start(bf16[5,256,2,256]{3,1,2,0:T(8,128)(2,1)} %bitcast_dynamic-update-slice_fusion), channel_id=1, source_target_pairs={{0,8},{8,0},{16,24},{24,16},{32,40},{40,32},{48,56},{56,48},{64,72... | collective-permute-start | bytes 3932168 | tf_op jit(solution)/shard_map/ppermute | solution.py:117
  162.6 35.8 %copy-start.2 = (bf16[256,256]{1,0:T(8,128)(2,1)S(1)}, bf16[256,256]{1,0:T(8,128)(2,1)}, u32[]{:S(2)}) copy-start(bf16[256,256]{1,0:T(8,128)(2,1)} %param.10) | copy-start | bytes 393220
  235.8 4.6 %copy-start.7 = (s32[16]{0:T(128)S(1)}, s32[16]{0:T(128)}, u32[]{:S(2)}) copy-start(s32[16]{0:T(128)} %param.12) | copy-start | bytes 196
  236.9 29.8 %all-to-all-start.3 = ((bf16[8,256,256]{2,1,0:T(8,128)(2,1)}), bf16[8,256,256]{2,1,0:T(8,128)(2,1)S(1)}, u32[]{:S(2)}, u32[]{:S(2)}) async-start(bf16[8,256,256]{2,1,0:T(8,128)(2,1)} %bitcast.85), calls=%async_computation.3 | async-start | bytes 2097152 | tf_op jit(solution)/shard_map/all_to_all | solution.py:34
  243.0 24.5 %copy-start = (bf16[2,16,16,256]{3,2,1,0:T(8,128)(2,1)}, bf16[2,16,16,256]{3,2,1,0:T(8,128)(2,1)S(1)}, u32[]{:S(2)}) copy-start(bf16[2,16,16,256]{3,2,1,0:T(8,128)(2,1)S(1)} %scatter_fusion) | copy-start | bytes 786436
Sparse Core Ops, SparseCore 0:
  12.0 88.6 all-gather.2
  104.6 88.8 all-gather.4

commit v9 on v8

--- a/solution.py
+++ b/solution.py
@@ -114,18 +114,13 @@
     chips_back = REACH // pairs_per_chip
     line = [shifted(packed, "wide", pairs_per_chip * step) for step in range(1, chips_back + 1)]
     count = lax.axis_size("wide")
-    partner = lax.ppermute(
-        jnp.stack(line + [packed], axis=0), "wide", [(i, i ^ 1) for i in range(count)]
-    )
+    mine = jnp.stack(line + [packed], axis=0)
+    partner = lax.ppermute(mine, "wide", [(i, i ^ 1) for i in range(count)])
     partner_rank = wide_rank ^ 1
-    order = []
     block_ids = []
-    for step in range(chips_back, 0, -1):
-        order += [line[step - 1], partner[step - 1]]
-        block_ids += [wide_rank - pairs_per_chip * step, partner_rank - pairs_per_chip * step]
-    order += [partner[chips_back], packed]
-    block_ids += [partner_rank, wide_rank]
-    kv_all = jnp.concatenate(order, axis=0)
+    for rank in (wide_rank, partner_rank):
+        block_ids += [rank - pairs_per_chip * step for step in range(1, chips_back + 1)] + [rank]
+    kv_all = jnp.concatenate([mine, partner], axis=0).reshape((-1,) + packed.shape[1:])
     key_index = (
         jnp.stack(block_ids)[:, None] * tok_rows + local_index[None, :]
     ).reshape(-1)

time: 275 us -> 275 us (level)
    unnamed x30 -> x23, local copies, waits for them, and re-layouts: 10.5 us -> 5.93 us
    concatenate x0 -> x2, local copies, waits for them, and re-layouts: none -> 3.1 us  [per_device(): jnp.concatenate([mine, partner], axis=0).reshape((-1,) + packed.shape[1:])]
  transfers between devices with their start and end apart: 17 -> 17, of which waited for: 8 -> 8; matrix products, arithmetic and copies ran while one was open for 14% -> 13% of each run, Pallas kernels for 0% -> 0%
where the time goes in v9:
time: 275 us; the launch traced here: 274 us
  waiting for transfers between devices  88.9 us (32%)
  blocking collectives  65.9 us (24%)
  starting transfers between devices  58.2 us (21%)
  matrix products  21.5 us (8%)
  local copies, waits for them, and re-layouts  15.9 us (6%)
  between operations  14.7 us (5%)
  other arithmetic  9.38 us (3%)
    ppermute x12, starting transfers between devices, shifted(): lax.ppermute(value, axis, [(source, source + steps) for source in range(f...  45.5 us
    all_to_all x1, blocking collectives, swap_sum(): got = lax.all_to_all(pieces, axis, 0, 0, tiled=True)  35.5 us
    all_to_all x1, blocking collectives, swap_gather(): got = lax.all_to_all(copies, axis, 0, 0, tiled=True)  30.4 us
    all_gather x1, waiting for transfers between devices, per_device(): lax.all_gather(jnp.concatenate(attn_pieces, axis=1), 'wide', axis=0, tile...  29.8 us
    all_to_all x1, waiting for transfers between devices, swap_sum(): got = lax.all_to_all(pieces, axis, 0, 0, tiled=True)  23.7 us
    ppermute x12, waiting for transfers between devices, shifted(): lax.ppermute(value, axis, [(source, source + steps) for source in range(f...  18.1 us
    all_to_all x1, waiting for transfers between devices, swap_gather(): got = lax.all_to_all(copies, axis, 0, 0, tiled=True)  15.9 us
    all_to_all x1, starting transfers between devices, swap_gather(): got = lax.all_to_all(copies, axis, 0, 0, tiled=True)  7.1 us
  transfers between devices with their start and end apart: 17, of which 8 were waited for; matrix products, arithmetic and copies ran while one was open for 13% of the time, Pallas kernels for 0%

profile of v9, /device:TPU:6, one launch (start us, length us, event | category | flops | bytes accessed | tf_op | source)
XLA Modules:
  0.0 274.3 jit_solution(12387315240279617832)
XLA Ops:
  8.7 4.3 %collective-permute-start = (s32[256]{0:T(256)}, s32[256]{0:T(256)S(1)}, u32[]{:S(2)}, u32[]{:S(2)}) collective-permute-start(s32[256]{0:T(256)} %param.11), channel_id=1, source_target_pairs={{0,64},{8,72},{16,80},{24,88},{32,96},{40,104},{48,112},{56,120},{... | collective-permute-start | bytes 3080 | tf_op jit(solution)/shard_map/ppermute | solution.py:18
  13.0 3.7 %collective-permute-start.1 = (s32[256]{0:T(256)}, s32[256]{0:T(256)S(1)}, u32[]{:S(2)}, u32[]{:S(2)}) collective-permute-start(s32[256]{0:T(256)} %param.11), channel_id=1, source_target_pairs={{0,56},{8,64},{16,72},{24,80},{32,88},{40,96},{48,104},{56,112},{6... | collective-permute-start | bytes 3080 | tf_op jit(solution)/shard_map/ppermute | solution.py:18
  16.7 4.3 %collective-permute-start.2 = (s32[256]{0:T(256)}, s32[256]{0:T(256)S(1)}, u32[]{:S(2)}, u32[]{:S(2)}) collective-permute-start(s32[256]{0:T(256)} %param.11), channel_id=1, source_target_pairs={{0,48},{8,56},{16,64},{24,72},{32,80},{40,88},{48,96},{56,104},{64... | collective-permute-start | bytes 3080 | tf_op jit(solution)/shard_map/ppermute | solution.py:18
  21.0 6.4 %collective-permute-start.3 = (s32[256]{0:T(256)}, s32[256]{0:T(256)S(1)}, u32[]{:S(2)}, u32[]{:S(2)}) collective-permute-start(s32[256]{0:T(256)} %param.11), channel_id=1, source_target_pairs={{0,40},{8,48},{16,56},{24,64},{32,72},{40,80},{48,88},{56,96},{64,... | collective-permute-start | bytes 3080 | tf_op jit(solution)/shard_map/ppermute | solution.py:18
  27.3 4.3 %collective-permute-start.4 = (s32[256]{0:T(256)}, s32[256]{0:T(256)S(1)}, u32[]{:S(2)}, u32[]{:S(2)}) collective-permute-start(s32[256]{0:T(256)} %param.11), channel_id=1, source_target_pairs={{0,32},{8,40},{16,48},{24,56},{32,64},{40,72},{48,80},{56,88},{64,... | collective-permute-start | bytes 3080 | tf_op jit(solution)/shard_map/ppermute | solution.py:18
  33.7 7.1 %all-to-all-start = ((bf16[8,256,256]{1,2,0:T(8,128)(2,1)}), bf16[8,256,256]{1,2,0:T(8,128)(2,1)S(1)}, u32[]{:S(2)}, u32[]{:S(2)}) async-start(bf16[8,256,256]{1,2,0:T(8,128)(2,1)} %broadcast_in_dim.37), calls=%async_computation | async-start | bytes 2097152 | tf_op jit(solution)/shard_map/all_to_all | solution.py:25
  41.7 3.2 %collective-permute-start.5 = (s32[256]{0:T(256)S(1)}, s32[256]{0:T(256)S(1)}, u32[]{:S(2)}, u32[]{:S(2)}) collective-permute-start(s32[256]{0:T(256)S(1)} %copy-done.7), channel_id=1, source_target_pairs={{0,24},{8,32},{16,40},{24,48},{32,56},{40,64},{48,72},{56,80},{64,... | collective-permute-start | bytes 3080 | tf_op jit(solution)/shard_map/ppermute | solution.py:18
  44.9 3.0 %collective-permute-start.6 = (s32[256]{0:T(256)S(1)}, s32[256]{0:T(256)S(1)}, u32[]{:S(2)}, u32[]{:S(2)}) collective-permute-start(s32[256]{0:T(256)S(1)} %copy-done.7), channel_id=1, source_target_pairs={{0,16},{8,24},{16,32},{24,40},{32,48},{40,56},{48,64},{56,72},{64,... | collective-permute-start | bytes 3080 | tf_op jit(solution)/shard_map/ppermute | solution.py:18
  48.0 3.4 %collective-permute-start.7 = (s32[256]{0:T(256)S(1)}, s32[256]{0:T(256)S(1)}, u32[]{:S(2)}, u32[]{:S(2)}) collective-permute-start(s32[256]{0:T(256)S(1)} %copy-done.7), channel_id=1, source_target_pairs={{0,8},{8,16},{16,24},{24,32},{32,40},{40,48},{48,56},{56,64},{64,7... | collective-permute-start | bytes 3080 | tf_op jit(solution)/shard_map/ppermute | solution.py:18
  54.0 15.9 %all-to-all-done = bf16[8,256,256]{1,2,0:T(8,128)(2,1)S(1)} async-done(((bf16[8,256,256]{1,2,0:T(8,128)(2,1)}), bf16[8,256,256]{1,2,0:T(8,128)(2,1)S(1)}, u32[]{:S(2)}, u32[]{:S(2)}) %all-to-all-start) | async-done | bytes 1048608 | tf_op jit(solution)/shard_map/all_to_all | solution.py:25
  70.8 29.8 %all-gather.3.cloned.1.call-done = bf16[2048,1024]{1,0:T(8,128)(2,1)} async-done(((bf16[32,1024]{1,0:T(8,128)(2,1)}), bf16[2048,1024]{1,0:T(8,128)(2,1)}) %all-gather.3.cloned.1.call-update) | async-done | bytes 4194320 | tf_op jit(solution)/shard_map/all_gather | solution.py:81
  100.7 3.5 %fusion.48 = f32[256,1024]{1,0:T(8,128)S(1)} fusion(bf16[256,2048]{0,1:T(8,128)(2,1)S(1)} %fusion.12, bf16[2048,1024]{1,0:T(8,128)(2,1)} %all-gather.3.cloned.1.call-done), kind=kOutput, calls=%fused_computation.101 | convolution fusion | flops 1073741824 | bytes 6291456 | tf_op jit(solution)/shard_map/dot_general | solution.py:64
  107.5 3.5 %collective-permute-start.8 = (bf16[256,2,256]{2,0,1:T(8,128)(2,1)}, bf16[256,2,256]{2,0,1:T(8,128)(2,1)}, u32[]{:S(2)}, u32[]{:S(2)}) collective-permute-start(bf16[256,2,256]{2,0,1:T(8,128)(2,1)} %pad_maximum_fusion), channel_id=1, source_target_pairs={{0,16},{8,24},{16,32},{24,40},{32,48},{40,56},{48,64},{56,72},{64,... | collective-permute-start | bytes 786440 | tf_op jit(solution)/shard_map/ppermute | solution.py:18
  111.1 3.3 %collective-permute-start.9 = (bf16[256,2,256]{2,0,1:T(8,128)(2,1)}, bf16[256,2,256]{2,0,1:T(8,128)(2,1)S(1)}, u32[]{:S(2)}, u32[]{:S(2)}) collective-permute-start(bf16[256,2,256]{2,0,1:T(8,128)(2,1)} %pad_maximum_fusion), channel_id=1, source_target_pairs={{0,32},{8,40},{16,48},{24,56},{32,64},{40,72},{48,80},{56,88},{64,... | collective-permute-start | bytes 786440 | tf_op jit(solution)/shard_map/ppermute | solution.py:18
  114.5 2.6 collective-permute-start.10
  117.1 3.5 %collective-permute-start.11 = (bf16[256,2,256]{2,0,1:T(8,128)(2,1)}, bf16[256,2,256]{2,0,1:T(8,128)(2,1)S(1)}, u32[]{:S(2)}, u32[]{:S(2)}) collective-permute-start(bf16[256,2,256]{2,0,1:T(8,128)(2,1)} %pad_maximum_fusion), channel_id=1, source_target_pairs={{0,64},{8,72},{16,80},{24,88},{32,96},{40,104},{48,112},{56,120},{... | collective-permute-start | bytes 786440 | tf_op jit(solution)/shard_map/ppermute | solution.py:18
  120.6 1.7 bitcast_dynamic-update-slice_fusion.9
  122.3 5.5 %collective-permute-done.9 = bf16[256,2,256]{2,0,1:T(8,128)(2,1)S(1)} collective-permute-done((bf16[256,2,256]{2,0,1:T(8,128)(2,1)}, bf16[256,2,256]{2,0,1:T(8,128)(2,1)S(1)}, u32[]{:S(2)}, u32[]{:S(2)}) %collective-permute-start.9) | collective-permute-done | bytes 262176 | tf_op jit(solution)/shard_map/ppermute | solution.py:18
  128.6 6.0 %collective-permute-done.10 = bf16[256,2,256]{2,0,1:T(8,128)(2,1)S(1)} collective-permute-done((bf16[256,2,256]{2,0,1:T(8,128)(2,1)}, bf16[256,2,256]{2,0,1:T(8,128)(2,1)S(1)}, u32[]{:S(2)}, u32[]{:S(2)}) %collective-permute-start.10) | collective-permute-done | bytes 262176 | tf_op jit(solution)/shard_map/ppermute | solution.py:18
  135.3 5.3 %collective-permute-done.11 = bf16[256,2,256]{2,0,1:T(8,128)(2,1)S(1)} collective-permute-done((bf16[256,2,256]{2,0,1:T(8,128)(2,1)}, bf16[256,2,256]{2,0,1:T(8,128)(2,1)S(1)}, u32[]{:S(2)}, u32[]{:S(2)}) %collective-permute-start.11) | collective-permute-done | bytes 262176 | tf_op jit(solution)/shard_map/ppermute | solution.py:18
  142.1 1.9 collective-permute-start.12
  144.1 1.4 compare_and_fusion
  148.8 1.7 copy.48
  150.4 6.8 %fusion.43 = (f32[2,256]{1,0:T(2,128)S(1)}, f32[2,256,2560]{2,1,0:T(8,128)}) fusion(pred[256,2560]{1,0:T(8,128)(4,1)} %compare_and_fusion, bf16[2560,2,256]{2,0,1:T(8,128)(2,1)} %bitcast.76, bf16[256,2,64]{2,0,1:T(8,128)(2,1)S(1)} %get-tuple-element.5, bf16[256,2,64]{2,0,1:T(8,128)(2,1)S(1)} %get-tuple-element.4), kind=kOutput, calls=%fused_computation.99 | convolution fusion | flops 342362624 | bytes 7997440 | tf_op jit(solution)/shard_map/sub | solution.py:139
  157.3 3.6 %fusion.23 = bf16[2,128,256]{2,1,0:T(8,128)(2,1)S(1)} fusion(f32[2,256,2560]{2,1,0:T(8,128)} %get-tuple-element.27, f32[2,256]{1,0:T(2,128)S(1)} %get-tuple-element.26, bf16[2560,2,256]{2,0,1:T(8,128)(2,1)S(1)} %bitcast.77), kind=kOutput, calls=%fused_computation.32 | convolution fusion | flops 338231296 | bytes 6686720 | tf_op jit(solution)/shard_map/hqk,khd->qhd/dot_general | solution.py:141
  160.8 1.7 convolution_convert_fusion.1
  162.6 35.5 %all_to_all.20 = bf16[8,256,256]{2,1,0:T(8,128)(2,1)S(1)} all-to-all(bf16[8,256,256]{2,1,0:T(8,128)(2,1)S(1)} %bitcast.75), channel_id=1, replica_groups=mesh['wide'=64,'narrow'=8] {'narrow'}, dimensions={0} | all-to-all | bytes 2097152 | tf_op jit(solution)/shard_map/all_to_all | solution.py:34
  198.5 30.4 %all_to_all.21 = bf16[8,256,256]{1,2,0:T(8,128)(2,1)S(1)} all-to-all(bf16[8,256,256]{1,2,0:T(8,128)(2,1)S(1)} %broadcast_in_dim.42), channel_id=1, replica_groups=mesh['wide'=64,'narrow'=8] {'narrow'}, dimensions={0} | all-to-all | bytes 2097152 | tf_op jit(solution)/shard_map/all_to_all | solution.py:25
  229.9 2.3 fusion.7
  232.2 3.6 %convolution_convert_fusion = bf16[256,2048]{1,0:T(8,128)(2,1)S(1)} fusion(bf16[2048,1536]{1,0:T(8,128)(2,1)} %all-gather.5.cloned.1.call-done, bf16[256,2048]{0,1:T(8,128)(2,1)S(1)} %fusion.10, f32[256,512]{1,0:T(8,128)S(1)} %fusion.7), kind=kOutput, calls=%fused_computation.8 | convolution fusion | flops 1075052544 | bytes 6815744 | tf_op jit(solution)/shard_map/dot_general | solution.py:154
  236.9 3.6 %all-to-all-start.3 = ((bf16[8,256,256]{2,1,0:T(8,128)(2,1)}), bf16[8,256,256]{2,1,0:T(8,128)(2,1)S(1)}, u32[]{:S(2)}, u32[]{:S(2)}) async-start(bf16[8,256,256]{2,1,0:T(8,128)(2,1)} %bitcast.71), calls=%async_computation.3 | async-start | bytes 2097152 | tf_op jit(solution)/shard_map/all_to_all | solution.py:34
  243.0 23.7 %all-to-all-done.3 = bf16[8,256,256]{2,1,0:T(8,128)(2,1)S(1)} async-done(((bf16[8,256,256]{2,1,0:T(8,128)(2,1)}), bf16[8,256,256]{2,1,0:T(8,128)(2,1)S(1)}, u32[]{:S(2)}, u32[]{:S(2)}) %all-to-all-start.3) | async-done | bytes 1048608 | tf_op jit(solution)/shard_map/all_to_all | solution.py:34
  (98 shorter events, 23.1 us)
Async XLA Ops:
  7.2 34.5 %copy-start.7 = (s32[256]{0:T(256)S(1)}, s32[256]{0:T(256)}, u32[]{:S(2)}) copy-start(s32[256]{0:T(256)} %param.11) | copy-start | bytes 3076
  7.2 33.7 %copy-start.4 = (bf16[512,32]{0,1:T(8,128)(2,1)S(1)}, bf16[512,32]{0,1:T(8,128)(2,1)}, u32[]{:S(2)}) copy-start(bf16[512,32]{0,1:T(8,128)(2,1)} %param.19) | copy-start | bytes 98308
  7.2 33.7 %copy-start.6 = (bf16[32,512]{1,0:T(8,128)(2,1)S(1)}, bf16[32,512]{1,0:T(8,128)(2,1)}, u32[]{:S(2)}) copy-start(bf16[32,512]{1,0:T(8,128)(2,1)} %param.17) | copy-start | bytes 98308
  7.2 33.7 %copy-start.5 = (bf16[32,512]{1,0:T(8,128)(2,1)S(1)}, bf16[32,512]{1,0:T(8,128)(2,1)}, u32[]{:S(2)}) copy-start(bf16[32,512]{1,0:T(8,128)(2,1)} %param.18) | copy-start | bytes 98308
  7.2 93.5 %all-gather.3.cloned.1.call-start = ((), (), s32[]{:S(2)}) async-start(), calls=%async_computation.4 | async-start | bytes 4259840 | tf_op jit(solution)/shard_map/all_gather | solution.py:81
  8.7 33.0 %collective-permute-start = (s32[256]{0:T(256)}, s32[256]{0:T(256)S(1)}, u32[]{:S(2)}, u32[]{:S(2)}) collective-permute-start(s32[256]{0:T(256)} %param.11), channel_id=1, source_target_pairs={{0,64},{8,72},{16,80},{24,88},{32,96},{40,104},{48,112},{56,120},{... | collective-permute-start | bytes 3080 | tf_op jit(solution)/shard_map/ppermute | solution.py:18
  13.0 31.9 %collective-permute-start.1 = (s32[256]{0:T(256)}, s32[256]{0:T(256)S(1)}, u32[]{:S(2)}, u32[]{:S(2)}) collective-permute-start(s32[256]{0:T(256)} %param.11), channel_id=1, source_target_pairs={{0,56},{8,64},{16,72},{24,80},{32,88},{40,96},{48,104},{56,112},{6... | collective-permute-start | bytes 3080 | tf_op jit(solution)/shard_map/ppermute | solution.py:18
  16.7 31.3 %collective-permute-start.2 = (s32[256]{0:T(256)}, s32[256]{0:T(256)S(1)}, u32[]{:S(2)}, u32[]{:S(2)}) collective-permute-start(s32[256]{0:T(256)} %param.11), channel_id=1, source_target_pairs={{0,48},{8,56},{16,64},{24,72},{32,80},{40,88},{48,96},{56,104},{64... | collective-permute-start | bytes 3080 | tf_op jit(solution)/shard_map/ppermute | solution.py:18
  21.0 30.5 %collective-permute-start.3 = (s32[256]{0:T(256)}, s32[256]{0:T(256)S(1)}, u32[]{:S(2)}, u32[]{:S(2)}) collective-permute-start(s32[256]{0:T(256)} %param.11), channel_id=1, source_target_pairs={{0,40},{8,48},{16,56},{24,64},{32,72},{40,80},{48,88},{56,96},{64,... | collective-permute-start | bytes 3080 | tf_op jit(solution)/shard_map/ppermute | solution.py:18
  27.3 24.1 %collective-permute-start.4 = (s32[256]{0:T(256)}, s32[256]{0:T(256)S(1)}, u32[]{:S(2)}, u32[]{:S(2)}) collective-permute-start(s32[256]{0:T(256)} %param.11), channel_id=1, source_target_pairs={{0,32},{8,40},{16,48},{24,56},{32,64},{40,72},{48,80},{56,88},{64,... | collective-permute-start | bytes 3080 | tf_op jit(solution)/shard_map/ppermute | solution.py:18
  33.7 36.2 %all-to-all-start = ((bf16[8,256,256]{1,2,0:T(8,128)(2,1)}), bf16[8,256,256]{1,2,0:T(8,128)(2,1)S(1)}, u32[]{:S(2)}, u32[]{:S(2)}) async-start(bf16[8,256,256]{1,2,0:T(8,128)(2,1)} %broadcast_in_dim.37), calls=%async_computation | async-start | bytes 2097152 | tf_op jit(solution)/shard_map/all_to_all | solution.py:25
  40.8 189.0 %all-gather.5.cloned.1.call-start = ((), (), s32[]{:S(2)}) async-start(), calls=%async_computation.5 | async-start | bytes 6389760 | tf_op jit(solution)/shard_map/all_gather | solution.py:76
  41.7 9.8 %collective-permute-start.5 = (s32[256]{0:T(256)S(1)}, s32[256]{0:T(256)S(1)}, u32[]{:S(2)}, u32[]{:S(2)}) collective-permute-start(s32[256]{0:T(256)S(1)} %copy-done.7), channel_id=1, source_target_pairs={{0,24},{8,32},{16,40},{24,48},{32,56},{40,64},{48,72},{56,80},{64,... | collective-permute-start | bytes 3080 | tf_op jit(solution)/shard_map/ppermute | solution.py:18
  44.9 6.6 %collective-permute-start.6 = (s32[256]{0:T(256)S(1)}, s32[256]{0:T(256)S(1)}, u32[]{:S(2)}, u32[]{:S(2)}) collective-permute-start(s32[256]{0:T(256)S(1)} %copy-done.7), channel_id=1, source_target_pairs={{0,16},{8,24},{16,32},{24,40},{32,48},{40,56},{48,64},{56,72},{64,... | collective-permute-start | bytes 3080 | tf_op jit(solution)/shard_map/ppermute | solution.py:18
  48.0 4.9 %collective-permute-start.7 = (s32[256]{0:T(256)S(1)}, s32[256]{0:T(256)S(1)}, u32[]{:S(2)}, u32[]{:S(2)}) collective-permute-start(s32[256]{0:T(256)S(1)} %copy-done.7), channel_id=1, source_target_pairs={{0,8},{8,16},{16,24},{24,32},{32,40},{40,48},{48,56},{56,64},{64,7... | collective-permute-start | bytes 3080 | tf_op jit(solution)/shard_map/ppermute | solution.py:18
  104.2 1.0 copy-start.2
  107.5 13.1 %collective-permute-start.8 = (bf16[256,2,256]{2,0,1:T(8,128)(2,1)}, bf16[256,2,256]{2,0,1:T(8,128)(2,1)}, u32[]{:S(2)}, u32[]{:S(2)}) collective-permute-start(bf16[256,2,256]{2,0,1:T(8,128)(2,1)} %pad_maximum_fusion), channel_id=1, source_target_pairs={{0,16},{8,24},{16,32},{24,40},{32,48},{40,56},{48,64},{56,72},{64,... | collective-permute-start | bytes 786440 | tf_op jit(solution)/shard_map/ppermute | solution.py:18
  111.1 16.7 %collective-permute-start.9 = (bf16[256,2,256]{2,0,1:T(8,128)(2,1)}, bf16[256,2,256]{2,0,1:T(8,128)(2,1)S(1)}, u32[]{:S(2)}, u32[]{:S(2)}) collective-permute-start(bf16[256,2,256]{2,0,1:T(8,128)(2,1)} %pad_maximum_fusion), channel_id=1, source_target_pairs={{0,32},{8,40},{16,48},{24,56},{32,64},{40,72},{48,80},{56,88},{64,... | collective-permute-start | bytes 786440 | tf_op jit(solution)/shard_map/ppermute | solution.py:18
  114.5 20.1 %collective-permute-start.10 = (bf16[256,2,256]{2,0,1:T(8,128)(2,1)}, bf16[256,2,256]{2,0,1:T(8,128)(2,1)S(1)}, u32[]{:S(2)}, u32[]{:S(2)}) collective-permute-start(bf16[256,2,256]{2,0,1:T(8,128)(2,1)} %pad_maximum_fusion), channel_id=1, source_target_pairs={{0,48},{8,56},{16,64},{24,72},{32,80},{40,88},{48,96},{56,104},{64... | collective-permute-start | bytes 786440 | tf_op jit(solution)/shard_map/ppermute | solution.py:18
  117.1 23.6 %collective-permute-start.11 = (bf16[256,2,256]{2,0,1:T(8,128)(2,1)}, bf16[256,2,256]{2,0,1:T(8,128)(2,1)S(1)}, u32[]{:S(2)}, u32[]{:S(2)}) collective-permute-start(bf16[256,2,256]{2,0,1:T(8,128)(2,1)} %pad_maximum_fusion), channel_id=1, source_target_pairs={{0,64},{8,72},{16,80},{24,88},{32,96},{40,104},{48,112},{56,120},{... | collective-permute-start | bytes 786440 | tf_op jit(solution)/shard_map/ppermute | solution.py:18
  142.1 5.3 %collective-permute-start.12 = (bf16[5,256,2,256]{3,1,2,0:T(8,128)(2,1)}, bf16[5,256,2,256]{3,1,2,0:T(8,128)(2,1)}, u32[]{:S(2)}, u32[]{:S(2)}) collective-permute-start(bf16[5,256,2,256]{3,1,2,0:T(8,128)(2,1)} %get-tuple-element.10), channel_id=1, source_target_pairs={{0,8},{8,0},{16,24},{24,16},{32,40},{40,32},{48,56},{56,48},{64,72... | collective-permute-start | bytes 3932168 | tf_op jit(solution)/shard_map/ppermute | solution.py:118
  150.4 6.8 %copy-start = (bf16[10,256,2,256]{3,1,0,2:T(8,128)(2,1)S(1)}, bf16[10,256,2,256]{3,1,0,2:T(8,128)(2,1)}, u32[]{:S(2)}) copy-start(bf16[10,256,2,256]{3,1,0,2:T(8,128)(2,1)} %copy.48) | copy-start | bytes 7864324
  162.5 35.8 %copy-start.3 = (bf16[256,256]{1,0:T(8,128)(2,1)S(1)}, bf16[256,256]{1,0:T(8,128)(2,1)}, u32[]{:S(2)}) copy-start(bf16[256,256]{1,0:T(8,128)(2,1)} %param.10) | copy-start | bytes 393220
  235.8 4.6 %copy-start.8 = (s32[16]{0:T(128)S(1)}, s32[16]{0:T(128)}, u32[]{:S(2)}) copy-start(s32[16]{0:T(128)} %param.12) | copy-start | bytes 196
  236.9 29.8 %all-to-all-start.3 = ((bf16[8,256,256]{2,1,0:T(8,128)(2,1)}), bf16[8,256,256]{2,1,0:T(8,128)(2,1)S(1)}, u32[]{:S(2)}, u32[]{:S(2)}) async-start(bf16[8,256,256]{2,1,0:T(8,128)(2,1)} %bitcast.71), calls=%async_computation.3 | async-start | bytes 2097152 | tf_op jit(solution)/shard_map/all_to_all | solution.py:34
  243.0 24.5 %copy-start.1 = (bf16[2,16,16,256]{3,2,1,0:T(8,128)(2,1)}, bf16[2,16,16,256]{3,2,1,0:T(8,128)(2,1)S(1)}, u32[]{:S(2)}) copy-start(bf16[2,16,16,256]{3,2,1,0:T(8,128)(2,1)S(1)} %scatter_fusion) | copy-start | bytes 786436
Sparse Core Ops, SparseCore 0:
  12.0 88.6 all-gather.2
  104.6 90.4 all-gather.4

commit v10 on v8

--- a/solution.py
+++ b/solution.py
@@ -95,7 +95,22 @@
     earlier = same & (window_index[None, :] < lead + local_index[:, None])
     positions = jnp.sum(earlier.astype(jnp.int32), axis=1)
 
-    whole = swap_gather(hidden_in, "narrow")
+    pairs_per_chip = 2
+    chips_back = REACH // pairs_per_chip
+    partner_rank = wide_rank ^ 1
+    block_ids = []
+    for step in range(chips_back, 0, -1):
+        block_ids += [wide_rank - pairs_per_chip * step, partner_rank - pairs_per_chip * step]
+    block_ids += [partner_rank, wide_rank]
+    key_index = (
+        jnp.stack(block_ids)[:, None] * tok_rows + local_index[None, :]
+    ).reshape(-1)
+    query_index = wide_rank * tok_rows + local_index
+    query_start = query_index - positions
+    allowed = (key_index[None, :] >= query_start[:, None]) & (key_index[None, :] <= query_index[:, None])
+    allowed, hidden_sent = lax.optimization_barrier((allowed, hidden_in))
+
+    whole = swap_gather(hidden_sent, "narrow")
     normed = norm_rows(whole)
     local_width = attn_width
     head_count = local_width // HEAD_DIM
@@ -110,28 +125,16 @@
     )
     values = v_proj.astype(jnp.bfloat16).reshape(tok_rows, head_count, HEAD_DIM)
     packed = jnp.concatenate([keys_rot, values], axis=2)
-    pairs_per_chip = 2
-    chips_back = REACH // pairs_per_chip
     line = [shifted(packed, "wide", pairs_per_chip * step) for step in range(1, chips_back + 1)]
     count = lax.axis_size("wide")
     partner = lax.ppermute(
         jnp.stack(line + [packed], axis=0), "wide", [(i, i ^ 1) for i in range(count)]
     )
-    partner_rank = wide_rank ^ 1
     order = []
-    block_ids = []
     for step in range(chips_back, 0, -1):
         order += [line[step - 1], partner[step - 1]]
-        block_ids += [wide_rank - pairs_per_chip * step, partner_rank - pairs_per_chip * step]
     order += [partner[chips_back], packed]
-    block_ids += [partner_rank, wide_rank]
     kv_all = jnp.concatenate(order, axis=0)
-    key_index = (
-        jnp.stack(block_ids)[:, None] * tok_rows + local_index[None, :]
-    ).reshape(-1)
-    query_index = wide_rank * tok_rows + local_index
-    query_start = query_index - positions
-    allowed = (key_index[None, :] >= query_start[:, None]) & (key_index[None, :] <= query_index[:, None])
     score_scale = HEAD_DIM ** (-0.5)
     key_all = kv_all[:, :, :HEAD_DIM]
     value_all = kv_all[:, :, HEAD_DIM:]

time: 275 us -> 275 us (level)
    all_gather x1, waiting for transfers between devices: 29.8 us -> 15.3 us  [per_device(): lax.all_gather(jnp.concatenate(attn_pieces, axis=1), 'wide', axis=0, tile...]
    all_to_all x1, waiting for transfers between devices: 15.8 us -> 27.3 us  [swap_gather(): got = lax.all_to_all(copies, axis, 0, 0, tiled=True)]
    unnamed x30 -> x27, local copies, waits for them, and re-layouts: 10.5 us -> 9.42 us
where the time goes in v10:
time: 275 us; the launch traced here: 274 us
  waiting for transfers between devices  86.7 us (32%)
  blocking collectives  66 us (24%)
  starting transfers between devices  58.3 us (21%)
  matrix products  21.7 us (8%)
  local copies, waits for them, and re-layouts  17 us (6%)
  between operations  14.6 us (5%)
  other arithmetic  10.1 us (4%)
    ppermute x12, starting transfers between devices, shifted(): lax.ppermute(value, axis, [(source, source + steps) for source in range(f...  45.7 us
    all_to_all x1, blocking collectives, swap_sum(): got = lax.all_to_all(pieces, axis, 0, 0, tiled=True)  35.6 us
    all_to_all x1, blocking collectives, swap_gather(): got = lax.all_to_all(copies, axis, 0, 0, tiled=True)  30.4 us
    all_to_all x1, waiting for transfers between devices, swap_gather(): got = lax.all_to_all(copies, axis, 0, 0, tiled=True)  27.3 us
    all_to_all x1, waiting for transfers between devices, swap_sum(): got = lax.all_to_all(pieces, axis, 0, 0, tiled=True)  23.7 us
    ppermute x12, waiting for transfers between devices, shifted(): lax.ppermute(value, axis, [(source, source + steps) for source in range(f...  18.4 us
    all_gather x1, waiting for transfers between devices, per_device(): lax.all_gather(jnp.concatenate(attn_pieces, axis=1), 'wide', axis=0, tile...  15.3 us
    unnamed x27, local copies, waits for them, and re-layouts  9.42 us
  transfers between devices with their start and end apart: 17, of which 8 were waited for; matrix products, arithmetic and copies ran while one was open for 14% of the time, Pallas kernels for 0%

profile of v10, /device:TPU:6, one launch (start us, length us, event | category | flops | bytes accessed | tf_op | source)
XLA Modules:
  0.0 274.4 jit_solution(14003843050453240541)
XLA Ops:
  8.7 4.3 %collective-permute-start = (s32[256]{0:T(256)}, s32[256]{0:T(256)S(1)}, u32[]{:S(2)}, u32[]{:S(2)}) collective-permute-start(s32[256]{0:T(256)} %param.11), channel_id=1, source_target_pairs={{0,64},{8,72},{16,80},{24,88},{32,96},{40,104},{48,112},{56,120},{... | collective-permute-start | bytes 3080 | tf_op jit(solution)/shard_map/ppermute | solution.py:18
  13.0 3.7 %collective-permute-start.1 = (s32[256]{0:T(256)}, s32[256]{0:T(256)S(1)}, u32[]{:S(2)}, u32[]{:S(2)}) collective-permute-start(s32[256]{0:T(256)} %param.11), channel_id=1, source_target_pairs={{0,56},{8,64},{16,72},{24,80},{32,88},{40,96},{48,104},{56,112},{6... | collective-permute-start | bytes 3080 | tf_op jit(solution)/shard_map/ppermute | solution.py:18
  16.7 4.3 %collective-permute-start.2 = (s32[256]{0:T(256)}, s32[256]{0:T(256)S(1)}, u32[]{:S(2)}, u32[]{:S(2)}) collective-permute-start(s32[256]{0:T(256)} %param.11), channel_id=1, source_target_pairs={{0,48},{8,56},{16,64},{24,72},{32,80},{40,88},{48,96},{56,104},{64... | collective-permute-start | bytes 3080 | tf_op jit(solution)/shard_map/ppermute | solution.py:18
  20.9 6.4 %collective-permute-start.3 = (s32[256]{0:T(256)}, s32[256]{0:T(256)S(1)}, u32[]{:S(2)}, u32[]{:S(2)}) collective-permute-start(s32[256]{0:T(256)} %param.11), channel_id=1, source_target_pairs={{0,40},{8,48},{16,56},{24,64},{32,72},{40,80},{48,88},{56,96},{64,... | collective-permute-start | bytes 3080 | tf_op jit(solution)/shard_map/ppermute | solution.py:18
  27.3 4.3 %collective-permute-start.4 = (s32[256]{0:T(256)}, s32[256]{0:T(256)S(1)}, u32[]{:S(2)}, u32[]{:S(2)}) collective-permute-start(s32[256]{0:T(256)} %param.11), channel_id=1, source_target_pairs={{0,32},{8,40},{16,48},{24,56},{32,64},{40,72},{48,80},{56,88},{64,... | collective-permute-start | bytes 3080 | tf_op jit(solution)/shard_map/ppermute | solution.py:18
  31.8 3.5 %collective-permute-start.5 = (s32[256]{0:T(256)}, s32[256]{0:T(256)S(1)}, u32[]{:S(2)}, u32[]{:S(2)}) collective-permute-start(s32[256]{0:T(256)} %param.11), channel_id=1, source_target_pairs={{0,24},{8,32},{16,40},{24,48},{32,56},{40,64},{48,72},{56,80},{64,... | collective-permute-start | bytes 3080 | tf_op jit(solution)/shard_map/ppermute | solution.py:18
  35.3 2.8 %collective-permute-start.6 = (s32[256]{0:T(256)}, s32[256]{0:T(256)S(1)}, u32[]{:S(2)}, u32[]{:S(2)}) collective-permute-start(s32[256]{0:T(256)} %param.11), channel_id=1, source_target_pairs={{0,16},{8,24},{16,32},{24,40},{32,48},{40,56},{48,64},{56,72},{64,... | collective-permute-start | bytes 3080 | tf_op jit(solution)/shard_map/ppermute | solution.py:18
  38.1 3.4 %collective-permute-start.7 = (s32[256]{0:T(256)}, s32[256]{0:T(256)S(1)}, u32[]{:S(2)}, u32[]{:S(2)}) collective-permute-start(s32[256]{0:T(256)} %param.11), channel_id=1, source_target_pairs={{0,8},{8,16},{16,24},{24,32},{32,40},{40,48},{48,56},{56,64},{64,7... | collective-permute-start | bytes 3080 | tf_op jit(solution)/shard_map/ppermute | solution.py:18
  41.7 1.5 collective-permute-done.7
  45.2 1.4 compare_and_fusion
  48.7 7.1 %all-to-all-start = ((bf16[8,256,256]{1,2,0:T(8,128)(2,1)}), bf16[8,256,256]{1,2,0:T(8,128)(2,1)S(1)}, u32[]{:S(2)}, u32[]{:S(2)}) async-start(bf16[8,256,256]{1,2,0:T(8,128)(2,1)} %broadcast_in_dim.38), calls=%async_computation | async-start | bytes 2097152 | tf_op jit(solution)/shard_map/all_to_all | solution.py:25
  57.1 27.3 %all-to-all-done = bf16[8,256,256]{1,2,0:T(8,128)(2,1)S(1)} async-done(((bf16[8,256,256]{1,2,0:T(8,128)(2,1)}), bf16[8,256,256]{1,2,0:T(8,128)(2,1)S(1)}, u32[]{:S(2)}, u32[]{:S(2)}) %all-to-all-start) | async-done | bytes 1048608 | tf_op jit(solution)/shard_map/all_to_all | solution.py:25
  85.3 15.3 %all-gather.3.cloned.1.call-done = bf16[2048,1024]{1,0:T(8,128)(2,1)} async-done(((bf16[32,1024]{1,0:T(8,128)(2,1)}), bf16[2048,1024]{1,0:T(8,128)(2,1)}) %all-gather.3.cloned.1.call-update) | async-done | bytes 4194320 | tf_op jit(solution)/shard_map/all_gather | solution.py:81
  100.7 3.5 %fusion.53 = f32[256,1024]{1,0:T(8,128)S(1)} fusion(bf16[256,2048]{0,1:T(8,128)(2,1)S(1)} %fusion.12, bf16[2048,1024]{1,0:T(8,128)(2,1)} %all-gather.3.cloned.1.call-done), kind=kOutput, calls=%fused_computation.110 | convolution fusion | flops 1073741824 | bytes 6291456 | tf_op jit(solution)/shard_map/dot_general | solution.py:64
  105.0 3.5 %collective-permute-start.9 = (bf16[256,2,256]{2,0,1:T(8,128)(2,1)S(1)}, bf16[256,2,256]{2,0,1:T(8,128)(2,1)S(1)}, u32[]{:S(2)}, u32[]{:S(2)}) collective-permute-start(bf16[256,2,256]{2,0,1:T(8,128)(2,1)S(1)} %pad_maximum_fusion), channel_id=1, source_target_pairs={{0,16},{8,24},{16,32},{24,40},{32,48},{40,56},{48,64},{56,72},{64,... | collective-permute-start | bytes 786440 | tf_op jit(solution)/shard_map/ppermute | solution.py:18
  108.5 3.4 %collective-permute-start.10 = (bf16[256,2,256]{2,0,1:T(8,128)(2,1)S(1)}, bf16[256,2,256]{2,0,1:T(8,128)(2,1)S(1)}, u32[]{:S(2)}, u32[]{:S(2)}) collective-permute-start(bf16[256,2,256]{2,0,1:T(8,128)(2,1)S(1)} %pad_maximum_fusion), channel_id=1, source_target_pairs={{0,32},{8,40},{16,48},{24,56},{32,64},{40,72},{48,80},{56,88},{64,... | collective-permute-start | bytes 786440 | tf_op jit(solution)/shard_map/ppermute | solution.py:18
  111.8 2.5 collective-permute-start.11
  114.4 3.7 %collective-permute-start.8 = (bf16[256,2,256]{2,0,1:T(8,128)(2,1)S(1)}, bf16[256,2,256]{2,0,1:T(8,128)(2,1)S(1)}, u32[]{:S(2)}, u32[]{:S(2)}) collective-permute-start(bf16[256,2,256]{2,0,1:T(8,128)(2,1)S(1)} %pad_maximum_fusion), channel_id=1, source_target_pairs={{0,64},{8,72},{16,80},{24,88},{32,96},{40,104},{48,112},{56,120},{... | collective-permute-start | bytes 786440 | tf_op jit(solution)/shard_map/ppermute | solution.py:18
  118.8 5.5 %collective-permute-done.10 = bf16[256,2,256]{2,0,1:T(8,128)(2,1)S(1)} collective-permute-done((bf16[256,2,256]{2,0,1:T(8,128)(2,1)S(1)}, bf16[256,2,256]{2,0,1:T(8,128)(2,1)S(1)}, u32[]{:S(2)}, u32[]{:S(2)}) %collective-permute-start.10) | collective-permute-done | bytes 262176 | tf_op jit(solution)/shard_map/ppermute | solution.py:18
  125.1 6.0 %collective-permute-done.11 = bf16[256,2,256]{2,0,1:T(8,128)(2,1)S(1)} collective-permute-done((bf16[256,2,256]{2,0,1:T(8,128)(2,1)S(1)}, bf16[256,2,256]{2,0,1:T(8,128)(2,1)S(1)}, u32[]{:S(2)}, u32[]{:S(2)}) %collective-permute-start.11) | collective-permute-done | bytes 262176 | tf_op jit(solution)/shard_map/ppermute | solution.py:18
  131.8 5.3 %collective-permute-done.8 = bf16[256,2,256]{2,0,1:T(8,128)(2,1)S(1)} collective-permute-done((bf16[256,2,256]{2,0,1:T(8,128)(2,1)S(1)}, bf16[256,2,256]{2,0,1:T(8,128)(2,1)S(1)}, u32[]{:S(2)}, u32[]{:S(2)}) %collective-permute-start.8) | collective-permute-done | bytes 262176 | tf_op jit(solution)/shard_map/ppermute | solution.py:18
  138.6 1.9 collective-permute-start.12
  141.8 1.9 collective-permute-done.12
  150.2 6.7 %fusion.48 = (f32[2,256]{1,0:T(2,128)S(1)}, f32[2,256,2560]{2,1,0:T(8,128)}) fusion(pred[256,2560]{1,0:T(8,128)(4,1)} %compare_and_fusion, bf16[2560,2,256]{2,0,1:T(8,128)(2,1)} %constant_dynamic-update-slice_fusion.1, bf16[256,2,64]{2,0,1:T(8,128)(2,1)S(1)} %get-tuple-element.9, bf16[256,2,64]{2,0,1:T(8,128)(2,1)S(1)} %get-tuple-element.8), kind=kOutput, calls=%fused_computation.108 | convolution fusion | flops 342362624 | bytes 7997440 | tf_op jit(solution)/shard_map/sub | solution.py:147
  156.9 4.0 %fusion.23 = bf16[2,128,256]{2,1,0:T(8,128)(2,1)S(1)} fusion(f32[2,256,2560]{2,1,0:T(8,128)} %get-tuple-element.21, f32[2,256]{1,0:T(2,128)S(1)} %get-tuple-element.20, bf16[2560,2,256]{2,0,1:T(8,128)(2,1)} %constant_dynamic-update-slice_fusion.1), kind=kOutput, calls=%fused_computation.32 | convolution fusion | flops 338231296 | bytes 6686720 | tf_op jit(solution)/shard_map/hqk,khd->qhd/dot_general | solution.py:149
  160.8 1.7 convolution_convert_fusion.1
  162.7 35.6 %all_to_all.20 = bf16[8,256,256]{2,1,0:T(8,128)(2,1)S(1)} all-to-all(bf16[8,256,256]{2,1,0:T(8,128)(2,1)S(1)} %bitcast.89), channel_id=1, replica_groups=mesh['wide'=64,'narrow'=8] {'narrow'}, dimensions={0} | all-to-all | bytes 2097152 | tf_op jit(solution)/shard_map/all_to_all | solution.py:34
  198.6 30.4 %all_to_all.21 = bf16[8,256,256]{1,2,0:T(8,128)(2,1)S(1)} all-to-all(bf16[8,256,256]{1,2,0:T(8,128)(2,1)S(1)} %broadcast_in_dim.42), channel_id=1, replica_groups=mesh['wide'=64,'narrow'=8] {'narrow'}, dimensions={0} | all-to-all | bytes 2097152 | tf_op jit(solution)/shard_map/all_to_all | solution.py:25
  230.0 2.3 fusion.7
  232.3 3.6 %convolution_convert_fusion = bf16[256,2048]{1,0:T(8,128)(2,1)S(1)} fusion(bf16[2048,1536]{1,0:T(8,128)(2,1)} %all-gather.5.cloned.1.call-done, bf16[256,2048]{0,1:T(8,128)(2,1)S(1)} %fusion.10, f32[256,512]{1,0:T(8,128)S(1)} %fusion.7), kind=kOutput, calls=%fused_computation.8 | convolution fusion | flops 1075052544 | bytes 6815744 | tf_op jit(solution)/shard_map/dot_general | solution.py:162
  236.9 3.6 %all-to-all-start.3 = ((bf16[8,256,256]{2,1,0:T(8,128)(2,1)}), bf16[8,256,256]{2,1,0:T(8,128)(2,1)S(1)}, u32[]{:S(2)}, u32[]{:S(2)}) async-start(bf16[8,256,256]{2,1,0:T(8,128)(2,1)} %bitcast.85), calls=%async_computation.3 | async-start | bytes 2097152 | tf_op jit(solution)/shard_map/all_to_all | solution.py:34
  243.1 23.7 %all-to-all-done.3 = bf16[8,256,256]{2,1,0:T(8,128)(2,1)S(1)} async-done(((bf16[8,256,256]{2,1,0:T(8,128)(2,1)}), bf16[8,256,256]{2,1,0:T(8,128)(2,1)S(1)}, u32[]{:S(2)}, u32[]{:S(2)}) %all-to-all-start.3) | async-done | bytes 1048608 | tf_op jit(solution)/shard_map/all_to_all | solution.py:34
  (101 shorter events, 25.7 us)
Async XLA Ops:
  7.2 48.7 %copy-start.3 = (bf16[512,32]{0,1:T(8,128)(2,1)S(1)}, bf16[512,32]{0,1:T(8,128)(2,1)}, u32[]{:S(2)}) copy-start(bf16[512,32]{0,1:T(8,128)(2,1)} %param.19) | copy-start | bytes 98308
  7.2 48.7 %copy-start.5 = (bf16[32,512]{1,0:T(8,128)(2,1)S(1)}, bf16[32,512]{1,0:T(8,128)(2,1)}, u32[]{:S(2)}) copy-start(bf16[32,512]{1,0:T(8,128)(2,1)} %param.17) | copy-start | bytes 98308
  7.2 48.7 %copy-start.4 = (bf16[32,512]{1,0:T(8,128)(2,1)S(1)}, bf16[32,512]{1,0:T(8,128)(2,1)}, u32[]{:S(2)}) copy-start(bf16[32,512]{1,0:T(8,128)(2,1)} %param.18) | copy-start | bytes 98308
  7.2 93.5 %all-gather.3.cloned.1.call-start = ((), (), s32[]{:S(2)}) async-start(), calls=%async_computation.4 | async-start | bytes 4259840 | tf_op jit(solution)/shard_map/all_gather | solution.py:81
  8.7 23.2 %collective-permute-start = (s32[256]{0:T(256)}, s32[256]{0:T(256)S(1)}, u32[]{:S(2)}, u32[]{:S(2)}) collective-permute-start(s32[256]{0:T(256)} %param.11), channel_id=1, source_target_pairs={{0,64},{8,72},{16,80},{24,88},{32,96},{40,104},{48,112},{56,120},{... | collective-permute-start | bytes 3080 | tf_op jit(solution)/shard_map/ppermute | solution.py:18
  13.0 22.4 %collective-permute-start.1 = (s32[256]{0:T(256)}, s32[256]{0:T(256)S(1)}, u32[]{:S(2)}, u32[]{:S(2)}) collective-permute-start(s32[256]{0:T(256)} %param.11), channel_id=1, source_target_pairs={{0,56},{8,64},{16,72},{24,80},{32,88},{40,96},{48,104},{56,112},{6... | collective-permute-start | bytes 3080 | tf_op jit(solution)/shard_map/ppermute | solution.py:18
  16.7 21.5 %collective-permute-start.2 = (s32[256]{0:T(256)}, s32[256]{0:T(256)S(1)}, u32[]{:S(2)}, u32[]{:S(2)}) collective-permute-start(s32[256]{0:T(256)} %param.11), channel_id=1, source_target_pairs={{0,48},{8,56},{16,64},{24,72},{32,80},{40,88},{48,96},{56,104},{64... | collective-permute-start | bytes 3080 | tf_op jit(solution)/shard_map/ppermute | solution.py:18
  20.9 20.7 %collective-permute-start.3 = (s32[256]{0:T(256)}, s32[256]{0:T(256)S(1)}, u32[]{:S(2)}, u32[]{:S(2)}) collective-permute-start(s32[256]{0:T(256)} %param.11), channel_id=1, source_target_pairs={{0,40},{8,48},{16,56},{24,64},{32,72},{40,80},{48,88},{56,96},{64,... | collective-permute-start | bytes 3080 | tf_op jit(solution)/shard_map/ppermute | solution.py:18
  27.3 14.3 %collective-permute-start.4 = (s32[256]{0:T(256)}, s32[256]{0:T(256)S(1)}, u32[]{:S(2)}, u32[]{:S(2)}) collective-permute-start(s32[256]{0:T(256)} %param.11), channel_id=1, source_target_pairs={{0,32},{8,40},{16,48},{24,56},{32,64},{40,72},{48,80},{56,88},{64,... | collective-permute-start | bytes 3080 | tf_op jit(solution)/shard_map/ppermute | solution.py:18
  31.8 9.8 %collective-permute-start.5 = (s32[256]{0:T(256)}, s32[256]{0:T(256)S(1)}, u32[]{:S(2)}, u32[]{:S(2)}) collective-permute-start(s32[256]{0:T(256)} %param.11), channel_id=1, source_target_pairs={{0,24},{8,32},{16,40},{24,48},{32,56},{40,64},{48,72},{56,80},{64,... | collective-permute-start | bytes 3080 | tf_op jit(solution)/shard_map/ppermute | solution.py:18
  35.3 6.3 %collective-permute-start.6 = (s32[256]{0:T(256)}, s32[256]{0:T(256)S(1)}, u32[]{:S(2)}, u32[]{:S(2)}) collective-permute-start(s32[256]{0:T(256)} %param.11), channel_id=1, source_target_pairs={{0,16},{8,24},{16,32},{24,40},{32,48},{40,56},{48,64},{56,72},{64,... | collective-permute-start | bytes 3080 | tf_op jit(solution)/shard_map/ppermute | solution.py:18
  38.1 5.1 %collective-permute-start.7 = (s32[256]{0:T(256)}, s32[256]{0:T(256)S(1)}, u32[]{:S(2)}, u32[]{:S(2)}) collective-permute-start(s32[256]{0:T(256)} %param.11), channel_id=1, source_target_pairs={{0,8},{8,16},{16,24},{24,32},{32,40},{40,48},{48,56},{56,64},{64,7... | collective-permute-start | bytes 3080 | tf_op jit(solution)/shard_map/ppermute | solution.py:18
  48.7 35.7 %all-to-all-start = ((bf16[8,256,256]{1,2,0:T(8,128)(2,1)}), bf16[8,256,256]{1,2,0:T(8,128)(2,1)S(1)}, u32[]{:S(2)}, u32[]{:S(2)}) async-start(bf16[8,256,256]{1,2,0:T(8,128)(2,1)} %broadcast_in_dim.38), calls=%async_computation | async-start | bytes 2097152 | tf_op jit(solution)/shard_map/all_to_all | solution.py:25
  55.8 174.1 %all-gather.5.cloned.1.call-start = ((), (), s32[]{:S(2)}) async-start(), calls=%async_computation.5 | async-start | bytes 6389760 | tf_op jit(solution)/shard_map/all_gather | solution.py:76
  104.1 14.7 %copy-start.1 = (f32[256,1024]{1,0:T(8,128)}, f32[256,1024]{1,0:T(8,128)S(1)}, u32[]{:S(2)}) copy-start(f32[256,1024]{1,0:T(8,128)S(1)} %fusion.53) | copy-start | bytes 3145732
  105.0 13.1 %collective-permute-start.9 = (bf16[256,2,256]{2,0,1:T(8,128)(2,1)S(1)}, bf16[256,2,256]{2,0,1:T(8,128)(2,1)S(1)}, u32[]{:S(2)}, u32[]{:S(2)}) collective-permute-start(bf16[256,2,256]{2,0,1:T(8,128)(2,1)S(1)} %pad_maximum_fusion), channel_id=1, source_target_pairs={{0,16},{8,24},{16,32},{24,40},{32,48},{40,56},{48,64},{56,72},{64,... | collective-permute-start | bytes 786440 | tf_op jit(solution)/shard_map/ppermute | solution.py:18
  108.5 15.9 %collective-permute-start.10 = (bf16[256,2,256]{2,0,1:T(8,128)(2,1)S(1)}, bf16[256,2,256]{2,0,1:T(8,128)(2,1)S(1)}, u32[]{:S(2)}, u32[]{:S(2)}) collective-permute-start(bf16[256,2,256]{2,0,1:T(8,128)(2,1)S(1)} %pad_maximum_fusion), channel_id=1, source_target_pairs={{0,32},{8,40},{16,48},{24,56},{32,64},{40,72},{48,80},{56,88},{64,... | collective-permute-start | bytes 786440 | tf_op jit(solution)/shard_map/ppermute | solution.py:18
  111.8 19.2 %collective-permute-start.11 = (bf16[256,2,256]{2,0,1:T(8,128)(2,1)S(1)}, bf16[256,2,256]{2,0,1:T(8,128)(2,1)S(1)}, u32[]{:S(2)}, u32[]{:S(2)}) collective-permute-start(bf16[256,2,256]{2,0,1:T(8,128)(2,1)S(1)} %pad_maximum_fusion), channel_id=1, source_target_pairs={{0,48},{8,56},{16,64},{24,72},{32,80},{40,88},{48,96},{56,104},{64... | collective-permute-start | bytes 786440 | tf_op jit(solution)/shard_map/ppermute | solution.py:18
  114.4 22.7 %collective-permute-start.8 = (bf16[256,2,256]{2,0,1:T(8,128)(2,1)S(1)}, bf16[256,2,256]{2,0,1:T(8,128)(2,1)S(1)}, u32[]{:S(2)}, u32[]{:S(2)}) collective-permute-start(bf16[256,2,256]{2,0,1:T(8,128)(2,1)S(1)} %pad_maximum_fusion), channel_id=1, source_target_pairs={{0,64},{8,72},{16,80},{24,88},{32,96},{40,104},{48,112},{56,120},{... | collective-permute-start | bytes 786440 | tf_op jit(solution)/shard_map/ppermute | solution.py:18
  138.6 5.1 %collective-permute-start.12 = (bf16[5,256,2,256]{3,1,2,0:T(8,128)(2,1)}, bf16[5,256,2,256]{3,1,2,0:T(8,128)(2,1)S(1)}, u32[]{:S(2)}, u32[]{:S(2)}) collective-permute-start(bf16[5,256,2,256]{3,1,2,0:T(8,128)(2,1)} %bitcast_dynamic-update-slice_fusion), channel_id=1, source_target_pairs={{0,8},{8,0},{16,24},{24,16},{32,40},{40,32},{48,56},{56,48},{64,72... | collective-permute-start | bytes 3932168 | tf_op jit(solution)/shard_map/ppermute | solution.py:130
  162.6 35.8 %copy-start.2 = (bf16[256,256]{1,0:T(8,128)(2,1)S(1)}, bf16[256,256]{1,0:T(8,128)(2,1)}, u32[]{:S(2)}) copy-start(bf16[256,256]{1,0:T(8,128)(2,1)} %param.10) | copy-start | bytes 393220
  235.9 4.6 %copy-start.6 = (s32[16]{0:T(128)S(1)}, s32[16]{0:T(128)}, u32[]{:S(2)}) copy-start(s32[16]{0:T(128)} %param.12) | copy-start | bytes 196
  236.9 29.8 %all-to-all-start.3 = ((bf16[8,256,256]{2,1,0:T(8,128)(2,1)}), bf16[8,256,256]{2,1,0:T(8,128)(2,1)S(1)}, u32[]{:S(2)}, u32[]{:S(2)}) async-start(bf16[8,256,256]{2,1,0:T(8,128)(2,1)} %bitcast.85), calls=%async_computation.3 | async-start | bytes 2097152 | tf_op jit(solution)/shard_map/all_to_all | solution.py:34
  243.0 24.5 %copy-start = (bf16[2,16,16,256]{3,2,1,0:T(8,128)(2,1)}, bf16[2,16,16,256]{3,2,1,0:T(8,128)(2,1)S(1)}, u32[]{:S(2)}) copy-start(bf16[2,16,16,256]{3,2,1,0:T(8,128)(2,1)S(1)} %scatter_fusion) | copy-start | bytes 786436
Sparse Core Ops, SparseCore 0:
  12.0 88.6 all-gather.2
  104.6 88.9 all-gather.4

commit v11 on v10

--- a/solution.py
+++ b/solution.py
@@ -124,7 +124,7 @@
         jnp.bfloat16
     )
     values = v_proj.astype(jnp.bfloat16).reshape(tok_rows, head_count, HEAD_DIM)
-    packed = jnp.concatenate([keys_rot, values], axis=2)
+    packed = jnp.transpose(jnp.concatenate([keys_rot, values], axis=2), (1, 2, 0))
     line = [shifted(packed, "wide", pairs_per_chip * step) for step in range(1, chips_back + 1)]
     count = lax.axis_size("wide")
     partner = lax.ppermute(
@@ -134,19 +134,19 @@
     for step in range(chips_back, 0, -1):
         order += [line[step - 1], partner[step - 1]]
     order += [partner[chips_back], packed]
-    kv_all = jnp.concatenate(order, axis=0)
+    kv_all = jnp.concatenate(order, axis=-1)
     score_scale = HEAD_DIM ** (-0.5)
-    key_all = kv_all[:, :, :HEAD_DIM]
-    value_all = kv_all[:, :, HEAD_DIM:]
+    key_all = kv_all[:, :HEAD_DIM, :]
+    value_all = kv_all[:, HEAD_DIM:, :]
     scores = (
-        jnp.einsum("qhd,khd->hqk", queries, key_all, preferred_element_type=jnp.float32)
+        jnp.einsum("qhd,hdk->hqk", queries, key_all, preferred_element_type=jnp.float32)
         * score_scale
     )
     scores = jnp.where(allowed[None], scores, -1e30)
     row_peak = jnp.max(scores, axis=-1, keepdims=True)
     exps = jnp.where(allowed[None], jnp.exp(scores - row_peak), 0.0)
     attn_probs = (exps / jnp.sum(exps, axis=-1, keepdims=True)).astype(jnp.bfloat16)
-    mixed = jnp.einsum("hqk,khd->qhd", attn_probs, value_all, preferred_element_type=jnp.float32)
+    mixed = jnp.einsum("hqk,hdk->qhd", attn_probs, value_all, preferred_element_type=jnp.float32)
     attended = mixed.astype(jnp.bfloat16).reshape(tok_rows, local_width)
     attn_terms = lax.dot_general(
         attended, wo_t, (((1,), (1,)), ((), ())), preferred_element_type=jnp.float32

time: 275 us -> 275 us (level)
  no operation moved by 1% of the time
where the time goes in v11:
time: 275 us; the launch traced here: 274 us
  waiting for transfers between devices  88.1 us (32%)
  blocking collectives  66 us (24%)
  starting transfers between devices  58.3 us (21%)
  matrix products  21.3 us (8%)
  local copies, waits for them, and re-layouts  15.8 us (6%)
  between operations  14.6 us (5%)
  other arithmetic  9.66 us (4%)
    ppermute x12, starting transfers between devices, shifted(): lax.ppermute(value, axis, [(source, source + steps) for source in range(f...  45.7 us
    all_to_all x1, blocking collectives, swap_sum(): got = lax.all_to_all(pieces, axis, 0, 0, tiled=True)  35.6 us
    all_to_all x1, blocking collectives, swap_gather(): got = lax.all_to_all(copies, axis, 0, 0, tiled=True)  30.4 us
    all_to_all x1, waiting for transfers between devices, swap_gather(): got = lax.all_to_all(copies, axis, 0, 0, tiled=True)  27.5 us
    all_to_all x1, waiting for transfers between devices, swap_sum(): got = lax.all_to_all(pieces, axis, 0, 0, tiled=True)  24.6 us
    ppermute x12, waiting for transfers between devices, shifted(): lax.ppermute(value, axis, [(source, source + steps) for source in range(f...  18.3 us
    all_gather x1, waiting for transfers between devices, per_device(): lax.all_gather(jnp.concatenate(attn_pieces, axis=1), 'wide', axis=0, tile...  15.3 us
    unnamed x27, local copies, waits for them, and re-layouts  9.78 us
  transfers between devices with their start and end apart: 17, of which 8 were waited for; matrix products, arithmetic and copies ran while one was open for 14% of the time, Pallas kernels for 0%

profile of v11, /device:TPU:6, one launch (start us, length us, event | category | flops | bytes accessed | tf_op | source)
XLA Modules:
  0.0 273.8 jit_solution(3558538110484402466)
XLA Ops:
  8.7 4.3 %collective-permute-start = (s32[256]{0:T(256)}, s32[256]{0:T(256)S(1)}, u32[]{:S(2)}, u32[]{:S(2)}) collective-permute-start(s32[256]{0:T(256)} %param.11), channel_id=1, source_target_pairs={{0,64},{8,72},{16,80},{24,88},{32,96},{40,104},{48,112},{56,120},{... | collective-permute-start | bytes 3080 | tf_op jit(solution)/shard_map/ppermute | solution.py:18
  13.0 3.7 %collective-permute-start.1 = (s32[256]{0:T(256)}, s32[256]{0:T(256)S(1)}, u32[]{:S(2)}, u32[]{:S(2)}) collective-permute-start(s32[256]{0:T(256)} %param.11), channel_id=1, source_target_pairs={{0,56},{8,64},{16,72},{24,80},{32,88},{40,96},{48,104},{56,112},{6... | collective-permute-start | bytes 3080 | tf_op jit(solution)/shard_map/ppermute | solution.py:18
  16.7 4.3 %collective-permute-start.2 = (s32[256]{0:T(256)}, s32[256]{0:T(256)S(1)}, u32[]{:S(2)}, u32[]{:S(2)}) collective-permute-start(s32[256]{0:T(256)} %param.11), channel_id=1, source_target_pairs={{0,48},{8,56},{16,64},{24,72},{32,80},{40,88},{48,96},{56,104},{64... | collective-permute-start | bytes 3080 | tf_op jit(solution)/shard_map/ppermute | solution.py:18
  20.9 6.4 %collective-permute-start.3 = (s32[256]{0:T(256)}, s32[256]{0:T(256)S(1)}, u32[]{:S(2)}, u32[]{:S(2)}) collective-permute-start(s32[256]{0:T(256)} %param.11), channel_id=1, source_target_pairs={{0,40},{8,48},{16,56},{24,64},{32,72},{40,80},{48,88},{56,96},{64,... | collective-permute-start | bytes 3080 | tf_op jit(solution)/shard_map/ppermute | solution.py:18
  27.3 4.3 %collective-permute-start.4 = (s32[256]{0:T(256)}, s32[256]{0:T(256)S(1)}, u32[]{:S(2)}, u32[]{:S(2)}) collective-permute-start(s32[256]{0:T(256)} %param.11), channel_id=1, source_target_pairs={{0,32},{8,40},{16,48},{24,56},{32,64},{40,72},{48,80},{56,88},{64,... | collective-permute-start | bytes 3080 | tf_op jit(solution)/shard_map/ppermute | solution.py:18
  31.8 3.5 %collective-permute-start.5 = (s32[256]{0:T(256)}, s32[256]{0:T(256)S(1)}, u32[]{:S(2)}, u32[]{:S(2)}) collective-permute-start(s32[256]{0:T(256)} %param.11), channel_id=1, source_target_pairs={{0,24},{8,32},{16,40},{24,48},{32,56},{40,64},{48,72},{56,80},{64,... | collective-permute-start | bytes 3080 | tf_op jit(solution)/shard_map/ppermute | solution.py:18
  35.3 2.8 %collective-permute-start.6 = (s32[256]{0:T(256)}, s32[256]{0:T(256)S(1)}, u32[]{:S(2)}, u32[]{:S(2)}) collective-permute-start(s32[256]{0:T(256)} %param.11), channel_id=1, source_target_pairs={{0,16},{8,24},{16,32},{24,40},{32,48},{40,56},{48,64},{56,72},{64,... | collective-permute-start | bytes 3080 | tf_op jit(solution)/shard_map/ppermute | solution.py:18
  38.1 3.4 %collective-permute-start.7 = (s32[256]{0:T(256)}, s32[256]{0:T(256)S(1)}, u32[]{:S(2)}, u32[]{:S(2)}) collective-permute-start(s32[256]{0:T(256)} %param.11), channel_id=1, source_target_pairs={{0,8},{8,16},{16,24},{24,32},{32,40},{40,48},{48,56},{56,64},{64,7... | collective-permute-start | bytes 3080 | tf_op jit(solution)/shard_map/ppermute | solution.py:18
  41.7 1.5 collective-permute-done.7
  45.2 1.5 compare_and_fusion
  48.8 7.1 %all-to-all-start = ((bf16[8,256,256]{1,2,0:T(8,128)(2,1)}), bf16[8,256,256]{1,2,0:T(8,128)(2,1)S(1)}, u32[]{:S(2)}, u32[]{:S(2)}) async-start(bf16[8,256,256]{1,2,0:T(8,128)(2,1)} %broadcast_in_dim.38), calls=%async_computation | async-start | bytes 2097152 | tf_op jit(solution)/shard_map/all_to_all | solution.py:25
  56.9 27.5 %all-to-all-done = bf16[8,256,256]{1,2,0:T(8,128)(2,1)S(1)} async-done(((bf16[8,256,256]{1,2,0:T(8,128)(2,1)}), bf16[8,256,256]{1,2,0:T(8,128)(2,1)S(1)}, u32[]{:S(2)}, u32[]{:S(2)}) %all-to-all-start) | async-done | bytes 1048608 | tf_op jit(solution)/shard_map/all_to_all | solution.py:25
  85.4 15.3 %all-gather.3.cloned.1.call-done = bf16[2048,1024]{1,0:T(8,128)(2,1)} async-done(((bf16[32,1024]{1,0:T(8,128)(2,1)}), bf16[2048,1024]{1,0:T(8,128)(2,1)}) %all-gather.3.cloned.1.call-update) | async-done | bytes 4194320 | tf_op jit(solution)/shard_map/all_gather | solution.py:81
  100.7 3.5 %fusion.52 = f32[256,1024]{1,0:T(8,128)S(1)} fusion(bf16[256,2048]{0,1:T(8,128)(2,1)S(1)} %fusion.12, bf16[2048,1024]{1,0:T(8,128)(2,1)} %all-gather.3.cloned.1.call-done), kind=kOutput, calls=%fused_computation.107 | convolution fusion | flops 1073741824 | bytes 6291456 | tf_op jit(solution)/shard_map/dot_general | solution.py:64
  104.5 3.5 %collective-permute-start.9 = (bf16[2,256,256]{2,1,0:T(8,128)(2,1)S(1)}, bf16[2,256,256]{2,1,0:T(8,128)(2,1)S(1)}, u32[]{:S(2)}, u32[]{:S(2)}) collective-permute-start(bf16[2,256,256]{2,1,0:T(8,128)(2,1)S(1)} %fusion.38), channel_id=1, source_target_pairs={{0,16},{8,24},{16,32},{24,40},{32,48},{40,56},{48,64},{56,72},{64,... | collective-permute-start | bytes 786440 | tf_op jit(solution)/shard_map/ppermute | solution.py:18
  108.0 3.4 %collective-permute-start.10 = (bf16[2,256,256]{2,1,0:T(8,128)(2,1)S(1)}, bf16[2,256,256]{2,1,0:T(8,128)(2,1)S(1)}, u32[]{:S(2)}, u32[]{:S(2)}) collective-permute-start(bf16[2,256,256]{2,1,0:T(8,128)(2,1)S(1)} %fusion.38), channel_id=1, source_target_pairs={{0,32},{8,40},{16,48},{24,56},{32,64},{40,72},{48,80},{56,88},{64,... | collective-permute-start | bytes 786440 | tf_op jit(solution)/shard_map/ppermute | solution.py:18
  111.4 2.5 collective-permute-start.11
  114.0 3.7 %collective-permute-start.8 = (bf16[2,256,256]{2,1,0:T(8,128)(2,1)S(1)}, bf16[2,256,256]{2,1,0:T(8,128)(2,1)S(1)}, u32[]{:S(2)}, u32[]{:S(2)}) collective-permute-start(bf16[2,256,256]{2,1,0:T(8,128)(2,1)S(1)} %fusion.38), channel_id=1, source_target_pairs={{0,64},{8,72},{16,80},{24,88},{32,96},{40,104},{48,112},{56,120},{... | collective-permute-start | bytes 786440 | tf_op jit(solution)/shard_map/ppermute | solution.py:18
  118.4 5.3 %collective-permute-done.10 = bf16[2,256,256]{2,1,0:T(8,128)(2,1)S(1)} collective-permute-done((bf16[2,256,256]{2,1,0:T(8,128)(2,1)S(1)}, bf16[2,256,256]{2,1,0:T(8,128)(2,1)S(1)}, u32[]{:S(2)}, u32[]{:S(2)}) %collective-permute-start.10) | collective-permute-done | bytes 262176 | tf_op jit(solution)/shard_map/ppermute | solution.py:18
  124.4 6.1 %collective-permute-done.11 = bf16[2,256,256]{2,1,0:T(8,128)(2,1)S(1)} collective-permute-done((bf16[2,256,256]{2,1,0:T(8,128)(2,1)S(1)}, bf16[2,256,256]{2,1,0:T(8,128)(2,1)S(1)}, u32[]{:S(2)}, u32[]{:S(2)}) %collective-permute-start.11) | collective-permute-done | bytes 262176 | tf_op jit(solution)/shard_map/ppermute | solution.py:18
  131.3 5.3 %collective-permute-done.8 = bf16[2,256,256]{2,1,0:T(8,128)(2,1)S(1)} collective-permute-done((bf16[2,256,256]{2,1,0:T(8,128)(2,1)S(1)}, bf16[2,256,256]{2,1,0:T(8,128)(2,1)S(1)}, u32[]{:S(2)}, u32[]{:S(2)}) %collective-permute-start.8) | collective-permute-done | bytes 262176 | tf_op jit(solution)/shard_map/ppermute | solution.py:18
  138.0 1.9 collective-permute-start.12
  140.9 2.3 collective-permute-done.12
  150.0 6.3 %fusion.47 = (f32[2,256]{1,0:T(2,128)S(1)}, f32[2,256,2560]{2,1,0:T(8,128)}) fusion(pred[256,2560]{1,0:T(8,128)(4,1)S(1)} %copy-done.1, bf16[2,256,2560]{2,1,0:T(8,128)(2,1)} %constant_dynamic-update-slice_fusion.1, bf16[256,2,64]{0,2,1:T(8,128)(2,1)S(1)} %get-tuple-element.9, bf16[256,2,64]{0,2,1:T(8,128)(2,1)S(1)} %get-tuple-element.8), kind=kOutput, calls=%fused_computation.106 | convolution fusion | flops 342362624 | bytes 7997440 | tf_op jit(solution)/shard_map/sub | solution.py:147
  156.3 4.0 %fusion.23 = bf16[2,128,256]{2,1,0:T(8,128)(2,1)S(1)} fusion(f32[2,256,2560]{2,1,0:T(8,128)} %get-tuple-element.17, f32[2,256]{1,0:T(2,128)S(1)} %get-tuple-element.16, bf16[2,256,2560]{2,1,0:T(8,128)(2,1)} %constant_dynamic-update-slice_fusion.1), kind=kOutput, calls=%fused_computation.32 | convolution fusion | flops 338231296 | bytes 6686720 | tf_op jit(solution)/shard_map/hqk,hdk->qhd/dot_general | solution.py:149
  160.3 1.7 convolution_convert_fusion.1
  162.1 35.6 %all_to_all.20 = bf16[8,256,256]{2,1,0:T(8,128)(2,1)S(1)} all-to-all(bf16[8,256,256]{2,1,0:T(8,128)(2,1)S(1)} %bitcast.92), channel_id=1, replica_groups=mesh['wide'=64,'narrow'=8] {'narrow'}, dimensions={0} | all-to-all | bytes 2097152 | tf_op jit(solution)/shard_map/all_to_all | solution.py:34
  198.1 30.4 %all_to_all.21 = bf16[8,256,256]{1,2,0:T(8,128)(2,1)S(1)} all-to-all(bf16[8,256,256]{1,2,0:T(8,128)(2,1)S(1)} %broadcast_in_dim.42), channel_id=1, replica_groups=mesh['wide'=64,'narrow'=8] {'narrow'}, dimensions={0} | all-to-all | bytes 2097152 | tf_op jit(solution)/shard_map/all_to_all | solution.py:25
  229.4 2.3 fusion.7
  231.7 3.6 %convolution_convert_fusion = bf16[256,2048]{1,0:T(8,128)(2,1)S(1)} fusion(bf16[2048,1536]{1,0:T(8,128)(2,1)} %all-gather.5.cloned.1.call-done, bf16[256,2048]{0,1:T(8,128)(2,1)S(1)} %fusion.10, f32[256,512]{1,0:T(8,128)S(1)} %fusion.7), kind=kOutput, calls=%fused_computation.8 | convolution fusion | flops 1075052544 | bytes 6815744 | tf_op jit(solution)/shard_map/dot_general | solution.py:162
  236.4 3.6 %all-to-all-start.3 = ((bf16[8,256,256]{2,1,0:T(8,128)(2,1)}), bf16[8,256,256]{2,1,0:T(8,128)(2,1)S(1)}, u32[]{:S(2)}, u32[]{:S(2)}) async-start(bf16[8,256,256]{2,1,0:T(8,128)(2,1)} %bitcast.88), calls=%async_computation.3 | async-start | bytes 2097152 | tf_op jit(solution)/shard_map/all_to_all | solution.py:34
  241.5 24.6 %all-to-all-done.3 = bf16[8,256,256]{2,1,0:T(8,128)(2,1)S(1)} async-done(((bf16[8,256,256]{2,1,0:T(8,128)(2,1)}), bf16[8,256,256]{2,1,0:T(8,128)(2,1)S(1)}, u32[]{:S(2)}, u32[]{:S(2)}) %all-to-all-start.3) | async-done | bytes 1048608 | tf_op jit(solution)/shard_map/all_to_all | solution.py:34
  (99 shorter events, 24.1 us)
Async XLA Ops:
  7.2 48.7 %copy-start.3 = (bf16[512,32]{0,1:T(8,128)(2,1)S(1)}, bf16[512,32]{0,1:T(8,128)(2,1)}, u32[]{:S(2)}) copy-start(bf16[512,32]{0,1:T(8,128)(2,1)} %param.19) | copy-start | bytes 98308
  7.2 48.7 %copy-start.5 = (bf16[32,512]{1,0:T(8,128)(2,1)S(1)}, bf16[32,512]{1,0:T(8,128)(2,1)}, u32[]{:S(2)}) copy-start(bf16[32,512]{1,0:T(8,128)(2,1)} %param.17) | copy-start | bytes 98308
  7.2 48.7 %copy-start.4 = (bf16[32,512]{1,0:T(8,128)(2,1)S(1)}, bf16[32,512]{1,0:T(8,128)(2,1)}, u32[]{:S(2)}) copy-start(bf16[32,512]{1,0:T(8,128)(2,1)} %param.18) | copy-start | bytes 98308
  7.2 93.5 %all-gather.3.cloned.1.call-start = ((), (), s32[]{:S(2)}) async-start(), calls=%async_computation.4 | async-start | bytes 4259840 | tf_op jit(solution)/shard_map/all_gather | solution.py:81
  8.7 23.2 %collective-permute-start = (s32[256]{0:T(256)}, s32[256]{0:T(256)S(1)}, u32[]{:S(2)}, u32[]{:S(2)}) collective-permute-start(s32[256]{0:T(256)} %param.11), channel_id=1, source_target_pairs={{0,64},{8,72},{16,80},{24,88},{32,96},{40,104},{48,112},{56,120},{... | collective-permute-start | bytes 3080 | tf_op jit(solution)/shard_map/ppermute | solution.py:18
  13.0 22.4 %collective-permute-start.1 = (s32[256]{0:T(256)}, s32[256]{0:T(256)S(1)}, u32[]{:S(2)}, u32[]{:S(2)}) collective-permute-start(s32[256]{0:T(256)} %param.11), channel_id=1, source_target_pairs={{0,56},{8,64},{16,72},{24,80},{32,88},{40,96},{48,104},{56,112},{6... | collective-permute-start | bytes 3080 | tf_op jit(solution)/shard_map/ppermute | solution.py:18
  16.7 21.5 %collective-permute-start.2 = (s32[256]{0:T(256)}, s32[256]{0:T(256)S(1)}, u32[]{:S(2)}, u32[]{:S(2)}) collective-permute-start(s32[256]{0:T(256)} %param.11), channel_id=1, source_target_pairs={{0,48},{8,56},{16,64},{24,72},{32,80},{40,88},{48,96},{56,104},{64... | collective-permute-start | bytes 3080 | tf_op jit(solution)/shard_map/ppermute | solution.py:18
  20.9 20.7 %collective-permute-start.3 = (s32[256]{0:T(256)}, s32[256]{0:T(256)S(1)}, u32[]{:S(2)}, u32[]{:S(2)}) collective-permute-start(s32[256]{0:T(256)} %param.11), channel_id=1, source_target_pairs={{0,40},{8,48},{16,56},{24,64},{32,72},{40,80},{48,88},{56,96},{64,... | collective-permute-start | bytes 3080 | tf_op jit(solution)/shard_map/ppermute | solution.py:18
  27.3 14.3 %collective-permute-start.4 = (s32[256]{0:T(256)}, s32[256]{0:T(256)S(1)}, u32[]{:S(2)}, u32[]{:S(2)}) collective-permute-start(s32[256]{0:T(256)} %param.11), channel_id=1, source_target_pairs={{0,32},{8,40},{16,48},{24,56},{32,64},{40,72},{48,80},{56,88},{64,... | collective-permute-start | bytes 3080 | tf_op jit(solution)/shard_map/ppermute | solution.py:18
  31.8 9.8 %collective-permute-start.5 = (s32[256]{0:T(256)}, s32[256]{0:T(256)S(1)}, u32[]{:S(2)}, u32[]{:S(2)}) collective-permute-start(s32[256]{0:T(256)} %param.11), channel_id=1, source_target_pairs={{0,24},{8,32},{16,40},{24,48},{32,56},{40,64},{48,72},{56,80},{64,... | collective-permute-start | bytes 3080 | tf_op jit(solution)/shard_map/ppermute | solution.py:18
  35.3 6.3 %collective-permute-start.6 = (s32[256]{0:T(256)}, s32[256]{0:T(256)S(1)}, u32[]{:S(2)}, u32[]{:S(2)}) collective-permute-start(s32[256]{0:T(256)} %param.11), channel_id=1, source_target_pairs={{0,16},{8,24},{16,32},{24,40},{32,48},{40,56},{48,64},{56,72},{64,... | collective-permute-start | bytes 3080 | tf_op jit(solution)/shard_map/ppermute | solution.py:18
  38.1 5.1 %collective-permute-start.7 = (s32[256]{0:T(256)}, s32[256]{0:T(256)S(1)}, u32[]{:S(2)}, u32[]{:S(2)}) collective-permute-start(s32[256]{0:T(256)} %param.11), channel_id=1, source_target_pairs={{0,8},{8,16},{16,24},{24,32},{32,40},{40,48},{48,56},{56,64},{64,7... | collective-permute-start | bytes 3080 | tf_op jit(solution)/shard_map/ppermute | solution.py:18
  48.8 35.7 %all-to-all-start = ((bf16[8,256,256]{1,2,0:T(8,128)(2,1)}), bf16[8,256,256]{1,2,0:T(8,128)(2,1)S(1)}, u32[]{:S(2)}, u32[]{:S(2)}) async-start(bf16[8,256,256]{1,2,0:T(8,128)(2,1)} %broadcast_in_dim.38), calls=%async_computation | async-start | bytes 2097152 | tf_op jit(solution)/shard_map/all_to_all | solution.py:25
  55.9 173.5 %all-gather.5.cloned.1.call-start = ((), (), s32[]{:S(2)}) async-start(), calls=%async_computation.5 | async-start | bytes 6389760 | tf_op jit(solution)/shard_map/all_gather | solution.py:76
  104.5 13.1 %collective-permute-start.9 = (bf16[2,256,256]{2,1,0:T(8,128)(2,1)S(1)}, bf16[2,256,256]{2,1,0:T(8,128)(2,1)S(1)}, u32[]{:S(2)}, u32[]{:S(2)}) collective-permute-start(bf16[2,256,256]{2,1,0:T(8,128)(2,1)S(1)} %fusion.38), channel_id=1, source_target_pairs={{0,16},{8,24},{16,32},{24,40},{32,48},{40,56},{48,64},{56,72},{64,... | collective-permute-start | bytes 786440 | tf_op jit(solution)/shard_map/ppermute | solution.py:18
  108.0 15.6 %collective-permute-start.10 = (bf16[2,256,256]{2,1,0:T(8,128)(2,1)S(1)}, bf16[2,256,256]{2,1,0:T(8,128)(2,1)S(1)}, u32[]{:S(2)}, u32[]{:S(2)}) collective-permute-start(bf16[2,256,256]{2,1,0:T(8,128)(2,1)S(1)} %fusion.38), channel_id=1, source_target_pairs={{0,32},{8,40},{16,48},{24,56},{32,64},{40,72},{48,80},{56,88},{64,... | collective-permute-start | bytes 786440 | tf_op jit(solution)/shard_map/ppermute | solution.py:18
  111.4 19.1 %collective-permute-start.11 = (bf16[2,256,256]{2,1,0:T(8,128)(2,1)S(1)}, bf16[2,256,256]{2,1,0:T(8,128)(2,1)S(1)}, u32[]{:S(2)}, u32[]{:S(2)}) collective-permute-start(bf16[2,256,256]{2,1,0:T(8,128)(2,1)S(1)} %fusion.38), channel_id=1, source_target_pairs={{0,48},{8,56},{16,64},{24,72},{32,80},{40,88},{48,96},{56,104},{64... | collective-permute-start | bytes 786440 | tf_op jit(solution)/shard_map/ppermute | solution.py:18
  114.0 22.6 %collective-permute-start.8 = (bf16[2,256,256]{2,1,0:T(8,128)(2,1)S(1)}, bf16[2,256,256]{2,1,0:T(8,128)(2,1)S(1)}, u32[]{:S(2)}, u32[]{:S(2)}) collective-permute-start(bf16[2,256,256]{2,1,0:T(8,128)(2,1)S(1)} %fusion.38), channel_id=1, source_target_pairs={{0,64},{8,72},{16,80},{24,88},{32,96},{40,104},{48,112},{56,120},{... | collective-permute-start | bytes 786440 | tf_op jit(solution)/shard_map/ppermute | solution.py:18
  138.0 5.1 %collective-permute-start.12 = (bf16[5,2,256,256]{3,2,1,0:T(8,128)(2,1)}, bf16[5,2,256,256]{3,2,1,0:T(8,128)(2,1)S(1)}, u32[]{:S(2)}, u32[]{:S(2)}) collective-permute-start(bf16[5,2,256,256]{3,2,1,0:T(8,128)(2,1)} %bitcast_dynamic-update-slice_fusion), channel_id=1, source_target_pairs={{0,8},{8,0},{16,24},{24,16},{32,40},{40,32},{48,56},{56,48},{64,72... | collective-permute-start | bytes 3932168 | tf_op jit(solution)/shard_map/ppermute | solution.py:130
  140.1 9.9 %copy-start.1 = (pred[256,2560]{1,0:T(8,128)(4,1)S(1)}, pred[256,2560]{1,0:T(8,128)(4,1)}, u32[]{:S(2)}) copy-start(pred[256,2560]{1,0:T(8,128)(4,1)} %compare_and_fusion) | copy-start | bytes 1966084
  162.0 35.9 %copy-start.2 = (bf16[256,256]{1,0:T(8,128)(2,1)S(1)}, bf16[256,256]{1,0:T(8,128)(2,1)}, u32[]{:S(2)}) copy-start(bf16[256,256]{1,0:T(8,128)(2,1)} %param.10) | copy-start | bytes 393220
  235.3 4.6 %copy-start.6 = (s32[16]{0:T(128)S(1)}, s32[16]{0:T(128)}, u32[]{:S(2)}) copy-start(s32[16]{0:T(128)} %param.12) | copy-start | bytes 196
  236.4 29.8 %all-to-all-start.3 = ((bf16[8,256,256]{2,1,0:T(8,128)(2,1)}), bf16[8,256,256]{2,1,0:T(8,128)(2,1)S(1)}, u32[]{:S(2)}, u32[]{:S(2)}) async-start(bf16[8,256,256]{2,1,0:T(8,128)(2,1)} %bitcast.88), calls=%async_computation.3 | async-start | bytes 2097152 | tf_op jit(solution)/shard_map/all_to_all | solution.py:34
  241.5 25.5 %copy-start = (bf16[2,16,16,256]{3,2,1,0:T(8,128)(2,1)}, bf16[2,16,16,256]{3,2,1,0:T(8,128)(2,1)S(1)}, u32[]{:S(2)}) copy-start(bf16[2,16,16,256]{3,2,1,0:T(8,128)(2,1)S(1)} %scatter_fusion) | copy-start | bytes 786436
Sparse Core Ops, SparseCore 0:
  12.0 88.6 all-gather.2
  104.6 88.5 all-gather.4

commit v12 on v11

--- a/solution.py
+++ b/solution.py
@@ -98,10 +98,14 @@
     pairs_per_chip = 2
     chips_back = REACH // pairs_per_chip
     partner_rank = wide_rank ^ 1
-    block_ids = []
-    for step in range(chips_back, 0, -1):
+    first_core = (wide_rank % pairs_per_chip) == 0
+    block_ids = [
+        wide_rank - pairs_per_chip * chips_back,
+        jnp.where(first_core, partner_rank - pairs_per_chip * chips_back, partner_rank),
+    ]
+    for step in range(chips_back - 1, 0, -1):
         block_ids += [wide_rank - pairs_per_chip * step, partner_rank - pairs_per_chip * step]
-    block_ids += [partner_rank, wide_rank]
+    block_ids += [wide_rank]
     key_index = (
         jnp.stack(block_ids)[:, None] * tok_rows + local_index[None, :]
     ).reshape(-1)
@@ -130,10 +134,10 @@
     partner = lax.ppermute(
         jnp.stack(line + [packed], axis=0), "wide", [(i, i ^ 1) for i in range(count)]
     )
-    order = []
-    for step in range(chips_back, 0, -1):
+    order = [line[chips_back - 1], jnp.where(first_core, partner[chips_back - 1], partner[chips_back])]
+    for step in range(chips_back - 1, 0, -1):
         order += [line[step - 1], partner[step - 1]]
-    order += [partner[chips_back], packed]
+    order += [packed]
     kv_all = jnp.concatenate(order, axis=-1)
     score_scale = HEAD_DIM ** (-0.5)
     key_all = kv_all[:, :HEAD_DIM, :]

time: 275 us -> 273 us (level)
    unnamed x27 -> x25, local copies, waits for them, and re-layouts: 9.78 us -> 8.17 us
  transfers between devices with their start and end apart: 17 -> 17, of which waited for: 8 -> 8; matrix products, arithmetic and copies ran while one was open for 14% -> 13% of each run, Pallas kernels for 0% -> 0%
where the time goes in v12:
time: 273 us; the launch traced here: 272 us
  waiting for transfers between devices  88.1 us (32%)
  blocking collectives  65.9 us (24%)
  starting transfers between devices  58.3 us (21%)
  matrix products  20.6 us (8%)
  between operations  14.6 us (5%)
  local copies, waits for them, and re-layouts  14.1 us (5%)
  other arithmetic  10.4 us (4%)
    ppermute x12, starting transfers between devices, shifted(): lax.ppermute(value, axis, [(source, source + steps) for source in range(f...  45.7 us
    all_to_all x1, blocking collectives, swap_sum(): got = lax.all_to_all(pieces, axis, 0, 0, tiled=True)  35.6 us
    all_to_all x1, blocking collectives, swap_gather(): got = lax.all_to_all(copies, axis, 0, 0, tiled=True)  30.3 us
    all_to_all x1, waiting for transfers between devices, swap_gather(): got = lax.all_to_all(copies, axis, 0, 0, tiled=True)  27.5 us
    all_to_all x1, waiting for transfers between devices, swap_sum(): got = lax.all_to_all(pieces, axis, 0, 0, tiled=True)  24.6 us
    ppermute x12, waiting for transfers between devices, shifted(): lax.ppermute(value, axis, [(source, source + steps) for source in range(f...  18.3 us
    all_gather x1, waiting for transfers between devices, per_device(): lax.all_gather(jnp.concatenate(attn_pieces, axis=1), 'wide', axis=0, tile...  15.4 us
    unnamed x25, local copies, waits for them, and re-layouts  8.17 us
  transfers between devices with their start and end apart: 17, of which 8 were waited for; matrix products, arithmetic and copies ran while one was open for 13% of the time, Pallas kernels for 0%

profile of v12, /device:TPU:6, one launch (start us, length us, event | category | flops | bytes accessed | tf_op | source)
XLA Modules:
  0.0 272.1 jit_solution(8196959645296494412)
XLA Ops:
  7.2 1.4 pad_maximum_fusion.2
  8.7 4.3 %collective-permute-start = (s32[256]{0:T(256)}, s32[256]{0:T(256)S(1)}, u32[]{:S(2)}, u32[]{:S(2)}) collective-permute-start(s32[256]{0:T(256)} %param.11), channel_id=1, source_target_pairs={{0,64},{8,72},{16,80},{24,88},{32,96},{40,104},{48,112},{56,120},{... | collective-permute-start | bytes 3080 | tf_op jit(solution)/shard_map/ppermute | solution.py:18
  13.0 3.7 %collective-permute-start.1 = (s32[256]{0:T(256)}, s32[256]{0:T(256)S(1)}, u32[]{:S(2)}, u32[]{:S(2)}) collective-permute-start(s32[256]{0:T(256)} %param.11), channel_id=1, source_target_pairs={{0,56},{8,64},{16,72},{24,80},{32,88},{40,96},{48,104},{56,112},{6... | collective-permute-start | bytes 3080 | tf_op jit(solution)/shard_map/ppermute | solution.py:18
  16.7 4.3 %collective-permute-start.2 = (s32[256]{0:T(256)}, s32[256]{0:T(256)S(1)}, u32[]{:S(2)}, u32[]{:S(2)}) collective-permute-start(s32[256]{0:T(256)} %param.11), channel_id=1, source_target_pairs={{0,48},{8,56},{16,64},{24,72},{32,80},{40,88},{48,96},{56,104},{64... | collective-permute-start | bytes 3080 | tf_op jit(solution)/shard_map/ppermute | solution.py:18
  20.9 6.4 %collective-permute-start.3 = (s32[256]{0:T(256)}, s32[256]{0:T(256)S(1)}, u32[]{:S(2)}, u32[]{:S(2)}) collective-permute-start(s32[256]{0:T(256)} %param.11), channel_id=1, source_target_pairs={{0,40},{8,48},{16,56},{24,64},{32,72},{40,80},{48,88},{56,96},{64,... | collective-permute-start | bytes 3080 | tf_op jit(solution)/shard_map/ppermute | solution.py:18
  27.3 4.3 %collective-permute-start.4 = (s32[256]{0:T(256)}, s32[256]{0:T(256)S(1)}, u32[]{:S(2)}, u32[]{:S(2)}) collective-permute-start(s32[256]{0:T(256)} %param.11), channel_id=1, source_target_pairs={{0,32},{8,40},{16,48},{24,56},{32,64},{40,72},{48,80},{56,88},{64,... | collective-permute-start | bytes 3080 | tf_op jit(solution)/shard_map/ppermute | solution.py:18
  31.9 3.5 %collective-permute-start.5 = (s32[256]{0:T(256)}, s32[256]{0:T(256)S(1)}, u32[]{:S(2)}, u32[]{:S(2)}) collective-permute-start(s32[256]{0:T(256)} %param.11), channel_id=1, source_target_pairs={{0,24},{8,32},{16,40},{24,48},{32,56},{40,64},{48,72},{56,80},{64,... | collective-permute-start | bytes 3080 | tf_op jit(solution)/shard_map/ppermute | solution.py:18
  35.4 2.8 %collective-permute-start.6 = (s32[256]{0:T(256)}, s32[256]{0:T(256)S(1)}, u32[]{:S(2)}, u32[]{:S(2)}) collective-permute-start(s32[256]{0:T(256)} %param.11), channel_id=1, source_target_pairs={{0,16},{8,24},{16,32},{24,40},{32,48},{40,56},{48,64},{56,72},{64,... | collective-permute-start | bytes 3080 | tf_op jit(solution)/shard_map/ppermute | solution.py:18
  38.2 3.4 %collective-permute-start.7 = (s32[256]{0:T(256)}, s32[256]{0:T(256)S(1)}, u32[]{:S(2)}, u32[]{:S(2)}) collective-permute-start(s32[256]{0:T(256)} %param.11), channel_id=1, source_target_pairs={{0,8},{8,16},{16,24},{24,32},{32,40},{40,48},{48,56},{56,64},{64,7... | collective-permute-start | bytes 3080 | tf_op jit(solution)/shard_map/ppermute | solution.py:18
  41.7 1.5 collective-permute-done.7
  48.7 7.1 %all-to-all-start = ((bf16[8,256,256]{1,2,0:T(8,128)(2,1)}), bf16[8,256,256]{1,2,0:T(8,128)(2,1)S(1)}, u32[]{:S(2)}, u32[]{:S(2)}) async-start(bf16[8,256,256]{1,2,0:T(8,128)(2,1)} %broadcast_in_dim.38), calls=%async_computation | async-start | bytes 2097152 | tf_op jit(solution)/shard_map/all_to_all | solution.py:25
  56.9 27.5 %all-to-all-done = bf16[8,256,256]{1,2,0:T(8,128)(2,1)S(1)} async-done(((bf16[8,256,256]{1,2,0:T(8,128)(2,1)}), bf16[8,256,256]{1,2,0:T(8,128)(2,1)S(1)}, u32[]{:S(2)}, u32[]{:S(2)}) %all-to-all-start) | async-done | bytes 1048608 | tf_op jit(solution)/shard_map/all_to_all | solution.py:25
  85.3 15.4 %all-gather.3.cloned.1.call-done = bf16[2048,1024]{1,0:T(8,128)(2,1)} async-done(((bf16[32,1024]{1,0:T(8,128)(2,1)}), bf16[2048,1024]{1,0:T(8,128)(2,1)}) %all-gather.3.cloned.1.call-update) | async-done | bytes 4194320 | tf_op jit(solution)/shard_map/all_gather | solution.py:81
  100.7 3.5 %fusion.55 = f32[256,1024]{1,0:T(8,128)S(1)} fusion(bf16[256,2048]{0,1:T(8,128)(2,1)S(1)} %fusion.15, bf16[2048,1024]{1,0:T(8,128)(2,1)} %all-gather.3.cloned.1.call-done), kind=kOutput, calls=%fused_computation.108 | convolution fusion | flops 1073741824 | bytes 6291456 | tf_op jit(solution)/shard_map/dot_general | solution.py:64
  104.6 3.5 %collective-permute-start.9 = (bf16[2,256,256]{2,1,0:T(8,128)(2,1)S(1)}, bf16[2,256,256]{2,1,0:T(8,128)(2,1)S(1)}, u32[]{:S(2)}, u32[]{:S(2)}) collective-permute-start(bf16[2,256,256]{2,1,0:T(8,128)(2,1)S(1)} %fusion.41), channel_id=1, source_target_pairs={{0,16},{8,24},{16,32},{24,40},{32,48},{40,56},{48,64},{56,72},{64,... | collective-permute-start | bytes 786440 | tf_op jit(solution)/shard_map/ppermute | solution.py:18
  108.1 3.4 %collective-permute-start.10 = (bf16[2,256,256]{2,1,0:T(8,128)(2,1)S(1)}, bf16[2,256,256]{2,1,0:T(8,128)(2,1)S(1)}, u32[]{:S(2)}, u32[]{:S(2)}) collective-permute-start(bf16[2,256,256]{2,1,0:T(8,128)(2,1)S(1)} %fusion.41), channel_id=1, source_target_pairs={{0,32},{8,40},{16,48},{24,56},{32,64},{40,72},{48,80},{56,88},{64,... | collective-permute-start | bytes 786440 | tf_op jit(solution)/shard_map/ppermute | solution.py:18
  111.4 2.5 collective-permute-start.11
  114.0 3.7 %collective-permute-start.8 = (bf16[2,256,256]{2,1,0:T(8,128)(2,1)S(1)}, bf16[2,256,256]{2,1,0:T(8,128)(2,1)S(1)}, u32[]{:S(2)}, u32[]{:S(2)}) collective-permute-start(bf16[2,256,256]{2,1,0:T(8,128)(2,1)S(1)} %fusion.41), channel_id=1, source_target_pairs={{0,64},{8,72},{16,80},{24,88},{32,96},{40,104},{48,112},{56,120},{... | collective-permute-start | bytes 786440 | tf_op jit(solution)/shard_map/ppermute | solution.py:18
  118.4 5.3 %collective-permute-done.10 = bf16[2,256,256]{2,1,0:T(8,128)(2,1)S(1)} collective-permute-done((bf16[2,256,256]{2,1,0:T(8,128)(2,1)S(1)}, bf16[2,256,256]{2,1,0:T(8,128)(2,1)S(1)}, u32[]{:S(2)}, u32[]{:S(2)}) %collective-permute-start.10) | collective-permute-done | bytes 262176 | tf_op jit(solution)/shard_map/ppermute | solution.py:18
  124.4 6.1 %collective-permute-done.11 = bf16[2,256,256]{2,1,0:T(8,128)(2,1)S(1)} collective-permute-done((bf16[2,256,256]{2,1,0:T(8,128)(2,1)S(1)}, bf16[2,256,256]{2,1,0:T(8,128)(2,1)S(1)}, u32[]{:S(2)}, u32[]{:S(2)}) %collective-permute-start.11) | collective-permute-done | bytes 262176 | tf_op jit(solution)/shard_map/ppermute | solution.py:18
  131.3 5.3 %collective-permute-done.8 = bf16[2,256,256]{2,1,0:T(8,128)(2,1)S(1)} collective-permute-done((bf16[2,256,256]{2,1,0:T(8,128)(2,1)S(1)}, bf16[2,256,256]{2,1,0:T(8,128)(2,1)S(1)}, u32[]{:S(2)}, u32[]{:S(2)}) %collective-permute-start.8) | collective-permute-done | bytes 262176 | tf_op jit(solution)/shard_map/ppermute | solution.py:18
  138.0 1.9 collective-permute-start.12
  140.9 2.2 collective-permute-done.12
  149.2 5.8 %fusion.50 = (f32[2,256]{1,0:T(2,128)S(1)}, f32[2,256,2304]{2,1,0:T(8,128)}) fusion(pred[256,2304]{1,0:T(8,128)(4,1)S(1)} %copy-done.1, bf16[2,256,2304]{2,1,0:T(8,128)(2,1)} %constant_dynamic-update-slice_fusion.1, bf16[256,2,64]{0,2,1:T(8,128)(2,1)S(1)} %get-tuple-element.9, bf16[256,2,64]{0,2,1:T(8,128)(2,1)S(1)} %get-tuple-element.8), kind=kOutput, calls=%fused_computation.107 | convolution fusion | flops 308152576 | bytes 7211008 | tf_op jit(solution)/shard_map/sub | solution.py:151
  155.0 3.7 %fusion.26 = bf16[2,128,256]{2,1,0:T(8,128)(2,1)S(1)} fusion(f32[2,256,2304]{2,1,0:T(8,128)} %get-tuple-element.17, f32[2,256]{1,0:T(2,128)S(1)} %get-tuple-element.16, bf16[2,256,2304]{2,1,0:T(8,128)(2,1)} %constant_dynamic-update-slice_fusion.1), kind=kOutput, calls=%fused_computation.34 | convolution fusion | flops 304414720 | bytes 6031360 | tf_op jit(solution)/shard_map/hqk,hdk->qhd/dot_general | solution.py:153
  158.7 1.7 convolution_convert_fusion.1
  160.5 35.6 %all_to_all.20 = bf16[8,256,256]{2,1,0:T(8,128)(2,1)S(1)} all-to-all(bf16[8,256,256]{2,1,0:T(8,128)(2,1)S(1)} %bitcast.87), channel_id=1, replica_groups=mesh['wide'=64,'narrow'=8] {'narrow'}, dimensions={0} | all-to-all | bytes 2097152 | tf_op jit(solution)/shard_map/all_to_all | solution.py:34
  196.5 30.3 %all_to_all.21 = bf16[8,256,256]{1,2,0:T(8,128)(2,1)S(1)} all-to-all(bf16[8,256,256]{1,2,0:T(8,128)(2,1)S(1)} %broadcast_in_dim.42), channel_id=1, replica_groups=mesh['wide'=64,'narrow'=8] {'narrow'}, dimensions={0} | all-to-all | bytes 2097152 | tf_op jit(solution)/shard_map/all_to_all | solution.py:25
  227.7 2.3 fusion.10
  230.1 3.6 %convolution_convert_fusion = bf16[256,2048]{1,0:T(8,128)(2,1)S(1)} fusion(bf16[2048,1536]{1,0:T(8,128)(2,1)} %all-gather.5.cloned.1.call-done, bf16[256,2048]{0,1:T(8,128)(2,1)S(1)} %fusion.13, f32[256,512]{1,0:T(8,128)S(1)} %fusion.10), kind=kOutput, calls=%fused_computation.8 | convolution fusion | flops 1075052544 | bytes 6815744 | tf_op jit(solution)/shard_map/dot_general | solution.py:166
  234.7 3.6 %all-to-all-start.3 = ((bf16[8,256,256]{2,1,0:T(8,128)(2,1)}), bf16[8,256,256]{2,1,0:T(8,128)(2,1)S(1)}, u32[]{:S(2)}, u32[]{:S(2)}) async-start(bf16[8,256,256]{2,1,0:T(8,128)(2,1)} %bitcast.83), calls=%async_computation.3 | async-start | bytes 2097152 | tf_op jit(solution)/shard_map/all_to_all | solution.py:34
  239.8 24.6 %all-to-all-done.3 = bf16[8,256,256]{2,1,0:T(8,128)(2,1)S(1)} async-done(((bf16[8,256,256]{2,1,0:T(8,128)(2,1)}), bf16[8,256,256]{2,1,0:T(8,128)(2,1)S(1)}, u32[]{:S(2)}, u32[]{:S(2)}) %all-to-all-start.3) | async-done | bytes 1048608 | tf_op jit(solution)/shard_map/all_to_all | solution.py:34
  (98 shorter events, 23.3 us)
Async XLA Ops:
  7.2 48.7 %copy-start.3 = (bf16[512,32]{0,1:T(8,128)(2,1)S(1)}, bf16[512,32]{0,1:T(8,128)(2,1)}, u32[]{:S(2)}) copy-start(bf16[512,32]{0,1:T(8,128)(2,1)} %param.19) | copy-start | bytes 98308
  7.2 48.7 %copy-start.5 = (bf16[32,512]{1,0:T(8,128)(2,1)S(1)}, bf16[32,512]{1,0:T(8,128)(2,1)}, u32[]{:S(2)}) copy-start(bf16[32,512]{1,0:T(8,128)(2,1)} %param.17) | copy-start | bytes 98308
  7.2 48.7 %copy-start.4 = (bf16[32,512]{1,0:T(8,128)(2,1)S(1)}, bf16[32,512]{1,0:T(8,128)(2,1)}, u32[]{:S(2)}) copy-start(bf16[32,512]{1,0:T(8,128)(2,1)} %param.18) | copy-start | bytes 98308
  7.2 93.5 %all-gather.3.cloned.1.call-start = ((), (), s32[]{:S(2)}) async-start(), calls=%async_computation.4 | async-start | bytes 4259840 | tf_op jit(solution)/shard_map/all_gather | solution.py:81
  8.7 23.2 %collective-permute-start = (s32[256]{0:T(256)}, s32[256]{0:T(256)S(1)}, u32[]{:S(2)}, u32[]{:S(2)}) collective-permute-start(s32[256]{0:T(256)} %param.11), channel_id=1, source_target_pairs={{0,64},{8,72},{16,80},{24,88},{32,96},{40,104},{48,112},{56,120},{... | collective-permute-start | bytes 3080 | tf_op jit(solution)/shard_map/ppermute | solution.py:18
  13.0 22.4 %collective-permute-start.1 = (s32[256]{0:T(256)}, s32[256]{0:T(256)S(1)}, u32[]{:S(2)}, u32[]{:S(2)}) collective-permute-start(s32[256]{0:T(256)} %param.11), channel_id=1, source_target_pairs={{0,56},{8,64},{16,72},{24,80},{32,88},{40,96},{48,104},{56,112},{6... | collective-permute-start | bytes 3080 | tf_op jit(solution)/shard_map/ppermute | solution.py:18
  16.7 21.5 %collective-permute-start.2 = (s32[256]{0:T(256)}, s32[256]{0:T(256)S(1)}, u32[]{:S(2)}, u32[]{:S(2)}) collective-permute-start(s32[256]{0:T(256)} %param.11), channel_id=1, source_target_pairs={{0,48},{8,56},{16,64},{24,72},{32,80},{40,88},{48,96},{56,104},{64... | collective-permute-start | bytes 3080 | tf_op jit(solution)/shard_map/ppermute | solution.py:18
  20.9 20.7 %collective-permute-start.3 = (s32[256]{0:T(256)}, s32[256]{0:T(256)S(1)}, u32[]{:S(2)}, u32[]{:S(2)}) collective-permute-start(s32[256]{0:T(256)} %param.11), channel_id=1, source_target_pairs={{0,40},{8,48},{16,56},{24,64},{32,72},{40,80},{48,88},{56,96},{64,... | collective-permute-start | bytes 3080 | tf_op jit(solution)/shard_map/ppermute | solution.py:18
  27.3 14.4 %collective-permute-start.4 = (s32[256]{0:T(256)}, s32[256]{0:T(256)S(1)}, u32[]{:S(2)}, u32[]{:S(2)}) collective-permute-start(s32[256]{0:T(256)} %param.11), channel_id=1, source_target_pairs={{0,32},{8,40},{16,48},{24,56},{32,64},{40,72},{48,80},{56,88},{64,... | collective-permute-start | bytes 3080 | tf_op jit(solution)/shard_map/ppermute | solution.py:18
  31.9 9.8 %collective-permute-start.5 = (s32[256]{0:T(256)}, s32[256]{0:T(256)S(1)}, u32[]{:S(2)}, u32[]{:S(2)}) collective-permute-start(s32[256]{0:T(256)} %param.11), channel_id=1, source_target_pairs={{0,24},{8,32},{16,40},{24,48},{32,56},{40,64},{48,72},{56,80},{64,... | collective-permute-start | bytes 3080 | tf_op jit(solution)/shard_map/ppermute | solution.py:18
  35.4 6.3 %collective-permute-start.6 = (s32[256]{0:T(256)}, s32[256]{0:T(256)S(1)}, u32[]{:S(2)}, u32[]{:S(2)}) collective-permute-start(s32[256]{0:T(256)} %param.11), channel_id=1, source_target_pairs={{0,16},{8,24},{16,32},{24,40},{32,48},{40,56},{48,64},{56,72},{64,... | collective-permute-start | bytes 3080 | tf_op jit(solution)/shard_map/ppermute | solution.py:18
  38.2 5.1 %collective-permute-start.7 = (s32[256]{0:T(256)}, s32[256]{0:T(256)S(1)}, u32[]{:S(2)}, u32[]{:S(2)}) collective-permute-start(s32[256]{0:T(256)} %param.11), channel_id=1, source_target_pairs={{0,8},{8,16},{16,24},{24,32},{32,40},{40,48},{48,56},{56,64},{64,7... | collective-permute-start | bytes 3080 | tf_op jit(solution)/shard_map/ppermute | solution.py:18
  48.7 35.7 %all-to-all-start = ((bf16[8,256,256]{1,2,0:T(8,128)(2,1)}), bf16[8,256,256]{1,2,0:T(8,128)(2,1)S(1)}, u32[]{:S(2)}, u32[]{:S(2)}) async-start(bf16[8,256,256]{1,2,0:T(8,128)(2,1)} %broadcast_in_dim.38), calls=%async_computation | async-start | bytes 2097152 | tf_op jit(solution)/shard_map/all_to_all | solution.py:25
  55.8 172.0 %all-gather.5.cloned.1.call-start = ((), (), s32[]{:S(2)}) async-start(), calls=%async_computation.5 | async-start | bytes 6389760 | tf_op jit(solution)/shard_map/all_gather | solution.py:76
  104.6 13.1 %collective-permute-start.9 = (bf16[2,256,256]{2,1,0:T(8,128)(2,1)S(1)}, bf16[2,256,256]{2,1,0:T(8,128)(2,1)S(1)}, u32[]{:S(2)}, u32[]{:S(2)}) collective-permute-start(bf16[2,256,256]{2,1,0:T(8,128)(2,1)S(1)} %fusion.41), channel_id=1, source_target_pairs={{0,16},{8,24},{16,32},{24,40},{32,48},{40,56},{48,64},{56,72},{64,... | collective-permute-start | bytes 786440 | tf_op jit(solution)/shard_map/ppermute | solution.py:18
  108.1 15.6 %collective-permute-start.10 = (bf16[2,256,256]{2,1,0:T(8,128)(2,1)S(1)}, bf16[2,256,256]{2,1,0:T(8,128)(2,1)S(1)}, u32[]{:S(2)}, u32[]{:S(2)}) collective-permute-start(bf16[2,256,256]{2,1,0:T(8,128)(2,1)S(1)} %fusion.41), channel_id=1, source_target_pairs={{0,32},{8,40},{16,48},{24,56},{32,64},{40,72},{48,80},{56,88},{64,... | collective-permute-start | bytes 786440 | tf_op jit(solution)/shard_map/ppermute | solution.py:18
  111.4 19.1 %collective-permute-start.11 = (bf16[2,256,256]{2,1,0:T(8,128)(2,1)S(1)}, bf16[2,256,256]{2,1,0:T(8,128)(2,1)S(1)}, u32[]{:S(2)}, u32[]{:S(2)}) collective-permute-start(bf16[2,256,256]{2,1,0:T(8,128)(2,1)S(1)} %fusion.41), channel_id=1, source_target_pairs={{0,48},{8,56},{16,64},{24,72},{32,80},{40,88},{48,96},{56,104},{64... | collective-permute-start | bytes 786440 | tf_op jit(solution)/shard_map/ppermute | solution.py:18
  114.0 22.6 %collective-permute-start.8 = (bf16[2,256,256]{2,1,0:T(8,128)(2,1)S(1)}, bf16[2,256,256]{2,1,0:T(8,128)(2,1)S(1)}, u32[]{:S(2)}, u32[]{:S(2)}) collective-permute-start(bf16[2,256,256]{2,1,0:T(8,128)(2,1)S(1)} %fusion.41), channel_id=1, source_target_pairs={{0,64},{8,72},{16,80},{24,88},{32,96},{40,104},{48,112},{56,120},{... | collective-permute-start | bytes 786440 | tf_op jit(solution)/shard_map/ppermute | solution.py:18
  138.0 5.1 %collective-permute-start.12 = (bf16[5,2,256,256]{3,2,1,0:T(8,128)(2,1)}, bf16[5,2,256,256]{3,2,1,0:T(8,128)(2,1)S(1)}, u32[]{:S(2)}, u32[]{:S(2)}) collective-permute-start(bf16[5,2,256,256]{3,2,1,0:T(8,128)(2,1)} %bitcast_dynamic-update-slice_fusion), channel_id=1, source_target_pairs={{0,8},{8,0},{16,24},{24,16},{32,40},{40,32},{48,56},{56,48},{64,72... | collective-permute-start | bytes 3932168 | tf_op jit(solution)/shard_map/ppermute | solution.py:134
  140.9 8.3 %copy-start.1 = (pred[256,2304]{1,0:T(8,128)(4,1)S(1)}, pred[256,2304]{1,0:T(8,128)(4,1)}, u32[]{:S(2)}) copy-start(pred[256,2304]{1,0:T(8,128)(4,1)} %compare_and_fusion) | copy-start | bytes 1769476
  160.5 35.8 %copy-start.2 = (bf16[256,256]{1,0:T(8,128)(2,1)S(1)}, bf16[256,256]{1,0:T(8,128)(2,1)}, u32[]{:S(2)}) copy-start(bf16[256,256]{1,0:T(8,128)(2,1)} %param.10) | copy-start | bytes 393220
  233.7 4.6 %copy-start.6 = (s32[16]{0:T(128)S(1)}, s32[16]{0:T(128)}, u32[]{:S(2)}) copy-start(s32[16]{0:T(128)} %param.12) | copy-start | bytes 196
  234.7 29.7 %all-to-all-start.3 = ((bf16[8,256,256]{2,1,0:T(8,128)(2,1)}), bf16[8,256,256]{2,1,0:T(8,128)(2,1)S(1)}, u32[]{:S(2)}, u32[]{:S(2)}) async-start(bf16[8,256,256]{2,1,0:T(8,128)(2,1)} %bitcast.83), calls=%async_computation.3 | async-start | bytes 2097152 | tf_op jit(solution)/shard_map/all_to_all | solution.py:34
  239.8 25.5 %copy-start = (bf16[2,16,16,256]{3,2,1,0:T(8,128)(2,1)}, bf16[2,16,16,256]{3,2,1,0:T(8,128)(2,1)S(1)}, u32[]{:S(2)}) copy-start(bf16[2,16,16,256]{3,2,1,0:T(8,128)(2,1)S(1)} %scatter_fusion) | copy-start | bytes 786436
Sparse Core Ops, SparseCore 0:
  12.0 88.6 all-gather.2
  104.6 88.5 all-gather.4

commit v13 on v12

--- a/solution.py
+++ b/solution.py
@@ -131,10 +131,9 @@
     packed = jnp.transpose(jnp.concatenate([keys_rot, values], axis=2), (1, 2, 0))
     line = [shifted(packed, "wide", pairs_per_chip * step) for step in range(1, chips_back + 1)]
     count = lax.axis_size("wide")
-    partner = lax.ppermute(
-        jnp.stack(line + [packed], axis=0), "wide", [(i, i ^ 1) for i in range(count)]
-    )
-    order = [line[chips_back - 1], jnp.where(first_core, partner[chips_back - 1], partner[chips_back])]
+    sent = line[:chips_back - 1] + [jnp.where(first_core, packed, line[chips_back - 1])]
+    partner = lax.ppermute(jnp.stack(sent, axis=0), "wide", [(i, i ^ 1) for i in range(count)])
+    order = [line[chips_back - 1], partner[chips_back - 1]]
     for step in range(chips_back - 1, 0, -1):
         order += [line[step - 1], partner[step - 1]]
     order += [packed]

time: 273 us -> 276 us (1.011)
    unnamed x25 -> x27, local copies, waits for them, and re-layouts: 8.17 us -> 7.01 us
where the time goes in v13:
time: 276 us; the launch traced here: 274 us
  waiting for transfers between devices  90 us (33%)
  blocking collectives  66.3 us (24%)
  starting transfers between devices  58.4 us (21%)
  matrix products  20.8 us (8%)
  between operations  14.7 us (5%)
  local copies, waits for them, and re-layouts  13 us (5%)
  other arithmetic  10.7 us (4%)
    ppermute x12, starting transfers between devices, shifted(): lax.ppermute(value, axis, [(source, source + steps) for source in range(f...  45.7 us
    all_to_all x1, blocking collectives, swap_sum(): got = lax.all_to_all(pieces, axis, 0, 0, tiled=True)  36.1 us
    all_to_all x1, blocking collectives, swap_gather(): got = lax.all_to_all(copies, axis, 0, 0, tiled=True)  30.2 us
    all_to_all x1, waiting for transfers between devices, swap_gather(): got = lax.all_to_all(copies, axis, 0, 0, tiled=True)  27.5 us
    all_to_all x1, waiting for transfers between devices, swap_sum(): got = lax.all_to_all(pieces, axis, 0, 0, tiled=True)  24.5 us
    ppermute x12, waiting for transfers between devices, shifted(): lax.ppermute(value, axis, [(source, source + steps) for source in range(f...  21 us
    all_gather x1, waiting for transfers between devices, per_device(): lax.all_gather(jnp.concatenate(attn_pieces, axis=1), 'wide', axis=0, tile...  15.4 us
    all_to_all x1, starting transfers between devices, swap_gather(): got = lax.all_to_all(copies, axis, 0, 0, tiled=True)  7.1 us
  transfers between devices with their start and end apart: 17, of which 8 were waited for; matrix products, arithmetic and copies ran while one was open for 13% of the time, Pallas kernels for 0%

profile of v13, /device:TPU:6, one launch (start us, length us, event | category | flops | bytes accessed | tf_op | source)
XLA Modules:
  0.0 273.9 jit_solution(16807549901051874719)
XLA Ops:
  8.7 4.3 %collective-permute-start = (s32[256]{0:T(256)}, s32[256]{0:T(256)S(1)}, u32[]{:S(2)}, u32[]{:S(2)}) collective-permute-start(s32[256]{0:T(256)} %param.11), channel_id=1, source_target_pairs={{0,64},{8,72},{16,80},{24,88},{32,96},{40,104},{48,112},{56,120},{... | collective-permute-start | bytes 3080 | tf_op jit(solution)/shard_map/ppermute | solution.py:18
  13.0 3.7 %collective-permute-start.1 = (s32[256]{0:T(256)}, s32[256]{0:T(256)S(1)}, u32[]{:S(2)}, u32[]{:S(2)}) collective-permute-start(s32[256]{0:T(256)} %param.11), channel_id=1, source_target_pairs={{0,56},{8,64},{16,72},{24,80},{32,88},{40,96},{48,104},{56,112},{6... | collective-permute-start | bytes 3080 | tf_op jit(solution)/shard_map/ppermute | solution.py:18
  16.7 4.3 %collective-permute-start.2 = (s32[256]{0:T(256)}, s32[256]{0:T(256)S(1)}, u32[]{:S(2)}, u32[]{:S(2)}) collective-permute-start(s32[256]{0:T(256)} %param.11), channel_id=1, source_target_pairs={{0,48},{8,56},{16,64},{24,72},{32,80},{40,88},{48,96},{56,104},{64... | collective-permute-start | bytes 3080 | tf_op jit(solution)/shard_map/ppermute | solution.py:18
  20.9 6.4 %collective-permute-start.3 = (s32[256]{0:T(256)}, s32[256]{0:T(256)S(1)}, u32[]{:S(2)}, u32[]{:S(2)}) collective-permute-start(s32[256]{0:T(256)} %param.11), channel_id=1, source_target_pairs={{0,40},{8,48},{16,56},{24,64},{32,72},{40,80},{48,88},{56,96},{64,... | collective-permute-start | bytes 3080 | tf_op jit(solution)/shard_map/ppermute | solution.py:18
  27.3 4.3 %collective-permute-start.4 = (s32[256]{0:T(256)}, s32[256]{0:T(256)S(1)}, u32[]{:S(2)}, u32[]{:S(2)}) collective-permute-start(s32[256]{0:T(256)} %param.11), channel_id=1, source_target_pairs={{0,32},{8,40},{16,48},{24,56},{32,64},{40,72},{48,80},{56,88},{64,... | collective-permute-start | bytes 3080 | tf_op jit(solution)/shard_map/ppermute | solution.py:18
  31.9 3.5 %collective-permute-start.5 = (s32[256]{0:T(256)}, s32[256]{0:T(256)S(1)}, u32[]{:S(2)}, u32[]{:S(2)}) collective-permute-start(s32[256]{0:T(256)} %param.11), channel_id=1, source_target_pairs={{0,24},{8,32},{16,40},{24,48},{32,56},{40,64},{48,72},{56,80},{64,... | collective-permute-start | bytes 3080 | tf_op jit(solution)/shard_map/ppermute | solution.py:18
  35.4 2.8 %collective-permute-start.6 = (s32[256]{0:T(256)}, s32[256]{0:T(256)S(1)}, u32[]{:S(2)}, u32[]{:S(2)}) collective-permute-start(s32[256]{0:T(256)} %param.11), channel_id=1, source_target_pairs={{0,16},{8,24},{16,32},{24,40},{32,48},{40,56},{48,64},{56,72},{64,... | collective-permute-start | bytes 3080 | tf_op jit(solution)/shard_map/ppermute | solution.py:18
  38.2 3.4 %collective-permute-start.7 = (s32[256]{0:T(256)}, s32[256]{0:T(256)S(1)}, u32[]{:S(2)}, u32[]{:S(2)}) collective-permute-start(s32[256]{0:T(256)} %param.11), channel_id=1, source_target_pairs={{0,8},{8,16},{16,24},{24,32},{32,40},{40,48},{48,56},{56,64},{64,7... | collective-permute-start | bytes 3080 | tf_op jit(solution)/shard_map/ppermute | solution.py:18
  41.7 1.5 collective-permute-done.7
  48.7 7.1 %all-to-all-start = ((bf16[8,256,256]{1,2,0:T(8,128)(2,1)}), bf16[8,256,256]{1,2,0:T(8,128)(2,1)S(1)}, u32[]{:S(2)}, u32[]{:S(2)}) async-start(bf16[8,256,256]{1,2,0:T(8,128)(2,1)} %broadcast_in_dim.38), calls=%async_computation | async-start | bytes 2097152 | tf_op jit(solution)/shard_map/all_to_all | solution.py:25
  56.9 27.5 %all-to-all-done = bf16[8,256,256]{1,2,0:T(8,128)(2,1)S(1)} async-done(((bf16[8,256,256]{1,2,0:T(8,128)(2,1)}), bf16[8,256,256]{1,2,0:T(8,128)(2,1)S(1)}, u32[]{:S(2)}, u32[]{:S(2)}) %all-to-all-start) | async-done | bytes 1048608 | tf_op jit(solution)/shard_map/all_to_all | solution.py:25
  85.3 15.4 %all-gather.3.cloned.1.call-done = bf16[2048,1024]{1,0:T(8,128)(2,1)} async-done(((bf16[32,1024]{1,0:T(8,128)(2,1)}), bf16[2048,1024]{1,0:T(8,128)(2,1)}) %all-gather.3.cloned.1.call-update) | async-done | bytes 4194320 | tf_op jit(solution)/shard_map/all_gather | solution.py:81
  100.7 3.5 %fusion.53 = f32[256,1024]{1,0:T(8,128)S(1)} fusion(bf16[256,2048]{0,1:T(8,128)(2,1)S(1)} %fusion.15, bf16[2048,1024]{1,0:T(8,128)(2,1)} %all-gather.3.cloned.1.call-done), kind=kOutput, calls=%fused_computation.103 | convolution fusion | flops 1073741824 | bytes 6291456 | tf_op jit(solution)/shard_map/dot_general | solution.py:64
  104.6 2.6 collective-permute-start.8
  107.2 4.6 %collective-permute-start.9 = (bf16[2,256,256]{2,1,0:T(8,128)(2,1)S(1)}, bf16[2,256,256]{2,1,0:T(8,128)(2,1)S(1)}, u32[]{:S(2)}, u32[]{:S(2)}) collective-permute-start(bf16[2,256,256]{2,1,0:T(8,128)(2,1)S(1)} %maximum_bitcast_fusion), channel_id=1, source_target_pairs={{0,16},{8,24},{16,32},{24,40},{32,48},{40,56},{48,64},{56,72},{64,... | collective-permute-start | bytes 786440 | tf_op jit(solution)/shard_map/ppermute | solution.py:18
  111.8 2.6 collective-permute-start.10
  114.3 3.4 %collective-permute-start.11 = (bf16[2,256,256]{2,1,0:T(8,128)(2,1)S(1)}, bf16[2,256,256]{2,1,0:T(8,128)(2,1)S(1)}, u32[]{:S(2)}, u32[]{:S(2)}) collective-permute-start(bf16[2,256,256]{2,1,0:T(8,128)(2,1)S(1)} %maximum_bitcast_fusion), channel_id=1, source_target_pairs={{0,48},{8,56},{16,64},{24,72},{32,80},{40,88},{48,96},{56,104},{64... | collective-permute-start | bytes 786440 | tf_op jit(solution)/shard_map/ppermute | solution.py:18
  118.5 4.7 %collective-permute-done.9 = bf16[2,256,256]{2,1,0:T(8,128)(2,1)S(1)} collective-permute-done((bf16[2,256,256]{2,1,0:T(8,128)(2,1)S(1)}, bf16[2,256,256]{2,1,0:T(8,128)(2,1)S(1)}, u32[]{:S(2)}, u32[]{:S(2)}) %collective-permute-start.9) | collective-permute-done | bytes 262176 | tf_op jit(solution)/shard_map/ppermute | solution.py:18
  123.2 8.8 %collective-permute-done.10 = bf16[2,256,256]{2,1,0:T(8,128)(2,1)S(1)} collective-permute-done((bf16[2,256,256]{2,1,0:T(8,128)(2,1)S(1)}, bf16[2,256,256]{2,1,0:T(8,128)(2,1)S(1)}, u32[]{:S(2)}, u32[]{:S(2)}) %collective-permute-start.10) | collective-permute-done | bytes 262176 | tf_op jit(solution)/shard_map/ppermute | solution.py:18
  132.1 5.9 %collective-permute-done.11 = bf16[2,256,256]{2,1,0:T(8,128)(2,1)S(1)} collective-permute-done((bf16[2,256,256]{2,1,0:T(8,128)(2,1)S(1)}, bf16[2,256,256]{2,1,0:T(8,128)(2,1)S(1)}, u32[]{:S(2)}, u32[]{:S(2)}) %collective-permute-start.11) | collective-permute-done | bytes 262176 | tf_op jit(solution)/shard_map/ppermute | solution.py:18
  138.8 1.9 collective-permute-start.12
  141.8 1.6 collective-permute-done.12
  144.1 1.7 constant_dynamic-update-slice_fusion.4
  150.4 6.3 %fusion.48 = (f32[2,256]{1,0:T(2,128)S(1)}, f32[2,256,2304]{2,1,0:T(8,128)}) fusion(pred[256,2304]{1,0:T(8,128)(4,1)} %compare_and_fusion, bf16[2,256,2304]{2,1,0:T(8,128)(2,1)} %constant_dynamic-update-slice_fusion.1, bf16[256,2,64]{0,2,1:T(8,128)(2,1)S(1)} %get-tuple-element.9, bf16[256,2,64]{0,2,1:T(8,128)(2,1)S(1)} %get-tuple-element.8), kind=kOutput, calls=%fused_computation.102 | convolution fusion | flops 308152576 | bytes 7211008 | tf_op jit(solution)/shard_map/sub | solution.py:150
  156.7 3.3 %fusion.26 = bf16[2,128,256]{2,1,0:T(8,128)(2,1)S(1)} fusion(f32[2,256,2304]{2,1,0:T(8,128)} %get-tuple-element.19, f32[2,256]{1,0:T(2,128)S(1)} %get-tuple-element.18, bf16[2,256,2304]{2,1,0:T(8,128)(2,1)S(1)} %copy-done.8), kind=kOutput, calls=%fused_computation.34 | convolution fusion | flops 304414720 | bytes 6031360 | tf_op jit(solution)/shard_map/hqk,hdk->qhd/dot_general | solution.py:152
  160.0 1.8 convolution_convert_fusion.1
  161.9 36.1 %all_to_all.20 = bf16[8,256,256]{2,1,0:T(8,128)(2,1)S(1)} all-to-all(bf16[8,256,256]{2,1,0:T(8,128)(2,1)S(1)} %bitcast.83), channel_id=1, replica_groups=mesh['wide'=64,'narrow'=8] {'narrow'}, dimensions={0} | all-to-all | bytes 2097152 | tf_op jit(solution)/shard_map/all_to_all | solution.py:34
  198.4 30.2 %all_to_all.21 = bf16[8,256,256]{1,2,0:T(8,128)(2,1)S(1)} all-to-all(bf16[8,256,256]{1,2,0:T(8,128)(2,1)S(1)} %broadcast_in_dim.42), channel_id=1, replica_groups=mesh['wide'=64,'narrow'=8] {'narrow'}, dimensions={0} | all-to-all | bytes 2097152 | tf_op jit(solution)/shard_map/all_to_all | solution.py:25
  229.5 2.3 fusion.10
  231.9 3.6 %convolution_convert_fusion = bf16[256,2048]{1,0:T(8,128)(2,1)S(1)} fusion(bf16[2048,1536]{1,0:T(8,128)(2,1)} %all-gather.5.cloned.1.call-done, bf16[256,2048]{0,1:T(8,128)(2,1)S(1)} %fusion.13, f32[256,512]{1,0:T(8,128)S(1)} %fusion.10), kind=kOutput, calls=%fused_computation.8 | convolution fusion | flops 1075052544 | bytes 6815744 | tf_op jit(solution)/shard_map/dot_general | solution.py:165
  236.5 3.6 %all-to-all-start.3 = ((bf16[8,256,256]{2,1,0:T(8,128)(2,1)}), bf16[8,256,256]{2,1,0:T(8,128)(2,1)S(1)}, u32[]{:S(2)}, u32[]{:S(2)}) async-start(bf16[8,256,256]{2,1,0:T(8,128)(2,1)} %bitcast.79), calls=%async_computation.3 | async-start | bytes 2097152 | tf_op jit(solution)/shard_map/all_to_all | solution.py:34
  241.7 24.5 %all-to-all-done.3 = bf16[8,256,256]{2,1,0:T(8,128)(2,1)S(1)} async-done(((bf16[8,256,256]{2,1,0:T(8,128)(2,1)}), bf16[8,256,256]{2,1,0:T(8,128)(2,1)S(1)}, u32[]{:S(2)}, u32[]{:S(2)}) %all-to-all-start.3) | async-done | bytes 1048608 | tf_op jit(solution)/shard_map/all_to_all | solution.py:34
  (100 shorter events, 22.1 us)
Async XLA Ops:
  7.2 48.7 %copy-start.5 = (bf16[512,32]{0,1:T(8,128)(2,1)S(1)}, bf16[512,32]{0,1:T(8,128)(2,1)}, u32[]{:S(2)}) copy-start(bf16[512,32]{0,1:T(8,128)(2,1)} %param.19) | copy-start | bytes 98308
  7.2 48.7 %copy-start.7 = (bf16[32,512]{1,0:T(8,128)(2,1)S(1)}, bf16[32,512]{1,0:T(8,128)(2,1)}, u32[]{:S(2)}) copy-start(bf16[32,512]{1,0:T(8,128)(2,1)} %param.17) | copy-start | bytes 98308
  7.2 48.7 %copy-start.6 = (bf16[32,512]{1,0:T(8,128)(2,1)S(1)}, bf16[32,512]{1,0:T(8,128)(2,1)}, u32[]{:S(2)}) copy-start(bf16[32,512]{1,0:T(8,128)(2,1)} %param.18) | copy-start | bytes 98308
  7.2 93.5 %all-gather.3.cloned.1.call-start = ((), (), s32[]{:S(2)}) async-start(), calls=%async_computation.4 | async-start | bytes 4259840 | tf_op jit(solution)/shard_map/all_gather | solution.py:81
  8.7 23.2 %collective-permute-start = (s32[256]{0:T(256)}, s32[256]{0:T(256)S(1)}, u32[]{:S(2)}, u32[]{:S(2)}) collective-permute-start(s32[256]{0:T(256)} %param.11), channel_id=1, source_target_pairs={{0,64},{8,72},{16,80},{24,88},{32,96},{40,104},{48,112},{56,120},{... | collective-permute-start | bytes 3080 | tf_op jit(solution)/shard_map/ppermute | solution.py:18
  13.0 22.4 %collective-permute-start.1 = (s32[256]{0:T(256)}, s32[256]{0:T(256)S(1)}, u32[]{:S(2)}, u32[]{:S(2)}) collective-permute-start(s32[256]{0:T(256)} %param.11), channel_id=1, source_target_pairs={{0,56},{8,64},{16,72},{24,80},{32,88},{40,96},{48,104},{56,112},{6... | collective-permute-start | bytes 3080 | tf_op jit(solution)/shard_map/ppermute | solution.py:18
  16.7 21.5 %collective-permute-start.2 = (s32[256]{0:T(256)}, s32[256]{0:T(256)S(1)}, u32[]{:S(2)}, u32[]{:S(2)}) collective-permute-start(s32[256]{0:T(256)} %param.11), channel_id=1, source_target_pairs={{0,48},{8,56},{16,64},{24,72},{32,80},{40,88},{48,96},{56,104},{64... | collective-permute-start | bytes 3080 | tf_op jit(solution)/shard_map/ppermute | solution.py:18
  20.9 20.7 %collective-permute-start.3 = (s32[256]{0:T(256)}, s32[256]{0:T(256)S(1)}, u32[]{:S(2)}, u32[]{:S(2)}) collective-permute-start(s32[256]{0:T(256)} %param.11), channel_id=1, source_target_pairs={{0,40},{8,48},{16,56},{24,64},{32,72},{40,80},{48,88},{56,96},{64,... | collective-permute-start | bytes 3080 | tf_op jit(solution)/shard_map/ppermute | solution.py:18
  27.3 14.4 %collective-permute-start.4 = (s32[256]{0:T(256)}, s32[256]{0:T(256)S(1)}, u32[]{:S(2)}, u32[]{:S(2)}) collective-permute-start(s32[256]{0:T(256)} %param.11), channel_id=1, source_target_pairs={{0,32},{8,40},{16,48},{24,56},{32,64},{40,72},{48,80},{56,88},{64,... | collective-permute-start | bytes 3080 | tf_op jit(solution)/shard_map/ppermute | solution.py:18
  31.9 9.8 %collective-permute-start.5 = (s32[256]{0:T(256)}, s32[256]{0:T(256)S(1)}, u32[]{:S(2)}, u32[]{:S(2)}) collective-permute-start(s32[256]{0:T(256)} %param.11), channel_id=1, source_target_pairs={{0,24},{8,32},{16,40},{24,48},{32,56},{40,64},{48,72},{56,80},{64,... | collective-permute-start | bytes 3080 | tf_op jit(solution)/shard_map/ppermute | solution.py:18
  35.4 6.3 %collective-permute-start.6 = (s32[256]{0:T(256)}, s32[256]{0:T(256)S(1)}, u32[]{:S(2)}, u32[]{:S(2)}) collective-permute-start(s32[256]{0:T(256)} %param.11), channel_id=1, source_target_pairs={{0,16},{8,24},{16,32},{24,40},{32,48},{40,56},{48,64},{56,72},{64,... | collective-permute-start | bytes 3080 | tf_op jit(solution)/shard_map/ppermute | solution.py:18
  38.2 5.1 %collective-permute-start.7 = (s32[256]{0:T(256)}, s32[256]{0:T(256)S(1)}, u32[]{:S(2)}, u32[]{:S(2)}) collective-permute-start(s32[256]{0:T(256)} %param.11), channel_id=1, source_target_pairs={{0,8},{8,16},{16,24},{24,32},{32,40},{40,48},{48,56},{56,64},{64,7... | collective-permute-start | bytes 3080 | tf_op jit(solution)/shard_map/ppermute | solution.py:18
  48.7 35.7 %all-to-all-start = ((bf16[8,256,256]{1,2,0:T(8,128)(2,1)}), bf16[8,256,256]{1,2,0:T(8,128)(2,1)S(1)}, u32[]{:S(2)}, u32[]{:S(2)}) async-start(bf16[8,256,256]{1,2,0:T(8,128)(2,1)} %broadcast_in_dim.38), calls=%async_computation | async-start | bytes 2097152 | tf_op jit(solution)/shard_map/all_to_all | solution.py:25
  55.8 173.7 %all-gather.5.cloned.1.call-start = ((), (), s32[]{:S(2)}) async-start(), calls=%async_computation.5 | async-start | bytes 6389760 | tf_op jit(solution)/shard_map/all_gather | solution.py:76
  56.9 47.6 %copy-start.2 = (f32[256,64]{0,1:T(8,128)}, f32[256,64]{0,1:T(8,128)S(1)}, u32[]{:S(2)}) copy-start(f32[256,64]{0,1:T(8,128)S(1)} %get-tuple-element.14) | copy-start | bytes 196612
  56.9 47.6 %copy-start.3 = (f32[256,64]{0,1:T(8,128)}, f32[256,64]{0,1:T(8,128)S(1)}, u32[]{:S(2)}) copy-start(f32[256,64]{0,1:T(8,128)S(1)} %get-tuple-element.15) | copy-start | bytes 196612
  104.6 13.1 %collective-permute-start.8 = (bf16[2,256,256]{2,1,0:T(8,128)(2,1)S(1)}, bf16[2,256,256]{2,1,0:T(8,128)(2,1)S(1)}, u32[]{:S(2)}, u32[]{:S(2)}) collective-permute-start(bf16[2,256,256]{2,1,0:T(8,128)(2,1)S(1)} %maximum_bitcast_fusion), channel_id=1, source_target_pairs={{0,64},{8,72},{16,80},{24,88},{32,96},{40,104},{48,112},{56,120},{... | collective-permute-start | bytes 786440 | tf_op jit(solution)/shard_map/ppermute | solution.py:18
  107.2 16.0 %collective-permute-start.9 = (bf16[2,256,256]{2,1,0:T(8,128)(2,1)S(1)}, bf16[2,256,256]{2,1,0:T(8,128)(2,1)S(1)}, u32[]{:S(2)}, u32[]{:S(2)}) collective-permute-start(bf16[2,256,256]{2,1,0:T(8,128)(2,1)S(1)} %maximum_bitcast_fusion), channel_id=1, source_target_pairs={{0,16},{8,24},{16,32},{24,40},{32,48},{40,56},{48,64},{56,72},{64,... | collective-permute-start | bytes 786440 | tf_op jit(solution)/shard_map/ppermute | solution.py:18
  111.8 20.3 %collective-permute-start.10 = (bf16[2,256,256]{2,1,0:T(8,128)(2,1)S(1)}, bf16[2,256,256]{2,1,0:T(8,128)(2,1)S(1)}, u32[]{:S(2)}, u32[]{:S(2)}) collective-permute-start(bf16[2,256,256]{2,1,0:T(8,128)(2,1)S(1)} %maximum_bitcast_fusion), channel_id=1, source_target_pairs={{0,32},{8,40},{16,48},{24,56},{32,64},{40,72},{48,80},{56,88},{64,... | collective-permute-start | bytes 786440 | tf_op jit(solution)/shard_map/ppermute | solution.py:18
  114.3 23.7 %collective-permute-start.11 = (bf16[2,256,256]{2,1,0:T(8,128)(2,1)S(1)}, bf16[2,256,256]{2,1,0:T(8,128)(2,1)S(1)}, u32[]{:S(2)}, u32[]{:S(2)}) collective-permute-start(bf16[2,256,256]{2,1,0:T(8,128)(2,1)S(1)} %maximum_bitcast_fusion), channel_id=1, source_target_pairs={{0,48},{8,56},{16,64},{24,72},{32,80},{40,88},{48,96},{56,104},{64... | collective-permute-start | bytes 786440 | tf_op jit(solution)/shard_map/ppermute | solution.py:18
  138.0 0.7 copy-start.1
  138.8 4.6 %collective-permute-start.12 = (bf16[4,2,256,256]{3,2,1,0:T(8,128)(2,1)S(1)}, bf16[4,2,256,256]{3,2,1,0:T(8,128)(2,1)S(1)}, u32[]{:S(2)}, u32[]{:S(2)}) collective-permute-start(bf16[4,2,256,256]{3,2,1,0:T(8,128)(2,1)S(1)} %pad_maximum_fusion), channel_id=1, source_target_pairs={{0,8},{8,0},{16,24},{24,16},{32,40},{40,32},{48,56},{56,48},{64,72... | collective-permute-start | bytes 3145736 | tf_op jit(solution)/shard_map/ppermute | solution.py:135
  150.4 6.3 %copy-start.8 = (bf16[2,256,2304]{2,1,0:T(8,128)(2,1)S(1)}, bf16[2,256,2304]{2,1,0:T(8,128)(2,1)}, u32[]{:S(2)}) copy-start(bf16[2,256,2304]{2,1,0:T(8,128)(2,1)} %constant_dynamic-update-slice_fusion.1) | copy-start | bytes 7077892
  161.8 36.3 %copy-start.4 = (bf16[256,256]{1,0:T(8,128)(2,1)S(1)}, bf16[256,256]{1,0:T(8,128)(2,1)}, u32[]{:S(2)}) copy-start(bf16[256,256]{1,0:T(8,128)(2,1)} %param.10) | copy-start | bytes 393220
  235.5 4.6 %copy-start.9 = (s32[16]{0:T(128)S(1)}, s32[16]{0:T(128)}, u32[]{:S(2)}) copy-start(s32[16]{0:T(128)} %param.12) | copy-start | bytes 196
  236.5 29.7 %all-to-all-start.3 = ((bf16[8,256,256]{2,1,0:T(8,128)(2,1)}), bf16[8,256,256]{2,1,0:T(8,128)(2,1)S(1)}, u32[]{:S(2)}, u32[]{:S(2)}) async-start(bf16[8,256,256]{2,1,0:T(8,128)(2,1)} %bitcast.79), calls=%async_computation.3 | async-start | bytes 2097152 | tf_op jit(solution)/shard_map/all_to_all | solution.py:34
  241.6 25.4 %copy-start = (bf16[2,16,16,256]{3,2,1,0:T(8,128)(2,1)}, bf16[2,16,16,256]{3,2,1,0:T(8,128)(2,1)S(1)}, u32[]{:S(2)}) copy-start(bf16[2,16,16,256]{3,2,1,0:T(8,128)(2,1)S(1)} %scatter_fusion) | copy-start | bytes 786436
Sparse Core Ops, SparseCore 0:
  12.0 88.6 all-gather.2
  104.6 87.1 all-gather.4

commit v14 on v12

--- a/solution.py
+++ b/solution.py
@@ -26,11 +26,7 @@
     return jnp.moveaxis(got, 0, 1).reshape(rows, cols * count)
 
 
-def swap_sum(value, axis):
-    count = lax.axis_size(axis)
-    rows, width = value.shape
-    cols = width // count
-    pieces = jnp.moveaxis(value.reshape(rows, count, cols), 1, 0)
+def swap_sum(pieces, axis):
     got = lax.all_to_all(pieces, axis, 0, 0, tiled=True)
     return jnp.sum(got.astype(jnp.float32), axis=0)
 
@@ -152,8 +148,10 @@
     attn_probs = (exps / jnp.sum(exps, axis=-1, keepdims=True)).astype(jnp.bfloat16)
     mixed = jnp.einsum("hqk,hdk->qhd", attn_probs, value_all, preferred_element_type=jnp.float32)
     attended = mixed.astype(jnp.bfloat16).reshape(tok_rows, local_width)
-    attn_terms = lax.dot_general(
-        attended, wo_t, (((1,), (1,)), ((), ())), preferred_element_type=jnp.float32
+    narrow_count = lax.axis_size("narrow")
+    attn_terms = jnp.einsum(
+        "tc,goc->gto", attended, wo_t.reshape(narrow_count, -1, wo_t.shape[1]),
+        preferred_element_type=jnp.float32,
     )
     attn_sum = swap_sum(attn_terms.astype(jnp.bfloat16), "narrow")
     first_res = (hidden_in.astype(jnp.float32) + attn_sum).astype(jnp.bfloat16)
@@ -163,8 +161,9 @@
     gate_proj = add_rows(normed_two, wg_all)
     up_proj = add_rows(normed_two, wu_all)
     hidden = (jax.nn.silu(gate_proj) * up_proj).astype(jnp.bfloat16)
-    down_terms = lax.dot_general(
-        hidden, wd_t, (((1,), (1,)), ((), ())), preferred_element_type=jnp.float32
+    down_terms = jnp.einsum(
+        "tc,goc->gto", hidden, wd_t.reshape(narrow_count, -1, wd_t.shape[1]),
+        preferred_element_type=jnp.float32,
     )
     down_sum = swap_sum(down_terms.astype(jnp.bfloat16), "narrow")
     result = (first_res.astype(jnp.float32) + down_sum).astype(jnp.bfloat16)

time: 273 us -> 273 us (level)
  blocking collectives: 65.9 us -> 0 us
  waiting for transfers between devices: 88.1 us -> 147 us
  starting transfers between devices: 58.3 us -> 69.1 us
  local copies, waits for them, and re-layouts: 14.1 us -> 11.1 us
    all_to_all x2 -> x0, blocking collectives: 65.9 us -> none  [the longest x1 35.6 us: swap_sum(): got = lax.all_to_all(pieces, axis, 0, 0, tiled=True)]
    all_to_all x1 -> x2, waiting for transfers between devices: 24.6 us -> 56.2 us  [swap_sum(): got = lax.all_to_all(pieces, axis, 0, 0, tiled=True)]
    all_to_all x1 -> x2, waiting for transfers between devices: 27.5 us -> 54.5 us  [swap_gather(): got = lax.all_to_all(copies, axis, 0, 0, tiled=True)]
    all_to_all x1 -> x2, starting transfers between devices: 3.56 us -> 10.6 us  [swap_sum(): got = lax.all_to_all(pieces, axis, 0, 0, tiled=True)]
    all_to_all x1 -> x2, starting transfers between devices: 7.1 us -> 10.8 us  [swap_gather(): got = lax.all_to_all(copies, axis, 0, 0, tiled=True)]
    unnamed x25 -> x31, local copies, waits for them, and re-layouts: 8.17 us -> 5.32 us
  transfers between devices with their start and end apart: 17 -> 19, of which waited for: 8 -> 10; matrix products, arithmetic and copies ran while one was open for 13% -> 11% of each run, Pallas kernels for 0% -> 0%
where the time goes in v14:
time: 273 us; the launch traced here: 272 us
  waiting for transfers between devices  147 us (54%)
  starting transfers between devices  69.1 us (25%)
  matrix products  21.5 us (8%)
  between operations  14.7 us (5%)
  local copies, waits for them, and re-layouts  11.1 us (4%)
  other arithmetic  8.31 us (3%)
    all_to_all x2, waiting for transfers between devices, swap_sum(): got = lax.all_to_all(pieces, axis, 0, 0, tiled=True)  56.2 us
    all_to_all x2, waiting for transfers between devices, swap_gather(): got = lax.all_to_all(copies, axis, 0, 0, tiled=True)  54.5 us
    ppermute x12, starting transfers between devices, shifted(): lax.ppermute(value, axis, [(source, source + steps) for source in range(f...  45.7 us
    ppermute x12, waiting for transfers between devices, shifted(): lax.ppermute(value, axis, [(source, source + steps) for source in range(f...  18.3 us
    all_gather x1, waiting for transfers between devices, per_device(): lax.all_gather(jnp.concatenate(attn_pieces, axis=1), 'wide', axis=0, tile...  15.4 us
    all_to_all x2, starting transfers between devices, swap_gather(): got = lax.all_to_all(copies, axis, 0, 0, tiled=True)  10.8 us
    all_to_all x2, starting transfers between devices, swap_sum(): got = lax.all_to_all(pieces, axis, 0, 0, tiled=True)  10.6 us
    dot_general x2, matrix products, add_rows(): return jnp.dot(source, piece, preferred_element_type=jnp.float32)  6.18 us
  transfers between devices with their start and end apart: 19, of which 10 were waited for; matrix products, arithmetic and copies ran while one was open for 11% of the time, Pallas kernels for 0%

profile of v14, /device:TPU:6, one launch (start us, length us, event | category | flops | bytes accessed | tf_op | source)
XLA Modules:
  0.0 272.1 jit_solution(15663368736942715722)
XLA Ops:
  8.7 4.3 %collective-permute-start = (s32[256]{0:T(256)}, s32[256]{0:T(256)S(1)}, u32[]{:S(2)}, u32[]{:S(2)}) collective-permute-start(s32[256]{0:T(256)} %param.11), channel_id=1, source_target_pairs={{0,64},{8,72},{16,80},{24,88},{32,96},{40,104},{48,112},{56,120},{... | collective-permute-start | bytes 3080 | tf_op jit(solution)/shard_map/ppermute | solution.py:18
  13.0 3.7 %collective-permute-start.1 = (s32[256]{0:T(256)}, s32[256]{0:T(256)S(1)}, u32[]{:S(2)}, u32[]{:S(2)}) collective-permute-start(s32[256]{0:T(256)} %param.11), channel_id=1, source_target_pairs={{0,56},{8,64},{16,72},{24,80},{32,88},{40,96},{48,104},{56,112},{6... | collective-permute-start | bytes 3080 | tf_op jit(solution)/shard_map/ppermute | solution.py:18
  16.7 4.3 %collective-permute-start.2 = (s32[256]{0:T(256)}, s32[256]{0:T(256)S(1)}, u32[]{:S(2)}, u32[]{:S(2)}) collective-permute-start(s32[256]{0:T(256)} %param.11), channel_id=1, source_target_pairs={{0,48},{8,56},{16,64},{24,72},{32,80},{40,88},{48,96},{56,104},{64... | collective-permute-start | bytes 3080 | tf_op jit(solution)/shard_map/ppermute | solution.py:18
  20.9 6.4 %collective-permute-start.3 = (s32[256]{0:T(256)}, s32[256]{0:T(256)S(1)}, u32[]{:S(2)}, u32[]{:S(2)}) collective-permute-start(s32[256]{0:T(256)} %param.11), channel_id=1, source_target_pairs={{0,40},{8,48},{16,56},{24,64},{32,72},{40,80},{48,88},{56,96},{64,... | collective-permute-start | bytes 3080 | tf_op jit(solution)/shard_map/ppermute | solution.py:18
  27.3 4.3 %collective-permute-start.4 = (s32[256]{0:T(256)}, s32[256]{0:T(256)S(1)}, u32[]{:S(2)}, u32[]{:S(2)}) collective-permute-start(s32[256]{0:T(256)} %param.11), channel_id=1, source_target_pairs={{0,32},{8,40},{16,48},{24,56},{32,64},{40,72},{48,80},{56,88},{64,... | collective-permute-start | bytes 3080 | tf_op jit(solution)/shard_map/ppermute | solution.py:18
  31.9 3.5 %collective-permute-start.5 = (s32[256]{0:T(256)}, s32[256]{0:T(256)S(1)}, u32[]{:S(2)}, u32[]{:S(2)}) collective-permute-start(s32[256]{0:T(256)} %param.11), channel_id=1, source_target_pairs={{0,24},{8,32},{16,40},{24,48},{32,56},{40,64},{48,72},{56,80},{64,... | collective-permute-start | bytes 3080 | tf_op jit(solution)/shard_map/ppermute | solution.py:18
  35.4 2.8 %collective-permute-start.6 = (s32[256]{0:T(256)}, s32[256]{0:T(256)S(1)}, u32[]{:S(2)}, u32[]{:S(2)}) collective-permute-start(s32[256]{0:T(256)} %param.11), channel_id=1, source_target_pairs={{0,16},{8,24},{16,32},{24,40},{32,48},{40,56},{48,64},{56,72},{64,... | collective-permute-start | bytes 3080 | tf_op jit(solution)/shard_map/ppermute | solution.py:18
  38.2 3.4 %collective-permute-start.7 = (s32[256]{0:T(256)}, s32[256]{0:T(256)S(1)}, u32[]{:S(2)}, u32[]{:S(2)}) collective-permute-start(s32[256]{0:T(256)} %param.11), channel_id=1, source_target_pairs={{0,8},{8,16},{16,24},{24,32},{32,40},{40,48},{48,56},{56,64},{64,7... | collective-permute-start | bytes 3080 | tf_op jit(solution)/shard_map/ppermute | solution.py:18
  41.7 1.5 collective-permute-done.7
  48.7 7.1 %all-to-all-start = ((bf16[8,256,256]{1,2,0:T(8,128)(2,1)}), bf16[8,256,256]{1,2,0:T(8,128)(2,1)S(1)}, u32[]{:S(2)}, u32[]{:S(2)}) async-start(bf16[8,256,256]{1,2,0:T(8,128)(2,1)} %broadcast_in_dim.38), calls=%async_computation | async-start | bytes 2097152 | tf_op jit(solution)/shard_map/all_to_all | solution.py:25
  56.9 27.5 %all-to-all-done = bf16[8,256,256]{1,2,0:T(8,128)(2,1)S(1)} async-done(((bf16[8,256,256]{1,2,0:T(8,128)(2,1)}), bf16[8,256,256]{1,2,0:T(8,128)(2,1)S(1)}, u32[]{:S(2)}, u32[]{:S(2)}) %all-to-all-start) | async-done | bytes 1048608 | tf_op jit(solution)/shard_map/all_to_all | solution.py:25
  85.3 15.4 %all-gather.3.cloned.1.call-done = bf16[2048,1024]{1,0:T(8,128)(2,1)} async-done(((bf16[32,1024]{1,0:T(8,128)(2,1)}), bf16[2048,1024]{1,0:T(8,128)(2,1)}) %all-gather.3.cloned.1.call-update) | async-done | bytes 4194320 | tf_op jit(solution)/shard_map/all_gather | solution.py:77
  100.7 3.5 %fusion.58 = f32[256,1024]{1,0:T(8,128)S(1)} fusion(bf16[256,2048]{0,1:T(8,128)(2,1)S(1)} %fusion.14, bf16[2048,1024]{1,0:T(8,128)(2,1)} %all-gather.3.cloned.1.call-done), kind=kOutput, calls=%fused_computation.107 | convolution fusion | flops 1073741824 | bytes 6291456 | tf_op jit(solution)/shard_map/dot_general | solution.py:60
  104.6 3.5 %collective-permute-start.9 = (bf16[2,256,256]{2,1,0:T(8,128)(2,1)S(1)}, bf16[2,256,256]{2,1,0:T(8,128)(2,1)S(1)}, u32[]{:S(2)}, u32[]{:S(2)}) collective-permute-start(bf16[2,256,256]{2,1,0:T(8,128)(2,1)S(1)} %fusion.44), channel_id=1, source_target_pairs={{0,16},{8,24},{16,32},{24,40},{32,48},{40,56},{48,64},{56,72},{64,... | collective-permute-start | bytes 786440 | tf_op jit(solution)/shard_map/ppermute | solution.py:18
  108.1 3.4 %collective-permute-start.10 = (bf16[2,256,256]{2,1,0:T(8,128)(2,1)S(1)}, bf16[2,256,256]{2,1,0:T(8,128)(2,1)S(1)}, u32[]{:S(2)}, u32[]{:S(2)}) collective-permute-start(bf16[2,256,256]{2,1,0:T(8,128)(2,1)S(1)} %fusion.44), channel_id=1, source_target_pairs={{0,32},{8,40},{16,48},{24,56},{32,64},{40,72},{48,80},{56,88},{64,... | collective-permute-start | bytes 786440 | tf_op jit(solution)/shard_map/ppermute | solution.py:18
  111.4 2.5 collective-permute-start.11
  114.0 3.7 %collective-permute-start.8 = (bf16[2,256,256]{2,1,0:T(8,128)(2,1)S(1)}, bf16[2,256,256]{2,1,0:T(8,128)(2,1)S(1)}, u32[]{:S(2)}, u32[]{:S(2)}) collective-permute-start(bf16[2,256,256]{2,1,0:T(8,128)(2,1)S(1)} %fusion.44), channel_id=1, source_target_pairs={{0,64},{8,72},{16,80},{24,88},{32,96},{40,104},{48,112},{56,120},{... | collective-permute-start | bytes 786440 | tf_op jit(solution)/shard_map/ppermute | solution.py:18
  118.4 5.2 %collective-permute-done.10 = bf16[2,256,256]{2,1,0:T(8,128)(2,1)S(1)} collective-permute-done((bf16[2,256,256]{2,1,0:T(8,128)(2,1)S(1)}, bf16[2,256,256]{2,1,0:T(8,128)(2,1)S(1)}, u32[]{:S(2)}, u32[]{:S(2)}) %collective-permute-start.10) | collective-permute-done | bytes 262176 | tf_op jit(solution)/shard_map/ppermute | solution.py:18
  124.4 6.1 %collective-permute-done.11 = bf16[2,256,256]{2,1,0:T(8,128)(2,1)S(1)} collective-permute-done((bf16[2,256,256]{2,1,0:T(8,128)(2,1)S(1)}, bf16[2,256,256]{2,1,0:T(8,128)(2,1)S(1)}, u32[]{:S(2)}, u32[]{:S(2)}) %collective-permute-start.11) | collective-permute-done | bytes 262176 | tf_op jit(solution)/shard_map/ppermute | solution.py:18
  131.3 5.3 %collective-permute-done.8 = bf16[2,256,256]{2,1,0:T(8,128)(2,1)S(1)} collective-permute-done((bf16[2,256,256]{2,1,0:T(8,128)(2,1)S(1)}, bf16[2,256,256]{2,1,0:T(8,128)(2,1)S(1)}, u32[]{:S(2)}, u32[]{:S(2)}) %collective-permute-start.8) | collective-permute-done | bytes 262176 | tf_op jit(solution)/shard_map/ppermute | solution.py:18
  138.0 1.9 collective-permute-start.12
  140.2 3.0 %collective-permute-done.12 = bf16[5,2,256,256]{3,2,1,0:T(8,128)(2,1)S(1)} collective-permute-done((bf16[5,2,256,256]{3,2,1,0:T(8,128)(2,1)}, bf16[5,2,256,256]{3,2,1,0:T(8,128)(2,1)S(1)}, u32[]{:S(2)}, u32[]{:S(2)}) %collective-permute-start.12) | collective-permute-done | bytes 1310752 | tf_op jit(solution)/shard_map/ppermute | solution.py:130
  144.8 5.8 %fusion.53 = (f32[2,256]{1,0:T(2,128)S(1)}, f32[2,256,2304]{2,1,0:T(8,128)}) fusion(pred[256,2304]{1,0:T(8,128)(4,1)S(1)} %copy-done.2, bf16[2,256,2304]{2,1,0:T(8,128)(2,1)} %copy-done.7, bf16[256,2,64]{0,2,1:T(8,128)(2,1)S(1)} %get-tuple-element.13, bf16[256,2,64]{0,2,1:T(8,128)(2,1)S(1)} %get-tuple-element.12), kind=kOutput, calls=%fused_computation.106 | convolution fusion | flops 308152576 | bytes 7211008 | tf_op jit(solution)/shard_map/sub | solution.py:147
  150.6 3.8 %fusion.28 = bf16[2,128,256]{2,1,0:T(8,128)(2,1)S(1)} fusion(f32[2,256,2304]{2,1,0:T(8,128)} %get-tuple-element.21, f32[2,256]{1,0:T(2,128)S(1)} %get-tuple-element.20, bf16[2,256,2304]{2,1,0:T(8,128)(2,1)} %copy-done.7), kind=kOutput, calls=%fused_computation.36 | convolution fusion | flops 304414720 | bytes 6031360 | tf_op jit(solution)/shard_map/hqk,hdk->qhd/dot_general | solution.py:149
  155.8 6.7 %all-to-all-start.1 = ((bf16[8,256,256]{1,2,0:T(8,128)(2,1)}), bf16[8,256,256]{1,2,0:T(8,128)(2,1)S(1)}, u32[]{:S(2)}, u32[]{:S(2)}) async-start(bf16[8,256,256]{1,2,0:T(8,128)(2,1)} %fusion.16), calls=%async_computation.1 | async-start | bytes 2097152 | tf_op jit(solution)/shard_map/all_to_all | solution.py:30
  162.7 29.0 %all-to-all-done.1 = bf16[8,256,256]{1,2,0:T(8,128)(2,1)S(1)} async-done(((bf16[8,256,256]{1,2,0:T(8,128)(2,1)}), bf16[8,256,256]{1,2,0:T(8,128)(2,1)S(1)}, u32[]{:S(2)}, u32[]{:S(2)}) %all-to-all-start.1) | async-done | bytes 1048608 | tf_op jit(solution)/shard_map/all_to_all | solution.py:30
  192.9 3.7 %all-to-all-start.2 = ((bf16[8,256,256]{1,2,0:T(8,128)(2,1)}), bf16[8,256,256]{1,2,0:T(8,128)(2,1)S(1)}, u32[]{:S(2)}, u32[]{:S(2)}) async-start(bf16[8,256,256]{1,2,0:T(8,128)(2,1)} %broadcast_in_dim.42), calls=%async_computation.2 | async-start | bytes 2097152 | tf_op jit(solution)/shard_map/all_to_all | solution.py:25
  196.7 27.0 %all-to-all-done.2 = bf16[8,256,256]{1,2,0:T(8,128)(2,1)S(1)} async-done(((bf16[8,256,256]{1,2,0:T(8,128)(2,1)}), bf16[8,256,256]{1,2,0:T(8,128)(2,1)S(1)}, u32[]{:S(2)}, u32[]{:S(2)}) %all-to-all-start.2) | async-done | bytes 1048608 | tf_op jit(solution)/shard_map/all_to_all | solution.py:25
  224.6 2.7 %fusion.9 = f32[256,512]{1,0:T(8,128)S(1)} fusion(bf16[256,2048]{0,1:T(8,128)(2,1)S(1)} %fusion.12, bf16[2048,1536]{1,0:T(8,128)(2,1)} %all-gather.5.cloned.1.call-done), kind=kOutput, calls=%fused_computation.15 | convolution fusion | flops 536870912 | bytes 3670016 | tf_op jit(solution)/shard_map/dot_general | solution.py:60
  227.4 4.3 %fusion.15 = bf16[8,256,256]{1,2,0:T(8,128)(2,1)} fusion(bf16[8,256,512]{2,1,0:T(8,128)(2,1)S(1)} %bitcast.87, bf16[256,2048]{0,1:T(8,128)(2,1)} %copy-done, bf16[2048,1536]{1,0:T(8,128)(2,1)} %all-gather.5.cloned.1.call-done, f32[256,512]{1,0:T(8,128)S(1)} %fusion.9), kind=kOutput, calls=%fused_computation.29 | convolution fusion | flops 1075052544 | bytes 6815744 | tf_op jit(solution)/shard_map/tc,goc->gto/dot_general | solution.py:164
  231.7 3.8 %all-to-all-start.3 = ((bf16[8,256,256]{1,2,0:T(8,128)(2,1)}), bf16[8,256,256]{1,2,0:T(8,128)(2,1)S(1)}, u32[]{:S(2)}, u32[]{:S(2)}) async-start(bf16[8,256,256]{1,2,0:T(8,128)(2,1)} %fusion.15), calls=%async_computation.3 | async-start | bytes 2097152 | tf_op jit(solution)/shard_map/all_to_all | solution.py:30
  237.1 27.3 %all-to-all-done.3 = bf16[8,256,256]{1,2,0:T(8,128)(2,1)S(1)} async-done(((bf16[8,256,256]{1,2,0:T(8,128)(2,1)}), bf16[8,256,256]{1,2,0:T(8,128)(2,1)S(1)}, u32[]{:S(2)}, u32[]{:S(2)}) %all-to-all-start.3) | async-done | bytes 1048608 | tf_op jit(solution)/shard_map/all_to_all | solution.py:30
  (107 shorter events, 21.0 us)
Async XLA Ops:
  7.2 48.7 %copy-start.4 = (bf16[512,32]{0,1:T(8,128)(2,1)S(1)}, bf16[512,32]{0,1:T(8,128)(2,1)}, u32[]{:S(2)}) copy-start(bf16[512,32]{0,1:T(8,128)(2,1)} %param.19) | copy-start | bytes 98308
  7.2 48.7 %copy-start.6 = (bf16[32,512]{1,0:T(8,128)(2,1)S(1)}, bf16[32,512]{1,0:T(8,128)(2,1)}, u32[]{:S(2)}) copy-start(bf16[32,512]{1,0:T(8,128)(2,1)} %param.17) | copy-start | bytes 98308
  7.2 48.7 %copy-start.5 = (bf16[32,512]{1,0:T(8,128)(2,1)S(1)}, bf16[32,512]{1,0:T(8,128)(2,1)}, u32[]{:S(2)}) copy-start(bf16[32,512]{1,0:T(8,128)(2,1)} %param.18) | copy-start | bytes 98308
  7.2 93.5 %all-gather.3.cloned.1.call-start = ((), (), s32[]{:S(2)}) async-start(), calls=%async_computation.4 | async-start | bytes 4259840 | tf_op jit(solution)/shard_map/all_gather | solution.py:77
  8.7 23.2 %collective-permute-start = (s32[256]{0:T(256)}, s32[256]{0:T(256)S(1)}, u32[]{:S(2)}, u32[]{:S(2)}) collective-permute-start(s32[256]{0:T(256)} %param.11), channel_id=1, source_target_pairs={{0,64},{8,72},{16,80},{24,88},{32,96},{40,104},{48,112},{56,120},{... | collective-permute-start | bytes 3080 | tf_op jit(solution)/shard_map/ppermute | solution.py:18
  13.0 22.4 %collective-permute-start.1 = (s32[256]{0:T(256)}, s32[256]{0:T(256)S(1)}, u32[]{:S(2)}, u32[]{:S(2)}) collective-permute-start(s32[256]{0:T(256)} %param.11), channel_id=1, source_target_pairs={{0,56},{8,64},{16,72},{24,80},{32,88},{40,96},{48,104},{56,112},{6... | collective-permute-start | bytes 3080 | tf_op jit(solution)/shard_map/ppermute | solution.py:18
  16.7 21.5 %collective-permute-start.2 = (s32[256]{0:T(256)}, s32[256]{0:T(256)S(1)}, u32[]{:S(2)}, u32[]{:S(2)}) collective-permute-start(s32[256]{0:T(256)} %param.11), channel_id=1, source_target_pairs={{0,48},{8,56},{16,64},{24,72},{32,80},{40,88},{48,96},{56,104},{64... | collective-permute-start | bytes 3080 | tf_op jit(solution)/shard_map/ppermute | solution.py:18
  20.9 20.7 %collective-permute-start.3 = (s32[256]{0:T(256)}, s32[256]{0:T(256)S(1)}, u32[]{:S(2)}, u32[]{:S(2)}) collective-permute-start(s32[256]{0:T(256)} %param.11), channel_id=1, source_target_pairs={{0,40},{8,48},{16,56},{24,64},{32,72},{40,80},{48,88},{56,96},{64,... | collective-permute-start | bytes 3080 | tf_op jit(solution)/shard_map/ppermute | solution.py:18
  27.3 14.4 %collective-permute-start.4 = (s32[256]{0:T(256)}, s32[256]{0:T(256)S(1)}, u32[]{:S(2)}, u32[]{:S(2)}) collective-permute-start(s32[256]{0:T(256)} %param.11), channel_id=1, source_target_pairs={{0,32},{8,40},{16,48},{24,56},{32,64},{40,72},{48,80},{56,88},{64,... | collective-permute-start | bytes 3080 | tf_op jit(solution)/shard_map/ppermute | solution.py:18
  31.9 9.8 %collective-permute-start.5 = (s32[256]{0:T(256)}, s32[256]{0:T(256)S(1)}, u32[]{:S(2)}, u32[]{:S(2)}) collective-permute-start(s32[256]{0:T(256)} %param.11), channel_id=1, source_target_pairs={{0,24},{8,32},{16,40},{24,48},{32,56},{40,64},{48,72},{56,80},{64,... | collective-permute-start | bytes 3080 | tf_op jit(solution)/shard_map/ppermute | solution.py:18
  35.4 6.3 %collective-permute-start.6 = (s32[256]{0:T(256)}, s32[256]{0:T(256)S(1)}, u32[]{:S(2)}, u32[]{:S(2)}) collective-permute-start(s32[256]{0:T(256)} %param.11), channel_id=1, source_target_pairs={{0,16},{8,24},{16,32},{24,40},{32,48},{40,56},{48,64},{56,72},{64,... | collective-permute-start | bytes 3080 | tf_op jit(solution)/shard_map/ppermute | solution.py:18
  38.2 5.1 %collective-permute-start.7 = (s32[256]{0:T(256)}, s32[256]{0:T(256)S(1)}, u32[]{:S(2)}, u32[]{:S(2)}) collective-permute-start(s32[256]{0:T(256)} %param.11), channel_id=1, source_target_pairs={{0,8},{8,16},{16,24},{24,32},{32,40},{40,48},{48,56},{56,64},{64,7... | collective-permute-start | bytes 3080 | tf_op jit(solution)/shard_map/ppermute | solution.py:18
  48.7 35.7 %all-to-all-start = ((bf16[8,256,256]{1,2,0:T(8,128)(2,1)}), bf16[8,256,256]{1,2,0:T(8,128)(2,1)S(1)}, u32[]{:S(2)}, u32[]{:S(2)}) async-start(bf16[8,256,256]{1,2,0:T(8,128)(2,1)} %broadcast_in_dim.38), calls=%async_computation | async-start | bytes 2097152 | tf_op jit(solution)/shard_map/all_to_all | solution.py:25
  55.8 140.8 %all-gather.5.cloned.1.call-start = ((), (), s32[]{:S(2)}) async-start(), calls=%async_computation.5 | async-start | bytes 6389760 | tf_op jit(solution)/shard_map/all_gather | solution.py:72
  104.6 13.1 %collective-permute-start.9 = (bf16[2,256,256]{2,1,0:T(8,128)(2,1)S(1)}, bf16[2,256,256]{2,1,0:T(8,128)(2,1)S(1)}, u32[]{:S(2)}, u32[]{:S(2)}) collective-permute-start(bf16[2,256,256]{2,1,0:T(8,128)(2,1)S(1)} %fusion.44), channel_id=1, source_target_pairs={{0,16},{8,24},{16,32},{24,40},{32,48},{40,56},{48,64},{56,72},{64,... | collective-permute-start | bytes 786440 | tf_op jit(solution)/shard_map/ppermute | solution.py:18
  108.1 15.6 %collective-permute-start.10 = (bf16[2,256,256]{2,1,0:T(8,128)(2,1)S(1)}, bf16[2,256,256]{2,1,0:T(8,128)(2,1)S(1)}, u32[]{:S(2)}, u32[]{:S(2)}) collective-permute-start(bf16[2,256,256]{2,1,0:T(8,128)(2,1)S(1)} %fusion.44), channel_id=1, source_target_pairs={{0,32},{8,40},{16,48},{24,56},{32,64},{40,72},{48,80},{56,88},{64,... | collective-permute-start | bytes 786440 | tf_op jit(solution)/shard_map/ppermute | solution.py:18
  111.4 19.1 %collective-permute-start.11 = (bf16[2,256,256]{2,1,0:T(8,128)(2,1)S(1)}, bf16[2,256,256]{2,1,0:T(8,128)(2,1)S(1)}, u32[]{:S(2)}, u32[]{:S(2)}) collective-permute-start(bf16[2,256,256]{2,1,0:T(8,128)(2,1)S(1)} %fusion.44), channel_id=1, source_target_pairs={{0,48},{8,56},{16,64},{24,72},{32,80},{40,88},{48,96},{56,104},{64... | collective-permute-start | bytes 786440 | tf_op jit(solution)/shard_map/ppermute | solution.py:18
  114.0 22.6 %collective-permute-start.8 = (bf16[2,256,256]{2,1,0:T(8,128)(2,1)S(1)}, bf16[2,256,256]{2,1,0:T(8,128)(2,1)S(1)}, u32[]{:S(2)}, u32[]{:S(2)}) collective-permute-start(bf16[2,256,256]{2,1,0:T(8,128)(2,1)S(1)} %fusion.44), channel_id=1, source_target_pairs={{0,64},{8,72},{16,80},{24,88},{32,96},{40,104},{48,112},{56,120},{... | collective-permute-start | bytes 786440 | tf_op jit(solution)/shard_map/ppermute | solution.py:18
  138.0 5.1 %collective-permute-start.12 = (bf16[5,2,256,256]{3,2,1,0:T(8,128)(2,1)}, bf16[5,2,256,256]{3,2,1,0:T(8,128)(2,1)S(1)}, u32[]{:S(2)}, u32[]{:S(2)}) collective-permute-start(bf16[5,2,256,256]{3,2,1,0:T(8,128)(2,1)} %bitcast_dynamic-update-slice_fusion), channel_id=1, source_target_pairs={{0,8},{8,0},{16,24},{24,16},{32,40},{40,32},{48,56},{56,48},{64,72... | collective-permute-start | bytes 3932168 | tf_op jit(solution)/shard_map/ppermute | solution.py:130
  140.2 4.6 %copy-start.2 = (pred[256,2304]{1,0:T(8,128)(4,1)S(1)}, pred[256,2304]{1,0:T(8,128)(4,1)}, u32[]{:S(2)}) copy-start(pred[256,2304]{1,0:T(8,128)(4,1)} %compare_and_fusion) | copy-start | bytes 1769476
  143.4 1.4 copy-start.7
  150.6 3.8 %slice-start = ((bf16[2048,1024]{1,0:T(8,128)(2,1)}), bf16[2048,256]{1,0:T(8,128)(2,1)S(1)}, s32[]{:S(2)}) async-start(bf16[2048,1024]{1,0:T(8,128)(2,1)} %all-gather.3.cloned.1.call-done), calls=%async_computation.6 | async-start | bytes 2097152 | tf_op jit(solution)/shard_map/slice | solution.py:78
  154.4 8.2 %copy-start.3 = (bf16[256,256]{1,0:T(8,128)(2,1)S(1)}, bf16[256,256]{1,0:T(8,128)(2,1)}, u32[]{:S(2)}) copy-start(bf16[256,256]{1,0:T(8,128)(2,1)} %param.10) | copy-start | bytes 393220
  155.8 35.8 %all-to-all-start.1 = ((bf16[8,256,256]{1,2,0:T(8,128)(2,1)}), bf16[8,256,256]{1,2,0:T(8,128)(2,1)S(1)}, u32[]{:S(2)}, u32[]{:S(2)}) async-start(bf16[8,256,256]{1,2,0:T(8,128)(2,1)} %fusion.16), calls=%async_computation.1 | async-start | bytes 2097152 | tf_op jit(solution)/shard_map/all_to_all | solution.py:30
  192.9 30.7 %all-to-all-start.2 = ((bf16[8,256,256]{1,2,0:T(8,128)(2,1)}), bf16[8,256,256]{1,2,0:T(8,128)(2,1)S(1)}, u32[]{:S(2)}, u32[]{:S(2)}) async-start(bf16[8,256,256]{1,2,0:T(8,128)(2,1)} %broadcast_in_dim.42), calls=%async_computation.2 | async-start | bytes 2097152 | tf_op jit(solution)/shard_map/all_to_all | solution.py:25
  224.6 2.8 %copy-start = (bf16[256,2048]{0,1:T(8,128)(2,1)}, bf16[256,2048]{0,1:T(8,128)(2,1)S(1)}, u32[]{:S(2)}) copy-start(bf16[256,2048]{0,1:T(8,128)(2,1)S(1)} %fusion.12) | copy-start | bytes 3145732
  224.6 2.8 %slice-start.1 = ((bf16[2048,1536]{1,0:T(8,128)(2,1)}), bf16[2048,512]{1,0:T(8,128)(2,1)S(1)}, s32[]{:S(2)}) async-start(bf16[2048,1536]{1,0:T(8,128)(2,1)} %all-gather.5.cloned.1.call-done), calls=%async_computation.7 | async-start | bytes 4194304 | tf_op jit(solution)/shard_map/slice | solution.py:74
  227.3 8.2 %copy-start.8 = (s32[16]{0:T(128)S(1)}, s32[16]{0:T(128)}, u32[]{:S(2)}) copy-start(s32[16]{0:T(128)} %param.12) | copy-start | bytes 196
  231.7 32.7 %all-to-all-start.3 = ((bf16[8,256,256]{1,2,0:T(8,128)(2,1)}), bf16[8,256,256]{1,2,0:T(8,128)(2,1)S(1)}, u32[]{:S(2)}, u32[]{:S(2)}) async-start(bf16[8,256,256]{1,2,0:T(8,128)(2,1)} %fusion.15), calls=%async_computation.3 | async-start | bytes 2097152 | tf_op jit(solution)/shard_map/all_to_all | solution.py:30
  237.1 28.2 %copy-start.1 = (bf16[2,16,16,256]{3,2,1,0:T(8,128)(2,1)}, bf16[2,16,16,256]{3,2,1,0:T(8,128)(2,1)S(1)}, u32[]{:S(2)}) copy-start(bf16[2,16,16,256]{3,2,1,0:T(8,128)(2,1)S(1)} %scatter_fusion) | copy-start | bytes 786436
Sparse Core Ops, SparseCore 0:
  12.0 88.6 all-gather.2
  104.6 88.5 all-gather.4

commit v15 on v14

--- a/solution.py
+++ b/solution.py
@@ -155,11 +155,20 @@
     )
     attn_sum = swap_sum(attn_terms.astype(jnp.bfloat16), "narrow")
     first_res = (hidden_in.astype(jnp.float32) + attn_sum).astype(jnp.bfloat16)
-    whole_two = swap_gather(first_res, "narrow")
-    normed_two = norm_rows(whole_two)
-
-    gate_proj = add_rows(normed_two, wg_all)
-    up_proj = add_rows(normed_two, wu_all)
+    copies = jnp.broadcast_to(first_res[None], (narrow_count,) + first_res.shape)
+    pieces_two = lax.all_to_all(copies, "narrow", 0, 0, tiled=True).astype(jnp.float32)
+    center = pieces_two - jnp.mean(pieces_two, axis=(0, 2), keepdims=True)
+    spread = jnp.mean(center * center, axis=(0, 2), keepdims=True)
+    normed_two = (center * lax.rsqrt(spread + epsilon)).astype(jnp.bfloat16)
+
+    def add_pieces(piece):
+        return jnp.einsum(
+            "gtc,gcu->tu", normed_two, piece.reshape(narrow_count, -1, piece.shape[1]),
+            preferred_element_type=jnp.float32,
+        )
+
+    gate_proj = add_pieces(wg_all)
+    up_proj = add_pieces(wu_all)
     hidden = (jax.nn.silu(gate_proj) * up_proj).astype(jnp.bfloat16)
     down_terms = jnp.einsum(
         "tc,goc->gto", hidden, wd_t.reshape(narrow_count, -1, wd_t.shape[1]),

time: 273 us -> 273 us (level)
  local copies, waits for them, and re-layouts: 11.1 us -> 17.5 us
  waiting for transfers between devices: 147 us -> 142 us
    all_to_all x2 -> x1, waiting for transfers between devices: 54.5 us -> 27.5 us  [swap_gather(): got = lax.all_to_all(copies, axis, 0, 0, tiled=True)]
    all_to_all x0 -> x1, waiting for transfers between devices: none -> 21.5 us  [per_device(): lax.all_to_all(copies, 'narrow', 0, 0, tiled=True).astype(jnp.float32)]
    slice x2 -> x1, local copies, waits for them, and re-layouts: 0.01 us -> 5.43 us  [gather_pieces(): return [gathered[:, o:o + w] for o, w in zip(offsets, widths)]]
    all_to_all x0 -> x1, starting transfers between devices: none -> 3.74 us  [per_device(): lax.all_to_all(copies, 'narrow', 0, 0, tiled=True).astype(jnp.float32)]
    all_to_all x2 -> x1, starting transfers between devices: 10.8 us -> 7.1 us  [swap_gather(): got = lax.all_to_all(copies, axis, 0, 0, tiled=True)]
    dot_general x2 -> x1, matrix products: 6.18 us -> 3.46 us  [add_rows(): return jnp.dot(source, piece, preferred_element_type=jnp.float32)]
  transfers between devices with their start and end apart: 19 -> 19, of which waited for: 10 -> 10; matrix products, arithmetic and copies ran while one was open for 11% -> 13% of each run, Pallas kernels for 0% -> 0%
where the time goes in v15:
time: 273 us; the launch traced here: 272 us
  waiting for transfers between devices  142 us (52%)
  starting transfers between devices  69.3 us (25%)
  matrix products  20.2 us (7%)
  local copies, waits for them, and re-layouts  17.5 us (6%)
  between operations  14.7 us (5%)
  other arithmetic  8.03 us (3%)
    all_to_all x2, waiting for transfers between devices, swap_sum(): got = lax.all_to_all(pieces, axis, 0, 0, tiled=True)  56.2 us
    ppermute x12, starting transfers between devices, shifted(): lax.ppermute(value, axis, [(source, source + steps) for source in range(f...  45.7 us
    all_to_all x1, waiting for transfers between devices, swap_gather(): got = lax.all_to_all(copies, axis, 0, 0, tiled=True)  27.5 us
    all_to_all x1, waiting for transfers between devices, per_device(): lax.all_to_all(copies, 'narrow', 0, 0, tiled=True).astype(jnp.float32)  21.5 us
    ppermute x12, waiting for transfers between devices, shifted(): lax.ppermute(value, axis, [(source, source + steps) for source in range(f...  18.3 us
    all_gather x1, waiting for transfers between devices, per_device(): lax.all_gather(jnp.concatenate(attn_pieces, axis=1), 'wide', axis=0, tile...  15.3 us
    all_to_all x2, starting transfers between devices, swap_sum(): got = lax.all_to_all(pieces, axis, 0, 0, tiled=True)  10.7 us
    all_to_all x1, starting transfers between devices, swap_gather(): got = lax.all_to_all(copies, axis, 0, 0, tiled=True)  7.1 us
  transfers between devices with their start and end apart: 19, of which 10 were waited for; matrix products, arithmetic and copies ran while one was open for 13% of the time, Pallas kernels for 0%

profile of v15, /device:TPU:6, one launch (start us, length us, event | category | flops | bytes accessed | tf_op | source)
XLA Modules:
  0.0 271.6 jit_solution(4911315427043289364)
XLA Ops:
  8.6 4.3 %collective-permute-start = (s32[256]{0:T(256)}, s32[256]{0:T(256)S(1)}, u32[]{:S(2)}, u32[]{:S(2)}) collective-permute-start(s32[256]{0:T(256)} %param.11), channel_id=1, source_target_pairs={{0,64},{8,72},{16,80},{24,88},{32,96},{40,104},{48,112},{56,120},{... | collective-permute-start | bytes 3080 | tf_op jit(solution)/shard_map/ppermute | solution.py:18
  12.9 3.7 %collective-permute-start.1 = (s32[256]{0:T(256)}, s32[256]{0:T(256)S(1)}, u32[]{:S(2)}, u32[]{:S(2)}) collective-permute-start(s32[256]{0:T(256)} %param.11), channel_id=1, source_target_pairs={{0,56},{8,64},{16,72},{24,80},{32,88},{40,96},{48,104},{56,112},{6... | collective-permute-start | bytes 3080 | tf_op jit(solution)/shard_map/ppermute | solution.py:18
  16.6 4.3 %collective-permute-start.2 = (s32[256]{0:T(256)}, s32[256]{0:T(256)S(1)}, u32[]{:S(2)}, u32[]{:S(2)}) collective-permute-start(s32[256]{0:T(256)} %param.11), channel_id=1, source_target_pairs={{0,48},{8,56},{16,64},{24,72},{32,80},{40,88},{48,96},{56,104},{64... | collective-permute-start | bytes 3080 | tf_op jit(solution)/shard_map/ppermute | solution.py:18
  20.9 6.4 %collective-permute-start.3 = (s32[256]{0:T(256)}, s32[256]{0:T(256)S(1)}, u32[]{:S(2)}, u32[]{:S(2)}) collective-permute-start(s32[256]{0:T(256)} %param.11), channel_id=1, source_target_pairs={{0,40},{8,48},{16,56},{24,64},{32,72},{40,80},{48,88},{56,96},{64,... | collective-permute-start | bytes 3080 | tf_op jit(solution)/shard_map/ppermute | solution.py:18
  27.3 4.3 %collective-permute-start.4 = (s32[256]{0:T(256)}, s32[256]{0:T(256)S(1)}, u32[]{:S(2)}, u32[]{:S(2)}) collective-permute-start(s32[256]{0:T(256)} %param.11), channel_id=1, source_target_pairs={{0,32},{8,40},{16,48},{24,56},{32,64},{40,72},{48,80},{56,88},{64,... | collective-permute-start | bytes 3080 | tf_op jit(solution)/shard_map/ppermute | solution.py:18
  31.9 3.5 %collective-permute-start.5 = (s32[256]{0:T(256)}, s32[256]{0:T(256)S(1)}, u32[]{:S(2)}, u32[]{:S(2)}) collective-permute-start(s32[256]{0:T(256)} %param.11), channel_id=1, source_target_pairs={{0,24},{8,32},{16,40},{24,48},{32,56},{40,64},{48,72},{56,80},{64,... | collective-permute-start | bytes 3080 | tf_op jit(solution)/shard_map/ppermute | solution.py:18
  35.4 2.8 %collective-permute-start.6 = (s32[256]{0:T(256)}, s32[256]{0:T(256)S(1)}, u32[]{:S(2)}, u32[]{:S(2)}) collective-permute-start(s32[256]{0:T(256)} %param.11), channel_id=1, source_target_pairs={{0,16},{8,24},{16,32},{24,40},{32,48},{40,56},{48,64},{56,72},{64,... | collective-permute-start | bytes 3080 | tf_op jit(solution)/shard_map/ppermute | solution.py:18
  38.2 3.4 %collective-permute-start.7 = (s32[256]{0:T(256)}, s32[256]{0:T(256)S(1)}, u32[]{:S(2)}, u32[]{:S(2)}) collective-permute-start(s32[256]{0:T(256)} %param.11), channel_id=1, source_target_pairs={{0,8},{8,16},{16,24},{24,32},{32,40},{40,48},{48,56},{56,64},{64,7... | collective-permute-start | bytes 3080 | tf_op jit(solution)/shard_map/ppermute | solution.py:18
  48.7 7.1 %all-to-all-start = ((bf16[8,256,256]{1,2,0:T(8,128)(2,1)}), bf16[8,256,256]{1,2,0:T(8,128)(2,1)S(1)}, u32[]{:S(2)}, u32[]{:S(2)}) async-start(bf16[8,256,256]{1,2,0:T(8,128)(2,1)} %broadcast_in_dim.38), calls=%async_computation | async-start | bytes 2097152 | tf_op jit(solution)/shard_map/all_to_all | solution.py:25
  56.9 27.5 %all-to-all-done = bf16[8,256,256]{1,2,0:T(8,128)(2,1)S(1)} async-done(((bf16[8,256,256]{1,2,0:T(8,128)(2,1)}), bf16[8,256,256]{1,2,0:T(8,128)(2,1)S(1)}, u32[]{:S(2)}, u32[]{:S(2)}) %all-to-all-start) | async-done | bytes 1048608 | tf_op jit(solution)/shard_map/all_to_all | solution.py:25
  85.3 15.3 %all-gather.3.cloned.1.call-done = bf16[2048,1024]{1,0:T(8,128)(2,1)} async-done(((bf16[32,1024]{1,0:T(8,128)(2,1)}), bf16[2048,1024]{1,0:T(8,128)(2,1)}) %all-gather.3.cloned.1.call-update) | async-done | bytes 4194320 | tf_op jit(solution)/shard_map/all_gather | solution.py:77
  100.6 3.5 %fusion.52 = f32[256,1024]{1,0:T(8,128)S(1)} fusion(bf16[256,2048]{0,1:T(8,128)(2,1)S(1)} %fusion.12, bf16[2048,1024]{1,0:T(8,128)(2,1)} %all-gather.3.cloned.1.call-done), kind=kOutput, calls=%fused_computation.107 | convolution fusion | flops 1073741824 | bytes 6291456 | tf_op jit(solution)/shard_map/dot_general | solution.py:60
  104.5 3.5 %collective-permute-start.9 = (bf16[2,256,256]{2,1,0:T(8,128)(2,1)S(1)}, bf16[2,256,256]{2,1,0:T(8,128)(2,1)S(1)}, u32[]{:S(2)}, u32[]{:S(2)}) collective-permute-start(bf16[2,256,256]{2,1,0:T(8,128)(2,1)S(1)} %fusion.34), channel_id=1, source_target_pairs={{0,16},{8,24},{16,32},{24,40},{32,48},{40,56},{48,64},{56,72},{64,... | collective-permute-start | bytes 786440 | tf_op jit(solution)/shard_map/ppermute | solution.py:18
  108.0 3.4 %collective-permute-start.10 = (bf16[2,256,256]{2,1,0:T(8,128)(2,1)S(1)}, bf16[2,256,256]{2,1,0:T(8,128)(2,1)S(1)}, u32[]{:S(2)}, u32[]{:S(2)}) collective-permute-start(bf16[2,256,256]{2,1,0:T(8,128)(2,1)S(1)} %fusion.34), channel_id=1, source_target_pairs={{0,32},{8,40},{16,48},{24,56},{32,64},{40,72},{48,80},{56,88},{64,... | collective-permute-start | bytes 786440 | tf_op jit(solution)/shard_map/ppermute | solution.py:18
  111.4 2.5 collective-permute-start.11
  113.9 3.7 %collective-permute-start.8 = (bf16[2,256,256]{2,1,0:T(8,128)(2,1)S(1)}, bf16[2,256,256]{2,1,0:T(8,128)(2,1)S(1)}, u32[]{:S(2)}, u32[]{:S(2)}) collective-permute-start(bf16[2,256,256]{2,1,0:T(8,128)(2,1)S(1)} %fusion.34), channel_id=1, source_target_pairs={{0,64},{8,72},{16,80},{24,88},{32,96},{40,104},{48,112},{56,120},{... | collective-permute-start | bytes 786440 | tf_op jit(solution)/shard_map/ppermute | solution.py:18
  118.4 5.2 %collective-permute-done.10 = bf16[2,256,256]{2,1,0:T(8,128)(2,1)S(1)} collective-permute-done((bf16[2,256,256]{2,1,0:T(8,128)(2,1)S(1)}, bf16[2,256,256]{2,1,0:T(8,128)(2,1)S(1)}, u32[]{:S(2)}, u32[]{:S(2)}) %collective-permute-start.10) | collective-permute-done | bytes 262176 | tf_op jit(solution)/shard_map/ppermute | solution.py:18
  124.4 6.1 %collective-permute-done.11 = bf16[2,256,256]{2,1,0:T(8,128)(2,1)S(1)} collective-permute-done((bf16[2,256,256]{2,1,0:T(8,128)(2,1)S(1)}, bf16[2,256,256]{2,1,0:T(8,128)(2,1)S(1)}, u32[]{:S(2)}, u32[]{:S(2)}) %collective-permute-start.11) | collective-permute-done | bytes 262176 | tf_op jit(solution)/shard_map/ppermute | solution.py:18
  131.2 5.3 %collective-permute-done.8 = bf16[2,256,256]{2,1,0:T(8,128)(2,1)S(1)} collective-permute-done((bf16[2,256,256]{2,1,0:T(8,128)(2,1)S(1)}, bf16[2,256,256]{2,1,0:T(8,128)(2,1)S(1)}, u32[]{:S(2)}, u32[]{:S(2)}) %collective-permute-start.8) | collective-permute-done | bytes 262176 | tf_op jit(solution)/shard_map/ppermute | solution.py:18
  138.0 1.9 collective-permute-start.12
  140.1 3.0 %collective-permute-done.12 = bf16[5,2,256,256]{3,2,1,0:T(8,128)(2,1)S(1)} collective-permute-done((bf16[5,2,256,256]{3,2,1,0:T(8,128)(2,1)}, bf16[5,2,256,256]{3,2,1,0:T(8,128)(2,1)S(1)}, u32[]{:S(2)}, u32[]{:S(2)}) %collective-permute-start.12) | collective-permute-done | bytes 1310752 | tf_op jit(solution)/shard_map/ppermute | solution.py:130
  144.8 5.8 %fusion.47 = (f32[2,256]{1,0:T(2,128)S(1)}, f32[2,256,2304]{2,1,0:T(8,128)}) fusion(pred[256,2304]{1,0:T(8,128)(4,1)S(1)} %copy-done.2, bf16[2,256,2304]{2,1,0:T(8,128)(2,1)} %copy-done.7, bf16[256,2,64]{0,2,1:T(8,128)(2,1)S(1)} %get-tuple-element.16, bf16[256,2,64]{0,2,1:T(8,128)(2,1)S(1)} %get-tuple-element.15), kind=kOutput, calls=%fused_computation.106 | convolution fusion | flops 308152576 | bytes 7211008 | tf_op jit(solution)/shard_map/sub | solution.py:147
  150.6 3.8 %fusion.20 = bf16[2,128,256]{2,1,0:T(8,128)(2,1)S(1)} fusion(f32[2,256,2304]{2,1,0:T(8,128)} %get-tuple-element.24, f32[2,256]{1,0:T(2,128)S(1)} %get-tuple-element.23, bf16[2,256,2304]{2,1,0:T(8,128)(2,1)} %copy-done.7), kind=kOutput, calls=%fused_computation.36 | convolution fusion | flops 304414720 | bytes 6031360 | tf_op jit(solution)/shard_map/hqk,hdk->qhd/dot_general | solution.py:149
  155.8 6.7 %all-to-all-start.1 = ((bf16[8,256,256]{1,2,0:T(8,128)(2,1)}), bf16[8,256,256]{1,2,0:T(8,128)(2,1)S(1)}, u32[]{:S(2)}, u32[]{:S(2)}) async-start(bf16[8,256,256]{1,2,0:T(8,128)(2,1)} %fusion.14), calls=%async_computation.1 | async-start | bytes 2097152 | tf_op jit(solution)/shard_map/all_to_all | solution.py:30
  162.6 29.0 %all-to-all-done.1 = bf16[8,256,256]{1,2,0:T(8,128)(2,1)S(1)} async-done(((bf16[8,256,256]{1,2,0:T(8,128)(2,1)}), bf16[8,256,256]{1,2,0:T(8,128)(2,1)S(1)}, u32[]{:S(2)}, u32[]{:S(2)}) %all-to-all-start.1) | async-done | bytes 1048608 | tf_op jit(solution)/shard_map/all_to_all | solution.py:30
  192.9 3.7 %all-to-all-start.2 = ((bf16[8,256,256]{2,1,0:T(8,128)(2,1)}), bf16[8,256,256]{2,1,0:T(8,128)(2,1)S(1)}, u32[]{:S(2)}, u32[]{:S(2)}) async-start(bf16[8,256,256]{2,1,0:T(8,128)(2,1)} %broadcast_in_dim.42), calls=%async_computation.2 | async-start | bytes 2097152 | tf_op jit(solution)/shard_map/all_to_all | solution.py:159
  196.7 5.4 %fusion.44 = (bf16[2048,512]{1,0:T(8,128)(2,1)}, bf16[2048,512]{1,0:T(8,128)(2,1)S(1)}, bf16[2048,512]{1,0:T(8,128)(2,1)}) fusion(bf16[2048,1536]{1,0:T(8,128)(2,1)} %all-gather.5.cloned.1.call-done), kind=kLoop, calls=%fused_computation.103 | loop fusion | bytes 12582912 | tf_op jit(solution)/shard_map/slice | solution.py:74
  202.2 21.5 %all-to-all-done.2 = bf16[8,256,256]{2,1,0:T(8,128)(2,1)S(1)} async-done(((bf16[8,256,256]{2,1,0:T(8,128)(2,1)}), bf16[8,256,256]{2,1,0:T(8,128)(2,1)S(1)}, u32[]{:S(2)}, u32[]{:S(2)}) %all-to-all-start.2) | async-done | bytes 1048608 | tf_op jit(solution)/shard_map/all_to_all | solution.py:159
  225.3 1.6 convolution_bitcast_fusion.1
  226.9 4.1 %fusion.13 = bf16[8,256,256]{1,2,0:T(8,128)(2,1)} fusion(bf16[8,256,512]{2,1,0:T(8,128)(2,1)} %bitcast.94, bf16[8,256,512]{2,1,0:T(8,128)(2,1)S(1)} %bitcast.93, f32[256,512]{1,0:T(8,128)} %convolution_bitcast_fusion.1, bf16[8,256,256]{2,1,0:T(8,128)(2,1)S(1)} %all-to-all-done.2, f32[256]{0:T(256)S(1)} %add_rsqrt_fusion, f32[256]{0:T(256)S(1)} %broadcast_multiply_fusion), kind=kOutput, calls=%fused_computation.27 | convolution fusion | flops 1077149696 | bytes 6817792 | tf_op jit(solution)/shard_map/tc,goc->gto/dot_general | solution.py:173
  231.0 4.0 %all-to-all-start.3 = ((bf16[8,256,256]{1,2,0:T(8,128)(2,1)}), bf16[8,256,256]{1,2,0:T(8,128)(2,1)S(1)}, u32[]{:S(2)}, u32[]{:S(2)}) async-start(bf16[8,256,256]{1,2,0:T(8,128)(2,1)} %fusion.13), calls=%async_computation.3 | async-start | bytes 2097152 | tf_op jit(solution)/shard_map/all_to_all | solution.py:30
  236.5 27.3 %all-to-all-done.3 = bf16[8,256,256]{1,2,0:T(8,128)(2,1)S(1)} async-done(((bf16[8,256,256]{1,2,0:T(8,128)(2,1)}), bf16[8,256,256]{1,2,0:T(8,128)(2,1)S(1)}, u32[]{:S(2)}, u32[]{:S(2)}) %all-to-all-start.3) | async-done | bytes 1048608 | tf_op jit(solution)/shard_map/all_to_all | solution.py:30
  (106 shorter events, 23.3 us)
Async XLA Ops:
  7.2 93.5 %all-gather.3.cloned.1.call-start = ((), (), s32[]{:S(2)}) async-start(), calls=%async_computation.4 | async-start | bytes 4259840 | tf_op jit(solution)/shard_map/all_gather | solution.py:77
  8.6 23.2 %collective-permute-start = (s32[256]{0:T(256)}, s32[256]{0:T(256)S(1)}, u32[]{:S(2)}, u32[]{:S(2)}) collective-permute-start(s32[256]{0:T(256)} %param.11), channel_id=1, source_target_pairs={{0,64},{8,72},{16,80},{24,88},{32,96},{40,104},{48,112},{56,120},{... | collective-permute-start | bytes 3080 | tf_op jit(solution)/shard_map/ppermute | solution.py:18
  12.9 22.4 %collective-permute-start.1 = (s32[256]{0:T(256)}, s32[256]{0:T(256)S(1)}, u32[]{:S(2)}, u32[]{:S(2)}) collective-permute-start(s32[256]{0:T(256)} %param.11), channel_id=1, source_target_pairs={{0,56},{8,64},{16,72},{24,80},{32,88},{40,96},{48,104},{56,112},{6... | collective-permute-start | bytes 3080 | tf_op jit(solution)/shard_map/ppermute | solution.py:18
  16.6 21.5 %collective-permute-start.2 = (s32[256]{0:T(256)}, s32[256]{0:T(256)S(1)}, u32[]{:S(2)}, u32[]{:S(2)}) collective-permute-start(s32[256]{0:T(256)} %param.11), channel_id=1, source_target_pairs={{0,48},{8,56},{16,64},{24,72},{32,80},{40,88},{48,96},{56,104},{64... | collective-permute-start | bytes 3080 | tf_op jit(solution)/shard_map/ppermute | solution.py:18
  20.9 20.7 %collective-permute-start.3 = (s32[256]{0:T(256)}, s32[256]{0:T(256)S(1)}, u32[]{:S(2)}, u32[]{:S(2)}) collective-permute-start(s32[256]{0:T(256)} %param.11), channel_id=1, source_target_pairs={{0,40},{8,48},{16,56},{24,64},{32,72},{40,80},{48,88},{56,96},{64,... | collective-permute-start | bytes 3080 | tf_op jit(solution)/shard_map/ppermute | solution.py:18
  27.3 14.4 %collective-permute-start.4 = (s32[256]{0:T(256)}, s32[256]{0:T(256)S(1)}, u32[]{:S(2)}, u32[]{:S(2)}) collective-permute-start(s32[256]{0:T(256)} %param.11), channel_id=1, source_target_pairs={{0,32},{8,40},{16,48},{24,56},{32,64},{40,72},{48,80},{56,88},{64,... | collective-permute-start | bytes 3080 | tf_op jit(solution)/shard_map/ppermute | solution.py:18
  31.8 24.1 %copy-start.4 = (bf16[512,32]{0,1:T(8,128)(2,1)S(1)}, bf16[512,32]{0,1:T(8,128)(2,1)}, u32[]{:S(2)}) copy-start(bf16[512,32]{0,1:T(8,128)(2,1)} %param.19) | copy-start | bytes 98308
  31.8 24.1 %copy-start.5 = (bf16[32,512]{1,0:T(8,128)(2,1)S(1)}, bf16[32,512]{1,0:T(8,128)(2,1)}, u32[]{:S(2)}) copy-start(bf16[32,512]{1,0:T(8,128)(2,1)} %param.18) | copy-start | bytes 98308
  31.8 24.1 %copy-start.6 = (bf16[32,512]{1,0:T(8,128)(2,1)S(1)}, bf16[32,512]{1,0:T(8,128)(2,1)}, u32[]{:S(2)}) copy-start(bf16[32,512]{1,0:T(8,128)(2,1)} %param.17) | copy-start | bytes 98308
  31.9 9.8 %collective-permute-start.5 = (s32[256]{0:T(256)}, s32[256]{0:T(256)S(1)}, u32[]{:S(2)}, u32[]{:S(2)}) collective-permute-start(s32[256]{0:T(256)} %param.11), channel_id=1, source_target_pairs={{0,24},{8,32},{16,40},{24,48},{32,56},{40,64},{48,72},{56,80},{64,... | collective-permute-start | bytes 3080 | tf_op jit(solution)/shard_map/ppermute | solution.py:18
  35.4 6.3 %collective-permute-start.6 = (s32[256]{0:T(256)}, s32[256]{0:T(256)S(1)}, u32[]{:S(2)}, u32[]{:S(2)}) collective-permute-start(s32[256]{0:T(256)} %param.11), channel_id=1, source_target_pairs={{0,16},{8,24},{16,32},{24,40},{32,48},{40,56},{48,64},{56,72},{64,... | collective-permute-start | bytes 3080 | tf_op jit(solution)/shard_map/ppermute | solution.py:18
  38.2 5.1 %collective-permute-start.7 = (s32[256]{0:T(256)}, s32[256]{0:T(256)S(1)}, u32[]{:S(2)}, u32[]{:S(2)}) collective-permute-start(s32[256]{0:T(256)} %param.11), channel_id=1, source_target_pairs={{0,8},{8,16},{16,24},{24,32},{32,40},{40,48},{48,56},{56,64},{64,7... | collective-permute-start | bytes 3080 | tf_op jit(solution)/shard_map/ppermute | solution.py:18
  48.7 35.7 %all-to-all-start = ((bf16[8,256,256]{1,2,0:T(8,128)(2,1)}), bf16[8,256,256]{1,2,0:T(8,128)(2,1)S(1)}, u32[]{:S(2)}, u32[]{:S(2)}) async-start(bf16[8,256,256]{1,2,0:T(8,128)(2,1)} %broadcast_in_dim.38), calls=%async_computation | async-start | bytes 2097152 | tf_op jit(solution)/shard_map/all_to_all | solution.py:25
  55.8 140.9 %all-gather.5.cloned.1.call-start = ((), (), s32[]{:S(2)}) async-start(), calls=%async_computation.5 | async-start | bytes 6389760 | tf_op jit(solution)/shard_map/all_gather | solution.py:72
  104.5 13.1 %collective-permute-start.9 = (bf16[2,256,256]{2,1,0:T(8,128)(2,1)S(1)}, bf16[2,256,256]{2,1,0:T(8,128)(2,1)S(1)}, u32[]{:S(2)}, u32[]{:S(2)}) collective-permute-start(bf16[2,256,256]{2,1,0:T(8,128)(2,1)S(1)} %fusion.34), channel_id=1, source_target_pairs={{0,16},{8,24},{16,32},{24,40},{32,48},{40,56},{48,64},{56,72},{64,... | collective-permute-start | bytes 786440 | tf_op jit(solution)/shard_map/ppermute | solution.py:18
  108.0 15.6 %collective-permute-start.10 = (bf16[2,256,256]{2,1,0:T(8,128)(2,1)S(1)}, bf16[2,256,256]{2,1,0:T(8,128)(2,1)S(1)}, u32[]{:S(2)}, u32[]{:S(2)}) collective-permute-start(bf16[2,256,256]{2,1,0:T(8,128)(2,1)S(1)} %fusion.34), channel_id=1, source_target_pairs={{0,32},{8,40},{16,48},{24,56},{32,64},{40,72},{48,80},{56,88},{64,... | collective-permute-start | bytes 786440 | tf_op jit(solution)/shard_map/ppermute | solution.py:18
  111.4 19.1 %collective-permute-start.11 = (bf16[2,256,256]{2,1,0:T(8,128)(2,1)S(1)}, bf16[2,256,256]{2,1,0:T(8,128)(2,1)S(1)}, u32[]{:S(2)}, u32[]{:S(2)}) collective-permute-start(bf16[2,256,256]{2,1,0:T(8,128)(2,1)S(1)} %fusion.34), channel_id=1, source_target_pairs={{0,48},{8,56},{16,64},{24,72},{32,80},{40,88},{48,96},{56,104},{64... | collective-permute-start | bytes 786440 | tf_op jit(solution)/shard_map/ppermute | solution.py:18
  113.9 22.6 %collective-permute-start.8 = (bf16[2,256,256]{2,1,0:T(8,128)(2,1)S(1)}, bf16[2,256,256]{2,1,0:T(8,128)(2,1)S(1)}, u32[]{:S(2)}, u32[]{:S(2)}) collective-permute-start(bf16[2,256,256]{2,1,0:T(8,128)(2,1)S(1)} %fusion.34), channel_id=1, source_target_pairs={{0,64},{8,72},{16,80},{24,88},{32,96},{40,104},{48,112},{56,120},{... | collective-permute-start | bytes 786440 | tf_op jit(solution)/shard_map/ppermute | solution.py:18
  138.0 5.1 %collective-permute-start.12 = (bf16[5,2,256,256]{3,2,1,0:T(8,128)(2,1)}, bf16[5,2,256,256]{3,2,1,0:T(8,128)(2,1)S(1)}, u32[]{:S(2)}, u32[]{:S(2)}) collective-permute-start(bf16[5,2,256,256]{3,2,1,0:T(8,128)(2,1)} %bitcast_dynamic-update-slice_fusion), channel_id=1, source_target_pairs={{0,8},{8,0},{16,24},{24,16},{32,40},{40,32},{48,56},{56,48},{64,72... | collective-permute-start | bytes 3932168 | tf_op jit(solution)/shard_map/ppermute | solution.py:130
  140.1 4.6 %copy-start.2 = (pred[256,2304]{1,0:T(8,128)(4,1)S(1)}, pred[256,2304]{1,0:T(8,128)(4,1)}, u32[]{:S(2)}) copy-start(pred[256,2304]{1,0:T(8,128)(4,1)} %compare_and_fusion) | copy-start | bytes 1769476
  143.4 1.4 copy-start.7
  150.6 3.8 %slice-start = ((bf16[2048,1024]{1,0:T(8,128)(2,1)}), bf16[2048,256]{1,0:T(8,128)(2,1)S(1)}, s32[]{:S(2)}) async-start(bf16[2048,1024]{1,0:T(8,128)(2,1)} %all-gather.3.cloned.1.call-done), calls=%async_computation.6 | async-start | bytes 2097152 | tf_op jit(solution)/shard_map/slice | solution.py:78
  154.3 8.2 %copy-start.3 = (bf16[256,256]{1,0:T(8,128)(2,1)S(1)}, bf16[256,256]{1,0:T(8,128)(2,1)}, u32[]{:S(2)}) copy-start(bf16[256,256]{1,0:T(8,128)(2,1)} %param.10) | copy-start | bytes 393220
  155.8 35.8 %all-to-all-start.1 = ((bf16[8,256,256]{1,2,0:T(8,128)(2,1)}), bf16[8,256,256]{1,2,0:T(8,128)(2,1)S(1)}, u32[]{:S(2)}, u32[]{:S(2)}) async-start(bf16[8,256,256]{1,2,0:T(8,128)(2,1)} %fusion.14), calls=%async_computation.1 | async-start | bytes 2097152 | tf_op jit(solution)/shard_map/all_to_all | solution.py:30
  192.9 30.7 %all-to-all-start.2 = ((bf16[8,256,256]{2,1,0:T(8,128)(2,1)}), bf16[8,256,256]{2,1,0:T(8,128)(2,1)S(1)}, u32[]{:S(2)}, u32[]{:S(2)}) async-start(bf16[8,256,256]{2,1,0:T(8,128)(2,1)} %broadcast_in_dim.42), calls=%async_computation.2 | async-start | bytes 2097152 | tf_op jit(solution)/shard_map/all_to_all | solution.py:159
  223.7 1.6 copy-start
  231.0 4.0 %copy-start.8 = (s32[16]{0:T(128)S(1)}, s32[16]{0:T(128)}, u32[]{:S(2)}) copy-start(s32[16]{0:T(128)} %param.12) | copy-start | bytes 196
  231.0 32.8 %all-to-all-start.3 = ((bf16[8,256,256]{1,2,0:T(8,128)(2,1)}), bf16[8,256,256]{1,2,0:T(8,128)(2,1)S(1)}, u32[]{:S(2)}, u32[]{:S(2)}) async-start(bf16[8,256,256]{1,2,0:T(8,128)(2,1)} %fusion.13), calls=%async_computation.3 | async-start | bytes 2097152 | tf_op jit(solution)/shard_map/all_to_all | solution.py:30
  236.5 28.2 %copy-start.1 = (bf16[2,16,16,256]{3,2,1,0:T(8,128)(2,1)}, bf16[2,16,16,256]{3,2,1,0:T(8,128)(2,1)S(1)}, u32[]{:S(2)}) copy-start(bf16[2,16,16,256]{3,2,1,0:T(8,128)(2,1)S(1)} %scatter_fusion) | copy-start | bytes 786436
Sparse Core Ops, SparseCore 0:
  11.9 88.6 all-gather.2
  104.6 88.5 all-gather.4
